TPU v7x, 512 devices: a whole 4x8x8 slice. The times are simulated.
512 devices in a mesh: dp: 32 (over y, x), tensor: 16 (over z, core).
Axes of the slice: x: 4, y: 8, z: 8, core: 2. Of those that a mesh axis runs over, the one named last changes fastest.
Arguments:
- patch_rows: bfloat16 [32, 3072, 1792], P('dp', 'tensor'), may hold values from -6 to 6
- send_rows: int32 [32, 16, 32, 6], P('dp', 'tensor'), may hold values from 0 to 192, as said below
- take_rows: int32 [32, 2048], P('dp', 'tensor'), may hold values from 0 to 191, as said below
- segments: int32 [32, 2048], P('dp', 'tensor'), may hold values from 0 to 41, never falling along the last dimension, each value on 1 to 96 neighbouring positions
- norm_gain: float32 [1792], replicated, may hold values from 0.5 to 5
- qkv_weight: bfloat16 [1792, 2688], P('tensor'), may hold values from -0.125 to 0.125
- out_weight: bfloat16 [896, 1792], P('tensor'), may hold values from -0.1875 to 0.1875
- grad_out: bfloat16 [32, 2048, 1792], P('dp', 'tensor'), may hold values from -6 to 6
Outputs:
- layer_out: bfloat16 [32, 2048, 1792], P('dp', 'tensor')
- patch_grad: bfloat16 [32, 3072, 1792], P('dp', 'tensor')
Inputs may be any that keep to these rules, and one draw needn't show every extreme that they name: `send_rows`: for each source device (s, t) the entries below 192 are distinct, 128 in all; for each group they fill slots from 0 on, the rest being 192; some device sends 6 rows to some group. `take_rows`: for each g and t the 128 entries are distinct and name exactly the slots s * 6 + c that hold a row (c below the number of rows that device (s, t) sends to group g). `segments`: along each row the ids never fall and each id covers 1 to 96 positions.
All inputs are finite; a program needn't handle non-finite values.
Results may differ from a plain program's by a relative error of at most 0.009.
The roundings to bfloat16 on the way count: a program that leaves them out, or rounds other values in their place, can miss the bound.
Values may be sent and summed in bfloat16 or wider, within the bound.
No kernel may reach another device: no remote copies, remote signals or barrier semaphores. Data moves between devices by JAX's collectives and lax.ppermute only.
A program may use at most 128 MiB of HBM per device.

v0:
```python
import jax
import jax.numpy as jnp
from jax import lax
from jax.sharding import PartitionSpec as P

HD = 112
HEADS = 8
MOST = 96


def extended(block, sides, width):
    for axis, dim in sides:
        count = lax.axis_size(axis)
        forward = [(i, i + 1) for i in range(count - 1)]
        backward = [(target, source) for source, target in forward]
        low = lax.ppermute(
            lax.slice_in_dim(block, block.shape[dim] - width, None, axis=dim), axis, forward
        )
        high = lax.ppermute(lax.slice_in_dim(block, 0, width, axis=dim), axis, backward)
        block = jnp.concatenate([low, block, high], axis=dim)
    return block


def normalize(rows_in, norm_gain):
    values = rows_in.astype(jnp.float32)
    center = values - jnp.mean(values, axis=-1, keepdims=True)
    inv_dev = lax.rsqrt(jnp.mean(center * center, axis=-1, keepdims=True) + 1e-06)
    unit_rows = center * inv_dev
    return (values, unit_rows, inv_dev, (unit_rows * norm_gain).astype(jnp.bfloat16))


def split_heads(rows_in):
    return rows_in.reshape(rows_in.shape[0], HEADS, HD)


def attend(queries, keyval, seg_query, seg_key):
    all_heads = HEADS * HD
    score_scale = HD ** (-0.5)
    query_heads = split_heads(queries)
    key_heads = split_heads(keyval[:, :all_heads])
    value_heads = split_heads(keyval[:, all_heads:])
    scores = (
        jnp.einsum("qhd,khd->hqk", query_heads, key_heads, preferred_element_type=jnp.float32)
        * score_scale
    )
    same_chart = seg_query[:, None] == seg_key[None, :]
    scores = jnp.where(same_chart[None], scores, -jnp.inf)
    row_max = jnp.max(scores, axis=2, keepdims=True)
    exp_scores = jnp.exp(scores - row_max)
    row_sum = jnp.sum(exp_scores, axis=2, keepdims=True)
    attn_probs = exp_scores / row_sum
    prob_low = attn_probs.astype(jnp.bfloat16)
    attended = jnp.einsum("hqk,khd->qhd", prob_low, value_heads, preferred_element_type=jnp.float32)
    return (
        attn_probs,
        prob_low,
        attended.astype(jnp.bfloat16).reshape(queries.shape[0], all_heads),
        row_max + jnp.log(row_sum),
    )


def local(patch_rows, send_rows, take_rows, segments, norm_gain, qkv_weight, out_weight, grad_out):
    groups = lax.axis_size("dp")
    src_count = patch_rows.shape[1]
    features = patch_rows.shape[2]
    slot_count = send_rows.shape[3]
    own_rows = take_rows.shape[1]
    all_heads = HEADS * HD
    score_scale = HD ** (-0.5)
    patches = patch_rows[0]
    send_flat = send_rows.reshape(groups * slot_count)
    outgoing = jnp.take(patches, send_flat, axis=0, mode="fill", fill_value=0).reshape(
        groups, slot_count, features
    )
    incoming = lax.all_to_all(outgoing, "dp", split_axis=0, concat_axis=0, tiled=True).reshape(
        groups * slot_count, features
    )
    pick_rows = take_rows[0]
    packed = jnp.take(incoming, pick_rows, axis=0)
    full_qkv, full_out = (
        lax.all_gather(qkv_weight, "tensor", axis=0, tiled=True),
        lax.all_gather(out_weight, "tensor", axis=0, tiled=True),
    )
    values, unit_rows, inv_dev, normed = normalize(packed, norm_gain)
    projected = jnp.dot(normed, full_qkv, preferred_element_type=jnp.float32).astype(jnp.bfloat16)
    queries = projected[:, :all_heads]
    keyval = projected[:, all_heads:]
    seg_plus = segments[0] + 1
    wide_kv, wide_seg = (
        extended(keyval, (("tensor", 0),), MOST),
        extended(seg_plus, (("tensor", 0),), MOST),
    )
    attn_probs, prob_low, attended, log_norm = attend(queries, wide_kv, seg_plus, wide_seg)
    layer_out = (values + jnp.dot(attended, full_out, preferred_element_type=jnp.float32)).astype(
        jnp.bfloat16
    )
    grad_rows = grad_out[0]
    grad_att = lax.dot_general(
        grad_rows, full_out, (((1,), (1,)), ((), ())), preferred_element_type=jnp.float32
    ).astype(jnp.bfloat16)
    query_heads = split_heads(queries)
    grad_heads = split_heads(grad_att)
    wide_keys = split_heads(wide_kv[:, :all_heads])
    wide_values = split_heads(wide_kv[:, all_heads:])
    dprobs = jnp.einsum("qhd,khd->hqk", grad_heads, wide_values, preferred_element_type=jnp.float32)
    row_inner = jnp.sum(attn_probs * dprobs, axis=2, keepdims=True)
    dscore = (attn_probs * (dprobs - row_inner) * score_scale).astype(jnp.bfloat16)
    grad_query = jnp.einsum(
        "hqk,khd->qhd", dscore, wide_keys, preferred_element_type=jnp.float32
    ).reshape(own_rows, all_heads)
    window_rows = wide_kv.shape[0]
    grad_key = jnp.einsum("hqk,qhd->khd", dscore, query_heads, preferred_element_type=jnp.float32)
    grad_value = jnp.einsum(
        "hqk,qhd->khd", prob_low, grad_heads, preferred_element_type=jnp.float32
    )
    grad_window = jnp.concatenate(
        [grad_key.reshape(window_rows, all_heads), grad_value.reshape(window_rows, all_heads)],
        axis=1,
    )
    center = grad_window[MOST : MOST + own_rows]
    rim_parts = jnp.concatenate([grad_window[:MOST], grad_window[MOST + own_rows :]], axis=0)
    arrived = extended(rim_parts, (("tensor", 0),), MOST)
    center = center.at[:MOST].add(arrived[:MOST])
    center = center.at[own_rows - MOST :].add(arrived[3 * MOST :])
    grad_proj = jnp.concatenate([grad_query, center], axis=1).astype(jnp.bfloat16)
    grad_normed = lax.dot_general(
        grad_proj, full_qkv, (((1,), (1,)), ((), ())), preferred_element_type=jnp.float32
    )
    scaled = grad_normed * norm_gain
    grad_unit = (
        scaled
        - jnp.mean(scaled, axis=-1, keepdims=True)
        - unit_rows * jnp.mean(scaled * unit_rows, axis=-1, keepdims=True)
    )
    grad_packed = (grad_rows.astype(jnp.float32) + inv_dev * grad_unit).astype(jnp.bfloat16)
    back_slots = (
        jnp.zeros((groups * slot_count, features), jnp.bfloat16).at[pick_rows].set(grad_packed)
    )
    back_slots = back_slots.reshape(groups, slot_count, features)
    returned = lax.all_to_all(back_slots, "dp", split_axis=0, concat_axis=0, tiled=True).reshape(
        groups * slot_count, features
    )
    patch_grad = (
        jnp.zeros((src_count + 1, features), jnp.bfloat16).at[send_flat].add(returned)[:src_count]
    )
    return (layer_out[None], patch_grad[None])


def solution(mesh):
    return jax.shard_map(
        local,
        mesh=mesh,
        in_specs=(
            P("dp", "tensor", None),
            P("dp", "tensor", None, None),
            P("dp", "tensor"),
            P("dp", "tensor"),
            P(),
            P("tensor", None),
            P("tensor", None),
            P("dp", "tensor", None),
        ),
        out_specs=(P("dp", "tensor", None), P("dp", "tensor", None)),
        check_vma=False,
    )
```

profile of v0, /device:TPU:1, one launch (start us, length us, event | category | flops | bytes accessed | tf_op | source)
XLA Modules:
  0.0 227.3 jit_solution(14492804435034020752)
XLA Ops:
  12.9 10.6 %all-to-all-start = ((bf16[32,6,1792]{2,1,0:T(8,128)(2,1)}), bf16[32,6,1792]{2,1,0:T(8,128)(2,1)S(1)}, u32[]{:S(2)}, u32[]{:S(2)}) async-start(bf16[32,6,1792]{2,1,0:T(8,128)(2,1)} %broadcast_select_fusion), calls=%async_computation | async-start | bytes 1835008 | tf_op jit(solution)/shard_map/all_to_all | solution.py:75
  23.6 4.8 %collective-permute-start.2 = (s32[96]{0:T(128)S(1)}, s32[96]{0:T(128)S(1)}, u32[]{:S(2)}, u32[]{:S(2)}) collective-permute-start(s32[96]{0:T(128)S(1)} %get-tuple-element.36), channel_id=1, source_target_pairs={{0,1},{1,2},{2,3},{3,4},{4,5},{5,6},{6,7},{7,8},{8,9},{9,10},{10,1... | collective-permute-start | bytes 1160 | tf_op jit(solution)/shard_map/ppermute | solution.py:16
  30.5 3.3 %collective-permute-done.3 = s32[96]{0:T(128)S(1)} collective-permute-done((s32[96]{0:T(128)S(1)}, s32[96]{0:T(128)S(1)}, u32[]{:S(2)}, u32[]{:S(2)}) %collective-permute-start.3) | collective-permute-done | bytes 416 | tf_op jit(solution)/shard_map/ppermute | solution.py:19
  33.8 13.2 %all-to-all-done = bf16[32,6,1792]{2,1,0:T(8,128)(2,1)S(1)} async-done(((bf16[32,6,1792]{2,1,0:T(8,128)(2,1)}), bf16[32,6,1792]{2,1,0:T(8,128)(2,1)S(1)}, u32[]{:S(2)}, u32[]{:S(2)}) %all-to-all-start) | async-done | bytes 688160 | tf_op jit(solution)/shard_map/all_to_all | solution.py:75
  48.7 32.6 %all-gather.3.cloned.1.call-done = bf16[1792,2688]{1,0:T(8,128)(2,1)} async-done(((bf16[112,2688]{1,0:T(8,128)(2,1)}), bf16[1792,2688]{1,0:T(8,128)(2,1)}) %all-gather.3.cloned.1.call-update) | async-done | bytes 9633808 | tf_op jit(solution)/shard_map/all_gather | solution.py:81
  81.3 5.4 %convolution_convert_fusion = bf16[128,2688]{1,0:T(8,128)(2,1)S(1)} fusion(bf16[1792,2688]{1,0:T(8,128)(2,1)} %all-gather.3.cloned.1.call-done, f32[1792]{0:T(1024)S(1)} %copy-done.10, f32[128]{0:T(128)S(1)} %add_rsqrt_fusion, f32[128]{0:T(128)S(1)} %broadcast_multiply_fusion.2, bf16[128,1792]{1,0:T(8,128)(2,1)S(1)} %gather_fusion.1, ...), kind=kOutput, calls=%fused_computation.6 | convolution fusion | flops 1234845696 | bytes 10788992 | tf_op jit(solution)/shard_map/dot_general | solution.py:85
  89.5 2.4 %collective-permute-start.1 = (bf16[96,1792]{1,0:T(8,128)(2,1)}, bf16[96,1792]{1,0:T(8,128)(2,1)}, u32[]{:S(2)}, u32[]{:S(2)}) collective-permute-start(bf16[96,1792]{1,0:T(8,128)(2,1)} %get-tuple-element.33), channel_id=1, source_target_pairs={{1,0},{2,1},{3,2},{4,3},{5,4},{6,5},{7,6},{8,7},{9,8},{10,9},{11,1... | collective-permute-start | bytes 1032200 | tf_op jit(solution)/shard_map/ppermute | solution.py:19
  92.1 34.0 %all-gather.5.cloned.1.call-done = bf16[896,1792]{1,0:T(8,128)(2,1)} async-done(((bf16[56,1792]{1,0:T(8,128)(2,1)}), bf16[896,1792]{1,0:T(8,128)(2,1)}) %all-gather.5.cloned.1.call-update) | async-done | bytes 3211280 | tf_op jit(solution)/shard_map/all_gather | solution.py:82
  126.0 3.0 %convolution_convert_fusion.1 = bf16[128,896]{1,0:T(8,128)(2,1)S(1)} fusion(bf16[896,1792]{1,0:T(8,128)(2,1)} %all-gather.5.cloned.1.call-done, bf16[1,128,1792]{2,1,0:T(8,128)(2,1)S(1)} %copy-done.4), kind=kOutput, calls=%fused_computation.28 | convolution fusion | flops 411156480 | bytes 3899392 | tf_op jit(solution)/shard_map/dot_general | solution.py:98
  134.0 3.2 %fusion.98 = (f32[8,128]{1,0:T(8,128)S(1)}, f32[8,128,320]{1,2,0:T(8,128)}) fusion(pred[128,320]{0,1:T(8,128)(4,1)S(1)} %broadcast_compare_fusion, bf16[128,8,112]{0,2,1:T(8,128)(2,1)} %bitcast.59, bf16[320,8,112]{2,1,0:T(8,128)(2,1)} %reshape.258), kind=kOutput, calls=%fused_computation.111 | convolution fusion | flops 74711360 | bytes 2158592 | tf_op jit(solution)/shard_map/sub | solution.py:49
  137.3 3.0 %convolution_bitcast_fusion = f32[320,8,112]{2,0,1:T(8,128)} fusion(bf16[128,8,112]{0,2,1:T(8,128)(2,1)S(1)} %bitcast.58, f32[8,128]{1,0:T(8,128)S(1)} %get-tuple-element.40, pred[128,320]{0,1:T(8,128)(4,1)S(1)} %broadcast_compare_fusion, bf16[128,8,112]{0,2,1:T(8,128)(2,1)} %bitcast.60, bf16[320,8,112]{2,1,0:T(8,128)(2,1)} %reshape.258), kind=kOutput, calls=%fused_computation.17 | convolution fusion | flops 148440384 | bytes 2224128 | tf_op jit(solution)/shard_map/hqk,qhd->khd/dot_general | solution.py:113
  140.3 3.4 %convolution_bitcast_fusion.1 = f32[320,8,112]{2,0,1:T(8,128)} fusion(bf16[128,8,112]{0,2,1:T(8,128)(2,1)S(1)} %bitcast.61, f32[8,128,320]{1,2,0:T(8,128)S(1)} %fusion.41, f32[8,128,320]{1,2,0:T(8,128)} %get-tuple-element.41, f32[8,128]{1,0:T(8,128)S(1)} %get-tuple-element.40), kind=kOutput, calls=%fused_computation.18 | convolution fusion | flops 75695424 | bytes 4001792 | tf_op jit(solution)/shard_map/hqk,qhd->khd/dot_general | solution.py:112
  143.7 2.1 copy.28
  147.2 2.1 copy.29
  153.6 3.4 %collective-permute-start.4 = (f32[96,1792]{1,0:T(8,128)}, f32[96,1792]{1,0:T(8,128)}, u32[]{:S(2)}, u32[]{:S(2)}) collective-permute-start(f32[96,1792]{1,0:T(8,128)} %get-tuple-element.29), channel_id=1, source_target_pairs={{0,1},{1,2},{2,3},{3,4},{4,5},{5,6},{6,7},{7,8},{8,9},{9,10},{10,1... | collective-permute-start | bytes 2064392 | tf_op jit(solution)/shard_map/ppermute | solution.py:16
  159.9 4.3 %fusion.17 = bf16[8,112,128]{2,1,0:T(8,128)(2,1)} fusion(f32[8,128,320]{1,2,0:T(8,128)} %copy-done.6, bf16[320,8,112]{2,1,0:T(8,128)(2,1)} %reshape.258, f32[8,128,320]{1,2,0:T(8,128)} %get-tuple-element.41, f32[8,128]{1,0:T(8,128)S(1)} %get-tuple-element.40), kind=kOutput, calls=%fused_computation.27 | convolution fusion | flops 75810112 | bytes 3428352 | tf_op jit(solution)/shard_map/hqk,khd->qhd/dot_general | solution.py:108
  166.0 2.0 fusion.33
  168.1 2.5 %collective-permute-done.5 = f32[96,1792]{1,0:T(8,128)} collective-permute-done((f32[96,1792]{1,0:T(8,128)}, f32[96,1792]{1,0:T(8,128)}, u32[]{:S(2)}, u32[]{:S(2)}) %collective-permute-start.5) | collective-permute-done | bytes 688160 | tf_op jit(solution)/shard_map/ppermute | solution.py:19
  170.6 2.3 fusion.32
  174.1 6.6 %fusion.94 = (f32[128]{0:T(128)S(1)}, f32[128]{0:T(128)S(1)}, f32[128,1792]{1,0:T(8,128)S(1)}) fusion(f32[128]{0:T(128)S(1)} %add_rsqrt_fusion, f32[128]{0:T(128)S(1)} %broadcast_multiply_fusion.2, bf16[128,1792]{1,0:T(8,128)(2,1)S(1)} %gather_fusion.1, pred[128]{0:T(512)(128)(4,1)S(1)} %compare_and_fusion.1, f32[1792]{0:T(1024)S(1)} %copy-done.10, ...), kind=kOutput, calls=%fused_computation.107 | convolution fusion | flops 1236336384 | bytes 11707520 | tf_op jit(solution)/shard_map/dot_general | solution.py:126
  183.8 9.4 %all-to-all-start.1 = ((bf16[32,6,1792]{2,1,0:T(8,128)(2,1)}), bf16[32,6,1792]{2,1,0:T(8,128)(2,1)S(1)}, u32[]{:S(2)}, u32[]{:S(2)}) async-start(bf16[32,6,1792]{2,1,0:T(8,128)(2,1)} %reshape.264), calls=%async_computation.1 | async-start | bytes 1835008 | tf_op jit(solution)/shard_map/all_to_all | solution.py:140
  195.2 3.3 %fusion.3 = bf16[1,128,1792]{2,1,0:T(8,128)(2,1)} fusion(bf16[128,896]{0,1:T(8,128)(2,1)S(1)} %bitcast.64, bf16[896,1792]{1,0:T(8,128)(2,1)} %all-gather.5.cloned.1.call-done, bf16[128,1792]{1,0:T(8,128)(2,1)S(1)} %gather_fusion.1, pred[128]{0:T(512)(128)(4,1)S(1)} %compare_and_fusion.1), kind=kOutput, calls=%fused_computation.10 | convolution fusion | flops 411959296 | bytes 4358272 | tf_op jit(solution)/shard_map/dot_general | solution.py:94
  198.5 17.8 %all-to-all-done.1 = bf16[32,6,1792]{2,1,0:T(8,128)(2,1)S(1)} async-done(((bf16[32,6,1792]{2,1,0:T(8,128)(2,1)}), bf16[32,6,1792]{2,1,0:T(8,128)(2,1)S(1)}, u32[]{:S(2)}, u32[]{:S(2)}) %all-to-all-start.1) | async-done | bytes 688160 | tf_op jit(solution)/shard_map/all_to_all | solution.py:140
  216.5 3.1 %scatter_custom_fusion.1 = bf16[193,1792]{1,0:T(8,128)(2,1)S(1)} fusion(s32[192]{0:T(256)S(1)} %bitcast.66, bf16[192,1792]{1,0:T(8,128)(2,1)S(1)} %reshape.294, bf16[]{:T(256)} %constant.97.clone.1), kind=kCustom, calls=%fused_computation.73 | custom fusion | flops 344064 | bytes 691714 | tf_op jit(solution)/shard_map/scatter-add | solution.py:144
  (83 shorter events, 35.1 us)
Async XLA Ops:
  7.2 3.2 %copy-start = (bf16[1,192,1792]{2,1,0:T(8,128)(2,1)S(1)}, bf16[1,192,1792]{2,1,0:T(8,128)(2,1)}, u32[]{:S(2)}) copy-start(bf16[1,192,1792]{2,1,0:T(8,128)(2,1)} %param.12) | copy-start | bytes 2064388
  7.2 74.1 %all-gather.3.cloned.1.call-start = ((), (), s32[]{:S(2)}) async-start(), calls=%async_computation.2 | async-start | bytes 10235904 | tf_op jit(solution)/shard_map/all_gather | solution.py:81
  7.9 118.1 %all-gather.5.cloned.1.call-start = ((), (), s32[]{:S(2)}) async-start(), calls=%async_computation.3 | async-start | bytes 3411968 | tf_op jit(solution)/shard_map/all_gather | solution.py:82
  12.9 10.6 %copy-start.11 = (s32[1,128]{1,0:T(1,128)S(1)}, s32[1,128]{1,0:T(1,128)}, u32[]{:S(2)}) copy-start(s32[1,128]{1,0:T(1,128)} %param.15) | copy-start | bytes 1540
  12.9 17.5 %copy-start.12 = (s32[1,128]{1,0:T(1,128)S(1)}, s32[1,128]{1,0:T(1,128)}, u32[]{:S(2)}) copy-start(s32[1,128]{1,0:T(1,128)} %param.14) | copy-start | bytes 1540
  12.9 34.1 %all-to-all-start = ((bf16[32,6,1792]{2,1,0:T(8,128)(2,1)}), bf16[32,6,1792]{2,1,0:T(8,128)(2,1)S(1)}, u32[]{:S(2)}, u32[]{:S(2)}) async-start(bf16[32,6,1792]{2,1,0:T(8,128)(2,1)} %broadcast_select_fusion), calls=%async_computation | async-start | bytes 1835008 | tf_op jit(solution)/shard_map/all_to_all | solution.py:75
  23.6 6.8 %collective-permute-start.2 = (s32[96]{0:T(128)S(1)}, s32[96]{0:T(128)S(1)}, u32[]{:S(2)}, u32[]{:S(2)}) collective-permute-start(s32[96]{0:T(128)S(1)} %get-tuple-element.36), channel_id=1, source_target_pairs={{0,1},{1,2},{2,3},{3,4},{4,5},{5,6},{6,7},{7,8},{8,9},{9,10},{10,1... | collective-permute-start | bytes 1160 | tf_op jit(solution)/shard_map/ppermute | solution.py:16
  28.5 5.3 %collective-permute-start.3 = (s32[96]{0:T(128)S(1)}, s32[96]{0:T(128)S(1)}, u32[]{:S(2)}, u32[]{:S(2)}) collective-permute-start(s32[96]{0:T(128)S(1)} %get-tuple-element.37), channel_id=1, source_target_pairs={{1,0},{2,1},{3,2},{4,3},{5,4},{6,5},{7,6},{8,7},{9,8},{10,9},{11,1... | collective-permute-start | bytes 1160 | tf_op jit(solution)/shard_map/ppermute | solution.py:19
  47.2 34.1 %copy-start.10 = (f32[1792]{0:T(1024)S(1)}, f32[1792]{0:T(1024)}, u32[]{:S(2)}) copy-start(f32[1792]{0:T(1024)} %param.16) | copy-start | bytes 21508
  86.7 39.3 %copy-start.4 = (bf16[1,128,1792]{2,1,0:T(8,128)(2,1)S(1)}, bf16[1,128,1792]{2,1,0:T(8,128)(2,1)}, u32[]{:S(2)}) copy-start(bf16[1,128,1792]{2,1,0:T(8,128)(2,1)} %param.19) | copy-start | bytes 1376260
  87.6 42.6 %collective-permute-start = (bf16[96,1792]{1,0:T(8,128)(2,1)}, bf16[96,1792]{1,0:T(8,128)(2,1)S(1)}, u32[]{:S(2)}, u32[]{:S(2)}) collective-permute-start(bf16[96,1792]{1,0:T(8,128)(2,1)} %get-tuple-element.32), channel_id=1, source_target_pairs={{0,1},{1,2},{2,3},{3,4},{4,5},{5,6},{6,7},{7,8},{8,9},{9,10},{10,1... | collective-permute-start | bytes 1032200 | tf_op jit(solution)/shard_map/ppermute | solution.py:16
  89.5 40.6 %collective-permute-start.1 = (bf16[96,1792]{1,0:T(8,128)(2,1)}, bf16[96,1792]{1,0:T(8,128)(2,1)}, u32[]{:S(2)}, u32[]{:S(2)}) collective-permute-start(bf16[96,1792]{1,0:T(8,128)(2,1)} %get-tuple-element.33), channel_id=1, source_target_pairs={{1,0},{2,1},{3,2},{4,3},{5,4},{6,5},{7,6},{8,7},{9,8},{10,9},{11,1... | collective-permute-start | bytes 1032200 | tf_op jit(solution)/shard_map/ppermute | solution.py:19
  133.7 3.6 %copy-start.2 = (bf16[320,8,112]{2,1,0:T(8,128)(2,1)}, bf16[320,8,112]{2,1,0:T(8,128)(2,1)S(1)}, u32[]{:S(2)}) copy-start(bf16[320,8,112]{2,1,0:T(8,128)(2,1)S(1)} %reshape.256) | copy-start | bytes 1720324
  134.0 6.3 %copy-start.6 = (f32[8,128,320]{1,2,0:T(8,128)}, f32[8,128,320]{1,2,0:T(8,128)S(1)}, u32[]{:S(2)}) copy-start(f32[8,128,320]{1,2,0:T(8,128)S(1)} %fusion.41) | copy-start | bytes 3932164
  137.3 3.0 %copy-start.7 = (bf16[128,896]{0,1:T(8,128)(2,1)S(1)}, bf16[128,896]{0,1:T(8,128)(2,1)}, u32[]{:S(2)}) copy-start(bf16[128,896]{0,1:T(8,128)(2,1)} %copy.22) | copy-start | bytes 688132
  150.7 1.6 copy-start.1
  153.6 12.5 %collective-permute-start.4 = (f32[96,1792]{1,0:T(8,128)}, f32[96,1792]{1,0:T(8,128)}, u32[]{:S(2)}, u32[]{:S(2)}) collective-permute-start(f32[96,1792]{1,0:T(8,128)} %get-tuple-element.29), channel_id=1, source_target_pairs={{0,1},{1,2},{2,3},{3,4},{4,5},{5,6},{6,7},{7,8},{8,9},{9,10},{10,1... | collective-permute-start | bytes 2064392 | tf_op jit(solution)/shard_map/ppermute | solution.py:16
  158.0 12.6 %collective-permute-start.5 = (f32[96,1792]{1,0:T(8,128)}, f32[96,1792]{1,0:T(8,128)}, u32[]{:S(2)}, u32[]{:S(2)}) collective-permute-start(f32[96,1792]{1,0:T(8,128)} %get-tuple-element.28), channel_id=1, source_target_pairs={{1,0},{2,1},{3,2},{4,3},{5,4},{6,5},{7,6},{8,7},{9,8},{10,9},{11,1... | collective-permute-start | bytes 2064392 | tf_op jit(solution)/shard_map/ppermute | solution.py:19
  168.1 6.0 %copy-start.9 = (bf16[128,896]{1,0:T(8,128)(2,1)S(1)}, bf16[128,896]{1,0:T(8,128)(2,1)}, u32[]{:S(2)}) copy-start(bf16[128,896]{1,0:T(8,128)(2,1)} %copy.30) | copy-start | bytes 688132
  174.1 6.7 %copy-start.5 = (bf16[1,128,1792]{2,1,0:T(8,128)(2,1)S(1)}, bf16[1,128,1792]{2,1,0:T(8,128)(2,1)}, u32[]{:S(2)}) copy-start(bf16[1,128,1792]{2,1,0:T(8,128)(2,1)} %param.19) | copy-start | bytes 1376260
  183.8 9.4 %copy-start.3 = (bf16[320,8,112]{2,1,0:T(8,128)(2,1)S(1)}, bf16[320,8,112]{2,1,0:T(8,128)(2,1)}, u32[]{:S(2)}) copy-start(bf16[320,8,112]{2,1,0:T(8,128)(2,1)} %copy-done.2) | copy-start | bytes 1720324
  183.8 9.4 %copy-start.8 = (bf16[128,896]{0,1:T(8,128)(2,1)S(1)}, bf16[128,896]{0,1:T(8,128)(2,1)}, u32[]{:S(2)}) copy-start(bf16[128,896]{0,1:T(8,128)(2,1)} %copy.22) | copy-start | bytes 688132
  183.8 32.5 %all-to-all-start.1 = ((bf16[32,6,1792]{2,1,0:T(8,128)(2,1)}), bf16[32,6,1792]{2,1,0:T(8,128)(2,1)S(1)}, u32[]{:S(2)}, u32[]{:S(2)}) async-start(bf16[32,6,1792]{2,1,0:T(8,128)(2,1)} %reshape.264), calls=%async_computation.1 | async-start | bytes 1835008 | tf_op jit(solution)/shard_map/all_to_all | solution.py:140
Sparse Core Ops, SparseCore 0:
  10.1 71.1 all-gather.2
  83.4 42.5 all-gather.4
where the time goes:
time: 228 us; the launch traced here: 227 us
  waiting for transfers between devices  105 us (46%)
  starting transfers between devices  36.5 us (16%)
  matrix products  34.7 us (15%)
  local copies, waits for them, and re-layouts  23 us (10%)
  between operations  14.4 us (6%)
  other arithmetic  14.2 us (6%)
    all_gather x1, waiting for transfers between devices, local(): lax.all_gather(out_weight, 'tensor', axis=0, tiled=True)  34 us
    all_gather x1, waiting for transfers between devices, local(): lax.all_gather(qkv_weight, 'tensor', axis=0, tiled=True)  32.6 us
    all_to_all x1, waiting for transfers between devices, local(): lax.all_to_all(back_slots, 'dp', split_axis=0, concat_axis=0, tiled=True)  17.8 us
    all_to_all x1, waiting for transfers between devices, local(): lax.all_to_all(outgoing, 'dp', split_axis=0, concat_axis=0, tiled=True)  13.2 us
    all_to_all x1, starting transfers between devices, local(): lax.all_to_all(outgoing, 'dp', split_axis=0, concat_axis=0, tiled=True)  10.6 us
    ppermute x3, starting transfers between devices, extended(): lax.ppermute(lax.slice_in_dim(block, block.shape[dim] - width, None, axis...  10.1 us
    all_to_all x1, starting transfers between devices, local(): lax.all_to_all(back_slots, 'dp', split_axis=0, concat_axis=0, tiled=True)  9.4 us
    dot_general x1, matrix products, local(): lax.dot_general(grad_proj, full_qkv, (((1,), (1,)), ((), ())), preferred_...  6.63 us
  transfers between devices with their start and end apart: 10, of which 6 were waited for; matrix products, arithmetic and copies ran while one was open for 14% of the time, Pallas kernels for 0%

commit v1 on v0

--- a/solution.py
+++ b/solution.py
@@ -1,7 +1,7 @@
 import jax
 import jax.numpy as jnp
 from jax import lax
-from jax.sharding import PartitionSpec as P
+from jax.sharding import Mesh, PartitionSpec as P
 
 HD = 112
 HEADS = 8
@@ -19,6 +19,15 @@
         high = lax.ppermute(lax.slice_in_dim(block, 0, width, axis=dim), axis, backward)
         block = jnp.concatenate([low, block, high], axis=dim)
     return block
+
+
+TENSOR = ("z", "c")
+
+
+def gather_rows(block):
+    along_z = lax.all_gather(block, "z", axis=0, tiled=False)
+    both = lax.all_gather(along_z, "c", axis=1, tiled=False)
+    return both.reshape(-1, block.shape[1])
 
 
 def normalize(rows_in, norm_gain):
@@ -77,18 +86,15 @@
     )
     pick_rows = take_rows[0]
     packed = jnp.take(incoming, pick_rows, axis=0)
-    full_qkv, full_out = (
-        lax.all_gather(qkv_weight, "tensor", axis=0, tiled=True),
-        lax.all_gather(out_weight, "tensor", axis=0, tiled=True),
-    )
+    full_qkv, full_out = (gather_rows(qkv_weight), gather_rows(out_weight))
     values, unit_rows, inv_dev, normed = normalize(packed, norm_gain)
     projected = jnp.dot(normed, full_qkv, preferred_element_type=jnp.float32).astype(jnp.bfloat16)
     queries = projected[:, :all_heads]
     keyval = projected[:, all_heads:]
     seg_plus = segments[0] + 1
     wide_kv, wide_seg = (
-        extended(keyval, (("tensor", 0),), MOST),
-        extended(seg_plus, (("tensor", 0),), MOST),
+        extended(keyval, ((TENSOR, 0),), MOST),
+        extended(seg_plus, ((TENSOR, 0),), MOST),
     )
     attn_probs, prob_low, attended, log_norm = attend(queries, wide_kv, seg_plus, wide_seg)
     layer_out = (values + jnp.dot(attended, full_out, preferred_element_type=jnp.float32)).astype(
@@ -119,7 +125,7 @@
     )
     center = grad_window[MOST : MOST + own_rows]
     rim_parts = jnp.concatenate([grad_window[:MOST], grad_window[MOST + own_rows :]], axis=0)
-    arrived = extended(rim_parts, (("tensor", 0),), MOST)
+    arrived = extended(rim_parts, ((TENSOR, 0),), MOST)
     center = center.at[:MOST].add(arrived[:MOST])
     center = center.at[own_rows - MOST :].add(arrived[3 * MOST :])
     grad_proj = jnp.concatenate([grad_query, center], axis=1).astype(jnp.bfloat16)
@@ -147,19 +153,23 @@
 
 
 def solution(mesh):
+    cores = 2
+    split = Mesh(
+        mesh.devices.reshape(mesh.devices.shape[0], -1, cores), ("dp", "z", "c")
+    )
     return jax.shard_map(
         local,
-        mesh=mesh,
+        mesh=split,
         in_specs=(
-            P("dp", "tensor", None),
-            P("dp", "tensor", None, None),
-            P("dp", "tensor"),
-            P("dp", "tensor"),
+            P("dp", TENSOR, None),
+            P("dp", TENSOR, None, None),
+            P("dp", TENSOR),
+            P("dp", TENSOR),
             P(),
-            P("tensor", None),
-            P("tensor", None),
-            P("dp", "tensor", None),
+            P(TENSOR, None),
+            P(TENSOR, None),
+            P("dp", TENSOR, None),
         ),
-        out_specs=(P("dp", "tensor", None), P("dp", "tensor", None)),
+        out_specs=(P("dp", TENSOR, None), P("dp", TENSOR, None)),
         check_vma=False,
     )

time: 228 us -> 280 us (1.23)
  the two profiles are of different devices: /device:TPU:1 before, /device:TPU:66 now
where the time goes in v1:
time: 280 us; the launch traced here: 278 us
  waiting for transfers between devices  156 us (56%)
  starting transfers between devices  37 us (13%)
  matrix products  34.3 us (12%)
  local copies, waits for them, and re-layouts  23 us (8%)
  between operations  14.2 us (5%)
  other arithmetic  13.4 us (5%)
    all_gather x2, waiting for transfers between devices, gather_rows(): along_z = lax.all_gather(block, 'z', axis=0, tiled=False)  98.9 us
    all_gather x2, waiting for transfers between devices, gather_rows(): both = lax.all_gather(along_z, 'c', axis=1, tiled=False)  33.2 us
    all_to_all x1, waiting for transfers between devices, local(): lax.all_to_all(back_slots, 'dp', split_axis=0, concat_axis=0, tiled=True)  20.4 us
    ppermute x3, starting transfers between devices, extended(): lax.ppermute(lax.slice_in_dim(block, 0, width, axis=dim), axis, backward)  10.3 us
    all_to_all x1, starting transfers between devices, local(): lax.all_to_all(outgoing, 'dp', split_axis=0, concat_axis=0, tiled=True)  10 us
    all_to_all x1, starting transfers between devices, local(): lax.all_to_all(back_slots, 'dp', split_axis=0, concat_axis=0, tiled=True)  10 us
    dot_general x1, matrix products, local(): lax.dot_general(grad_proj, full_qkv, (((1,), (1,)), ((), ())), preferred_...  6.61 us
    ppermute x3, starting transfers between devices, extended(): lax.ppermute(lax.slice_in_dim(block, block.shape[dim] - width, None, axis...  6.48 us
  transfers between devices with their start and end apart: 12, of which 8 were waited for; matrix products, arithmetic and copies ran while one was open for 11% of the time, Pallas kernels for 0%

profile of v1, /device:TPU:66, one launch (start us, length us, event | category | flops | bytes accessed | tf_op | source)
XLA Modules:
  0.0 277.8 jit_solution(679922066373219123)
XLA Ops:
  8.7 67.1 %all-gather.9.cloned.1.call-done = bf16[896,2688]{1,0:T(8,128)(2,1)} async-done(((bf16[112,2688]{1,0:T(8,128)(2,1)}), bf16[896,2688]{1,0:T(8,128)(2,1)}) %all-gather.9.cloned.1.call-update) | async-done | bytes 4816912 | tf_op jit(solution)/shard_map/all_gather | solution.py:28
  79.3 10.0 %all-to-all-start = ((bf16[32,6,1792]{2,1,0:T(8,128)(2,1)}), bf16[32,6,1792]{2,1,0:T(8,128)(2,1)S(1)}, u32[]{:S(2)}, u32[]{:S(2)}) async-start(bf16[32,6,1792]{2,1,0:T(8,128)(2,1)} %broadcast_select_fusion), calls=%async_computation | async-start | bytes 1835008 | tf_op jit(solution)/shard_map/all_to_all | solution.py:84
  89.4 31.8 %all-gather.13.cloned.1.call-done = bf16[448,1792]{1,0:T(8,128)(2,1)} async-done(((bf16[56,1792]{1,0:T(8,128)(2,1)}), bf16[448,1792]{1,0:T(8,128)(2,1)}) %all-gather.13.cloned.1.call-update) | async-done | bytes 1605648 | tf_op jit(solution)/shard_map/all_gather | solution.py:28
  123.2 3.6 %collective-permute-start.3 = (s32[96]{0:T(128)S(1)}, s32[96]{0:T(128)S(1)}, u32[]{:S(2)}, u32[]{:S(2)}) collective-permute-start(s32[96]{0:T(128)S(1)} %get-tuple-element.37), channel_id=1, source_target_pairs={{1,0},{2,1},{3,2},{4,3},{5,4},{6,5},{7,6},{8,7},{9,8},{10,9},{11,1... | collective-permute-start | bytes 1160 | tf_op jit(solution)/shard_map/ppermute | solution.py:19
  129.9 21.6 %all-gather.11.cloned.1.call-done = bf16[8,224,2688]{2,1,0:T(8,128)(2,1)} async-done(((bf16[8,112,2688]{2,1,0:T(8,128)(2,1)}), bf16[8,224,2688]{2,1,0:T(8,128)(2,1)}) %all-gather.11.cloned.1.call-update) | async-done | bytes 9633808 | tf_op jit(solution)/shard_map/all_gather | solution.py:29
  151.5 5.4 %convolution_convert_fusion = bf16[128,2688]{1,0:T(8,128)(2,1)S(1)} fusion(bf16[1792,2688]{1,0:T(8,128)(2,1)} %bitcast.75, f32[1792]{0:T(1024)S(1)} %copy-done.11, f32[128]{0:T(128)S(1)} %add_rsqrt_fusion, f32[128]{0:T(128)S(1)} %broadcast_multiply_fusion.2, bf16[128,1792]{1,0:T(8,128)(2,1)S(1)} %gather_fusion.1, pred[128]{0:T(512)(128)(4,1)S(1)} %compare_and_fusion.1), kind=kOutput, calls=%fused_computation.6 | convolution fusion | flops 1234845696 | bytes 10788992 | tf_op jit(solution)/shard_map/dot_general | solution.py:91
  157.8 2.2 collective-permute-start
  160.0 3.4 %collective-permute-start.1 = (bf16[96,1792]{1,0:T(8,128)(2,1)}, bf16[96,1792]{1,0:T(8,128)(2,1)}, u32[]{:S(2)}, u32[]{:S(2)}) collective-permute-start(bf16[96,1792]{1,0:T(8,128)(2,1)} %get-tuple-element.33), channel_id=1, source_target_pairs={{1,0},{2,1},{3,2},{4,3},{5,4},{6,5},{7,6},{8,7},{9,8},{10,9},{11,1... | collective-permute-start | bytes 1032200 | tf_op jit(solution)/shard_map/ppermute | solution.py:19
  163.5 11.6 %all-gather.15.cloned.1.call-done = bf16[8,112,1792]{2,1,0:T(8,128)(2,1)} async-done(((bf16[8,56,1792]{2,1,0:T(8,128)(2,1)}), bf16[8,112,1792]{2,1,0:T(8,128)(2,1)}) %all-gather.15.cloned.1.call-update) | async-done | bytes 3211280 | tf_op jit(solution)/shard_map/all_gather | solution.py:29
  175.1 3.0 %convolution_convert_fusion.1 = bf16[128,896]{1,0:T(8,128)(2,1)S(1)} fusion(bf16[896,1792]{1,0:T(8,128)(2,1)} %bitcast.61, bf16[1,128,1792]{2,1,0:T(8,128)(2,1)S(1)} %copy-done.4), kind=kOutput, calls=%fused_computation.28 | convolution fusion | flops 411156480 | bytes 3899392 | tf_op jit(solution)/shard_map/dot_general | solution.py:104
  183.1 3.2 %fusion.98 = (f32[8,128]{1,0:T(8,128)S(1)}, f32[8,128,320]{1,2,0:T(8,128)}) fusion(pred[128,320]{0,1:T(8,128)(4,1)S(1)} %broadcast_compare_fusion, bf16[128,8,112]{0,2,1:T(8,128)(2,1)} %bitcast.67, bf16[320,8,112]{2,1,0:T(8,128)(2,1)} %reshape.265), kind=kOutput, calls=%fused_computation.111 | convolution fusion | flops 74711360 | bytes 2158592 | tf_op jit(solution)/shard_map/sub | solution.py:58
  186.3 3.0 %convolution_bitcast_fusion = f32[320,8,112]{2,0,1:T(8,128)} fusion(bf16[128,8,112]{0,2,1:T(8,128)(2,1)S(1)} %bitcast.66, f32[8,128]{1,0:T(8,128)S(1)} %get-tuple-element.40, pred[128,320]{0,1:T(8,128)(4,1)S(1)} %broadcast_compare_fusion, bf16[128,8,112]{0,2,1:T(8,128)(2,1)} %bitcast.68, bf16[320,8,112]{2,1,0:T(8,128)(2,1)} %reshape.265), kind=kOutput, calls=%fused_computation.17 | convolution fusion | flops 148440384 | bytes 2224128 | tf_op jit(solution)/shard_map/hqk,qhd->khd/dot_general | solution.py:119
  189.4 3.3 %convolution_bitcast_fusion.1 = f32[320,8,112]{2,0,1:T(8,128)} fusion(bf16[128,8,112]{0,2,1:T(8,128)(2,1)S(1)} %bitcast.69, f32[8,128,320]{1,2,0:T(8,128)S(1)} %fusion.41, f32[8,128,320]{1,2,0:T(8,128)} %get-tuple-element.41, f32[8,128]{1,0:T(8,128)S(1)} %get-tuple-element.40), kind=kOutput, calls=%fused_computation.18 | convolution fusion | flops 75695424 | bytes 4001792 | tf_op jit(solution)/shard_map/hqk,qhd->khd/dot_general | solution.py:118
  192.7 2.1 copy.28
  196.2 2.1 copy.29
  202.6 2.4 collective-permute-start.4
  206.0 3.3 %collective-permute-start.5 = (f32[96,1792]{1,0:T(8,128)}, f32[96,1792]{1,0:T(8,128)}, u32[]{:S(2)}, u32[]{:S(2)}) collective-permute-start(f32[96,1792]{1,0:T(8,128)} %get-tuple-element.28), channel_id=1, source_target_pairs={{1,0},{2,1},{3,2},{4,3},{5,4},{6,5},{7,6},{8,7},{9,8},{10,9},{11,1... | collective-permute-start | bytes 2064392 | tf_op jit(solution)/shard_map/ppermute | solution.py:19
  209.3 4.1 %fusion.17 = bf16[8,112,128]{2,1,0:T(8,128)(2,1)} fusion(f32[8,128,320]{1,2,0:T(8,128)} %copy-done.6, bf16[320,8,112]{2,1,0:T(8,128)(2,1)} %reshape.265, f32[8,128,320]{1,2,0:T(8,128)} %get-tuple-element.41, f32[8,128]{1,0:T(8,128)S(1)} %get-tuple-element.40), kind=kOutput, calls=%fused_computation.27 | convolution fusion | flops 75810112 | bytes 3428352 | tf_op jit(solution)/shard_map/hqk,khd->qhd/dot_general | solution.py:114
  218.1 2.2 fusion.32
  221.6 6.6 %fusion.94 = (f32[128]{0:T(128)S(1)}, f32[128]{0:T(128)S(1)}, f32[128,1792]{1,0:T(8,128)S(1)}) fusion(f32[128]{0:T(128)S(1)} %add_rsqrt_fusion, f32[128]{0:T(128)S(1)} %broadcast_multiply_fusion.2, bf16[128,1792]{1,0:T(8,128)(2,1)S(1)} %gather_fusion.1, pred[128]{0:T(512)(128)(4,1)S(1)} %compare_and_fusion.1, f32[1792]{0:T(1024)S(1)} %copy-done.11, ...), kind=kOutput, calls=%fused_computation.107 | convolution fusion | flops 1236336384 | bytes 11707520 | tf_op jit(solution)/shard_map/dot_general | solution.py:132
  231.3 10.0 %all-to-all-start.1 = ((bf16[32,6,1792]{2,1,0:T(8,128)(2,1)}), bf16[32,6,1792]{2,1,0:T(8,128)(2,1)S(1)}, u32[]{:S(2)}, u32[]{:S(2)}) async-start(bf16[32,6,1792]{2,1,0:T(8,128)(2,1)} %reshape.272), calls=%async_computation.1 | async-start | bytes 1835008 | tf_op jit(solution)/shard_map/all_to_all | solution.py:146
  243.2 3.4 %fusion.3 = bf16[1,128,1792]{2,1,0:T(8,128)(2,1)} fusion(bf16[128,896]{0,1:T(8,128)(2,1)S(1)} %bitcast.72, bf16[896,1792]{1,0:T(8,128)(2,1)} %bitcast.62, bf16[128,1792]{1,0:T(8,128)(2,1)S(1)} %gather_fusion.1, pred[128]{0:T(512)(128)(4,1)S(1)} %compare_and_fusion.1), kind=kOutput, calls=%fused_computation.10 | convolution fusion | flops 411959296 | bytes 4358272 | tf_op jit(solution)/shard_map/dot_general | solution.py:100
  246.6 20.4 %all-to-all-done.1 = bf16[32,6,1792]{2,1,0:T(8,128)(2,1)S(1)} async-done(((bf16[32,6,1792]{2,1,0:T(8,128)(2,1)}), bf16[32,6,1792]{2,1,0:T(8,128)(2,1)S(1)}, u32[]{:S(2)}, u32[]{:S(2)}) %all-to-all-start.1) | async-done | bytes 688160 | tf_op jit(solution)/shard_map/all_to_all | solution.py:146
  267.2 3.1 %scatter_custom_fusion.1 = bf16[193,1792]{1,0:T(8,128)(2,1)S(1)} fusion(s32[192]{0:T(256)S(1)} %bitcast.74, bf16[192,1792]{1,0:T(8,128)(2,1)S(1)} %reshape.302, bf16[]{:T(256)} %constant.97.clone.1), kind=kCustom, calls=%fused_computation.73 | custom fusion | flops 344064 | bytes 691714 | tf_op jit(solution)/shard_map/scatter-add | solution.py:150
  (91 shorter events, 34.7 us)
Async XLA Ops:
  7.2 69.6 %copy-start = (bf16[1,192,1792]{2,1,0:T(8,128)(2,1)S(1)}, bf16[1,192,1792]{2,1,0:T(8,128)(2,1)}, u32[]{:S(2)}) copy-start(bf16[1,192,1792]{2,1,0:T(8,128)(2,1)} %param.12) | copy-start | bytes 2064388
  7.2 68.6 %all-gather.9.cloned.1.call-start = ((), (), s32[]{:S(2)}) async-start(), calls=%async_computation.2 | async-start | bytes 5419008 | tf_op jit(solution)/shard_map/all_gather | solution.py:28
  7.9 113.2 %all-gather.13.cloned.1.call-start = ((), (), s32[]{:S(2)}) async-start(), calls=%async_computation.4 | async-start | bytes 1806336 | tf_op jit(solution)/shard_map/all_gather | solution.py:28
  8.7 142.8 %all-gather.11.cloned.1.call-start = ((), (), s32[]{:S(2)}) async-start(), calls=%async_computation.3 | async-start | bytes 14450688 | tf_op jit(solution)/shard_map/all_gather | solution.py:29
  79.3 41.9 %copy-start.12 = (s32[1,128]{1,0:T(1,128)S(1)}, s32[1,128]{1,0:T(1,128)}, u32[]{:S(2)}) copy-start(s32[1,128]{1,0:T(1,128)} %param.15) | copy-start | bytes 1540
  79.3 47.5 %copy-start.13 = (s32[1,128]{1,0:T(1,128)S(1)}, s32[1,128]{1,0:T(1,128)}, u32[]{:S(2)}) copy-start(s32[1,128]{1,0:T(1,128)} %param.14) | copy-start | bytes 1540
  79.3 48.9 %all-to-all-start = ((bf16[32,6,1792]{2,1,0:T(8,128)(2,1)}), bf16[32,6,1792]{2,1,0:T(8,128)(2,1)S(1)}, u32[]{:S(2)}, u32[]{:S(2)}) async-start(bf16[32,6,1792]{2,1,0:T(8,128)(2,1)} %broadcast_select_fusion), calls=%async_computation | async-start | bytes 1835008 | tf_op jit(solution)/shard_map/all_to_all | solution.py:84
  89.3 85.8 %all-gather.15.cloned.1.call-start = ((), (), s32[]{:S(2)}) async-start(), calls=%async_computation.5 | async-start | bytes 4816896 | tf_op jit(solution)/shard_map/all_gather | solution.py:29
  121.3 5.6 %collective-permute-start.2 = (s32[96]{0:T(128)S(1)}, s32[96]{0:T(128)S(1)}, u32[]{:S(2)}, u32[]{:S(2)}) collective-permute-start(s32[96]{0:T(128)S(1)} %get-tuple-element.36), channel_id=1, source_target_pairs={{0,1},{1,2},{2,3},{3,4},{4,5},{5,6},{6,7},{7,8},{8,9},{9,10},{10,1... | collective-permute-start | bytes 1160 | tf_op jit(solution)/shard_map/ppermute | solution.py:16
  123.2 4.9 %collective-permute-start.3 = (s32[96]{0:T(128)S(1)}, s32[96]{0:T(128)S(1)}, u32[]{:S(2)}, u32[]{:S(2)}) collective-permute-start(s32[96]{0:T(128)S(1)} %get-tuple-element.37), channel_id=1, source_target_pairs={{1,0},{2,1},{3,2},{4,3},{5,4},{6,5},{7,6},{8,7},{9,8},{10,9},{11,1... | collective-permute-start | bytes 1160 | tf_op jit(solution)/shard_map/ppermute | solution.py:19
  128.4 23.1 %copy-start.11 = (f32[1792]{0:T(1024)S(1)}, f32[1792]{0:T(1024)}, u32[]{:S(2)}) copy-start(f32[1792]{0:T(1024)} %param.16) | copy-start | bytes 21508
  156.9 18.2 %copy-start.4 = (bf16[1,128,1792]{2,1,0:T(8,128)(2,1)S(1)}, bf16[1,128,1792]{2,1,0:T(8,128)(2,1)}, u32[]{:S(2)}) copy-start(bf16[1,128,1792]{2,1,0:T(8,128)(2,1)} %param.19) | copy-start | bytes 1376260
  157.8 21.5 %collective-permute-start = (bf16[96,1792]{1,0:T(8,128)(2,1)}, bf16[96,1792]{1,0:T(8,128)(2,1)S(1)}, u32[]{:S(2)}, u32[]{:S(2)}) collective-permute-start(bf16[96,1792]{1,0:T(8,128)(2,1)} %get-tuple-element.32), channel_id=1, source_target_pairs={{0,1},{1,2},{2,3},{3,4},{4,5},{5,6},{6,7},{7,8},{8,9},{9,10},{10,1... | collective-permute-start | bytes 1032200 | tf_op jit(solution)/shard_map/ppermute | solution.py:16
  160.0 19.3 %collective-permute-start.1 = (bf16[96,1792]{1,0:T(8,128)(2,1)}, bf16[96,1792]{1,0:T(8,128)(2,1)}, u32[]{:S(2)}, u32[]{:S(2)}) collective-permute-start(bf16[96,1792]{1,0:T(8,128)(2,1)} %get-tuple-element.33), channel_id=1, source_target_pairs={{1,0},{2,1},{3,2},{4,3},{5,4},{6,5},{7,6},{8,7},{9,8},{10,9},{11,1... | collective-permute-start | bytes 1032200 | tf_op jit(solution)/shard_map/ppermute | solution.py:19
  182.8 3.5 %copy-start.2 = (bf16[320,8,112]{2,1,0:T(8,128)(2,1)}, bf16[320,8,112]{2,1,0:T(8,128)(2,1)S(1)}, u32[]{:S(2)}) copy-start(bf16[320,8,112]{2,1,0:T(8,128)(2,1)S(1)} %reshape.263) | copy-start | bytes 1720324
  183.1 6.2 %copy-start.6 = (f32[8,128,320]{1,2,0:T(8,128)}, f32[8,128,320]{1,2,0:T(8,128)S(1)}, u32[]{:S(2)}) copy-start(f32[8,128,320]{1,2,0:T(8,128)S(1)} %fusion.41) | copy-start | bytes 3932164
  186.3 3.0 %copy-start.7 = (bf16[128,896]{0,1:T(8,128)(2,1)S(1)}, bf16[128,896]{0,1:T(8,128)(2,1)}, u32[]{:S(2)}) copy-start(bf16[128,896]{0,1:T(8,128)(2,1)} %copy.22) | copy-start | bytes 688132
  202.6 12.7 %collective-permute-start.4 = (f32[96,1792]{1,0:T(8,128)}, f32[96,1792]{1,0:T(8,128)}, u32[]{:S(2)}, u32[]{:S(2)}) collective-permute-start(f32[96,1792]{1,0:T(8,128)} %get-tuple-element.29), channel_id=1, source_target_pairs={{0,1},{1,2},{2,3},{3,4},{4,5},{5,6},{6,7},{7,8},{8,9},{9,10},{10,1... | collective-permute-start | bytes 2064392 | tf_op jit(solution)/shard_map/ppermute | solution.py:16
  206.0 12.1 %collective-permute-start.5 = (f32[96,1792]{1,0:T(8,128)}, f32[96,1792]{1,0:T(8,128)}, u32[]{:S(2)}, u32[]{:S(2)}) collective-permute-start(f32[96,1792]{1,0:T(8,128)} %get-tuple-element.28), channel_id=1, source_target_pairs={{1,0},{2,1},{3,2},{4,3},{5,4},{6,5},{7,6},{8,7},{9,8},{10,9},{11,1... | collective-permute-start | bytes 2064392 | tf_op jit(solution)/shard_map/ppermute | solution.py:19
  217.4 4.2 %copy-start.9 = (bf16[128,896]{1,0:T(8,128)(2,1)S(1)}, bf16[128,896]{1,0:T(8,128)(2,1)}, u32[]{:S(2)}) copy-start(bf16[128,896]{1,0:T(8,128)(2,1)} %copy.30) | copy-start | bytes 688132
  221.5 6.6 %copy-start.5 = (bf16[1,128,1792]{2,1,0:T(8,128)(2,1)S(1)}, bf16[1,128,1792]{2,1,0:T(8,128)(2,1)}, u32[]{:S(2)}) copy-start(bf16[1,128,1792]{2,1,0:T(8,128)(2,1)} %param.19) | copy-start | bytes 1376260
  231.2 10.0 %copy-start.3 = (bf16[320,8,112]{2,1,0:T(8,128)(2,1)S(1)}, bf16[320,8,112]{2,1,0:T(8,128)(2,1)}, u32[]{:S(2)}) copy-start(bf16[320,8,112]{2,1,0:T(8,128)(2,1)} %copy-done.2) | copy-start | bytes 1720324
  231.3 10.0 %copy-start.8 = (bf16[128,896]{0,1:T(8,128)(2,1)S(1)}, bf16[128,896]{0,1:T(8,128)(2,1)}, u32[]{:S(2)}) copy-start(bf16[128,896]{0,1:T(8,128)(2,1)} %copy.22) | copy-start | bytes 688132
  231.3 35.8 %all-to-all-start.1 = ((bf16[32,6,1792]{2,1,0:T(8,128)(2,1)}), bf16[32,6,1792]{2,1,0:T(8,128)(2,1)S(1)}, u32[]{:S(2)}, u32[]{:S(2)}) async-start(bf16[32,6,1792]{2,1,0:T(8,128)(2,1)} %reshape.272), calls=%async_computation.1 | async-start | bytes 1835008 | tf_op jit(solution)/shard_map/all_to_all | solution.py:146
  (2 other events, 2.3 us)
Sparse Core Ops, SparseCore 0:
  10.1 65.6 all-gather.8
  77.9 43.2 all-gather.12
  123.2 28.2 all-gather.10
  153.4 21.6 all-gather.14

commit v2 on v0

--- a/solution.py
+++ b/solution.py
@@ -19,6 +19,19 @@
         high = lax.ppermute(lax.slice_in_dim(block, 0, width, axis=dim), axis, backward)
         block = jnp.concatenate([low, block, high], axis=dim)
     return block
+
+
+def gather_weights(qkv_weight, out_weight):
+    parts = lax.axis_size("tensor")
+    qkv_rows, qkv_cols = qkv_weight.shape
+    out_rows, out_cols = out_weight.shape
+    out_wide = out_weight.reshape(qkv_rows, out_rows * out_cols // qkv_rows)
+    both = lax.all_gather(
+        jnp.concatenate([qkv_weight, out_wide], axis=1), "tensor", axis=0, tiled=True
+    )
+    full_qkv = both[:, :qkv_cols]
+    full_out = both[:, qkv_cols:].reshape(parts * out_rows, out_cols)
+    return full_qkv, full_out
 
 
 def normalize(rows_in, norm_gain):
@@ -77,10 +90,7 @@
     )
     pick_rows = take_rows[0]
     packed = jnp.take(incoming, pick_rows, axis=0)
-    full_qkv, full_out = (
-        lax.all_gather(qkv_weight, "tensor", axis=0, tiled=True),
-        lax.all_gather(out_weight, "tensor", axis=0, tiled=True),
-    )
+    full_qkv, full_out = gather_weights(qkv_weight, out_weight)
     values, unit_rows, inv_dev, normed = normalize(packed, norm_gain)
     projected = jnp.dot(normed, full_qkv, preferred_element_type=jnp.float32).astype(jnp.bfloat16)
     queries = projected[:, :all_heads]

time: 228 us -> 217 us (0.952)
  the two profiles are of different devices: /device:TPU:1 before, /device:TPU:66 now
where the time goes in v2:
time: 217 us; the launch traced here: 216 us
  waiting for transfers between devices  83 us (38%)
  starting transfers between devices  38.2 us (18%)
  matrix products  34 us (16%)
  local copies, waits for them, and re-layouts  31.9 us (15%)
  other arithmetic  14.5 us (7%)
  between operations  14.5 us (7%)
    all_gather x1, waiting for transfers between devices, gather_weights(): lax.all_gather(jnp.concatenate([qkv_weight, out_wide], axis=1), 'tensor',...  41.7 us
    all_to_all x1, waiting for transfers between devices, local(): lax.all_to_all(back_slots, 'dp', split_axis=0, concat_axis=0, tiled=True)  21.1 us
    all_to_all x1, waiting for transfers between devices, local(): lax.all_to_all(outgoing, 'dp', split_axis=0, concat_axis=0, tiled=True)  18.2 us
    ppermute x3, starting transfers between devices, extended(): lax.ppermute(lax.slice_in_dim(block, 0, width, axis=dim), axis, backward)  11.8 us
    all_to_all x1, starting transfers between devices, local(): lax.all_to_all(outgoing, 'dp', split_axis=0, concat_axis=0, tiled=True)  10.4 us
    all_to_all x1, starting transfers between devices, local(): lax.all_to_all(back_slots, 'dp', split_axis=0, concat_axis=0, tiled=True)  10 us
    ppermute x3, starting transfers between devices, extended(): lax.ppermute(lax.slice_in_dim(block, block.shape[dim] - width, None, axis...  5.97 us
    reshape x1, local copies, waits for them, and re-layouts, gather_weights(): full_out = both[:, qkv_cols:].reshape(parts * out_rows, out_cols)  5.77 us
  transfers between devices with their start and end apart: 9, of which 5 were waited for; matrix products, arithmetic and copies ran while one was open for 15% of the time, Pallas kernels for 0%

profile of v2, /device:TPU:66, one launch (start us, length us, event | category | flops | bytes accessed | tf_op | source)
XLA Modules:
  0.0 216.1 jit_solution(14854768060977749511)
XLA Ops:
  8.3 2.0 pad_maximum_fusion.1
  13.2 10.4 %all-to-all-start = ((bf16[32,6,1792]{2,1,0:T(8,128)(2,1)}), bf16[32,6,1792]{2,1,0:T(8,128)(2,1)S(1)}, u32[]{:S(2)}, u32[]{:S(2)}) async-start(bf16[32,6,1792]{2,1,0:T(8,128)(2,1)} %broadcast_select_fusion), calls=%async_computation | async-start | bytes 1835008 | tf_op jit(solution)/shard_map/all_to_all | solution.py:88
  25.6 3.6 %collective-permute-start.3 = (s32[96]{0:T(128)S(1)}, s32[96]{0:T(128)S(1)}, u32[]{:S(2)}, u32[]{:S(2)}) collective-permute-start(s32[96]{0:T(128)S(1)} %get-tuple-element.37), channel_id=1, source_target_pairs={{1,0},{2,1},{3,2},{4,3},{5,4},{6,5},{7,6},{8,7},{9,8},{10,9},{11,1... | collective-permute-start | bytes 1160 | tf_op jit(solution)/shard_map/ppermute | solution.py:19
  30.7 18.2 %all-to-all-done = bf16[32,6,1792]{2,1,0:T(8,128)(2,1)S(1)} async-done(((bf16[32,6,1792]{2,1,0:T(8,128)(2,1)}), bf16[32,6,1792]{2,1,0:T(8,128)(2,1)S(1)}, u32[]{:S(2)}, u32[]{:S(2)}) %all-to-all-start) | async-done | bytes 688160 | tf_op jit(solution)/shard_map/all_to_all | solution.py:88
  50.6 41.7 %all-gather.2.cloned.1.call-done = bf16[1792,3584]{1,0:T(8,128)(2,1)} async-done(((bf16[112,3584]{1,0:T(8,128)(2,1)}), bf16[1792,3584]{1,0:T(8,128)(2,1)}) %all-gather.2.cloned.1.call-update) | async-done | bytes 12845072 | tf_op jit(solution)/shard_map/all_gather | solution.py:29
  92.3 5.4 %fusion.6 = bf16[128,2688]{1,0:T(8,128)(2,1)S(1)} fusion(bf16[1792,3584]{1,0:T(8,128)(2,1)} %all-gather.2.cloned.1.call-done, f32[1792]{0:T(1024)S(1)} %copy-done.13, f32[128]{0:T(128)S(1)} %add_rsqrt_fusion, f32[128]{0:T(128)S(1)} %broadcast_multiply_fusion.2, bf16[128,1792]{1,0:T(8,128)(2,1)S(1)} %gather_fusion.1, pred[128]{0:T(512)(128)(4,1)S(1)} %compare_and_fusion.1), kind=kOutput, calls=%fused_computation.10 | convolution fusion | flops 1234845696 | bytes 10788992 | tf_op jit(solution)/shard_map/dot_general | solution.py:95
  97.8 2.2 collective-permute-start
  99.9 4.5 %collective-permute-start.1 = (bf16[96,1792]{1,0:T(8,128)(2,1)S(1)}, bf16[96,1792]{1,0:T(8,128)(2,1)S(1)}, u32[]{:S(2)}, u32[]{:S(2)}) collective-permute-start(bf16[96,1792]{1,0:T(8,128)(2,1)S(1)} %get-tuple-element.33), channel_id=1, source_target_pairs={{1,0},{2,1},{3,2},{4,3},{5,4},{6,5},{7,6},{8,7},{9,8},{10,9},{11,1... | collective-permute-start | bytes 1032200 | tf_op jit(solution)/shard_map/ppermute | solution.py:19
  105.4 3.8 %slice.120 = bf16[1792,896]{1,0:T(8,128)(2,1)} slice(bf16[1792,3584]{1,0:T(8,128)(2,1)} %all-gather.2.cloned.1.call-done), slice={[0:1792], [2688:3584]} | slice | bytes 6422528 | tf_op jit(solution)/shard_map/slice | solution.py:33
  109.3 5.8 %reshape.267 = bf16[896,1792]{1,0:T(8,128)(2,1)} reshape(bf16[1792,896]{1,0:T(8,128)(2,1)} %slice.120) | data formatting | bytes 6422528 | tf_op jit(solution)/shard_map/reshape | solution.py:33
  115.1 3.6 %convolution_convert_fusion = bf16[896,128]{1,0:T(8,128)(2,1)} fusion(bf16[896,1792]{1,0:T(8,128)(2,1)} %reshape.267, bf16[1,128,1792]{2,1,0:T(8,128)(2,1)S(1)} %copy-done.6), kind=kOutput, calls=%fused_computation.32 | convolution fusion | flops 411156480 | bytes 3899392 | tf_op jit(solution)/shard_map/dot_general | solution.py:108
  121.6 3.2 %fusion.108 = (f32[8,128]{1,0:T(8,128)S(1)}, f32[8,128,320]{1,2,0:T(8,128)}) fusion(pred[128,320]{0,1:T(8,128)(4,1)S(1)} %broadcast_compare_fusion, bf16[128,8,112]{0,2,1:T(8,128)(2,1)} %bitcast.59, bf16[320,8,112]{2,1,0:T(8,128)(2,1)} %reshape.265), kind=kOutput, calls=%fused_computation.116 | convolution fusion | flops 74711360 | bytes 2158592 | tf_op jit(solution)/shard_map/sub | solution.py:62
  124.8 3.0 %convolution_bitcast_fusion = f32[320,8,112]{2,0,1:T(8,128)} fusion(bf16[128,8,112]{0,2,1:T(8,128)(2,1)S(1)} %bitcast.58, f32[8,128]{1,0:T(8,128)S(1)} %get-tuple-element.40, pred[128,320]{0,1:T(8,128)(4,1)S(1)} %broadcast_compare_fusion, bf16[128,8,112]{0,2,1:T(8,128)(2,1)} %bitcast.60, bf16[320,8,112]{2,1,0:T(8,128)(2,1)} %reshape.265), kind=kOutput, calls=%fused_computation.21 | convolution fusion | flops 148440384 | bytes 2224128 | tf_op jit(solution)/shard_map/hqk,qhd->khd/dot_general | solution.py:123
  127.8 3.4 %convolution_bitcast_fusion.1 = f32[320,8,112]{2,0,1:T(8,128)} fusion(bf16[128,8,112]{0,2,1:T(8,128)(2,1)S(1)} %bitcast.61, f32[8,128,320]{1,2,0:T(8,128)S(1)} %fusion.51, f32[8,128,320]{1,2,0:T(8,128)} %get-tuple-element.41, f32[8,128]{1,0:T(8,128)S(1)} %get-tuple-element.40), kind=kOutput, calls=%fused_computation.22 | convolution fusion | flops 75695424 | bytes 4001792 | tf_op jit(solution)/shard_map/hqk,qhd->khd/dot_general | solution.py:122
  131.2 2.1 copy.25
  134.7 2.1 copy.26
  144.0 3.6 %collective-permute-start.5 = (f32[96,1792]{1,0:T(8,128)}, f32[96,1792]{1,0:T(8,128)}, u32[]{:S(2)}, u32[]{:S(2)}) collective-permute-start(f32[96,1792]{1,0:T(8,128)} %get-tuple-element.28), channel_id=1, source_target_pairs={{1,0},{2,1},{3,2},{4,3},{5,4},{6,5},{7,6},{8,7},{9,8},{10,9},{11,1... | collective-permute-start | bytes 2064392 | tf_op jit(solution)/shard_map/ppermute | solution.py:19
  147.7 4.2 %fusion.27 = bf16[8,112,128]{2,1,0:T(8,128)(2,1)} fusion(f32[8,128,320]{1,2,0:T(8,128)} %copy-done.5, bf16[320,8,112]{2,1,0:T(8,128)(2,1)} %reshape.265, f32[8,128,320]{1,2,0:T(8,128)} %get-tuple-element.41, f32[8,128]{1,0:T(8,128)S(1)} %get-tuple-element.40), kind=kOutput, calls=%fused_computation.31 | convolution fusion | flops 75810112 | bytes 3428352 | tf_op jit(solution)/shard_map/hqk,khd->qhd/dot_general | solution.py:118
  156.4 2.2 %fusion.42 = f32[128,1792]{1,0:T(8,128)} fusion(f32[128,1792]{1,0:T(8,128)} %fusion.43, f32[96,1792]{1,0:T(8,128)} %collective-permute-done.5), kind=kLoop, calls=%fused_computation.51 | loop fusion | flops 172032 | bytes 2064384 | tf_op jit(solution)/shard_map/scatter-add | solution.py:134
  159.9 5.6 %fusion.104 = (f32[128]{0:T(128)S(1)}, f32[128]{0:T(128)S(1)}, f32[128,1792]{1,0:T(8,128)S(1)}) fusion(f32[128]{0:T(128)S(1)} %add_rsqrt_fusion, f32[128]{0:T(128)S(1)} %broadcast_multiply_fusion.2, bf16[128,1792]{1,0:T(8,128)(2,1)S(1)} %gather_fusion.1, pred[128]{0:T(512)(128)(4,1)S(1)} %compare_and_fusion.1, f32[1792]{0:T(1024)S(1)} %copy-done.13, ...), kind=kOutput, calls=%fused_computation.112 | convolution fusion | flops 1236336384 | bytes 11707520 | tf_op jit(solution)/shard_map/dot_general | solution.py:136
  168.6 10.0 %all-to-all-start.1 = ((bf16[32,6,1792]{2,1,0:T(8,128)(2,1)}), bf16[32,6,1792]{2,1,0:T(8,128)(2,1)S(1)}, u32[]{:S(2)}, u32[]{:S(2)}) async-start(bf16[32,6,1792]{2,1,0:T(8,128)(2,1)} %reshape.272), calls=%async_computation.1 | async-start | bytes 1835008 | tf_op jit(solution)/shard_map/all_to_all | solution.py:150
  180.6 3.4 %fusion.13 = bf16[1,128,1792]{2,1,0:T(8,128)(2,1)} fusion(bf16[128,896]{0,1:T(8,128)(2,1)S(1)} %bitcast.64, bf16[896,1792]{1,0:T(8,128)(2,1)} %reshape.267, bf16[128,1792]{1,0:T(8,128)(2,1)S(1)} %gather_fusion.1, pred[128]{0:T(512)(128)(4,1)S(1)} %compare_and_fusion.1), kind=kOutput, calls=%fused_computation.14 | convolution fusion | flops 411959296 | bytes 4358272 | tf_op jit(solution)/shard_map/dot_general | solution.py:104
  183.9 21.1 %all-to-all-done.1 = bf16[32,6,1792]{2,1,0:T(8,128)(2,1)S(1)} async-done(((bf16[32,6,1792]{2,1,0:T(8,128)(2,1)}), bf16[32,6,1792]{2,1,0:T(8,128)(2,1)S(1)}, u32[]{:S(2)}, u32[]{:S(2)}) %all-to-all-start.1) | async-done | bytes 688160 | tf_op jit(solution)/shard_map/all_to_all | solution.py:150
  205.2 3.1 %scatter_custom_fusion.1 = bf16[193,1792]{1,0:T(8,128)(2,1)S(1)} fusion(s32[192]{0:T(256)S(1)} %bitcast.66, bf16[192,1792]{1,0:T(8,128)(2,1)S(1)} %reshape.302, bf16[]{:T(256)} %constant.97.clone.1), kind=kCustom, calls=%fused_computation.78 | custom fusion | flops 344064 | bytes 691714 | tf_op jit(solution)/shard_map/scatter-add | solution.py:154
  (90 shorter events, 33.5 us)
Async XLA Ops:
  7.2 3.5 %copy-start = (bf16[1,192,1792]{2,1,0:T(8,128)(2,1)S(1)}, bf16[1,192,1792]{2,1,0:T(8,128)(2,1)}, u32[]{:S(2)}) copy-start(bf16[1,192,1792]{2,1,0:T(8,128)(2,1)} %param.12) | copy-start | bytes 2064388
  7.2 3.2 %copy-start.12 = (s32[1,1,32,6]{2,1,3,0:T(1,128)S(1)}, s32[1,1,32,6]{2,1,3,0:T(1,128)}, u32[]{:S(2)}) copy-start(s32[1,1,32,6]{2,1,3,0:T(1,128)} %param.13) | copy-start | bytes 2308
  7.2 85.1 %all-gather.2.cloned.1.call-start = ((), (), s32[]{:S(2)}) async-start(), calls=%async_computation.2 | async-start | bytes 13647872 | tf_op jit(solution)/shard_map/all_gather | solution.py:29
  13.2 10.4 %copy-start.14 = (s32[1,128]{1,0:T(1,128)S(1)}, s32[1,128]{1,0:T(1,128)}, u32[]{:S(2)}) copy-start(s32[1,128]{1,0:T(1,128)} %param.15) | copy-start | bytes 1540
  13.2 16.1 %copy-start.15 = (s32[1,128]{1,0:T(1,128)S(1)}, s32[1,128]{1,0:T(1,128)}, u32[]{:S(2)}) copy-start(s32[1,128]{1,0:T(1,128)} %param.14) | copy-start | bytes 1540
  13.2 35.6 %all-to-all-start = ((bf16[32,6,1792]{2,1,0:T(8,128)(2,1)}), bf16[32,6,1792]{2,1,0:T(8,128)(2,1)S(1)}, u32[]{:S(2)}, u32[]{:S(2)}) async-start(bf16[32,6,1792]{2,1,0:T(8,128)(2,1)} %broadcast_select_fusion), calls=%async_computation | async-start | bytes 1835008 | tf_op jit(solution)/shard_map/all_to_all | solution.py:88
  23.7 5.6 %collective-permute-start.2 = (s32[96]{0:T(128)S(1)}, s32[96]{0:T(128)S(1)}, u32[]{:S(2)}, u32[]{:S(2)}) collective-permute-start(s32[96]{0:T(128)S(1)} %get-tuple-element.36), channel_id=1, source_target_pairs={{0,1},{1,2},{2,3},{3,4},{4,5},{5,6},{6,7},{7,8},{8,9},{9,10},{10,1... | collective-permute-start | bytes 1160 | tf_op jit(solution)/shard_map/ppermute | solution.py:16
  25.6 5.0 %collective-permute-start.3 = (s32[96]{0:T(128)S(1)}, s32[96]{0:T(128)S(1)}, u32[]{:S(2)}, u32[]{:S(2)}) collective-permute-start(s32[96]{0:T(128)S(1)} %get-tuple-element.37), channel_id=1, source_target_pairs={{1,0},{2,1},{3,2},{4,3},{5,4},{6,5},{7,6},{8,7},{9,8},{10,9},{11,1... | collective-permute-start | bytes 1160 | tf_op jit(solution)/shard_map/ppermute | solution.py:19
  49.1 43.2 %copy-start.13 = (f32[1792]{0:T(1024)S(1)}, f32[1792]{0:T(1024)}, u32[]{:S(2)}) copy-start(f32[1792]{0:T(1024)} %param.16) | copy-start | bytes 21508
  97.7 6.9 %copy-start.2 = (bf16[128,2688]{1,0:T(8,128)(2,1)}, bf16[128,2688]{1,0:T(8,128)(2,1)S(1)}, u32[]{:S(2)}) copy-start(bf16[128,2688]{1,0:T(8,128)(2,1)S(1)} %fusion.6) | copy-start | bytes 2064388
  97.8 20.9 %collective-permute-start = (bf16[96,1792]{1,0:T(8,128)(2,1)S(1)}, bf16[96,1792]{1,0:T(8,128)(2,1)S(1)}, u32[]{:S(2)}, u32[]{:S(2)}) collective-permute-start(bf16[96,1792]{1,0:T(8,128)(2,1)S(1)} %get-tuple-element.32), channel_id=1, source_target_pairs={{0,1},{1,2},{2,3},{3,4},{4,5},{5,6},{6,7},{7,8},{8,9},{9,10},{10,1... | collective-permute-start | bytes 1032200 | tf_op jit(solution)/shard_map/ppermute | solution.py:16
  99.9 18.8 %collective-permute-start.1 = (bf16[96,1792]{1,0:T(8,128)(2,1)S(1)}, bf16[96,1792]{1,0:T(8,128)(2,1)S(1)}, u32[]{:S(2)}, u32[]{:S(2)}) collective-permute-start(bf16[96,1792]{1,0:T(8,128)(2,1)S(1)} %get-tuple-element.33), channel_id=1, source_target_pairs={{1,0},{2,1},{3,2},{4,3},{5,4},{6,5},{7,6},{8,7},{9,8},{10,9},{11,1... | collective-permute-start | bytes 1032200 | tf_op jit(solution)/shard_map/ppermute | solution.py:19
  109.3 5.8 %copy-start.6 = (bf16[1,128,1792]{2,1,0:T(8,128)(2,1)S(1)}, bf16[1,128,1792]{2,1,0:T(8,128)(2,1)}, u32[]{:S(2)}) copy-start(bf16[1,128,1792]{2,1,0:T(8,128)(2,1)} %param.19) | copy-start | bytes 1376260
  115.1 3.6 %slice-start = ((bf16[128,2688]{1,0:T(8,128)(2,1)}), bf16[128,1792]{1,0:T(8,128)(2,1)S(1)}, s32[]{:S(2)}) async-start(bf16[128,2688]{1,0:T(8,128)(2,1)} %copy-done.2), calls=%async_computation.3 | async-start | bytes 917504 | tf_op jit(solution)/shard_map/slice | solution.py:97
  121.3 3.5 %copy-start.3 = (bf16[320,8,112]{2,1,0:T(8,128)(2,1)}, bf16[320,8,112]{2,1,0:T(8,128)(2,1)S(1)}, u32[]{:S(2)}) copy-start(bf16[320,8,112]{2,1,0:T(8,128)(2,1)S(1)} %reshape.263) | copy-start | bytes 1720324
  121.6 6.2 %copy-start.5 = (f32[8,128,320]{1,2,0:T(8,128)}, f32[8,128,320]{1,2,0:T(8,128)S(1)}, u32[]{:S(2)}) copy-start(f32[8,128,320]{1,2,0:T(8,128)S(1)} %fusion.51) | copy-start | bytes 3932164
  124.8 3.0 %copy-start.9 = (bf16[128,896]{0,1:T(8,128)(2,1)S(1)}, bf16[128,896]{0,1:T(8,128)(2,1)}, u32[]{:S(2)}) copy-start(bf16[128,896]{0,1:T(8,128)(2,1)} %copy.20) | copy-start | bytes 688132
  141.1 12.6 %collective-permute-start.4 = (f32[96,1792]{1,0:T(8,128)}, f32[96,1792]{1,0:T(8,128)}, u32[]{:S(2)}, u32[]{:S(2)}) collective-permute-start(f32[96,1792]{1,0:T(8,128)} %get-tuple-element.29), channel_id=1, source_target_pairs={{0,1},{1,2},{2,3},{3,4},{4,5},{5,6},{6,7},{7,8},{8,9},{9,10},{10,1... | collective-permute-start | bytes 2064392 | tf_op jit(solution)/shard_map/ppermute | solution.py:16
  144.0 12.4 %collective-permute-start.5 = (f32[96,1792]{1,0:T(8,128)}, f32[96,1792]{1,0:T(8,128)}, u32[]{:S(2)}, u32[]{:S(2)}) collective-permute-start(f32[96,1792]{1,0:T(8,128)} %get-tuple-element.28), channel_id=1, source_target_pairs={{1,0},{2,1},{3,2},{4,3},{5,4},{6,5},{7,6},{8,7},{9,8},{10,9},{11,1... | collective-permute-start | bytes 2064392 | tf_op jit(solution)/shard_map/ppermute | solution.py:19
  155.7 4.2 %copy-start.11 = (bf16[128,896]{1,0:T(8,128)(2,1)S(1)}, bf16[128,896]{1,0:T(8,128)(2,1)}, u32[]{:S(2)}) copy-start(bf16[128,896]{1,0:T(8,128)(2,1)} %copy.27) | copy-start | bytes 688132
  159.9 5.6 %copy-start.7 = (bf16[1,128,1792]{2,1,0:T(8,128)(2,1)S(1)}, bf16[1,128,1792]{2,1,0:T(8,128)(2,1)}, u32[]{:S(2)}) copy-start(bf16[1,128,1792]{2,1,0:T(8,128)(2,1)} %param.19) | copy-start | bytes 1376260
  168.6 10.0 %copy-start.4 = (bf16[320,8,112]{2,1,0:T(8,128)(2,1)S(1)}, bf16[320,8,112]{2,1,0:T(8,128)(2,1)}, u32[]{:S(2)}) copy-start(bf16[320,8,112]{2,1,0:T(8,128)(2,1)} %copy-done.3) | copy-start | bytes 1720324
  168.6 10.0 %copy-start.10 = (bf16[128,896]{0,1:T(8,128)(2,1)S(1)}, bf16[128,896]{0,1:T(8,128)(2,1)}, u32[]{:S(2)}) copy-start(bf16[128,896]{0,1:T(8,128)(2,1)} %copy.20) | copy-start | bytes 688132
  168.6 36.4 %all-to-all-start.1 = ((bf16[32,6,1792]{2,1,0:T(8,128)(2,1)}), bf16[32,6,1792]{2,1,0:T(8,128)(2,1)S(1)}, u32[]{:S(2)}, u32[]{:S(2)}) async-start(bf16[32,6,1792]{2,1,0:T(8,128)(2,1)} %reshape.272), calls=%async_computation.1 | async-start | bytes 1835008 | tf_op jit(solution)/shard_map/all_to_all | solution.py:150
  (2 other events, 4.0 us)
Sparse Core Ops, SparseCore 0:
  10.5 81.8 all-gather.1

commit v3 on v2

--- a/solution.py
+++ b/solution.py
@@ -22,7 +22,6 @@
 
 
 def gather_weights(qkv_weight, out_weight):
-    parts = lax.axis_size("tensor")
     qkv_rows, qkv_cols = qkv_weight.shape
     out_rows, out_cols = out_weight.shape
     out_wide = out_weight.reshape(qkv_rows, out_rows * out_cols // qkv_rows)
@@ -30,8 +29,38 @@
         jnp.concatenate([qkv_weight, out_wide], axis=1), "tensor", axis=0, tiled=True
     )
     full_qkv = both[:, :qkv_cols]
-    full_out = both[:, qkv_cols:].reshape(parts * out_rows, out_cols)
-    return full_qkv, full_out
+    out_pairs = both[:, qkv_cols:]
+    return full_qkv, out_pairs
+
+
+def spread(cols, side):
+    rows = cols.shape[0]
+    none = jnp.zeros_like(cols)
+    pair = (cols, none) if side == 0 else (none, cols)
+    return jnp.stack(pair, axis=-1).reshape(rows, 2 * cols.shape[1])
+
+
+def times_out(attended, out_pairs):
+    halves = [
+        jnp.dot(spread(attended, side), out_pairs, preferred_element_type=jnp.float32)
+        for side in range(2)
+    ]
+    return jnp.concatenate(halves, axis=1)
+
+
+def times_out_t(grad_rows, out_pairs):
+    half = out_pairs.shape[1]
+    rows = grad_rows.shape[0]
+    parts = [
+        lax.dot_general(
+            grad_rows[:, side * half : (side + 1) * half],
+            out_pairs,
+            (((1,), (1,)), ((), ())),
+            preferred_element_type=jnp.float32,
+        ).reshape(rows, -1, 2)[:, :, side]
+        for side in range(2)
+    ]
+    return parts[0] + parts[1]
 
 
 def normalize(rows_in, norm_gain):
@@ -101,13 +130,9 @@
         extended(seg_plus, (("tensor", 0),), MOST),
     )
     attn_probs, prob_low, attended, log_norm = attend(queries, wide_kv, seg_plus, wide_seg)
-    layer_out = (values + jnp.dot(attended, full_out, preferred_element_type=jnp.float32)).astype(
-        jnp.bfloat16
-    )
+    layer_out = (values + times_out(attended, full_out)).astype(jnp.bfloat16)
     grad_rows = grad_out[0]
-    grad_att = lax.dot_general(
-        grad_rows, full_out, (((1,), (1,)), ((), ())), preferred_element_type=jnp.float32
-    ).astype(jnp.bfloat16)
+    grad_att = times_out_t(grad_rows, full_out).astype(jnp.bfloat16)
     query_heads = split_heads(queries)
     grad_heads = split_heads(grad_att)
     wide_keys = split_heads(wide_kv[:, :all_heads])

time: 217 us -> 213 us (0.982)
  the two profiles are of different devices: /device:TPU:66 before, /device:TPU:1 now
where the time goes in v3:
time: 213 us; the launch traced here: 212 us
  waiting for transfers between devices  80.3 us (38%)
  starting transfers between devices  36.8 us (17%)
  matrix products  36.5 us (17%)
  local copies, waits for them, and re-layouts  27.9 us (13%)
  other arithmetic  15.5 us (7%)
  between operations  14.5 us (7%)
    all_gather x1, waiting for transfers between devices, gather_weights(): lax.all_gather(jnp.concatenate([qkv_weight, out_wide], axis=1), 'tensor',...  47.7 us
    all_to_all x1, waiting for transfers between devices, local(): lax.all_to_all(back_slots, 'dp', split_axis=0, concat_axis=0, tiled=True)  14.1 us
    all_to_all x1, waiting for transfers between devices, local(): lax.all_to_all(outgoing, 'dp', split_axis=0, concat_axis=0, tiled=True)  13 us
    all_to_all x1, starting transfers between devices, local(): lax.all_to_all(outgoing, 'dp', split_axis=0, concat_axis=0, tiled=True)  10.6 us
    ppermute x3, starting transfers between devices, extended(): lax.ppermute(lax.slice_in_dim(block, block.shape[dim] - width, None, axis...  10 us
    all_to_all x1, starting transfers between devices, local(): lax.all_to_all(back_slots, 'dp', split_axis=0, concat_axis=0, tiled=True)  9.37 us
    ppermute x3, starting transfers between devices, extended(): lax.ppermute(lax.slice_in_dim(block, 0, width, axis=dim), axis, backward)  6.77 us
    dot_general x1, matrix products, local(): lax.dot_general(grad_proj, full_qkv, (((1,), (1,)), ((), ())), preferred_...  5.59 us
  transfers between devices with their start and end apart: 9, of which 5 were waited for; matrix products, arithmetic and copies ran while one was open for 15% of the time, Pallas kernels for 0%

profile of v3, /device:TPU:1, one launch (start us, length us, event | category | flops | bytes accessed | tf_op | source)
XLA Modules:
  0.0 211.5 jit_solution(15546488134168619678)
XLA Ops:
  13.2 10.6 %all-to-all-start = ((bf16[32,6,1792]{2,1,0:T(8,128)(2,1)}), bf16[32,6,1792]{2,1,0:T(8,128)(2,1)S(1)}, u32[]{:S(2)}, u32[]{:S(2)}) async-start(bf16[32,6,1792]{2,1,0:T(8,128)(2,1)} %broadcast_select_fusion), calls=%async_computation | async-start | bytes 1835008 | tf_op jit(solution)/shard_map/all_to_all | solution.py:117
  24.0 4.8 %collective-permute-start.2 = (s32[96]{0:T(128)S(1)}, s32[96]{0:T(128)S(1)}, u32[]{:S(2)}, u32[]{:S(2)}) collective-permute-start(s32[96]{0:T(128)S(1)} %get-tuple-element.38), channel_id=1, source_target_pairs={{0,1},{1,2},{2,3},{3,4},{4,5},{5,6},{6,7},{7,8},{8,9},{9,10},{10,1... | collective-permute-start | bytes 1160 | tf_op jit(solution)/shard_map/ppermute | solution.py:16
  30.8 3.3 %collective-permute-done.3 = s32[96]{0:T(128)S(1)} collective-permute-done((s32[96]{0:T(128)S(1)}, s32[96]{0:T(128)S(1)}, u32[]{:S(2)}, u32[]{:S(2)}) %collective-permute-start.3) | collective-permute-done | bytes 416 | tf_op jit(solution)/shard_map/ppermute | solution.py:19
  34.3 13.0 %all-to-all-done = bf16[32,6,1792]{2,1,0:T(8,128)(2,1)S(1)} async-done(((bf16[32,6,1792]{2,1,0:T(8,128)(2,1)}), bf16[32,6,1792]{2,1,0:T(8,128)(2,1)S(1)}, u32[]{:S(2)}, u32[]{:S(2)}) %all-to-all-start) | async-done | bytes 688160 | tf_op jit(solution)/shard_map/all_to_all | solution.py:117
  49.0 47.7 %all-gather.2.cloned.1.call-done = bf16[1792,3584]{1,0:T(8,128)(2,1)} async-done(((bf16[112,3584]{1,0:T(8,128)(2,1)}), bf16[1792,3584]{1,0:T(8,128)(2,1)}) %all-gather.2.cloned.1.call-update) | async-done | bytes 12845072 | tf_op jit(solution)/shard_map/all_gather | solution.py:28
  96.7 5.5 %fusion.6 = bf16[128,2688]{1,0:T(8,128)(2,1)S(1)} fusion(bf16[1792,3584]{1,0:T(8,128)(2,1)} %all-gather.2.cloned.1.call-done, f32[1792]{0:T(1024)S(1)} %copy-done.13, f32[128]{0:T(128)S(1)} %add_rsqrt_fusion, f32[128]{0:T(128)S(1)} %broadcast_multiply_fusion.2, bf16[128,1792]{1,0:T(8,128)(2,1)S(1)} %gather_fusion.1, pred[128]{0:T(512)(128)(4,1)S(1)} %compare_and_fusion.1), kind=kOutput, calls=%fused_computation.10 | convolution fusion | flops 1234845696 | bytes 10788992 | tf_op jit(solution)/shard_map/dot_general | solution.py:124
  103.1 2.0 collective-permute-start
  105.1 2.6 %collective-permute-start.1 = (bf16[96,1792]{1,0:T(8,128)(2,1)S(1)}, bf16[96,1792]{1,0:T(8,128)(2,1)S(1)}, u32[]{:S(2)}, u32[]{:S(2)}) collective-permute-start(bf16[96,1792]{1,0:T(8,128)(2,1)S(1)} %get-tuple-element.33), channel_id=1, source_target_pairs={{1,0},{2,1},{3,2},{4,3},{5,4},{6,5},{7,6},{8,7},{9,8},{10,9},{11,1... | collective-permute-start | bytes 1032200 | tf_op jit(solution)/shard_map/ppermute | solution.py:19
  118.8 3.2 %fusion.123 = (f32[8,128]{1,0:T(8,128)S(1)}, f32[8,128,320]{1,2,0:T(8,128)}) fusion(pred[128,320]{0,1:T(8,128)(4,1)S(1)} %broadcast_compare_fusion, bf16[128,8,112]{0,2,1:T(8,128)(2,1)} %bitcast.78, bf16[320,8,112]{2,1,0:T(8,128)(2,1)} %reshape.331), kind=kOutput, calls=%fused_computation.128 | convolution fusion | flops 74711360 | bytes 2158592 | tf_op jit(solution)/shard_map/sub | solution.py:91
  122.0 3.0 %convolution_bitcast_fusion = f32[320,8,112]{2,0,1:T(8,128)} fusion(bf16[128,8,112]{0,2,1:T(8,128)(2,1)S(1)} %bitcast.73, f32[8,128]{1,0:T(8,128)S(1)} %get-tuple-element.42, pred[128,320]{0,1:T(8,128)(4,1)S(1)} %broadcast_compare_fusion, bf16[128,8,112]{0,2,1:T(8,128)(2,1)} %bitcast.79, bf16[320,8,112]{2,1,0:T(8,128)(2,1)} %reshape.331), kind=kOutput, calls=%fused_computation.26 | convolution fusion | flops 148440384 | bytes 2224128 | tf_op jit(solution)/shard_map/hqk,qhd->khd/dot_general | solution.py:148
  125.0 3.4 %convolution_bitcast_fusion.1 = f32[320,8,112]{2,0,1:T(8,128)} fusion(bf16[128,8,112]{0,2,1:T(8,128)(2,1)S(1)} %bitcast.80, f32[8,128,320]{1,2,0:T(8,128)S(1)} %fusion.64, f32[8,128,320]{1,2,0:T(8,128)} %get-tuple-element.43, f32[8,128]{1,0:T(8,128)S(1)} %get-tuple-element.42), kind=kOutput, calls=%fused_computation.27 | convolution fusion | flops 75695424 | bytes 4001792 | tf_op jit(solution)/shard_map/hqk,qhd->khd/dot_general | solution.py:147
  128.4 2.1 copy.29
  131.9 2.1 copy.30
  138.3 3.1 %collective-permute-start.4 = (f32[96,1792]{1,0:T(8,128)}, f32[96,1792]{1,0:T(8,128)}, u32[]{:S(2)}, u32[]{:S(2)}) collective-permute-start(f32[96,1792]{1,0:T(8,128)} %get-tuple-element.29), channel_id=1, source_target_pairs={{0,1},{1,2},{2,3},{3,4},{4,5},{5,6},{6,7},{7,8},{8,9},{9,10},{10,1... | collective-permute-start | bytes 2064392 | tf_op jit(solution)/shard_map/ppermute | solution.py:16
  142.5 2.2 %collective-permute-start.5 = (f32[96,1792]{1,0:T(8,128)}, f32[96,1792]{1,0:T(8,128)}, u32[]{:S(2)}, u32[]{:S(2)}) collective-permute-start(f32[96,1792]{1,0:T(8,128)} %get-tuple-element.28), channel_id=1, source_target_pairs={{1,0},{2,1},{3,2},{4,3},{5,4},{6,5},{7,6},{8,7},{9,8},{10,9},{11,1... | collective-permute-start | bytes 2064392 | tf_op jit(solution)/shard_map/ppermute | solution.py:19
  144.8 4.4 %fusion.39 = bf16[8,112,128]{2,1,0:T(8,128)(2,1)} fusion(f32[8,128,320]{1,2,0:T(8,128)} %copy-done.6, bf16[320,8,112]{2,1,0:T(8,128)(2,1)} %reshape.331, f32[8,128,320]{1,2,0:T(8,128)} %get-tuple-element.43, f32[8,128]{1,0:T(8,128)S(1)} %get-tuple-element.42), kind=kOutput, calls=%fused_computation.36 | convolution fusion | flops 75810112 | bytes 3428352 | tf_op jit(solution)/shard_map/hqk,khd->qhd/dot_general | solution.py:143
  152.9 2.1 %collective-permute-done.5 = f32[96,1792]{1,0:T(8,128)} collective-permute-done((f32[96,1792]{1,0:T(8,128)}, f32[96,1792]{1,0:T(8,128)}, u32[]{:S(2)}, u32[]{:S(2)}) %collective-permute-start.5) | collective-permute-done | bytes 688160 | tf_op jit(solution)/shard_map/ppermute | solution.py:19
  155.1 2.3 %fusion.55 = f32[128,1792]{1,0:T(8,128)} fusion(f32[128,1792]{1,0:T(8,128)} %fusion.56, f32[96,1792]{1,0:T(8,128)} %collective-permute-done.5), kind=kLoop, calls=%fused_computation.59 | loop fusion | flops 172032 | bytes 2064384 | tf_op jit(solution)/shard_map/scatter-add | solution.py:159
  158.6 5.6 %fusion.118 = (f32[128]{0:T(128)S(1)}, f32[128]{0:T(128)S(1)}, f32[128,1792]{1,0:T(8,128)S(1)}) fusion(f32[128]{0:T(128)S(1)} %add_rsqrt_fusion, f32[128]{0:T(128)S(1)} %broadcast_multiply_fusion.2, bf16[128,1792]{1,0:T(8,128)(2,1)S(1)} %gather_fusion.1, pred[128]{0:T(512)(128)(4,1)S(1)} %compare_and_fusion.1, f32[1792]{0:T(1024)S(1)} %copy-done.13, ...), kind=kOutput, calls=%fused_computation.123 | convolution fusion | flops 1236336384 | bytes 11707520 | tf_op jit(solution)/shard_map/dot_general | solution.py:161
  167.3 9.4 %all-to-all-start.1 = ((bf16[32,6,1792]{2,1,0:T(8,128)(2,1)}), bf16[32,6,1792]{2,1,0:T(8,128)(2,1)S(1)}, u32[]{:S(2)}, u32[]{:S(2)}) async-start(bf16[32,6,1792]{2,1,0:T(8,128)(2,1)} %reshape.339), calls=%async_computation.1 | async-start | bytes 1835008 | tf_op jit(solution)/shard_map/all_to_all | solution.py:175
  180.2 2.6 %fusion.33 = f32[1,128,896]{2,1,0:T(8,128)S(1)} fusion(bf16[128,1792]{0,1:T(8,128)(2,1)S(1)} %bitcast.71, bf16[1792,3584]{1,0:T(8,128)(2,1)} %all-gather.2.cloned.1.call-done), kind=kOutput, calls=%fused_computation.34 | convolution fusion | flops 411041792 | bytes 4128768 | tf_op jit(solution)/shard_map/dot_general | solution.py:45
  182.8 2.6 %fusion.36 = f32[1,128,896]{2,1,0:T(8,128)S(1)} fusion(bf16[128,1792]{0,1:T(8,128)(2,1)S(1)} %bitcast.70, bf16[1792,3584]{1,0:T(8,128)(2,1)} %all-gather.2.cloned.1.call-done), kind=kOutput, calls=%fused_computation.35 | convolution fusion | flops 411041792 | bytes 4128768 | tf_op jit(solution)/shard_map/dot_general | solution.py:45
  186.3 14.1 %all-to-all-done.1 = bf16[32,6,1792]{2,1,0:T(8,128)(2,1)S(1)} async-done(((bf16[32,6,1792]{2,1,0:T(8,128)(2,1)}), bf16[32,6,1792]{2,1,0:T(8,128)(2,1)S(1)}, u32[]{:S(2)}, u32[]{:S(2)}) %all-to-all-start.1) | async-done | bytes 688160 | tf_op jit(solution)/shard_map/all_to_all | solution.py:175
  200.7 3.1 %scatter_custom_fusion.1 = bf16[193,1792]{1,0:T(8,128)(2,1)S(1)} fusion(s32[192]{0:T(256)S(1)} %bitcast.85, bf16[192,1792]{1,0:T(8,128)(2,1)S(1)} %reshape.369, bf16[]{:T(256)} %constant.98.clone.1), kind=kCustom, calls=%fused_computation.86 | custom fusion | flops 344064 | bytes 691714 | tf_op jit(solution)/shard_map/scatter-add | solution.py:179
  (96 shorter events, 42.1 us)
Async XLA Ops:
  7.2 3.5 %copy-start = (bf16[1,192,1792]{2,1,0:T(8,128)(2,1)S(1)}, bf16[1,192,1792]{2,1,0:T(8,128)(2,1)}, u32[]{:S(2)}) copy-start(bf16[1,192,1792]{2,1,0:T(8,128)(2,1)} %param.12) | copy-start | bytes 2064388
  7.2 3.2 %copy-start.12 = (s32[1,1,32,6]{2,1,3,0:T(1,128)S(1)}, s32[1,1,32,6]{2,1,3,0:T(1,128)}, u32[]{:S(2)}) copy-start(s32[1,1,32,6]{2,1,3,0:T(1,128)} %param.13) | copy-start | bytes 2308
  7.2 89.5 %all-gather.2.cloned.1.call-start = ((), (), s32[]{:S(2)}) async-start(), calls=%async_computation.2 | async-start | bytes 13647872 | tf_op jit(solution)/shard_map/all_gather | solution.py:28
  13.2 10.6 %copy-start.14 = (s32[1,128]{1,0:T(1,128)S(1)}, s32[1,128]{1,0:T(1,128)}, u32[]{:S(2)}) copy-start(s32[1,128]{1,0:T(1,128)} %param.15) | copy-start | bytes 1540
  13.2 17.5 %copy-start.15 = (s32[1,128]{1,0:T(1,128)S(1)}, s32[1,128]{1,0:T(1,128)}, u32[]{:S(2)}) copy-start(s32[1,128]{1,0:T(1,128)} %param.14) | copy-start | bytes 1540
  13.2 34.1 %all-to-all-start = ((bf16[32,6,1792]{2,1,0:T(8,128)(2,1)}), bf16[32,6,1792]{2,1,0:T(8,128)(2,1)S(1)}, u32[]{:S(2)}, u32[]{:S(2)}) async-start(bf16[32,6,1792]{2,1,0:T(8,128)(2,1)} %broadcast_select_fusion), calls=%async_computation | async-start | bytes 1835008 | tf_op jit(solution)/shard_map/all_to_all | solution.py:117
  24.0 6.8 %collective-permute-start.2 = (s32[96]{0:T(128)S(1)}, s32[96]{0:T(128)S(1)}, u32[]{:S(2)}, u32[]{:S(2)}) collective-permute-start(s32[96]{0:T(128)S(1)} %get-tuple-element.38), channel_id=1, source_target_pairs={{0,1},{1,2},{2,3},{3,4},{4,5},{5,6},{6,7},{7,8},{8,9},{9,10},{10,1... | collective-permute-start | bytes 1160 | tf_op jit(solution)/shard_map/ppermute | solution.py:16
  28.8 5.3 %collective-permute-start.3 = (s32[96]{0:T(128)S(1)}, s32[96]{0:T(128)S(1)}, u32[]{:S(2)}, u32[]{:S(2)}) collective-permute-start(s32[96]{0:T(128)S(1)} %get-tuple-element.39), channel_id=1, source_target_pairs={{1,0},{2,1},{3,2},{4,3},{5,4},{6,5},{7,6},{8,7},{9,8},{10,9},{11,1... | collective-permute-start | bytes 1160 | tf_op jit(solution)/shard_map/ppermute | solution.py:19
  47.5 49.2 %copy-start.13 = (f32[1792]{0:T(1024)S(1)}, f32[1792]{0:T(1024)}, u32[]{:S(2)}) copy-start(f32[1792]{0:T(1024)} %param.16) | copy-start | bytes 21508
  96.7 11.0 %copy-start.2 = (bf16[1792,3584]{1,0:T(8,128)(2,1)S(1)}, bf16[1792,3584]{1,0:T(8,128)(2,1)}, u32[]{:S(2)}) copy-start(bf16[1792,3584]{1,0:T(8,128)(2,1)} %all-gather.2.cloned.1.call-done) | copy-start | bytes 38535172
  102.3 9.4 %copy-start.3 = (bf16[128,2688]{1,0:T(8,128)(2,1)}, bf16[128,2688]{1,0:T(8,128)(2,1)S(1)}, u32[]{:S(2)}) copy-start(bf16[128,2688]{1,0:T(8,128)(2,1)S(1)} %fusion.6) | copy-start | bytes 2064388
  102.3 5.5 %copy-start.7 = (bf16[1,128,1792]{2,1,0:T(8,128)(2,1)S(1)}, bf16[1,128,1792]{2,1,0:T(8,128)(2,1)}, u32[]{:S(2)}) copy-start(bf16[1,128,1792]{2,1,0:T(8,128)(2,1)} %param.19) | copy-start | bytes 1376260
  103.1 12.8 %collective-permute-start = (bf16[96,1792]{1,0:T(8,128)(2,1)}, bf16[96,1792]{1,0:T(8,128)(2,1)S(1)}, u32[]{:S(2)}, u32[]{:S(2)}) collective-permute-start(bf16[96,1792]{1,0:T(8,128)(2,1)} %get-tuple-element.32), channel_id=1, source_target_pairs={{0,1},{1,2},{2,3},{3,4},{4,5},{5,6},{6,7},{7,8},{8,9},{9,10},{10,1... | collective-permute-start | bytes 1032200 | tf_op jit(solution)/shard_map/ppermute | solution.py:16
  105.1 10.7 %collective-permute-start.1 = (bf16[96,1792]{1,0:T(8,128)(2,1)S(1)}, bf16[96,1792]{1,0:T(8,128)(2,1)S(1)}, u32[]{:S(2)}, u32[]{:S(2)}) collective-permute-start(bf16[96,1792]{1,0:T(8,128)(2,1)S(1)} %get-tuple-element.33), channel_id=1, source_target_pairs={{1,0},{2,1},{3,2},{4,3},{5,4},{6,5},{7,6},{8,7},{9,8},{10,9},{11,1... | collective-permute-start | bytes 1032200 | tf_op jit(solution)/shard_map/ppermute | solution.py:19
  112.6 3.3 %slice-start = ((bf16[128,2688]{1,0:T(8,128)(2,1)}), bf16[128,1792]{1,0:T(8,128)(2,1)S(1)}, s32[]{:S(2)}) async-start(bf16[128,2688]{1,0:T(8,128)(2,1)} %copy-done.3), calls=%async_computation.3 | async-start | bytes 917504 | tf_op jit(solution)/shard_map/slice | solution.py:126
  118.4 3.6 %copy-start.4 = (bf16[320,8,112]{2,1,0:T(8,128)(2,1)}, bf16[320,8,112]{2,1,0:T(8,128)(2,1)S(1)}, u32[]{:S(2)}) copy-start(bf16[320,8,112]{2,1,0:T(8,128)(2,1)S(1)} %reshape.329) | copy-start | bytes 1720324
  118.8 6.3 %copy-start.6 = (f32[8,128,320]{1,2,0:T(8,128)}, f32[8,128,320]{1,2,0:T(8,128)S(1)}, u32[]{:S(2)}) copy-start(f32[8,128,320]{1,2,0:T(8,128)S(1)} %fusion.64) | copy-start | bytes 3932164
  138.3 12.6 %collective-permute-start.4 = (f32[96,1792]{1,0:T(8,128)}, f32[96,1792]{1,0:T(8,128)}, u32[]{:S(2)}, u32[]{:S(2)}) collective-permute-start(f32[96,1792]{1,0:T(8,128)} %get-tuple-element.29), channel_id=1, source_target_pairs={{0,1},{1,2},{2,3},{3,4},{4,5},{5,6},{6,7},{7,8},{8,9},{9,10},{10,1... | collective-permute-start | bytes 2064392 | tf_op jit(solution)/shard_map/ppermute | solution.py:16
  142.5 12.6 %collective-permute-start.5 = (f32[96,1792]{1,0:T(8,128)}, f32[96,1792]{1,0:T(8,128)}, u32[]{:S(2)}, u32[]{:S(2)}) collective-permute-start(f32[96,1792]{1,0:T(8,128)} %get-tuple-element.28), channel_id=1, source_target_pairs={{1,0},{2,1},{3,2},{4,3},{5,4},{6,5},{7,6},{8,7},{9,8},{10,9},{11,1... | collective-permute-start | bytes 2064392 | tf_op jit(solution)/shard_map/ppermute | solution.py:19
  152.9 5.6 %copy-start.11 = (bf16[128,896]{1,0:T(8,128)(2,1)S(1)}, bf16[128,896]{1,0:T(8,128)(2,1)}, u32[]{:S(2)}) copy-start(bf16[128,896]{1,0:T(8,128)(2,1)} %copy.31) | copy-start | bytes 688132
  158.6 5.6 %copy-start.8 = (bf16[1,128,1792]{2,1,0:T(8,128)(2,1)S(1)}, bf16[1,128,1792]{2,1,0:T(8,128)(2,1)}, u32[]{:S(2)}) copy-start(bf16[1,128,1792]{2,1,0:T(8,128)(2,1)} %param.19) | copy-start | bytes 1376260
  167.3 9.4 %copy-start.5 = (bf16[320,8,112]{2,1,0:T(8,128)(2,1)S(1)}, bf16[320,8,112]{2,1,0:T(8,128)(2,1)}, u32[]{:S(2)}) copy-start(bf16[320,8,112]{2,1,0:T(8,128)(2,1)} %copy-done.4) | copy-start | bytes 1720324
  167.3 9.4 %copy-start.10 = (bf16[128,896]{0,1:T(8,128)(2,1)S(1)}, bf16[128,896]{0,1:T(8,128)(2,1)}, u32[]{:S(2)}) copy-start(bf16[128,896]{0,1:T(8,128)(2,1)} %copy.20) | copy-start | bytes 688132
  167.3 33.1 %all-to-all-start.1 = ((bf16[32,6,1792]{2,1,0:T(8,128)(2,1)}), bf16[32,6,1792]{2,1,0:T(8,128)(2,1)S(1)}, u32[]{:S(2)}, u32[]{:S(2)}) async-start(bf16[32,6,1792]{2,1,0:T(8,128)(2,1)} %reshape.339), calls=%async_computation.1 | async-start | bytes 1835008 | tf_op jit(solution)/shard_map/all_to_all | solution.py:175
  (2 other events, 4.6 us)
Sparse Core Ops, SparseCore 0:
  10.5 86.2 all-gather.1

commit v4 on v3

--- a/solution.py
+++ b/solution.py
@@ -71,34 +71,44 @@
     return (values, unit_rows, inv_dev, (unit_rows * norm_gain).astype(jnp.bfloat16))
 
 
-def split_heads(rows_in):
-    return rows_in.reshape(rows_in.shape[0], HEADS, HD)
+def head_blocks(rows_in, count):
+    tiled = jnp.tile(rows_in, (HEADS, 1))
+    row_head = lax.broadcasted_iota(jnp.int32, tiled.shape, 0) // count
+    col_head = lax.broadcasted_iota(jnp.int32, tiled.shape, 1) // HD
+    return jnp.where(row_head == col_head, tiled, jnp.zeros_like(tiled))
+
+
+def own_heads(stacked, count):
+    row_head = lax.broadcasted_iota(jnp.int32, stacked.shape, 0) // count
+    col_head = lax.broadcasted_iota(jnp.int32, stacked.shape, 1) // HD
+    kept = jnp.where(row_head == col_head, stacked, jnp.zeros_like(stacked))
+    return kept.reshape(HEADS, count, stacked.shape[1]).sum(axis=0)
+
+
+def rows_dot(a, b):
+    return lax.dot_general(a, b, (((1,), (1,)), ((), ())), preferred_element_type=jnp.float32)
+
+
+def cols_dot(a, b):
+    return lax.dot_general(a, b, (((0,), (0,)), ((), ())), preferred_element_type=jnp.float32)
 
 
 def attend(queries, keyval, seg_query, seg_key):
     all_heads = HEADS * HD
     score_scale = HD ** (-0.5)
-    query_heads = split_heads(queries)
-    key_heads = split_heads(keyval[:, :all_heads])
-    value_heads = split_heads(keyval[:, all_heads:])
-    scores = (
-        jnp.einsum("qhd,khd->hqk", query_heads, key_heads, preferred_element_type=jnp.float32)
-        * score_scale
-    )
-    same_chart = seg_query[:, None] == seg_key[None, :]
-    scores = jnp.where(same_chart[None], scores, -jnp.inf)
-    row_max = jnp.max(scores, axis=2, keepdims=True)
+    count = queries.shape[0]
+    query_blocks = head_blocks(queries, count)
+    scores = rows_dot(query_blocks, keyval[:, :all_heads]) * score_scale
+    same_chart = jnp.tile(seg_query[:, None] == seg_key[None, :], (HEADS, 1))
+    scores = jnp.where(same_chart, scores, -jnp.inf)
+    row_max = jnp.max(scores, axis=1, keepdims=True)
     exp_scores = jnp.exp(scores - row_max)
-    row_sum = jnp.sum(exp_scores, axis=2, keepdims=True)
+    row_sum = jnp.sum(exp_scores, axis=1, keepdims=True)
     attn_probs = exp_scores / row_sum
     prob_low = attn_probs.astype(jnp.bfloat16)
-    attended = jnp.einsum("hqk,khd->qhd", prob_low, value_heads, preferred_element_type=jnp.float32)
-    return (
-        attn_probs,
-        prob_low,
-        attended.astype(jnp.bfloat16).reshape(queries.shape[0], all_heads),
-        row_max + jnp.log(row_sum),
-    )
+    mixed = jnp.dot(prob_low, keyval[:, all_heads:], preferred_element_type=jnp.float32)
+    attended = own_heads(mixed, count)
+    return (attn_probs, prob_low, attended.astype(jnp.bfloat16), query_blocks)
 
 
 def local(patch_rows, send_rows, take_rows, segments, norm_gain, qkv_weight, out_weight, grad_out):
@@ -129,29 +139,20 @@
         extended(keyval, (("tensor", 0),), MOST),
         extended(seg_plus, (("tensor", 0),), MOST),
     )
-    attn_probs, prob_low, attended, log_norm = attend(queries, wide_kv, seg_plus, wide_seg)
+    attn_probs, prob_low, attended, query_blocks = attend(queries, wide_kv, seg_plus, wide_seg)
     layer_out = (values + times_out(attended, full_out)).astype(jnp.bfloat16)
     grad_rows = grad_out[0]
     grad_att = times_out_t(grad_rows, full_out).astype(jnp.bfloat16)
-    query_heads = split_heads(queries)
-    grad_heads = split_heads(grad_att)
-    wide_keys = split_heads(wide_kv[:, :all_heads])
-    wide_values = split_heads(wide_kv[:, all_heads:])
-    dprobs = jnp.einsum("qhd,khd->hqk", grad_heads, wide_values, preferred_element_type=jnp.float32)
-    row_inner = jnp.sum(attn_probs * dprobs, axis=2, keepdims=True)
+    grad_blocks = head_blocks(grad_att, own_rows)
+    dprobs = rows_dot(grad_blocks, wide_kv[:, all_heads:])
+    row_inner = jnp.sum(attn_probs * dprobs, axis=1, keepdims=True)
     dscore = (attn_probs * (dprobs - row_inner) * score_scale).astype(jnp.bfloat16)
-    grad_query = jnp.einsum(
-        "hqk,khd->qhd", dscore, wide_keys, preferred_element_type=jnp.float32
-    ).reshape(own_rows, all_heads)
-    window_rows = wide_kv.shape[0]
-    grad_key = jnp.einsum("hqk,qhd->khd", dscore, query_heads, preferred_element_type=jnp.float32)
-    grad_value = jnp.einsum(
-        "hqk,qhd->khd", prob_low, grad_heads, preferred_element_type=jnp.float32
-    )
-    grad_window = jnp.concatenate(
-        [grad_key.reshape(window_rows, all_heads), grad_value.reshape(window_rows, all_heads)],
-        axis=1,
-    )
+    grad_query = own_heads(
+        jnp.dot(dscore, wide_kv[:, :all_heads], preferred_element_type=jnp.float32), own_rows
+    )
+    grad_key = cols_dot(dscore, query_blocks)
+    grad_value = cols_dot(prob_low, grad_blocks)
+    grad_window = jnp.concatenate([grad_key, grad_value], axis=1)
     center = grad_window[MOST : MOST + own_rows]
     rim_parts = jnp.concatenate([grad_window[:MOST], grad_window[MOST + own_rows :]], axis=0)
     arrived = extended(rim_parts, (("tensor", 0),), MOST)

time: 213 us -> 199 us (0.934)
  the two profiles are of different devices: /device:TPU:1 before, /device:TPU:66 now
where the time goes in v4:
time: 199 us; the launch traced here: 198 us
  waiting for transfers between devices  86.4 us (43%)
  starting transfers between devices  36.4 us (18%)
  matrix products  29.4 us (15%)
  other arithmetic  17.8 us (9%)
  between operations  14.6 us (7%)
  local copies, waits for them, and re-layouts  13.8 us (7%)
    all_gather x1, waiting for transfers between devices, gather_weights(): lax.all_gather(jnp.concatenate([qkv_weight, out_wide], axis=1), 'tensor',...  35.2 us
    all_to_all x1, waiting for transfers between devices, local(): lax.all_to_all(outgoing, 'dp', split_axis=0, concat_axis=0, tiled=True)  25.9 us
    all_to_all x1, waiting for transfers between devices, local(): lax.all_to_all(back_slots, 'dp', split_axis=0, concat_axis=0, tiled=True)  12.3 us
    ppermute x3, waiting for transfers between devices, extended(): lax.ppermute(lax.slice_in_dim(block, block.shape[dim] - width, None, axis...  10.3 us
    all_to_all x1, starting transfers between devices, local(): lax.all_to_all(outgoing, 'dp', split_axis=0, concat_axis=0, tiled=True)  10.3 us
    ppermute x3, starting transfers between devices, extended(): lax.ppermute(lax.slice_in_dim(block, 0, width, axis=dim), axis, backward)  10.1 us
    all_to_all x1, starting transfers between devices, local(): lax.all_to_all(back_slots, 'dp', split_axis=0, concat_axis=0, tiled=True)  9.93 us
    ppermute x3, starting transfers between devices, extended(): lax.ppermute(lax.slice_in_dim(block, block.shape[dim] - width, None, axis...  6.1 us
  transfers between devices with their start and end apart: 9, of which 5 were waited for; matrix products, arithmetic and copies ran while one was open for 16% of the time, Pallas kernels for 0%

profile of v4, /device:TPU:66, one launch (start us, length us, event | category | flops | bytes accessed | tf_op | source)
XLA Modules:
  0.0 198.4 jit_solution(11745641170105711453)
XLA Ops:
  8.3 2.0 %pad_maximum_fusion.1 = bf16[112,3584]{1,0:T(8,128)(2,1)} fusion(bf16[112,896]{1,0:T(8,128)(2,1)S(1)} %reshape.335, bf16[112,2688]{1,0:T(8,128)(2,1)} %param.17), kind=kLoop, calls=%fused_computation.57 | loop fusion | flops 1605632 | bytes 1605632 | tf_op jit(solution)/shard_map/concatenate | solution.py:29
  12.4 3.6 %collective-permute-start.1 = (s32[96]{0:T(128)S(1)}, s32[96]{0:T(128)S(1)}, u32[]{:S(2)}, u32[]{:S(2)}) collective-permute-start(s32[96]{0:T(128)S(1)} %get-tuple-element.39), channel_id=1, source_target_pairs={{1,0},{2,1},{3,2},{4,3},{5,4},{6,5},{7,6},{8,7},{9,8},{10,9},{11,1... | collective-permute-start | bytes 1160 | tf_op jit(solution)/shard_map/ppermute | solution.py:19
  18.9 10.3 %all-to-all-start = ((bf16[32,6,1792]{2,1,0:T(8,128)(2,1)}), bf16[32,6,1792]{2,1,0:T(8,128)(2,1)S(1)}, u32[]{:S(2)}, u32[]{:S(2)}) async-start(bf16[32,6,1792]{2,1,0:T(8,128)(2,1)} %broadcast_select_fusion), calls=%async_computation | async-start | bytes 1835008 | tf_op jit(solution)/shard_map/all_to_all | solution.py:127
  29.5 25.9 %all-to-all-done = bf16[32,6,1792]{2,1,0:T(8,128)(2,1)S(1)} async-done(((bf16[32,6,1792]{2,1,0:T(8,128)(2,1)}), bf16[32,6,1792]{2,1,0:T(8,128)(2,1)S(1)}, u32[]{:S(2)}, u32[]{:S(2)}) %all-to-all-start) | async-done | bytes 688160 | tf_op jit(solution)/shard_map/all_to_all | solution.py:127
  57.1 35.2 %all-gather.2.cloned.1.call-done = bf16[1792,3584]{1,0:T(8,128)(2,1)} async-done(((bf16[112,3584]{1,0:T(8,128)(2,1)}), bf16[1792,3584]{1,0:T(8,128)(2,1)}) %all-gather.2.cloned.1.call-update) | async-done | bytes 12845072 | tf_op jit(solution)/shard_map/all_gather | solution.py:28
  92.3 5.5 %fusion.4 = bf16[128,2688]{1,0:T(8,128)(2,1)S(1)} fusion(bf16[1792,3584]{1,0:T(8,128)(2,1)} %all-gather.2.cloned.1.call-done, f32[1792]{0:T(1024)S(1)} %copy-done.9, f32[128]{0:T(128)S(1)} %add_rsqrt_fusion, f32[128]{0:T(128)S(1)} %broadcast_multiply_fusion.2, bf16[128,1792]{1,0:T(8,128)(2,1)S(1)} %gather_fusion.1, pred[128]{0:T(512)(128)(4,1)S(1)} %compare_and_fusion.1), kind=kOutput, calls=%fused_computation.9 | convolution fusion | flops 1234845696 | bytes 10788992 | tf_op jit(solution)/shard_map/dot_general | solution.py:134
  98.8 2.3 %collective-permute-start.2 = (bf16[96,1792]{1,0:T(8,128)(2,1)}, bf16[96,1792]{1,0:T(8,128)(2,1)S(1)}, u32[]{:S(2)}, u32[]{:S(2)}) collective-permute-start(bf16[96,1792]{1,0:T(8,128)(2,1)} %get-tuple-element.30), channel_id=1, source_target_pairs={{0,1},{1,2},{2,3},{3,4},{4,5},{5,6},{6,7},{7,8},{8,9},{9,10},{10,1... | collective-permute-start | bytes 1032200 | tf_op jit(solution)/shard_map/ppermute | solution.py:16
  101.1 4.5 %collective-permute-start.3 = (bf16[96,1792]{1,0:T(8,128)(2,1)}, bf16[96,1792]{1,0:T(8,128)(2,1)S(1)}, u32[]{:S(2)}, u32[]{:S(2)}) collective-permute-start(bf16[96,1792]{1,0:T(8,128)(2,1)} %get-tuple-element.31), channel_id=1, source_target_pairs={{1,0},{2,1},{3,2},{4,3},{5,4},{6,5},{7,6},{8,7},{9,8},{10,9},{11,1... | collective-permute-start | bytes 1032200 | tf_op jit(solution)/shard_map/ppermute | solution.py:19
  106.6 2.0 %fusion.10 = f32[1792,128]{1,0:T(8,128)} fusion(bf16[1792,3584]{1,0:T(8,128)(2,1)S(1)} %copy-done.3, bf16[128,1792]{1,0:T(8,128)(2,1)S(1)} %bitcast.76), kind=kOutput, calls=%fused_computation.17 | convolution fusion | flops 411041792 | bytes 4358144 | tf_op jit(solution)/shard_map/dot_general | solution.py:55
  117.7 1.9 collective-permute-start.4
  119.7 10.3 %collective-permute-done.4 = f32[96,1792]{1,0:T(8,128)S(1)} collective-permute-done((f32[96,1792]{1,0:T(8,128)S(1)}, f32[96,1792]{1,0:T(8,128)S(1)}, u32[]{:S(2)}, u32[]{:S(2)}) %collective-permute-start.4) | collective-permute-done | bytes 688160 | tf_op jit(solution)/shard_map/ppermute | solution.py:16
  130.1 1.9 collective-permute-start.5
  132.0 2.7 %convolution_select_fusion = f32[1024,896]{1,0:T(8,128)} fusion(bf16[1024,320]{0,1:T(8,128)(2,1)S(1)} %multiply_convert_fusion, bf16[320,1792]{1,0:T(8,128)(2,1)S(1)} %pad_maximum_fusion, s32[896]{0:T(1024)S(1)} %get-tuple-element.47, s32[896]{0:T(1024)S(1)} %get-tuple-element.48, pred[896]{0:T(1024)(128)(4,1)S(1)} %fusion.77, ...), kind=kOutput, calls=%fused_computation.25 | convolution fusion | flops 590872576 | bytes 4917248 | tf_op jit(solution)/shard_map/dot_general | solution.py:151
  134.8 3.0 %reduce_sum.77 = bf16[128,896]{1,0:T(8,128)(2,1)} reduce(f32[8,128,896]{2,1,0:T(8,128)} %bitcast.71, f32[]{:T(128)} %constant.139.clone.1), dimensions={0}, to_apply=%region_6.7 | reduce | flops 802816 | bytes 3899396 | tf_op jit(solution)/shard_map/reduce_sum | solution.py:85
  137.7 2.7 %collective-permute-done.5 = f32[96,1792]{1,0:T(8,128)S(1)} collective-permute-done((f32[96,1792]{1,0:T(8,128)S(1)}, f32[96,1792]{1,0:T(8,128)S(1)}, u32[]{:S(2)}, u32[]{:S(2)}) %collective-permute-start.5) | collective-permute-done | bytes 688160 | tf_op jit(solution)/shard_map/ppermute | solution.py:19
  140.7 5.5 %fusion.85 = (f32[128]{0:T(128)S(1)}, f32[128]{0:T(128)S(1)}, f32[128,1792]{1,0:T(8,128)S(1)}) fusion(f32[128]{0:T(128)S(1)} %add_rsqrt_fusion, f32[128]{0:T(128)S(1)} %broadcast_multiply_fusion.2, bf16[128,1792]{1,0:T(8,128)(2,1)S(1)} %gather_fusion.1, pred[128]{0:T(512)(128)(4,1)S(1)} %compare_and_fusion.1, f32[1792]{0:T(1024)S(1)} %copy-done.9, ...), kind=kOutput, calls=%fused_computation.131 | convolution fusion | flops 1236336384 | bytes 11707520 | tf_op jit(solution)/shard_map/dot_general | solution.py:162
  146.2 2.4 %scatter_custom_fusion = bf16[192,1792]{1,0:T(8,128)(2,1)S(1)} fusion(s32[128]{0:T(128)S(1)} %fusion.79, f32[128,1792]{1,0:T(8,128)S(1)} %get-tuple-element.46, f32[128]{0:T(128)S(1)} %broadcast_multiply_fusion, f32[128]{0:T(128)S(1)} %broadcast_multiply_fusion.1, f32[128]{0:T(128)S(1)} %add_rsqrt_fusion, f32[128]{0:T(128)S(1)} %broadcast_multiply_fusion.2, ...), kind=kCustom, calls=%fused_computation.74 | custom fusion | flops 2523136 | bytes 2525698 | tf_op jit(solution)/shard_map/scatter | solution.py:173
  149.8 9.9 %all-to-all-start.1 = ((bf16[32,6,1792]{2,1,0:T(8,128)(2,1)}), bf16[32,6,1792]{2,1,0:T(8,128)(2,1)}, u32[]{:S(2)}, u32[]{:S(2)}) async-start(bf16[32,6,1792]{2,1,0:T(8,128)(2,1)} %reshape.342), calls=%async_computation.1 | async-start | bytes 1835008 | tf_op jit(solution)/shard_map/all_to_all | solution.py:176
  159.7 3.8 %convolution_select_fusion.1 = f32[1024,896]{1,0:T(8,128)} fusion(bf16[320,1792]{1,0:T(8,128)(2,1)} %copy-done.5, f32[1024,320]{0,1:T(8,128)S(1)} %copy-done.2, f32[1024]{0:T(1024)S(1)} %fusion.26, f32[1024]{0:T(1024)S(1)} %get-tuple-element.42, s32[896]{0:T(1024)S(1)} %get-tuple-element.47, s32[896]{0:T(1024)S(1)} %get-tuple-element.48, ...), kind=kOutput, calls=%fused_computation.26 | convolution fusion | flops 591855616 | bytes 5579648 | tf_op jit(solution)/shard_map/dot_general | solution.py:109
  163.5 2.2 %reduce_sum.75 = bf16[128,896]{1,0:T(8,128)(2,1)S(1)} reduce(f32[8,128,896]{2,1,0:T(8,128)} %bitcast.70, f32[]{:T(128)} %constant.139.clone.1), dimensions={0}, to_apply=%region_4.5 | reduce | flops 802816 | bytes 3899396 | tf_op jit(solution)/shard_map/reduce_sum | solution.py:85
  167.7 2.6 %fusion.19 = f32[1,128,896]{2,1,0:T(8,128)S(1)} fusion(bf16[128,1792]{0,1:T(8,128)(2,1)S(1)} %bitcast.73, bf16[1792,3584]{1,0:T(8,128)(2,1)} %all-gather.2.cloned.1.call-done), kind=kOutput, calls=%fused_computation.34 | convolution fusion | flops 411041792 | bytes 4128768 | tf_op jit(solution)/shard_map/dot_general | solution.py:45
  170.3 2.6 %fusion.22 = f32[1,128,896]{2,1,0:T(8,128)S(1)} fusion(bf16[128,1792]{0,1:T(8,128)(2,1)S(1)} %bitcast.72, bf16[1792,3584]{1,0:T(8,128)(2,1)} %all-gather.2.cloned.1.call-done), kind=kOutput, calls=%fused_computation.35 | convolution fusion | flops 411041792 | bytes 4128768 | tf_op jit(solution)/shard_map/dot_general | solution.py:45
  173.8 12.3 %all-to-all-done.1 = bf16[32,6,1792]{2,1,0:T(8,128)(2,1)} async-done(((bf16[32,6,1792]{2,1,0:T(8,128)(2,1)}), bf16[32,6,1792]{2,1,0:T(8,128)(2,1)}, u32[]{:S(2)}, u32[]{:S(2)}) %all-to-all-start.1) | async-done | bytes 688160 | tf_op jit(solution)/shard_map/all_to_all | solution.py:176
  187.5 3.1 %scatter_custom_fusion.1 = bf16[193,1792]{1,0:T(8,128)(2,1)S(1)} fusion(s32[192]{0:T(256)S(1)} %bitcast.81, bf16[192,1792]{1,0:T(8,128)(2,1)S(1)} %reshape.372, bf16[]{:T(256)} %constant.132.clone.1), kind=kCustom, calls=%fused_computation.85 | custom fusion | flops 344064 | bytes 691714 | tf_op jit(solution)/shard_map/scatter-add | solution.py:180
  (91 shorter events, 25.4 us)
Async XLA Ops:
  7.2 9.2 %copy-start = (bf16[1,192,1792]{2,1,0:T(8,128)(2,1)S(1)}, bf16[1,192,1792]{2,1,0:T(8,128)(2,1)}, u32[]{:S(2)}) copy-start(bf16[1,192,1792]{2,1,0:T(8,128)(2,1)} %param.12) | copy-start | bytes 2064388
  7.2 3.2 %copy-start.10 = (s32[1,128]{1,0:T(1,128)S(1)}, s32[1,128]{1,0:T(1,128)}, u32[]{:S(2)}) copy-start(s32[1,128]{1,0:T(1,128)} %param.15) | copy-start | bytes 1540
  7.2 8.8 %copy-start.8 = (s32[1,1,32,6]{2,1,3,0:T(1,128)S(1)}, s32[1,1,32,6]{2,1,3,0:T(1,128)}, u32[]{:S(2)}) copy-start(s32[1,1,32,6]{2,1,3,0:T(1,128)} %param.13) | copy-start | bytes 2308
  7.2 85.1 %all-gather.2.cloned.1.call-start = ((), (), s32[]{:S(2)}) async-start(), calls=%async_computation.2 | async-start | bytes 13647872 | tf_op jit(solution)/shard_map/all_gather | solution.py:28
  10.5 18.8 %collective-permute-start = (s32[96]{0:T(128)S(1)}, s32[96]{0:T(128)S(1)}, u32[]{:S(2)}, u32[]{:S(2)}) collective-permute-start(s32[96]{0:T(128)S(1)} %get-tuple-element.38), channel_id=1, source_target_pairs={{0,1},{1,2},{2,3},{3,4},{4,5},{5,6},{6,7},{7,8},{8,9},{9,10},{10,1... | collective-permute-start | bytes 1160 | tf_op jit(solution)/shard_map/ppermute | solution.py:16
  12.4 16.9 %collective-permute-start.1 = (s32[96]{0:T(128)S(1)}, s32[96]{0:T(128)S(1)}, u32[]{:S(2)}, u32[]{:S(2)}) collective-permute-start(s32[96]{0:T(128)S(1)} %get-tuple-element.39), channel_id=1, source_target_pairs={{1,0},{2,1},{3,2},{4,3},{5,4},{6,5},{7,6},{8,7},{9,8},{10,9},{11,1... | collective-permute-start | bytes 1160 | tf_op jit(solution)/shard_map/ppermute | solution.py:19
  17.8 11.4 %copy-start.11 = (s32[1,128]{1,0:T(1,128)S(1)}, s32[1,128]{1,0:T(1,128)}, u32[]{:S(2)}) copy-start(s32[1,128]{1,0:T(1,128)} %param.14) | copy-start | bytes 1540
  18.9 36.4 %all-to-all-start = ((bf16[32,6,1792]{2,1,0:T(8,128)(2,1)}), bf16[32,6,1792]{2,1,0:T(8,128)(2,1)S(1)}, u32[]{:S(2)}, u32[]{:S(2)}) async-start(bf16[32,6,1792]{2,1,0:T(8,128)(2,1)} %broadcast_select_fusion), calls=%async_computation | async-start | bytes 1835008 | tf_op jit(solution)/shard_map/all_to_all | solution.py:127
  55.6 36.8 %copy-start.9 = (f32[1792]{0:T(1024)S(1)}, f32[1792]{0:T(1024)}, u32[]{:S(2)}) copy-start(f32[1792]{0:T(1024)} %param.16) | copy-start | bytes 21508
  57.1 48.5 %copy-start.6 = (bf16[1,128,1792]{2,1,0:T(8,128)(2,1)S(1)}, bf16[1,128,1792]{2,1,0:T(8,128)(2,1)}, u32[]{:S(2)}) copy-start(bf16[1,128,1792]{2,1,0:T(8,128)(2,1)} %param.19) | copy-start | bytes 1376260
  92.3 13.3 %copy-start.3 = (bf16[1792,3584]{1,0:T(8,128)(2,1)S(1)}, bf16[1792,3584]{1,0:T(8,128)(2,1)}, u32[]{:S(2)}) copy-start(bf16[1792,3584]{1,0:T(8,128)(2,1)} %all-gather.2.cloned.1.call-done) | copy-start | bytes 38535172
  97.9 10.8 %copy-start.4 = (bf16[128,2688]{1,0:T(8,128)(2,1)}, bf16[128,2688]{1,0:T(8,128)(2,1)S(1)}, u32[]{:S(2)}) copy-start(bf16[128,2688]{1,0:T(8,128)(2,1)S(1)} %fusion.4) | copy-start | bytes 2064388
  98.8 14.4 %collective-permute-start.2 = (bf16[96,1792]{1,0:T(8,128)(2,1)}, bf16[96,1792]{1,0:T(8,128)(2,1)S(1)}, u32[]{:S(2)}, u32[]{:S(2)}) collective-permute-start(bf16[96,1792]{1,0:T(8,128)(2,1)} %get-tuple-element.30), channel_id=1, source_target_pairs={{0,1},{1,2},{2,3},{3,4},{4,5},{5,6},{6,7},{7,8},{8,9},{9,10},{10,1... | collective-permute-start | bytes 1032200 | tf_op jit(solution)/shard_map/ppermute | solution.py:16
  101.1 12.2 %collective-permute-start.3 = (bf16[96,1792]{1,0:T(8,128)(2,1)}, bf16[96,1792]{1,0:T(8,128)(2,1)S(1)}, u32[]{:S(2)}, u32[]{:S(2)}) collective-permute-start(bf16[96,1792]{1,0:T(8,128)(2,1)} %get-tuple-element.31), channel_id=1, source_target_pairs={{1,0},{2,1},{3,2},{4,3},{5,4},{6,5},{7,6},{8,7},{9,8},{10,9},{11,1... | collective-permute-start | bytes 1032200 | tf_op jit(solution)/shard_map/ppermute | solution.py:19
  108.9 3.2 %slice-start = ((bf16[128,2688]{1,0:T(8,128)(2,1)}), bf16[128,896]{1,0:T(8,128)(2,1)S(1)}, s32[]{:S(2)}) async-start(bf16[128,2688]{1,0:T(8,128)(2,1)} %copy-done.4), calls=%async_computation.3 | async-start | bytes 458752 | tf_op jit(solution)/shard_map/slice | solution.py:135
  112.1 1.1 slice-start.1
  113.3 18.7 %copy-start.5 = (bf16[320,1792]{1,0:T(8,128)(2,1)}, bf16[320,1792]{1,0:T(8,128)(2,1)S(1)}, u32[]{:S(2)}) copy-start(bf16[320,1792]{1,0:T(8,128)(2,1)S(1)} %pad_maximum_fusion) | copy-start | bytes 3440644
  114.4 2.0 copy-start.1
  117.7 12.3 %collective-permute-start.4 = (f32[96,1792]{1,0:T(8,128)S(1)}, f32[96,1792]{1,0:T(8,128)S(1)}, u32[]{:S(2)}, u32[]{:S(2)}) collective-permute-start(f32[96,1792]{1,0:T(8,128)S(1)} %fusion.41), channel_id=1, source_target_pairs={{0,1},{1,2},{2,3},{3,4},{4,5},{5,6},{6,7},{7,8},{8,9},{9,10},{10,1... | collective-permute-start | bytes 2064392 | tf_op jit(solution)/shard_map/ppermute | solution.py:16
  130.1 10.4 %collective-permute-start.5 = (f32[96,1792]{1,0:T(8,128)S(1)}, f32[96,1792]{1,0:T(8,128)S(1)}, u32[]{:S(2)}, u32[]{:S(2)}) collective-permute-start(f32[96,1792]{1,0:T(8,128)S(1)} %get-tuple-element.28), channel_id=1, source_target_pairs={{1,0},{2,1},{3,2},{4,3},{5,4},{6,5},{7,6},{8,7},{9,8},{10,9},{11,1... | collective-permute-start | bytes 2064392 | tf_op jit(solution)/shard_map/ppermute | solution.py:19
  137.7 2.9 %copy-start.7 = (bf16[128,896]{1,0:T(8,128)(2,1)S(1)}, bf16[128,896]{1,0:T(8,128)(2,1)}, u32[]{:S(2)}) copy-start(bf16[128,896]{1,0:T(8,128)(2,1)} %reduce_sum.77) | copy-start | bytes 688132
  148.6 11.1 %copy-start.2 = (f32[1024,320]{0,1:T(8,128)S(1)}, f32[1024,320]{0,1:T(8,128)}, u32[]{:S(2)}) copy-start(f32[1024,320]{0,1:T(8,128)} %copy-done.1) | copy-start | bytes 3932164
  149.8 36.4 %all-to-all-start.1 = ((bf16[32,6,1792]{2,1,0:T(8,128)(2,1)}), bf16[32,6,1792]{2,1,0:T(8,128)(2,1)}, u32[]{:S(2)}, u32[]{:S(2)}) async-start(bf16[32,6,1792]{2,1,0:T(8,128)(2,1)} %reshape.342), calls=%async_computation.1 | async-start | bytes 1835008 | tf_op jit(solution)/shard_map/all_to_all | solution.py:176
Sparse Core Ops, SparseCore 0:
  10.5 81.7 all-gather.1

commit v5 on v4

--- a/solution.py
+++ b/solution.py
@@ -21,46 +21,39 @@
     return block
 
 
-def gather_weights(qkv_weight, out_weight):
-    qkv_rows, qkv_cols = qkv_weight.shape
-    out_rows, out_cols = out_weight.shape
-    out_wide = out_weight.reshape(qkv_rows, out_rows * out_cols // qkv_rows)
-    both = lax.all_gather(
-        jnp.concatenate([qkv_weight, out_wide], axis=1), "tensor", axis=0, tiled=True
-    )
-    full_qkv = both[:, :qkv_cols]
-    out_pairs = both[:, qkv_cols:]
-    return full_qkv, out_pairs
+def ring_gather(block, axis_name):
+    count = lax.axis_size(axis_name)
+    half = count // 2
+    ahead = [(i, (i + 1) % count) for i in range(count)]
+    behind = [(i, (i - 1) % count) for i in range(count)]
+    forward, backward = block, block
+    lower, upper = [], []
+    for step in range(1, half + 1):
+        forward = lax.ppermute(forward, axis_name, ahead)
+        lower.append(forward)
+        if step < count - half:
+            backward = lax.ppermute(backward, axis_name, behind)
+            upper.append(backward)
+    offset = ((lax.axis_index(axis_name) - half) % count) * block.shape[0]
+    return jnp.concatenate(lower[::-1] + [block] + upper, axis=0), offset
 
 
-def spread(cols, side):
-    rows = cols.shape[0]
-    none = jnp.zeros_like(cols)
-    pair = (cols, none) if side == 0 else (none, cols)
-    return jnp.stack(pair, axis=-1).reshape(rows, 2 * cols.shape[1])
+def gather_weights(qkv_weight, out_weight):
+    full_qkv = lax.all_gather(qkv_weight, "tensor", axis=0, tiled=True)
+    return full_qkv, ring_gather(out_weight, "tensor")
 
 
-def times_out(attended, out_pairs):
-    halves = [
-        jnp.dot(spread(attended, side), out_pairs, preferred_element_type=jnp.float32)
-        for side in range(2)
-    ]
-    return jnp.concatenate(halves, axis=1)
+def times_out(attended, out_ring):
+    rows, offset = out_ring
+    return jnp.dot(jnp.roll(attended, -offset, axis=1), rows, preferred_element_type=jnp.float32)
 
 
-def times_out_t(grad_rows, out_pairs):
-    half = out_pairs.shape[1]
-    rows = grad_rows.shape[0]
-    parts = [
-        lax.dot_general(
-            grad_rows[:, side * half : (side + 1) * half],
-            out_pairs,
-            (((1,), (1,)), ((), ())),
-            preferred_element_type=jnp.float32,
-        ).reshape(rows, -1, 2)[:, :, side]
-        for side in range(2)
-    ]
-    return parts[0] + parts[1]
+def times_out_t(grad_rows, out_ring):
+    rows, offset = out_ring
+    turned = lax.dot_general(
+        grad_rows, rows, (((1,), (1,)), ((), ())), preferred_element_type=jnp.float32
+    )
+    return jnp.roll(turned, offset, axis=1)
 
 
 def normalize(rows_in, norm_gain):

time: 199 us -> 216 us (1.085)
  the two profiles are of different devices: /device:TPU:66 before, /device:TPU:258 now
where the time goes in v5:
time: 216 us; the launch traced here: 215 us
  waiting for transfers between devices  66 us (31%)
  starting transfers between devices  60.7 us (28%)
  matrix products  28.5 us (13%)
  local copies, waits for them, and re-layouts  24.5 us (11%)
  other arithmetic  20.9 us (10%)
  between operations  14.7 us (7%)
    ppermute x8, waiting for transfers between devices, ring_gather(): forward = lax.ppermute(forward, axis_name, ahead)  33.8 us
    ppermute x7, starting transfers between devices, ring_gather(): backward = lax.ppermute(backward, axis_name, behind)  23 us
    unnamed x66, local copies, waits for them, and re-layouts  15.4 us
    all_to_all x1, waiting for transfers between devices, local(): lax.all_to_all(back_slots, 'dp', split_axis=0, concat_axis=0, tiled=True)  14.8 us
    ppermute x3, starting transfers between devices, extended(): lax.ppermute(lax.slice_in_dim(block, 0, width, axis=dim), axis, backward)  11.8 us
    ppermute x3, waiting for transfers between devices, extended(): lax.ppermute(lax.slice_in_dim(block, block.shape[dim] - width, None, axis...  11.5 us
    all_to_all x1, starting transfers between devices, local(): lax.all_to_all(outgoing, 'dp', split_axis=0, concat_axis=0, tiled=True)  10.2 us
    all_to_all x1, starting transfers between devices, local(): lax.all_to_all(back_slots, 'dp', split_axis=0, concat_axis=0, tiled=True)  9.83 us
  transfers between devices with their start and end apart: 24, of which 14 were waited for; matrix products, arithmetic and copies ran while one was open for 22% of the time, Pallas kernels for 0%

profile of v5, /device:TPU:258, one launch (start us, length us, event | category | flops | bytes accessed | tf_op | source)
XLA Modules:
  0.0 215.4 jit_solution(13080875107436120081)
XLA Ops:
  7.9 2.9 %collective-permute-start.12 = (bf16[56,1792]{1,0:T(8,128)(2,1)}, bf16[56,1792]{1,0:T(8,128)(2,1)S(1)}, u32[]{:S(2)}, u32[]{:S(2)}) collective-permute-start(bf16[56,1792]{1,0:T(8,128)(2,1)} %param.18), channel_id=1, source_target_pairs={{0,15},{1,0},{2,1},{3,2},{4,3},{5,4},{6,5},{7,6},{8,7},{9,8},{10,9... | collective-permute-start | bytes 602120 | tf_op jit(solution)/shard_map/ppermute | solution.py:35
  13.5 4.9 %collective-permute-start.1 = (s32[96]{0:T(128)S(1)}, s32[96]{0:T(128)S(1)}, u32[]{:S(2)}, u32[]{:S(2)}) collective-permute-start(s32[96]{0:T(128)S(1)} %get-tuple-element.37), channel_id=1, source_target_pairs={{1,0},{2,1},{3,2},{4,3},{5,4},{6,5},{7,6},{8,7},{9,8},{10,9},{11,1... | collective-permute-start | bytes 1160 | tf_op jit(solution)/shard_map/ppermute | solution.py:19
  23.1 10.2 %all-to-all-start = ((bf16[32,6,1792]{2,1,0:T(8,128)(2,1)}), bf16[32,6,1792]{2,1,0:T(8,128)(2,1)S(1)}, u32[]{:S(2)}, u32[]{:S(2)}) async-start(bf16[32,6,1792]{2,1,0:T(8,128)(2,1)} %broadcast_select_fusion), calls=%async_computation | async-start | bytes 1835008 | tf_op jit(solution)/shard_map/all_to_all | solution.py:120
  33.5 2.9 %collective-permute-start.13 = (bf16[56,1792]{1,0:T(8,128)(2,1)S(1)}, bf16[56,1792]{1,0:T(8,128)(2,1)S(1)}, u32[]{:S(2)}, u32[]{:S(2)}) collective-permute-start(bf16[56,1792]{1,0:T(8,128)(2,1)S(1)} %collective-permute-done.12), channel_id=1, source_target_pairs={{0,15},{1,0},{2,1},{3,2},{4,3},{5,4},{6,5},{7,6},{8,7},{9,8},{10,9... | collective-permute-start | bytes 602120 | tf_op jit(solution)/shard_map/ppermute | solution.py:35
  37.1 7.1 %collective-permute-done.5 = bf16[56,1792]{1,0:T(8,128)(2,1)S(1)} collective-permute-done((bf16[56,1792]{1,0:T(8,128)(2,1)S(1)}, bf16[56,1792]{1,0:T(8,128)(2,1)S(1)}, u32[]{:S(2)}, u32[]{:S(2)}) %collective-permute-start.5) | collective-permute-done | bytes 200736 | tf_op jit(solution)/shard_map/ppermute | solution.py:32
  44.1 3.3 %collective-permute-start.14 = (bf16[56,1792]{1,0:T(8,128)(2,1)S(1)}, bf16[56,1792]{1,0:T(8,128)(2,1)S(1)}, u32[]{:S(2)}, u32[]{:S(2)}) collective-permute-start(bf16[56,1792]{1,0:T(8,128)(2,1)S(1)} %collective-permute-done.13), channel_id=1, source_target_pairs={{0,15},{1,0},{2,1},{3,2},{4,3},{5,4},{6,5},{7,6},{8,7},{9,8},{10,9... | collective-permute-start | bytes 602120 | tf_op jit(solution)/shard_map/ppermute | solution.py:35
  48.0 6.7 %collective-permute-done.6 = bf16[56,1792]{1,0:T(8,128)(2,1)S(1)} collective-permute-done((bf16[56,1792]{1,0:T(8,128)(2,1)S(1)}, bf16[56,1792]{1,0:T(8,128)(2,1)S(1)}, u32[]{:S(2)}, u32[]{:S(2)}) %collective-permute-start.6) | collective-permute-done | bytes 200736 | tf_op jit(solution)/shard_map/ppermute | solution.py:32
  55.0 3.5 %collective-permute-start.15 = (bf16[56,1792]{1,0:T(8,128)(2,1)S(1)}, bf16[56,1792]{1,0:T(8,128)(2,1)S(1)}, u32[]{:S(2)}, u32[]{:S(2)}) collective-permute-start(bf16[56,1792]{1,0:T(8,128)(2,1)S(1)} %collective-permute-done.14), channel_id=1, source_target_pairs={{0,15},{1,0},{2,1},{3,2},{4,3},{5,4},{6,5},{7,6},{8,7},{9,8},{10,9... | collective-permute-start | bytes 602120 | tf_op jit(solution)/shard_map/ppermute | solution.py:35
  59.0 6.3 %collective-permute-done.7 = bf16[56,1792]{1,0:T(8,128)(2,1)S(1)} collective-permute-done((bf16[56,1792]{1,0:T(8,128)(2,1)S(1)}, bf16[56,1792]{1,0:T(8,128)(2,1)S(1)}, u32[]{:S(2)}, u32[]{:S(2)}) %collective-permute-start.7) | collective-permute-done | bytes 200736 | tf_op jit(solution)/shard_map/ppermute | solution.py:32
  66.0 3.5 %collective-permute-start.16 = (bf16[56,1792]{1,0:T(8,128)(2,1)S(1)}, bf16[56,1792]{1,0:T(8,128)(2,1)S(1)}, u32[]{:S(2)}, u32[]{:S(2)}) collective-permute-start(bf16[56,1792]{1,0:T(8,128)(2,1)S(1)} %collective-permute-done.15), channel_id=1, source_target_pairs={{0,15},{1,0},{2,1},{3,2},{4,3},{5,4},{6,5},{7,6},{8,7},{9,8},{10,9... | collective-permute-start | bytes 602120 | tf_op jit(solution)/shard_map/ppermute | solution.py:35
  70.1 5.9 %collective-permute-done.8 = bf16[56,1792]{1,0:T(8,128)(2,1)} collective-permute-done((bf16[56,1792]{1,0:T(8,128)(2,1)S(1)}, bf16[56,1792]{1,0:T(8,128)(2,1)}, u32[]{:S(2)}, u32[]{:S(2)}) %collective-permute-start.8) | collective-permute-done | bytes 200736 | tf_op jit(solution)/shard_map/ppermute | solution.py:32
  77.0 3.5 %collective-permute-start.17 = (bf16[56,1792]{1,0:T(8,128)(2,1)S(1)}, bf16[56,1792]{1,0:T(8,128)(2,1)}, u32[]{:S(2)}, u32[]{:S(2)}) collective-permute-start(bf16[56,1792]{1,0:T(8,128)(2,1)S(1)} %collective-permute-done.16), channel_id=1, source_target_pairs={{0,15},{1,0},{2,1},{3,2},{4,3},{5,4},{6,5},{7,6},{8,7},{9,8},{10,9... | collective-permute-start | bytes 602120 | tf_op jit(solution)/shard_map/ppermute | solution.py:35
  83.8 3.2 %collective-permute-start.18 = (bf16[56,1792]{1,0:T(8,128)(2,1)}, bf16[56,1792]{1,0:T(8,128)(2,1)}, u32[]{:S(2)}, u32[]{:S(2)}) collective-permute-start(bf16[56,1792]{1,0:T(8,128)(2,1)} %collective-permute-done.17), channel_id=1, source_target_pairs={{0,15},{1,0},{2,1},{3,2},{4,3},{5,4},{6,5},{7,6},{8,7},{9,8},{10,9... | collective-permute-start | bytes 602120 | tf_op jit(solution)/shard_map/ppermute | solution.py:35
  89.9 6.1 %collective-permute-done.11 = bf16[56,1792]{1,0:T(8,128)(2,1)S(1)} collective-permute-done((bf16[56,1792]{1,0:T(8,128)(2,1)}, bf16[56,1792]{1,0:T(8,128)(2,1)S(1)}, u32[]{:S(2)}, u32[]{:S(2)}) %collective-permute-start.11) | collective-permute-done | bytes 200736 | tf_op jit(solution)/shard_map/ppermute | solution.py:32
  111.9 5.4 %convolution_convert_fusion = bf16[128,2688]{1,0:T(8,128)(2,1)S(1)} fusion(bf16[1792,2688]{1,0:T(8,128)(2,1)} %all-gather.2.cloned.1.call-done, f32[1792]{0:T(1024)S(1)} %copy-done.23, f32[128]{0:T(128)S(1)} %copy-done.22, f32[128]{0:T(128)S(1)} %copy-done.18, bf16[128,1792]{1,0:T(8,128)(2,1)S(1)} %gather_fusion.1, pred[128]{0:T(512)(128)(4,1)S(1)} %copy-done.15), kind=kOutput, calls=%fused_computation.5 | convolution fusion | flops 1234845696 | bytes 10788992 | tf_op jit(solution)/shard_map/dot_general | solution.py:127
  120.1 4.9 %collective-permute-start.3 = (bf16[96,1792]{1,0:T(8,128)(2,1)S(1)}, bf16[96,1792]{1,0:T(8,128)(2,1)S(1)}, u32[]{:S(2)}, u32[]{:S(2)}) collective-permute-start(bf16[96,1792]{1,0:T(8,128)(2,1)S(1)} %get-tuple-element.31), channel_id=1, source_target_pairs={{1,0},{2,1},{3,2},{4,3},{5,4},{6,5},{7,6},{8,7},{9,8},{10,9},{11,1... | collective-permute-start | bytes 1032200 | tf_op jit(solution)/shard_map/ppermute | solution.py:19
  136.5 11.5 %collective-permute-done.19 = f32[96,1792]{1,0:T(8,128)S(1)} collective-permute-done((f32[96,1792]{1,0:T(8,128)S(1)}, f32[96,1792]{1,0:T(8,128)S(1)}, u32[]{:S(2)}, u32[]{:S(2)}) %collective-permute-start.19) | collective-permute-done | bytes 688160 | tf_op jit(solution)/shard_map/ppermute | solution.py:16
  153.1 3.0 %reduce_sum.77 = bf16[128,896]{1,0:T(8,128)(2,1)} reduce(f32[8,128,896]{2,1,0:T(8,128)} %bitcast.58, f32[]{:T(128)} %constant.181.clone.1), dimensions={0}, to_apply=%region_6.7 | reduce | flops 802816 | bytes 3899396 | tf_op jit(solution)/shard_map/reduce_sum | solution.py:78
  158.7 6.6 %fusion.66 = (f32[128]{0:T(128)S(1)}, f32[128]{0:T(128)S(1)}, f32[128,1792]{1,0:T(8,128)S(1)}) fusion(f32[128]{0:T(128)S(1)} %copy-done.22, f32[128]{0:T(128)S(1)} %copy-done.18, bf16[128,1792]{1,0:T(8,128)(2,1)S(1)} %gather_fusion.1, pred[128]{0:T(512)(128)(4,1)S(1)} %copy-done.15, f32[1792]{0:T(1024)S(1)} %copy-done.23, ...), kind=kOutput, calls=%fused_computation.138 | convolution fusion | flops 1236336384 | bytes 11707520 | tf_op jit(solution)/shard_map/dot_general | solution.py:155
  168.9 9.8 %all-to-all-start.1 = ((bf16[32,6,1792]{2,1,0:T(8,128)(2,1)}), bf16[32,6,1792]{2,1,0:T(8,128)(2,1)}, u32[]{:S(2)}, u32[]{:S(2)}) async-start(bf16[32,6,1792]{2,1,0:T(8,128)(2,1)} %reshape.245), calls=%async_computation.1 | async-start | bytes 1835008 | tf_op jit(solution)/shard_map/all_to_all | solution.py:169
  178.7 3.8 %convolution_select_fusion.1 = f32[1024,896]{1,0:T(8,128)} fusion(bf16[320,1792]{1,0:T(8,128)(2,1)} %copy-done.4, f32[1024,320]{0,1:T(8,128)S(1)} %copy-done.2, f32[1024]{0:T(1024)S(1)} %fusion.4, f32[1024]{0:T(1024)S(1)} %get-tuple-element.40, s32[896]{0:T(1024)S(1)} %get-tuple-element.45, s32[896]{0:T(1024)S(1)} %get-tuple-element.46, ...), kind=kOutput, calls=%fused_computation.17 | convolution fusion | flops 591855616 | bytes 5579648 | tf_op jit(solution)/shard_map/dot_general | solution.py:102
  184.8 3.4 %fusion.1 = bf16[1,128,1792]{2,1,0:T(8,128)(2,1)} fusion(bf16[896,1792]{1,0:T(8,128)(2,1)} %constant_dynamic-update-slice_fusion, s32[]{:T(128)S(6)} %select_n.139, bf16[128,896]{1,0:T(8,128)(2,1)S(1)} %reduce_sum.75, bf16[128,1792]{1,0:T(8,128)(2,1)S(1)} %gather_fusion.1, pred[128]{0:T(512)(128)(4,1)S(1)} %copy-done.15), kind=kOutput, calls=%fused_computation.15 | convolution fusion | flops 412418048 | bytes 4358276 | tf_op jit(solution)/shard_map/dot_general | solution.py:48
  188.2 14.8 %all-to-all-done.1 = bf16[32,6,1792]{2,1,0:T(8,128)(2,1)} async-done(((bf16[32,6,1792]{2,1,0:T(8,128)(2,1)}), bf16[32,6,1792]{2,1,0:T(8,128)(2,1)}, u32[]{:S(2)}, u32[]{:S(2)}) %all-to-all-start.1) | async-done | bytes 688160 | tf_op jit(solution)/shard_map/all_to_all | solution.py:169
  204.4 3.2 %scatter_custom_fusion.1 = bf16[193,1792]{1,0:T(8,128)(2,1)S(1)} fusion(s32[192]{0:T(256)} %bitcast.61, bf16[192,1792]{1,0:T(8,128)(2,1)S(1)} %reshape.275, bf16[]{:T(256)} %constant.174.clone.1), kind=kCustom, calls=%fused_computation.78 | custom fusion | flops 344064 | bytes 692224 | tf_op jit(solution)/shard_map/scatter-add | solution.py:173
  (152 shorter events, 64.0 us)
Async XLA Ops:
  7.2 104.6 %all-gather.2.cloned.1.call-start = ((), (), s32[]{:S(2)}) async-start(), calls=%async_computation.2 | async-start | bytes 10235904 | tf_op jit(solution)/shard_map/all_gather | solution.py:42
  7.9 25.6 %collective-permute-start.4 = (bf16[56,1792]{1,0:T(8,128)(2,1)}, bf16[56,1792]{1,0:T(8,128)(2,1)S(1)}, u32[]{:S(2)}, u32[]{:S(2)}) collective-permute-start(bf16[56,1792]{1,0:T(8,128)(2,1)} %param.18), channel_id=1, source_target_pairs={{0,1},{1,2},{2,3},{3,4},{4,5},{5,6},{6,7},{7,8},{8,9},{9,10},{10,1... | collective-permute-start | bytes 602120 | tf_op jit(solution)/shard_map/ppermute | solution.py:32
  7.9 25.6 %collective-permute-start.12 = (bf16[56,1792]{1,0:T(8,128)(2,1)}, bf16[56,1792]{1,0:T(8,128)(2,1)S(1)}, u32[]{:S(2)}, u32[]{:S(2)}) collective-permute-start(bf16[56,1792]{1,0:T(8,128)(2,1)} %param.18), channel_id=1, source_target_pairs={{0,15},{1,0},{2,1},{3,2},{4,3},{5,4},{6,5},{7,6},{8,7},{9,8},{10,9... | collective-permute-start | bytes 602120 | tf_op jit(solution)/shard_map/ppermute | solution.py:35
  11.6 58.4 %collective-permute-start = (s32[96]{0:T(128)S(1)}, s32[96]{0:T(128)S(1)}, u32[]{:S(2)}, u32[]{:S(2)}) collective-permute-start(s32[96]{0:T(128)S(1)} %get-tuple-element.36), channel_id=1, source_target_pairs={{0,1},{1,2},{2,3},{3,4},{4,5},{5,6},{6,7},{7,8},{8,9},{9,10},{10,1... | collective-permute-start | bytes 1160 | tf_op jit(solution)/shard_map/ppermute | solution.py:16
  13.5 56.5 %collective-permute-start.1 = (s32[96]{0:T(128)S(1)}, s32[96]{0:T(128)S(1)}, u32[]{:S(2)}, u32[]{:S(2)}) collective-permute-start(s32[96]{0:T(128)S(1)} %get-tuple-element.37), channel_id=1, source_target_pairs={{1,0},{2,1},{3,2},{4,3},{5,4},{6,5},{7,6},{8,7},{9,8},{10,9},{11,1... | collective-permute-start | bytes 1160 | tf_op jit(solution)/shard_map/ppermute | solution.py:19
  23.1 63.9 %all-to-all-start = ((bf16[32,6,1792]{2,1,0:T(8,128)(2,1)}), bf16[32,6,1792]{2,1,0:T(8,128)(2,1)S(1)}, u32[]{:S(2)}, u32[]{:S(2)}) async-start(bf16[32,6,1792]{2,1,0:T(8,128)(2,1)} %broadcast_select_fusion), calls=%async_computation | async-start | bytes 1835008 | tf_op jit(solution)/shard_map/all_to_all | solution.py:120
  33.5 10.6 %collective-permute-start.5 = (bf16[56,1792]{1,0:T(8,128)(2,1)S(1)}, bf16[56,1792]{1,0:T(8,128)(2,1)S(1)}, u32[]{:S(2)}, u32[]{:S(2)}) collective-permute-start(bf16[56,1792]{1,0:T(8,128)(2,1)S(1)} %collective-permute-done.4), channel_id=1, source_target_pairs={{0,1},{1,2},{2,3},{3,4},{4,5},{5,6},{6,7},{7,8},{8,9},{9,10},{10,1... | collective-permute-start | bytes 602120 | tf_op jit(solution)/shard_map/ppermute | solution.py:32
  33.5 10.6 %collective-permute-start.13 = (bf16[56,1792]{1,0:T(8,128)(2,1)S(1)}, bf16[56,1792]{1,0:T(8,128)(2,1)S(1)}, u32[]{:S(2)}, u32[]{:S(2)}) collective-permute-start(bf16[56,1792]{1,0:T(8,128)(2,1)S(1)} %collective-permute-done.12), channel_id=1, source_target_pairs={{0,15},{1,0},{2,1},{3,2},{4,3},{5,4},{6,5},{7,6},{8,7},{9,8},{10,9... | collective-permute-start | bytes 602120 | tf_op jit(solution)/shard_map/ppermute | solution.py:35
  44.1 10.6 %collective-permute-start.6 = (bf16[56,1792]{1,0:T(8,128)(2,1)S(1)}, bf16[56,1792]{1,0:T(8,128)(2,1)S(1)}, u32[]{:S(2)}, u32[]{:S(2)}) collective-permute-start(bf16[56,1792]{1,0:T(8,128)(2,1)S(1)} %collective-permute-done.5), channel_id=1, source_target_pairs={{0,1},{1,2},{2,3},{3,4},{4,5},{5,6},{6,7},{7,8},{8,9},{9,10},{10,1... | collective-permute-start | bytes 602120 | tf_op jit(solution)/shard_map/ppermute | solution.py:32
  44.1 10.9 %collective-permute-start.14 = (bf16[56,1792]{1,0:T(8,128)(2,1)S(1)}, bf16[56,1792]{1,0:T(8,128)(2,1)S(1)}, u32[]{:S(2)}, u32[]{:S(2)}) collective-permute-start(bf16[56,1792]{1,0:T(8,128)(2,1)S(1)} %collective-permute-done.13), channel_id=1, source_target_pairs={{0,15},{1,0},{2,1},{3,2},{4,3},{5,4},{6,5},{7,6},{8,7},{9,8},{10,9... | collective-permute-start | bytes 602120 | tf_op jit(solution)/shard_map/ppermute | solution.py:35
  54.7 10.6 %collective-permute-start.7 = (bf16[56,1792]{1,0:T(8,128)(2,1)S(1)}, bf16[56,1792]{1,0:T(8,128)(2,1)S(1)}, u32[]{:S(2)}, u32[]{:S(2)}) collective-permute-start(bf16[56,1792]{1,0:T(8,128)(2,1)S(1)} %collective-permute-done.6), channel_id=1, source_target_pairs={{0,1},{1,2},{2,3},{3,4},{4,5},{5,6},{6,7},{7,8},{8,9},{9,10},{10,1... | collective-permute-start | bytes 602120 | tf_op jit(solution)/shard_map/ppermute | solution.py:32
  55.0 11.0 %collective-permute-start.15 = (bf16[56,1792]{1,0:T(8,128)(2,1)S(1)}, bf16[56,1792]{1,0:T(8,128)(2,1)S(1)}, u32[]{:S(2)}, u32[]{:S(2)}) collective-permute-start(bf16[56,1792]{1,0:T(8,128)(2,1)S(1)} %collective-permute-done.14), channel_id=1, source_target_pairs={{0,15},{1,0},{2,1},{3,2},{4,3},{5,4},{6,5},{7,6},{8,7},{9,8},{10,9... | collective-permute-start | bytes 602120 | tf_op jit(solution)/shard_map/ppermute | solution.py:35
  65.4 10.7 %collective-permute-start.8 = (bf16[56,1792]{1,0:T(8,128)(2,1)S(1)}, bf16[56,1792]{1,0:T(8,128)(2,1)}, u32[]{:S(2)}, u32[]{:S(2)}) collective-permute-start(bf16[56,1792]{1,0:T(8,128)(2,1)S(1)} %collective-permute-done.7), channel_id=1, source_target_pairs={{0,1},{1,2},{2,3},{3,4},{4,5},{5,6},{6,7},{7,8},{8,9},{9,10},{10,1... | collective-permute-start | bytes 602120 | tf_op jit(solution)/shard_map/ppermute | solution.py:32
  66.0 11.0 %collective-permute-start.16 = (bf16[56,1792]{1,0:T(8,128)(2,1)S(1)}, bf16[56,1792]{1,0:T(8,128)(2,1)S(1)}, u32[]{:S(2)}, u32[]{:S(2)}) collective-permute-start(bf16[56,1792]{1,0:T(8,128)(2,1)S(1)} %collective-permute-done.15), channel_id=1, source_target_pairs={{0,15},{1,0},{2,1},{3,2},{4,3},{5,4},{6,5},{7,6},{8,7},{9,8},{10,9... | collective-permute-start | bytes 602120 | tf_op jit(solution)/shard_map/ppermute | solution.py:35
  76.1 6.7 %collective-permute-start.9 = (bf16[56,1792]{1,0:T(8,128)(2,1)}, bf16[56,1792]{1,0:T(8,128)(2,1)}, u32[]{:S(2)}, u32[]{:S(2)}) collective-permute-start(bf16[56,1792]{1,0:T(8,128)(2,1)} %collective-permute-done.8), channel_id=1, source_target_pairs={{0,1},{1,2},{2,3},{3,4},{4,5},{5,6},{6,7},{7,8},{8,9},{9,10},{10,1... | collective-permute-start | bytes 602120 | tf_op jit(solution)/shard_map/ppermute | solution.py:32
  77.0 6.7 %collective-permute-start.17 = (bf16[56,1792]{1,0:T(8,128)(2,1)S(1)}, bf16[56,1792]{1,0:T(8,128)(2,1)}, u32[]{:S(2)}, u32[]{:S(2)}) collective-permute-start(bf16[56,1792]{1,0:T(8,128)(2,1)S(1)} %collective-permute-done.16), channel_id=1, source_target_pairs={{0,15},{1,0},{2,1},{3,2},{4,3},{5,4},{6,5},{7,6},{8,7},{9,8},{10,9... | collective-permute-start | bytes 602120 | tf_op jit(solution)/shard_map/ppermute | solution.py:35
  82.7 6.7 %collective-permute-start.10 = (bf16[56,1792]{1,0:T(8,128)(2,1)}, bf16[56,1792]{1,0:T(8,128)(2,1)}, u32[]{:S(2)}, u32[]{:S(2)}) collective-permute-start(bf16[56,1792]{1,0:T(8,128)(2,1)} %collective-permute-done.9), channel_id=1, source_target_pairs={{0,1},{1,2},{2,3},{3,4},{4,5},{5,6},{6,7},{7,8},{8,9},{9,10},{10,1... | collective-permute-start | bytes 602120 | tf_op jit(solution)/shard_map/ppermute | solution.py:32
  83.8 26.4 %collective-permute-start.18 = (bf16[56,1792]{1,0:T(8,128)(2,1)}, bf16[56,1792]{1,0:T(8,128)(2,1)}, u32[]{:S(2)}, u32[]{:S(2)}) collective-permute-start(bf16[56,1792]{1,0:T(8,128)(2,1)} %collective-permute-done.17), channel_id=1, source_target_pairs={{0,15},{1,0},{2,1},{3,2},{4,3},{5,4},{6,5},{7,6},{8,7},{9,8},{10,9... | collective-permute-start | bytes 602120 | tf_op jit(solution)/shard_map/ppermute | solution.py:35
  89.4 6.6 %collective-permute-start.11 = (bf16[56,1792]{1,0:T(8,128)(2,1)}, bf16[56,1792]{1,0:T(8,128)(2,1)S(1)}, u32[]{:S(2)}, u32[]{:S(2)}) collective-permute-start(bf16[56,1792]{1,0:T(8,128)(2,1)} %collective-permute-done.10), channel_id=1, source_target_pairs={{0,1},{1,2},{2,3},{3,4},{4,5},{5,6},{6,7},{7,8},{8,9},{9,10},{10,1... | collective-permute-start | bytes 602120 | tf_op jit(solution)/shard_map/ppermute | solution.py:32
  118.2 11.9 %collective-permute-start.2 = (bf16[96,1792]{1,0:T(8,128)(2,1)}, bf16[96,1792]{1,0:T(8,128)(2,1)S(1)}, u32[]{:S(2)}, u32[]{:S(2)}) collective-permute-start(bf16[96,1792]{1,0:T(8,128)(2,1)} %get-tuple-element.30), channel_id=1, source_target_pairs={{0,1},{1,2},{2,3},{3,4},{4,5},{5,6},{6,7},{7,8},{8,9},{9,10},{10,1... | collective-permute-start | bytes 1032200 | tf_op jit(solution)/shard_map/ppermute | solution.py:16
  120.1 10.0 %collective-permute-start.3 = (bf16[96,1792]{1,0:T(8,128)(2,1)S(1)}, bf16[96,1792]{1,0:T(8,128)(2,1)S(1)}, u32[]{:S(2)}, u32[]{:S(2)}) collective-permute-start(bf16[96,1792]{1,0:T(8,128)(2,1)S(1)} %get-tuple-element.31), channel_id=1, source_target_pairs={{1,0},{2,1},{3,2},{4,3},{5,4},{6,5},{7,6},{8,7},{9,8},{10,9},{11,1... | collective-permute-start | bytes 1032200 | tf_op jit(solution)/shard_map/ppermute | solution.py:19
  134.5 13.5 %collective-permute-start.19 = (f32[96,1792]{1,0:T(8,128)S(1)}, f32[96,1792]{1,0:T(8,128)S(1)}, u32[]{:S(2)}, u32[]{:S(2)}) collective-permute-start(f32[96,1792]{1,0:T(8,128)S(1)} %fusion.18), channel_id=1, source_target_pairs={{0,1},{1,2},{2,3},{3,4},{4,5},{5,6},{6,7},{7,8},{8,9},{9,10},{10,1... | collective-permute-start | bytes 2064392 | tf_op jit(solution)/shard_map/ppermute | solution.py:16
  148.1 10.4 %collective-permute-start.20 = (f32[96,1792]{1,0:T(8,128)S(1)}, f32[96,1792]{1,0:T(8,128)S(1)}, u32[]{:S(2)}, u32[]{:S(2)}) collective-permute-start(f32[96,1792]{1,0:T(8,128)S(1)} %get-tuple-element.28), channel_id=1, source_target_pairs={{1,0},{2,1},{3,2},{4,3},{5,4},{6,5},{7,6},{8,7},{9,8},{10,9},{11,1... | collective-permute-start | bytes 2064392 | tf_op jit(solution)/shard_map/ppermute | solution.py:19
  168.9 34.1 %all-to-all-start.1 = ((bf16[32,6,1792]{2,1,0:T(8,128)(2,1)}), bf16[32,6,1792]{2,1,0:T(8,128)(2,1)}, u32[]{:S(2)}, u32[]{:S(2)}) async-start(bf16[32,6,1792]{2,1,0:T(8,128)(2,1)} %reshape.245), calls=%async_computation.1 | async-start | bytes 1835008 | tf_op jit(solution)/shard_map/all_to_all | solution.py:169
  (26 other events, 297.1 us)
Sparse Core Ops, SparseCore 0:
  10.1 74.3 all-gather.1

commit v6 on v4

--- a/solution.py
+++ b/solution.py
@@ -1,7 +1,7 @@
 import jax
 import jax.numpy as jnp
 from jax import lax
-from jax.sharding import PartitionSpec as P
+from jax.sharding import Mesh, PartitionSpec as P
 
 HD = 112
 HEADS = 8
@@ -21,16 +21,20 @@
     return block
 
 
+DP = ("dh", "dl")
+
+
 def gather_weights(qkv_weight, out_weight):
     qkv_rows, qkv_cols = qkv_weight.shape
     out_rows, out_cols = out_weight.shape
     out_wide = out_weight.reshape(qkv_rows, out_rows * out_cols // qkv_rows)
-    both = lax.all_gather(
-        jnp.concatenate([qkv_weight, out_wide], axis=1), "tensor", axis=0, tiled=True
-    )
-    full_qkv = both[:, :qkv_cols]
-    out_pairs = both[:, qkv_cols:]
-    return full_qkv, out_pairs
+    both = jnp.concatenate([qkv_weight, out_wide], axis=1)
+    half = both.shape[1] // 2
+    mine = lax.dynamic_slice_in_dim(both, lax.axis_index("dl") * half, half, axis=1)
+    got = lax.all_gather(mine, ("dl", "tensor"), axis=0, tiled=False)
+    sides = got.reshape(2, -1, half)
+    rest = qkv_cols - half
+    return sides[0], sides[1][:, :rest], sides[1][:, rest:]
 
 
 def spread(cols, side):
@@ -112,7 +116,7 @@
 
 
 def local(patch_rows, send_rows, take_rows, segments, norm_gain, qkv_weight, out_weight, grad_out):
-    groups = lax.axis_size("dp")
+    groups = lax.axis_size(DP)
     src_count = patch_rows.shape[1]
     features = patch_rows.shape[2]
     slot_count = send_rows.shape[3]
@@ -124,16 +128,17 @@
     outgoing = jnp.take(patches, send_flat, axis=0, mode="fill", fill_value=0).reshape(
         groups, slot_count, features
     )
-    incoming = lax.all_to_all(outgoing, "dp", split_axis=0, concat_axis=0, tiled=True).reshape(
+    incoming = lax.all_to_all(outgoing, DP, split_axis=0, concat_axis=0, tiled=True).reshape(
         groups * slot_count, features
     )
     pick_rows = take_rows[0]
     packed = jnp.take(incoming, pick_rows, axis=0)
-    full_qkv, full_out = gather_weights(qkv_weight, out_weight)
+    qkv_low, qkv_high, full_out = gather_weights(qkv_weight, out_weight)
     values, unit_rows, inv_dev, normed = normalize(packed, norm_gain)
-    projected = jnp.dot(normed, full_qkv, preferred_element_type=jnp.float32).astype(jnp.bfloat16)
-    queries = projected[:, :all_heads]
-    keyval = projected[:, all_heads:]
+    proj_low = jnp.dot(normed, qkv_low, preferred_element_type=jnp.float32).astype(jnp.bfloat16)
+    proj_high = jnp.dot(normed, qkv_high, preferred_element_type=jnp.float32).astype(jnp.bfloat16)
+    queries = proj_low[:, :all_heads]
+    keyval = jnp.concatenate([proj_low[:, all_heads:], proj_high], axis=1)
     seg_plus = segments[0] + 1
     wide_kv, wide_seg = (
         extended(keyval, (("tensor", 0),), MOST),
@@ -159,8 +164,9 @@
     center = center.at[:MOST].add(arrived[:MOST])
     center = center.at[own_rows - MOST :].add(arrived[3 * MOST :])
     grad_proj = jnp.concatenate([grad_query, center], axis=1).astype(jnp.bfloat16)
-    grad_normed = lax.dot_general(
-        grad_proj, full_qkv, (((1,), (1,)), ((), ())), preferred_element_type=jnp.float32
+    low_cols = qkv_low.shape[1]
+    grad_normed = rows_dot(grad_proj[:, :low_cols], qkv_low) + rows_dot(
+        grad_proj[:, low_cols:], qkv_high
     )
     scaled = grad_normed * norm_gain
     grad_unit = (
@@ -173,7 +179,7 @@
         jnp.zeros((groups * slot_count, features), jnp.bfloat16).at[pick_rows].set(grad_packed)
     )
     back_slots = back_slots.reshape(groups, slot_count, features)
-    returned = lax.all_to_all(back_slots, "dp", split_axis=0, concat_axis=0, tiled=True).reshape(
+    returned = lax.all_to_all(back_slots, DP, split_axis=0, concat_axis=0, tiled=True).reshape(
         groups * slot_count, features
     )
     patch_grad = (
@@ -183,19 +189,21 @@
 
 
 def solution(mesh):
+    rows, cols = mesh.devices.shape
+    split = Mesh(mesh.devices.reshape(rows // 2, 2, cols), DP + ("tensor",))
     return jax.shard_map(
         local,
-        mesh=mesh,
+        mesh=split,
         in_specs=(
-            P("dp", "tensor", None),
-            P("dp", "tensor", None, None),
-            P("dp", "tensor"),
-            P("dp", "tensor"),
+            P(DP, "tensor", None),
+            P(DP, "tensor", None, None),
+            P(DP, "tensor"),
+            P(DP, "tensor"),
             P(),
             P("tensor", None),
             P("tensor", None),
-            P("dp", "tensor", None),
+            P(DP, "tensor", None),
         ),
-        out_specs=(P("dp", "tensor", None), P("dp", "tensor", None)),
+        out_specs=(P(DP, "tensor", None), P(DP, "tensor", None)),
         check_vma=False,
     )

time: 199 us -> 219 us (1.10)
  waiting for transfers between devices: 86.4 us -> 96.3 us
  other arithmetic: 17.8 us -> 24 us
  matrix products: 29.4 us -> 33.8 us
    all_gather x1, waiting for transfers between devices: 35.2 us -> 48.5 us  [gather_weights(): got = lax.all_gather(mine, ('dl', 'tensor'), axis=0, tiled=False)]
    dot_general x2 -> x4, matrix products: 1.84 us -> 9.91 us  [rows_dot(): lax.dot_general(a, b, (((1,), (1,)), ((), ())), preferred_element_type=jn...]
    dot_general x2, matrix products: 11.1 us -> 7.47 us  [the longest x1 4.05 us: local(): jnp.dot(normed, qkv_low, preferred_element_type=jnp.float32)]
    all_to_all x2, waiting for transfers between devices: 38.2 us -> 35 us  [the longest x1 23 us: local(): lax.all_to_all(outgoing, DP, split_axis=0, concat_axis=0, tiled=True)]
  transfers between devices with their start and end apart: 9 -> 9, of which waited for: 5 -> 5; matrix products, arithmetic and copies ran while one was open for 16% -> 17% of each run, Pallas kernels for 0% -> 0%
where the time goes in v6:
time: 219 us; the launch traced here: 217 us
  waiting for transfers between devices  96.3 us (44%)
  starting transfers between devices  35.6 us (16%)
  matrix products  33.8 us (15%)
  other arithmetic  24 us (11%)
  between operations  14.7 us (7%)
  local copies, waits for them, and re-layouts  13 us (6%)
    all_gather x1, waiting for transfers between devices, gather_weights(): got = lax.all_gather(mine, ('dl', 'tensor'), axis=0, tiled=False)  48.5 us
    all_to_all x1, waiting for transfers between devices, local(): lax.all_to_all(outgoing, DP, split_axis=0, concat_axis=0, tiled=True)  23 us
    all_to_all x1, waiting for transfers between devices, local(): lax.all_to_all(back_slots, DP, split_axis=0, concat_axis=0, tiled=True)  12 us
    all_to_all x1, starting transfers between devices, local(): lax.all_to_all(outgoing, DP, split_axis=0, concat_axis=0, tiled=True)  10.3 us
    ppermute x3, waiting for transfers between devices, extended(): lax.ppermute(lax.slice_in_dim(block, block.shape[dim] - width, None, axis...  10.2 us
    all_to_all x1, starting transfers between devices, local(): lax.all_to_all(back_slots, DP, split_axis=0, concat_axis=0, tiled=True)  10.1 us
    dot_general x4, matrix products, rows_dot(): lax.dot_general(a, b, (((1,), (1,)), ((), ())), preferred_element_type=jn...  9.91 us
    ppermute x3, starting transfers between devices, extended(): lax.ppermute(lax.slice_in_dim(block, 0, width, axis=dim), axis, backward)  9.16 us
  transfers between devices with their start and end apart: 9, of which 5 were waited for; matrix products, arithmetic and copies ran while one was open for 17% of the time, Pallas kernels for 0%

profile of v6, /device:TPU:66, one launch (start us, length us, event | category | flops | bytes accessed | tf_op | source)
XLA Modules:
  0.0 217.4 jit_solution(283247854983421351)
XLA Ops:
  12.2 3.6 %collective-permute-start.1 = (s32[96]{0:T(128)S(1)}, s32[96]{0:T(128)S(1)}, u32[]{:S(2)}, u32[]{:S(2)}) collective-permute-start(s32[96]{0:T(128)S(1)} %get-tuple-element.41), channel_id=1, source_target_pairs={{1,0},{2,1},{3,2},{4,3},{5,4},{6,5},{7,6},{8,7},{9,8},{10,9},{11,1... | collective-permute-start | bytes 1160 | tf_op jit(solution)/shard_map/ppermute | solution.py:19
  19.3 10.3 %all-to-all-start = ((bf16[32,6,1792]{2,1,0:T(8,128)(2,1)}), bf16[32,6,1792]{2,1,0:T(8,128)(2,1)S(1)}, u32[]{:S(2)}, u32[]{:S(2)}) async-start(bf16[32,6,1792]{2,1,0:T(8,128)(2,1)} %broadcast_select_fusion), calls=%async_computation | async-start | bytes 1835008 | tf_op jit(solution)/shard_map/all_to_all | solution.py:131
  32.8 23.0 %all-to-all-done = bf16[32,6,1792]{2,1,0:T(8,128)(2,1)S(1)} async-done(((bf16[32,6,1792]{2,1,0:T(8,128)(2,1)}), bf16[32,6,1792]{2,1,0:T(8,128)(2,1)S(1)}, u32[]{:S(2)}, u32[]{:S(2)}) %all-to-all-start) | async-done | bytes 688160 | tf_op jit(solution)/shard_map/all_to_all | solution.py:131
  57.5 48.5 %all-gather.3.cloned.1.call-done = bf16[3584,1792]{1,0:T(8,128)(2,1)} async-done(((bf16[112,1792]{1,0:T(8,128)(2,1)}), bf16[3584,1792]{1,0:T(8,128)(2,1)}) %all-gather.3.cloned.1.call-update) | async-done | bytes 12845072 | tf_op jit(solution)/shard_map/all_gather | solution.py:34
  106.0 4.1 %fusion.14 = bf16[128,1792]{1,0:T(8,128)(2,1)S(1)} fusion(bf16[3584,1792]{1,0:T(8,128)(2,1)} %all-gather.3.cloned.1.call-done, f32[1792]{0:T(1024)S(1)} %copy-done.22, f32[128]{0:T(128)S(1)} %add_rsqrt_fusion, f32[128]{0:T(128)S(1)} %broadcast_multiply_fusion.2, bf16[128,1792]{1,0:T(8,128)(2,1)S(1)} %gather_fusion.1, pred[128]{0:T(512)(128)(4,1)S(1)} %compare_and_fusion.1), kind=kOutput, calls=%fused_computation.21 | convolution fusion | flops 823689216 | bytes 7348352 | tf_op jit(solution)/shard_map/dot_general | solution.py:138
  110.1 3.4 %fusion.32 = bf16[128,896]{1,0:T(8,128)(2,1)S(1)} fusion(bf16[3584,1792]{1,0:T(8,128)(2,1)} %all-gather.3.cloned.1.call-done, f32[1792]{0:T(1024)S(1)} %copy-done.22, f32[128]{0:T(128)S(1)} %add_rsqrt_fusion, f32[128]{0:T(128)S(1)} %broadcast_multiply_fusion.2, bf16[128,1792]{1,0:T(8,128)(2,1)S(1)} %gather_fusion.1, pred[128]{0:T(512)(128)(4,1)S(1)} %compare_and_fusion.1), kind=kOutput, calls=%fused_computation.41 | convolution fusion | flops 412532736 | bytes 3907712 | tf_op jit(solution)/shard_map/dot_general | solution.py:139
  114.5 2.1 collective-permute-start.2
  116.6 3.6 %collective-permute-start.3 = (bf16[96,1792]{1,0:T(8,128)(2,1)}, bf16[96,1792]{1,0:T(8,128)(2,1)}, u32[]{:S(2)}, u32[]{:S(2)}) collective-permute-start(bf16[96,1792]{1,0:T(8,128)(2,1)} %get-tuple-element.35), channel_id=1, source_target_pairs={{1,0},{2,1},{3,2},{4,3},{5,4},{6,5},{7,6},{8,7},{9,8},{10,9},{11,1... | collective-permute-start | bytes 1032200 | tf_op jit(solution)/shard_map/ppermute | solution.py:19
  121.2 2.0 fusion.17
  133.9 1.9 collective-permute-start.4
  136.0 10.2 %collective-permute-done.4 = f32[96,1792]{1,0:T(8,128)S(1)} collective-permute-done((f32[96,1792]{1,0:T(8,128)S(1)}, f32[96,1792]{1,0:T(8,128)S(1)}, u32[]{:S(2)}, u32[]{:S(2)}) %collective-permute-start.4) | collective-permute-done | bytes 688160 | tf_op jit(solution)/shard_map/ppermute | solution.py:16
  148.3 2.7 %convolution_select_fusion = f32[1024,896]{1,0:T(8,128)} fusion(bf16[1024,320]{0,1:T(8,128)(2,1)S(1)} %multiply_convert_fusion, bf16[320,1792]{1,0:T(8,128)(2,1)S(1)} %pad_maximum_fusion, s32[896]{0:T(1024)S(1)} %copy-done.10, s32[896]{0:T(1024)S(1)} %copy-done.11, pred[896]{0:T(1024)(128)(4,1)S(1)} %copy-done.18, s32[1024]{0:T(1024)S(1)} %copy-done.8, ...), kind=kOutput, calls=%fused_computation.30 | convolution fusion | flops 590872576 | bytes 4917248 | tf_op jit(solution)/shard_map/dot_general | solution.py:156
  151.1 3.0 %reduce_sum.77 = bf16[128,896]{1,0:T(8,128)(2,1)} reduce(f32[8,128,896]{2,1,0:T(8,128)} %bitcast.71, f32[]{:T(128)} %constant.146.clone.1), dimensions={0}, to_apply=%region_6.7 | reduce | flops 802816 | bytes 3899396 | tf_op jit(solution)/shard_map/reduce_sum | solution.py:89
  154.0 2.7 %collective-permute-done.5 = f32[96,1792]{1,0:T(8,128)S(1)} collective-permute-done((f32[96,1792]{1,0:T(8,128)S(1)}, f32[96,1792]{1,0:T(8,128)S(1)}, u32[]{:S(2)}, u32[]{:S(2)}) %collective-permute-start.5) | collective-permute-done | bytes 688160 | tf_op jit(solution)/shard_map/ppermute | solution.py:19
  156.9 5.0 %fusion.2 = f32[128,1792]{1,0:T(8,128)S(1)} fusion(bf16[3584,1792]{1,0:T(8,128)(2,1)} %all-gather.3.cloned.1.call-done, bf16[128,1792]{1,0:T(8,128)(2,1)S(1)} %convert.7, bf16[128,896]{1,0:T(8,128)(2,1)S(1)} %copy-done.6), kind=kOutput, calls=%fused_computation.6 | convolution fusion | flops 823001088 | bytes 8028160 | tf_op jit(solution)/shard_map/dot_general | solution.py:93
  162.0 3.0 %fusion.94 = (f32[128]{0:T(128)S(1)}, f32[128]{0:T(128)S(1)}, f32[128,1792]{1,0:T(8,128)S(1)}) fusion(f32[128]{0:T(128)S(1)} %copy-done.21, f32[128]{0:T(128)S(1)} %copy-done.16, bf16[128,1792]{1,0:T(8,128)(2,1)S(1)} %gather_fusion.1, pred[128]{0:T(512)(128)(4,1)S(1)} %copy-done.14, f32[1792]{0:T(1024)S(1)} %copy-done.23, f32[128,1792]{1,0:T(8,128)S(1)} %fusion.2, ...), kind=kOutput, calls=%fused_computation.140 | convolution fusion | flops 413105920 | bytes 5745152 | tf_op jit(solution)/shard_map/dot_general | solution.py:93
  165.1 2.6 %scatter_custom_fusion = bf16[192,1792]{1,0:T(8,128)(2,1)S(1)} fusion(s32[128]{0:T(128)} %copy-done.19, f32[128,1792]{1,0:T(8,128)S(1)} %get-tuple-element.48, f32[128]{0:T(128)S(1)} %broadcast_multiply_fusion, f32[128]{0:T(128)S(1)} %broadcast_multiply_fusion.1, f32[128]{0:T(128)S(1)} %copy-done.21, f32[128]{0:T(128)S(1)} %copy-done.16, ...), kind=kCustom, calls=%fused_computation.78 | custom fusion | flops 2523136 | bytes 2525824 | tf_op jit(solution)/shard_map/scatter | solution.py:179
  168.8 10.1 %all-to-all-start.1 = ((bf16[32,6,1792]{2,1,0:T(8,128)(2,1)}), bf16[32,6,1792]{2,1,0:T(8,128)(2,1)}, u32[]{:S(2)}, u32[]{:S(2)}) async-start(bf16[32,6,1792]{2,1,0:T(8,128)(2,1)} %reshape.347), calls=%async_computation.1 | async-start | bytes 1835008 | tf_op jit(solution)/shard_map/all_to_all | solution.py:182
  179.0 3.8 %convolution_select_fusion.1 = f32[1024,896]{1,0:T(8,128)} fusion(bf16[320,1792]{1,0:T(8,128)(2,1)} %copy-done.4, f32[1024,320]{0,1:T(8,128)S(1)} %copy-done.2, f32[1024]{0:T(1024)S(1)} %fusion.36, f32[1024]{0:T(1024)S(1)} %get-tuple-element.44, s32[896]{0:T(1024)S(1)} %copy-done.10, s32[896]{0:T(1024)S(1)} %copy-done.11, ...), kind=kOutput, calls=%fused_computation.31 | convolution fusion | flops 591855616 | bytes 5579648 | tf_op jit(solution)/shard_map/dot_general | solution.py:113
  182.8 2.2 %reduce_sum.75 = bf16[128,896]{1,0:T(8,128)(2,1)S(1)} reduce(f32[8,128,896]{2,1,0:T(8,128)} %bitcast.70, f32[]{:T(128)} %constant.146.clone.1), dimensions={0}, to_apply=%region_4.5 | reduce | flops 802816 | bytes 3899396 | tf_op jit(solution)/shard_map/reduce_sum | solution.py:89
  186.9 2.6 %fusion.26 = f32[1,128,896]{2,1,0:T(8,128)S(1)} fusion(bf16[128,1792]{0,1:T(8,128)(2,1)S(1)} %bitcast.73, bf16[3584,1792]{1,0:T(8,128)(2,1)} %all-gather.3.cloned.1.call-done), kind=kOutput, calls=%fused_computation.39 | convolution fusion | flops 411041792 | bytes 4128768 | tf_op jit(solution)/shard_map/dot_general | solution.py:49
  189.5 2.6 %fusion.29 = f32[1,128,896]{2,1,0:T(8,128)S(1)} fusion(bf16[128,1792]{0,1:T(8,128)(2,1)S(1)} %bitcast.72, bf16[3584,1792]{1,0:T(8,128)(2,1)} %all-gather.3.cloned.1.call-done), kind=kOutput, calls=%fused_computation.40 | convolution fusion | flops 411041792 | bytes 4128768 | tf_op jit(solution)/shard_map/dot_general | solution.py:49
  193.1 12.0 %all-to-all-done.1 = bf16[32,6,1792]{2,1,0:T(8,128)(2,1)} async-done(((bf16[32,6,1792]{2,1,0:T(8,128)(2,1)}), bf16[32,6,1792]{2,1,0:T(8,128)(2,1)}, u32[]{:S(2)}, u32[]{:S(2)}) %all-to-all-start.1) | async-done | bytes 688160 | tf_op jit(solution)/shard_map/all_to_all | solution.py:182
  206.4 3.2 %scatter_custom_fusion.1 = bf16[193,1792]{1,0:T(8,128)(2,1)S(1)} fusion(s32[192]{0:T(256)} %bitcast.81, bf16[192,1792]{1,0:T(8,128)(2,1)S(1)} %reshape.377, bf16[]{:T(256)} %constant.139.clone.1), kind=kCustom, calls=%fused_computation.91 | custom fusion | flops 344064 | bytes 692224 | tf_op jit(solution)/shard_map/scatter-add | solution.py:186
  (118 shorter events, 34.4 us)
Async XLA Ops:
  7.2 98.8 %all-gather.3.cloned.1.call-start = ((), (), s32[]{:S(2)}) async-start(), calls=%async_computation.2 | async-start | bytes 13246464 | tf_op jit(solution)/shard_map/all_gather | solution.py:34
  10.3 21.7 %collective-permute-start = (s32[96]{0:T(128)S(1)}, s32[96]{0:T(128)S(1)}, u32[]{:S(2)}, u32[]{:S(2)}) collective-permute-start(s32[96]{0:T(128)S(1)} %get-tuple-element.40), channel_id=1, source_target_pairs={{0,1},{1,2},{2,3},{3,4},{4,5},{5,6},{6,7},{7,8},{8,9},{9,10},{10,1... | collective-permute-start | bytes 1160 | tf_op jit(solution)/shard_map/ppermute | solution.py:16
  12.2 19.8 %collective-permute-start.1 = (s32[96]{0:T(128)S(1)}, s32[96]{0:T(128)S(1)}, u32[]{:S(2)}, u32[]{:S(2)}) collective-permute-start(s32[96]{0:T(128)S(1)} %get-tuple-element.41), channel_id=1, source_target_pairs={{1,0},{2,1},{3,2},{4,3},{5,4},{6,5},{7,6},{8,7},{9,8},{10,9},{11,1... | collective-permute-start | bytes 1160 | tf_op jit(solution)/shard_map/ppermute | solution.py:19
  18.1 12.0 %copy-start.25 = (s32[1,128]{1,0:T(1,128)S(1)}, s32[1,128]{1,0:T(1,128)}, u32[]{:S(2)}) copy-start(s32[1,128]{1,0:T(1,128)} %param.14) | copy-start | bytes 1540
  19.3 36.5 %all-to-all-start = ((bf16[32,6,1792]{2,1,0:T(8,128)(2,1)}), bf16[32,6,1792]{2,1,0:T(8,128)(2,1)S(1)}, u32[]{:S(2)}, u32[]{:S(2)}) async-start(bf16[32,6,1792]{2,1,0:T(8,128)(2,1)} %broadcast_select_fusion), calls=%async_computation | async-start | bytes 1835008 | tf_op jit(solution)/shard_map/all_to_all | solution.py:131
  31.4 78.7 %copy-start.13 = (pred[128]{0:T(512)(128)(4,1)}, pred[128]{0:T(512)(128)(4,1)S(1)}, u32[]{:S(2)}) copy-start(pred[128]{0:T(512)(128)(4,1)S(1)} %compare_and_fusion.1) | copy-start | bytes 388
  56.0 50.0 %copy-start.22 = (f32[1792]{0:T(1024)S(1)}, f32[1792]{0:T(1024)}, u32[]{:S(2)}) copy-start(f32[1792]{0:T(1024)} %param.16) | copy-start | bytes 21508
  57.2 52.9 %copy-start.15 = (f32[128]{0:T(128)}, f32[128]{0:T(128)S(1)}, u32[]{:S(2)}) copy-start(f32[128]{0:T(128)S(1)} %broadcast_multiply_fusion.2) | copy-start | bytes 1540
  57.5 52.6 %copy-start.20 = (f32[128]{0:T(128)}, f32[128]{0:T(128)S(1)}, u32[]{:S(2)}) copy-start(f32[128]{0:T(128)S(1)} %add_rsqrt_fusion) | copy-start | bytes 1540
  106.0 14.2 %copy-start.3 = (bf16[3584,1792]{1,0:T(8,128)(2,1)S(1)}, bf16[3584,1792]{1,0:T(8,128)(2,1)}, u32[]{:S(2)}) copy-start(bf16[3584,1792]{1,0:T(8,128)(2,1)} %all-gather.3.cloned.1.call-done) | copy-start | bytes 38535172
  110.1 10.1 %copy-start.5 = (bf16[1,128,1792]{2,1,0:T(8,128)(2,1)S(1)}, bf16[1,128,1792]{2,1,0:T(8,128)(2,1)}, u32[]{:S(2)}) copy-start(bf16[1,128,1792]{2,1,0:T(8,128)(2,1)} %param.19) | copy-start | bytes 1376260
  114.5 14.0 %collective-permute-start.2 = (bf16[96,1792]{1,0:T(8,128)(2,1)}, bf16[96,1792]{1,0:T(8,128)(2,1)S(1)}, u32[]{:S(2)}, u32[]{:S(2)}) collective-permute-start(bf16[96,1792]{1,0:T(8,128)(2,1)} %get-tuple-element.34), channel_id=1, source_target_pairs={{0,1},{1,2},{2,3},{3,4},{4,5},{5,6},{6,7},{7,8},{8,9},{9,10},{10,1... | collective-permute-start | bytes 1032200 | tf_op jit(solution)/shard_map/ppermute | solution.py:16
  116.6 11.9 %collective-permute-start.3 = (bf16[96,1792]{1,0:T(8,128)(2,1)}, bf16[96,1792]{1,0:T(8,128)(2,1)}, u32[]{:S(2)}, u32[]{:S(2)}) collective-permute-start(bf16[96,1792]{1,0:T(8,128)(2,1)} %get-tuple-element.35), channel_id=1, source_target_pairs={{1,0},{2,1},{3,2},{4,3},{5,4},{6,5},{7,6},{8,7},{9,8},{10,9},{11,1... | collective-permute-start | bytes 1032200 | tf_op jit(solution)/shard_map/ppermute | solution.py:19
  129.6 18.7 %copy-start.4 = (bf16[320,1792]{1,0:T(8,128)(2,1)}, bf16[320,1792]{1,0:T(8,128)(2,1)S(1)}, u32[]{:S(2)}) copy-start(bf16[320,1792]{1,0:T(8,128)(2,1)S(1)} %pad_maximum_fusion) | copy-start | bytes 3440644
  133.9 12.3 %collective-permute-start.4 = (f32[96,1792]{1,0:T(8,128)S(1)}, f32[96,1792]{1,0:T(8,128)S(1)}, u32[]{:S(2)}, u32[]{:S(2)}) collective-permute-start(f32[96,1792]{1,0:T(8,128)S(1)} %fusion.51), channel_id=1, source_target_pairs={{0,1},{1,2},{2,3},{3,4},{4,5},{5,6},{6,7},{7,8},{8,9},{9,10},{10,1... | collective-permute-start | bytes 2064392 | tf_op jit(solution)/shard_map/ppermute | solution.py:16
  135.9 12.3 %copy-start.8 = (s32[1024]{0:T(1024)S(1)}, s32[1024]{0:T(1024)}, u32[]{:S(2)}) copy-start(s32[1024]{0:T(1024)} %get-tuple-element.51) | copy-start | bytes 12292
  135.9 12.3 %copy-start.9 = (s32[1024]{0:T(1024)S(1)}, s32[1024]{0:T(1024)}, u32[]{:S(2)}) copy-start(s32[1024]{0:T(1024)} %get-tuple-element.52) | copy-start | bytes 12292
  135.9 12.3 %copy-start.10 = (s32[896]{0:T(1024)S(1)}, s32[896]{0:T(1024)}, u32[]{:S(2)}) copy-start(s32[896]{0:T(1024)} %get-tuple-element.49) | copy-start | bytes 10756
  136.0 12.3 %copy-start.11 = (s32[896]{0:T(1024)S(1)}, s32[896]{0:T(1024)}, u32[]{:S(2)}) copy-start(s32[896]{0:T(1024)} %get-tuple-element.50) | copy-start | bytes 10756
  136.0 12.3 %copy-start.17 = (pred[1024]{0:T(1024)(128)(4,1)S(1)}, pred[1024]{0:T(1024)(128)(4,1)}, u32[]{:S(2)}) copy-start(pred[1024]{0:T(1024)(128)(4,1)} %fusion.85) | copy-start | bytes 3076
  136.0 12.3 %copy-start.18 = (pred[896]{0:T(1024)(128)(4,1)S(1)}, pred[896]{0:T(1024)(128)(4,1)}, u32[]{:S(2)}) copy-start(pred[896]{0:T(1024)(128)(4,1)} %fusion.84) | copy-start | bytes 2692
  146.3 10.4 %collective-permute-start.5 = (f32[96,1792]{1,0:T(8,128)S(1)}, f32[96,1792]{1,0:T(8,128)S(1)}, u32[]{:S(2)}, u32[]{:S(2)}) collective-permute-start(f32[96,1792]{1,0:T(8,128)S(1)} %get-tuple-element.28), channel_id=1, source_target_pairs={{1,0},{2,1},{3,2},{4,3},{5,4},{6,5},{7,6},{8,7},{9,8},{10,9},{11,1... | collective-permute-start | bytes 2064392 | tf_op jit(solution)/shard_map/ppermute | solution.py:19
  167.7 11.3 %copy-start.2 = (f32[1024,320]{0,1:T(8,128)S(1)}, f32[1024,320]{0,1:T(8,128)}, u32[]{:S(2)}) copy-start(f32[1024,320]{0,1:T(8,128)} %copy-done.1) | copy-start | bytes 3932164
  168.8 36.2 %all-to-all-start.1 = ((bf16[32,6,1792]{2,1,0:T(8,128)(2,1)}), bf16[32,6,1792]{2,1,0:T(8,128)(2,1)}, u32[]{:S(2)}, u32[]{:S(2)}) async-start(bf16[32,6,1792]{2,1,0:T(8,128)(2,1)} %reshape.347), calls=%async_computation.1 | async-start | bytes 1835008 | tf_op jit(solution)/shard_map/all_to_all | solution.py:182
  (11 other events, 50.1 us)
Sparse Core Ops, SparseCore 0:
  10.8 95.1 all-gather.2

commit v7 on v4

--- a/solution.py
+++ b/solution.py
@@ -121,13 +121,21 @@
     score_scale = HD ** (-0.5)
     patches = patch_rows[0]
     send_flat = send_rows.reshape(groups * slot_count)
+    lanes = 128
     outgoing = jnp.take(patches, send_flat, axis=0, mode="fill", fill_value=0).reshape(
-        groups, slot_count, features
+        groups, -1, lanes
     )
     incoming = lax.all_to_all(outgoing, "dp", split_axis=0, concat_axis=0, tiled=True).reshape(
         groups * slot_count, features
     )
     pick_rows = take_rows[0]
+    slot_total = groups * slot_count
+    slot_source = jnp.full((slot_total,), own_rows, jnp.int32).at[pick_rows].set(
+        jnp.arange(own_rows, dtype=jnp.int32)
+    )
+    row_slot = jnp.full((src_count + 1,), slot_total, jnp.int32).at[send_flat].set(
+        jnp.arange(slot_total, dtype=jnp.int32)
+    )[:src_count]
     packed = jnp.take(incoming, pick_rows, axis=0)
     full_qkv, full_out = gather_weights(qkv_weight, out_weight)
     values, unit_rows, inv_dev, normed = normalize(packed, norm_gain)
@@ -169,16 +177,12 @@
         - unit_rows * jnp.mean(scaled * unit_rows, axis=-1, keepdims=True)
     )
     grad_packed = (grad_rows.astype(jnp.float32) + inv_dev * grad_unit).astype(jnp.bfloat16)
-    back_slots = (
-        jnp.zeros((groups * slot_count, features), jnp.bfloat16).at[pick_rows].set(grad_packed)
-    )
-    back_slots = back_slots.reshape(groups, slot_count, features)
+    back_slots = jnp.take(grad_packed, slot_source, axis=0, mode="fill", fill_value=0)
+    back_slots = back_slots.reshape(groups, -1, lanes)
     returned = lax.all_to_all(back_slots, "dp", split_axis=0, concat_axis=0, tiled=True).reshape(
-        groups * slot_count, features
-    )
-    patch_grad = (
-        jnp.zeros((src_count + 1, features), jnp.bfloat16).at[send_flat].add(returned)[:src_count]
-    )
+        slot_total, features
+    )
+    patch_grad = jnp.take(returned, row_slot, axis=0, mode="fill", fill_value=0)
     return (layer_out[None], patch_grad[None])
 
 

time: 199 us -> 198 us (level)
  local copies, waits for them, and re-layouts: 13.8 us -> 20.9 us
  waiting for transfers between devices: 86.4 us -> 79.4 us
    all_to_all x1, waiting for transfers between devices: 25.9 us -> 20.5 us  [local(): lax.all_to_all(outgoing, 'dp', split_axis=0, concat_axis=0, tiled=True)]
    gather x0 -> x3, local copies, waits for them, and re-layouts: none -> 5.2 us  [the longest x2 4.06 us: local(): jnp.take(grad_packed, slot_source, axis=0, mode='fill', fill_value=0)]
    all_to_all x1, waiting for transfers between devices: 12.3 us -> 7.96 us  [local(): lax.all_to_all(back_slots, 'dp', split_axis=0, concat_axis=0, tiled=True)]
    all_gather x1, waiting for transfers between devices: 35.2 us -> 38.5 us  [gather_weights(): lax.all_gather(jnp.concatenate([qkv_weight, out_wide], axis=1), 'tensor',...]
    scatter-add x1 -> x0, other arithmetic: 3.1 us -> none  [local(): jnp.zeros((src_count + 1, features), jnp.bfloat16).at[send_flat]]
    concatenate x3, other arithmetic: 0.26 us -> 3.01 us  [local(): grad_window = jnp.concatenate([grad_key, grad_value], axis=1)]
    scatter x1 -> x0, other arithmetic: 2.36 us -> none  [local(): jnp.zeros((groups * slot_count, features), jnp.bfloat16).at[pick_rows]]
    scatter x0 -> x2, local copies, waits for them, and re-layouts: none -> 2.17 us  [the longest x1 1.2 us: local(): jnp.full((src_count + 1,), slot_total, jnp.int32).at[send_flat]]
  transfers between devices with their start and end apart: 9 -> 9, of which waited for: 5 -> 5; matrix products, arithmetic and copies ran while one was open for 16% -> 18% of each run, Pallas kernels for 0% -> 0%
where the time goes in v7:
time: 198 us; the launch traced here: 197 us
  waiting for transfers between devices  79.4 us (40%)
  starting transfers between devices  36.5 us (18%)
  matrix products  29.4 us (15%)
  local copies, waits for them, and re-layouts  20.9 us (11%)
  other arithmetic  16.3 us (8%)
  between operations  14.8 us (7%)
    all_gather x1, waiting for transfers between devices, gather_weights(): lax.all_gather(jnp.concatenate([qkv_weight, out_wide], axis=1), 'tensor',...  38.5 us
    all_to_all x1, waiting for transfers between devices, local(): lax.all_to_all(outgoing, 'dp', split_axis=0, concat_axis=0, tiled=True)  20.5 us
    ppermute x3, starting transfers between devices, extended(): lax.ppermute(lax.slice_in_dim(block, 0, width, axis=dim), axis, backward)  10.3 us
    all_to_all x1, starting transfers between devices, local(): lax.all_to_all(outgoing, 'dp', split_axis=0, concat_axis=0, tiled=True)  10.3 us
    all_to_all x1, starting transfers between devices, local(): lax.all_to_all(back_slots, 'dp', split_axis=0, concat_axis=0, tiled=True)  9.85 us
    ppermute x3, waiting for transfers between devices, extended(): lax.ppermute(lax.slice_in_dim(block, block.shape[dim] - width, None, axis...  8.96 us
    all_to_all x1, waiting for transfers between devices, local(): lax.all_to_all(back_slots, 'dp', split_axis=0, concat_axis=0, tiled=True)  7.96 us
    ppermute x3, starting transfers between devices, extended(): lax.ppermute(lax.slice_in_dim(block, block.shape[dim] - width, None, axis...  6.09 us
  transfers between devices with their start and end apart: 9, of which 5 were waited for; matrix products, arithmetic and copies ran while one was open for 18% of the time, Pallas kernels for 0%

profile of v7, /device:TPU:66, one launch (start us, length us, event | category | flops | bytes accessed | tf_op | source)
XLA Modules:
  0.0 197.3 jit_solution(15238915642124723779)
XLA Ops:
  8.3 2.1 %pad_maximum_fusion.1 = bf16[112,3584]{1,0:T(8,128)(2,1)} fusion(bf16[112,896]{1,0:T(8,128)(2,1)S(1)} %reshape.315, bf16[112,2688]{1,0:T(8,128)(2,1)} %param.19), kind=kLoop, calls=%fused_computation.58 | loop fusion | flops 1605632 | bytes 1605632 | tf_op jit(solution)/shard_map/concatenate | solution.py:29
  12.4 3.6 %collective-permute-start.1 = (s32[96]{0:T(128)S(1)}, s32[96]{0:T(128)S(1)}, u32[]{:S(2)}, u32[]{:S(2)}) collective-permute-start(s32[96]{0:T(128)S(1)} %get-tuple-element.38), channel_id=1, source_target_pairs={{1,0},{2,1},{3,2},{4,3},{5,4},{6,5},{7,6},{8,7},{9,8},{10,9},{11,1... | collective-permute-start | bytes 1160 | tf_op jit(solution)/shard_map/ppermute | solution.py:19
  19.3 10.3 %all-to-all-start = ((bf16[32,84,128]{2,1,0:T(8,128)(2,1)}), bf16[32,84,128]{2,1,0:T(8,128)(2,1)S(1)}, u32[]{:S(2)}, u32[]{:S(2)}) async-start(bf16[32,84,128]{2,1,0:T(8,128)(2,1)} %reshape.313), calls=%async_computation | async-start | bytes 1441792 | tf_op jit(solution)/shard_map/all_to_all | solution.py:128
  31.0 20.5 %all-to-all-done = bf16[32,84,128]{2,1,0:T(8,128)(2,1)S(1)} async-done(((bf16[32,84,128]{2,1,0:T(8,128)(2,1)}), bf16[32,84,128]{2,1,0:T(8,128)(2,1)S(1)}, u32[]{:S(2)}, u32[]{:S(2)}) %all-to-all-start) | async-done | bytes 688160 | tf_op jit(solution)/shard_map/all_to_all | solution.py:128
  53.8 38.5 %all-gather.2.cloned.1.call-done = bf16[1792,3584]{1,0:T(8,128)(2,1)} async-done(((bf16[112,3584]{1,0:T(8,128)(2,1)}), bf16[1792,3584]{1,0:T(8,128)(2,1)}) %all-gather.2.cloned.1.call-update) | async-done | bytes 12845072 | tf_op jit(solution)/shard_map/all_gather | solution.py:28
  92.4 5.5 %fusion.4 = bf16[128,2688]{1,0:T(8,128)(2,1)S(1)} fusion(bf16[1792,3584]{1,0:T(8,128)(2,1)} %all-gather.2.cloned.1.call-done, f32[1792]{0:T(1024)S(1)} %copy-done.14, f32[128]{0:T(128)S(1)} %add_rsqrt_fusion, f32[128]{0:T(128)S(1)} %broadcast_multiply_fusion.2, bf16[128,1792]{1,0:T(8,128)(2,1)S(1)} %gather_fusion, pred[128]{0:T(512)(128)(4,1)S(1)} %compare_and_fusion.3), kind=kOutput, calls=%fused_computation.11 | convolution fusion | flops 1234845696 | bytes 10788992 | tf_op jit(solution)/shard_map/dot_general | solution.py:142
  98.8 2.3 %collective-permute-start.2 = (bf16[96,1792]{1,0:T(8,128)(2,1)}, bf16[96,1792]{1,0:T(8,128)(2,1)S(1)}, u32[]{:S(2)}, u32[]{:S(2)}) collective-permute-start(bf16[96,1792]{1,0:T(8,128)(2,1)} %get-tuple-element.31), channel_id=1, source_target_pairs={{0,1},{1,2},{2,3},{3,4},{4,5},{5,6},{6,7},{7,8},{8,9},{9,10},{10,1... | collective-permute-start | bytes 1032200 | tf_op jit(solution)/shard_map/ppermute | solution.py:16
  101.1 4.5 %collective-permute-start.3 = (bf16[96,1792]{1,0:T(8,128)(2,1)}, bf16[96,1792]{1,0:T(8,128)(2,1)S(1)}, u32[]{:S(2)}, u32[]{:S(2)}) collective-permute-start(bf16[96,1792]{1,0:T(8,128)(2,1)} %get-tuple-element.32), channel_id=1, source_target_pairs={{1,0},{2,1},{3,2},{4,3},{5,4},{6,5},{7,6},{8,7},{9,8},{10,9},{11,1... | collective-permute-start | bytes 1032200 | tf_op jit(solution)/shard_map/ppermute | solution.py:19
  106.7 2.0 %fusion.10 = f32[1792,128]{1,0:T(8,128)} fusion(bf16[1792,3584]{1,0:T(8,128)(2,1)S(1)} %copy-done.5, bf16[128,1792]{1,0:T(8,128)(2,1)S(1)} %bitcast.73), kind=kOutput, calls=%fused_computation.19 | convolution fusion | flops 411041792 | bytes 4358144 | tf_op jit(solution)/shard_map/dot_general | solution.py:55
  122.2 9.0 %collective-permute-done.4 = f32[96,1792]{1,0:T(8,128)} collective-permute-done((f32[96,1792]{1,0:T(8,128)}, f32[96,1792]{1,0:T(8,128)}, u32[]{:S(2)}, u32[]{:S(2)}) %collective-permute-start.4) | collective-permute-done | bytes 688160 | tf_op jit(solution)/shard_map/ppermute | solution.py:16
  131.2 2.1 %pad_maximum_fusion.2 = (f32[96,1792]{1,0:T(8,128)}, f32[128,1792]{1,0:T(8,128)S(1)}) fusion(f32[320,896]{1,0:T(8,128)S(1)} %fusion.58, f32[320,896]{1,0:T(8,128)S(1)} %fusion.83, f32[128,1792]{1,0:T(8,128)S(1)} %fusion.39, f32[96,1792]{1,0:T(8,128)} %collective-permute-done.4), kind=kLoop, calls=%fused_computation.64 | loop fusion | flops 516096 | bytes 4358144 | tf_op jit(solution)/shard_map/concatenate | solution.py:163
  133.2 2.1 %collective-permute-start.5 = (f32[96,1792]{1,0:T(8,128)}, f32[96,1792]{1,0:T(8,128)S(1)}, u32[]{:S(2)}, u32[]{:S(2)}) collective-permute-start(f32[96,1792]{1,0:T(8,128)} %get-tuple-element.29), channel_id=1, source_target_pairs={{1,0},{2,1},{3,2},{4,3},{5,4},{6,5},{7,6},{8,7},{9,8},{10,9},{11,1... | collective-permute-start | bytes 2064392 | tf_op jit(solution)/shard_map/ppermute | solution.py:19
  135.4 2.8 %convolution_select_fusion = f32[1024,896]{1,0:T(8,128)} fusion(bf16[1024,320]{0,1:T(8,128)(2,1)S(1)} %copy-done.10, bf16[320,1792]{1,0:T(8,128)(2,1)S(1)} %copy-done.8, s32[896]{0:T(1024)S(1)} %get-tuple-element.46, s32[896]{0:T(1024)S(1)} %get-tuple-element.47, pred[896]{0:T(1024)(128)(4,1)S(1)} %fusion.68, s32[1024]{0:T(1024)S(1)} %get-tuple-element.48, ...), kind=kOutput, calls=%fused_computation.27 | convolution fusion | flops 590872576 | bytes 4917248 | tf_op jit(solution)/shard_map/dot_general | solution.py:159
  138.2 2.3 %reduce_sum.77 = bf16[128,896]{1,0:T(8,128)(2,1)S(1)} reduce(f32[8,128,896]{2,1,0:T(8,128)} %bitcast.68, f32[]{:T(128)} %constant.148.clone.1), dimensions={0}, to_apply=%region_7.9 | reduce | flops 802816 | bytes 3899396 | tf_op jit(solution)/shard_map/reduce_sum | solution.py:85
  140.5 3.4 %collective-permute-done.5 = f32[96,1792]{1,0:T(8,128)S(1)} collective-permute-done((f32[96,1792]{1,0:T(8,128)}, f32[96,1792]{1,0:T(8,128)S(1)}, u32[]{:S(2)}, u32[]{:S(2)}) %collective-permute-start.5) | collective-permute-done | bytes 688160 | tf_op jit(solution)/shard_map/ppermute | solution.py:19
  144.1 5.6 %fusion.79 = (f32[128]{0:T(128)S(1)}, f32[128]{0:T(128)S(1)}, f32[128,1792]{1,0:T(8,128)S(1)}) fusion(f32[128]{0:T(128)S(1)} %add_rsqrt_fusion, f32[128]{0:T(128)S(1)} %broadcast_multiply_fusion.2, bf16[128,1792]{1,0:T(8,128)(2,1)S(1)} %gather_fusion, pred[128]{0:T(512)(128)(4,1)S(1)} %compare_and_fusion.3, f32[1792]{0:T(1024)S(1)} %copy-done.14, ...), kind=kOutput, calls=%fused_computation.134 | convolution fusion | flops 1236336384 | bytes 11707520 | tf_op jit(solution)/shard_map/dot_general | solution.py:170
  150.2 2.0 %gather_fusion.1 = bf16[192,1792]{1,0:T(8,128)(2,1)} fusion(bf16[128,1792]{1,0:T(8,128)(2,1)S(1)} %fusion.37, s32[1024]{0:T(1024)S(1)} %pad_clamp_fusion.1), kind=kCustom, calls=%fused_computation.3 | custom fusion | bytes 1377024 | tf_op jit(solution)/shard_map/jit(_take)/gather | solution.py:180
  152.2 2.1 %gather.18 = bf16[32,84,128]{2,1,0:T(8,128)(2,1)S(1)} reshape(bf16[192,1792]{1,0:T(8,128)(2,1)} %gather_fusion.1) | data formatting | bytes 1376256 | tf_op jit(solution)/shard_map/jit(_take)/gather | solution.py:180
  155.6 9.9 %all-to-all-start.1 = ((bf16[32,84,128]{2,1,0:T(8,128)(2,1)}), bf16[32,84,128]{2,1,0:T(8,128)(2,1)S(1)}, u32[]{:S(2)}, u32[]{:S(2)}) async-start(bf16[32,84,128]{2,1,0:T(8,128)(2,1)} %broadcast_select_fusion), calls=%async_computation.1 | async-start | bytes 1441792 | tf_op jit(solution)/shard_map/all_to_all | solution.py:182
  165.5 3.8 %convolution_select_fusion.1 = f32[1024,896]{1,0:T(8,128)} fusion(bf16[320,1792]{1,0:T(8,128)(2,1)} %copy-done.7, f32[1024,320]{0,1:T(8,128)S(1)} %copy-done.4, f32[1024]{0:T(1024)S(1)} %fusion.26, f32[1024]{0:T(1024)S(1)} %get-tuple-element.41, s32[896]{0:T(1024)S(1)} %get-tuple-element.46, s32[896]{0:T(1024)S(1)} %get-tuple-element.47, ...), kind=kOutput, calls=%fused_computation.28 | convolution fusion | flops 591855616 | bytes 5579648 | tf_op jit(solution)/shard_map/dot_general | solution.py:109
  169.3 2.2 %reduce_sum.75 = bf16[128,896]{1,0:T(8,128)(2,1)S(1)} reduce(f32[8,128,896]{2,1,0:T(8,128)} %bitcast.67, f32[]{:T(128)} %constant.148.clone.1), dimensions={0}, to_apply=%region_4.6 | reduce | flops 802816 | bytes 3899396 | tf_op jit(solution)/shard_map/reduce_sum | solution.py:85
  173.5 2.6 %fusion.19 = f32[1,128,896]{2,1,0:T(8,128)S(1)} fusion(bf16[128,1792]{0,1:T(8,128)(2,1)S(1)} %bitcast.70, bf16[1792,3584]{1,0:T(8,128)(2,1)} %all-gather.2.cloned.1.call-done), kind=kOutput, calls=%fused_computation.36 | convolution fusion | flops 411041792 | bytes 4128768 | tf_op jit(solution)/shard_map/dot_general | solution.py:45
  176.1 2.6 %fusion.22 = f32[1,128,896]{2,1,0:T(8,128)S(1)} fusion(bf16[128,1792]{0,1:T(8,128)(2,1)S(1)} %bitcast.69, bf16[1792,3584]{1,0:T(8,128)(2,1)} %all-gather.2.cloned.1.call-done), kind=kOutput, calls=%fused_computation.37 | convolution fusion | flops 411041792 | bytes 4128768 | tf_op jit(solution)/shard_map/dot_general | solution.py:45
  179.6 8.0 %all-to-all-done.1 = bf16[32,84,128]{2,1,0:T(8,128)(2,1)S(1)} async-done(((bf16[32,84,128]{2,1,0:T(8,128)(2,1)}), bf16[32,84,128]{2,1,0:T(8,128)(2,1)S(1)}, u32[]{:S(2)}, u32[]{:S(2)}) %all-to-all-start.1) | async-done | bytes 688160 | tf_op jit(solution)/shard_map/all_to_all | solution.py:182
  (119 shorter events, 32.9 us)
Async XLA Ops:
  7.2 9.1 %copy-start = (bf16[1,192,1792]{2,1,0:T(8,128)(2,1)S(1)}, bf16[1,192,1792]{2,1,0:T(8,128)(2,1)}, u32[]{:S(2)}) copy-start(bf16[1,192,1792]{2,1,0:T(8,128)(2,1)} %param.14) | copy-start | bytes 2064388
  7.2 3.2 %copy-start.15 = (s32[1,128]{1,0:T(1,128)S(1)}, s32[1,128]{1,0:T(1,128)}, u32[]{:S(2)}) copy-start(s32[1,128]{1,0:T(1,128)} %param.17) | copy-start | bytes 1540
  7.2 8.9 %copy-start.13 = (s32[1,1,32,6]{2,1,3,0:T(1,128)S(1)}, s32[1,1,32,6]{2,1,3,0:T(1,128)}, u32[]{:S(2)}) copy-start(s32[1,1,32,6]{2,1,3,0:T(1,128)} %param.15) | copy-start | bytes 2308
  7.2 85.2 %all-gather.2.cloned.1.call-start = ((), (), s32[]{:S(2)}) async-start(), calls=%async_computation.2 | async-start | bytes 13647872 | tf_op jit(solution)/shard_map/all_gather | solution.py:28
  10.5 20.3 %collective-permute-start = (s32[96]{0:T(128)S(1)}, s32[96]{0:T(128)S(1)}, u32[]{:S(2)}, u32[]{:S(2)}) collective-permute-start(s32[96]{0:T(128)S(1)} %get-tuple-element.37), channel_id=1, source_target_pairs={{0,1},{1,2},{2,3},{3,4},{4,5},{5,6},{6,7},{7,8},{8,9},{9,10},{10,1... | collective-permute-start | bytes 1160 | tf_op jit(solution)/shard_map/ppermute | solution.py:16
  12.4 18.4 %collective-permute-start.1 = (s32[96]{0:T(128)S(1)}, s32[96]{0:T(128)S(1)}, u32[]{:S(2)}, u32[]{:S(2)}) collective-permute-start(s32[96]{0:T(128)S(1)} %get-tuple-element.38), channel_id=1, source_target_pairs={{1,0},{2,1},{3,2},{4,3},{5,4},{6,5},{7,6},{8,7},{9,8},{10,9},{11,1... | collective-permute-start | bytes 1160 | tf_op jit(solution)/shard_map/ppermute | solution.py:19
  17.5 12.2 %copy-start.16 = (s32[1,128]{1,0:T(1,128)S(1)}, s32[1,128]{1,0:T(1,128)}, u32[]{:S(2)}) copy-start(s32[1,128]{1,0:T(1,128)} %param.16) | copy-start | bytes 1540
  19.3 32.2 %all-to-all-start = ((bf16[32,84,128]{2,1,0:T(8,128)(2,1)}), bf16[32,84,128]{2,1,0:T(8,128)(2,1)S(1)}, u32[]{:S(2)}, u32[]{:S(2)}) async-start(bf16[32,84,128]{2,1,0:T(8,128)(2,1)} %reshape.313), calls=%async_computation | async-start | bytes 1441792 | tf_op jit(solution)/shard_map/all_to_all | solution.py:128
  52.3 40.1 %copy-start.14 = (f32[1792]{0:T(1024)S(1)}, f32[1792]{0:T(1024)}, u32[]{:S(2)}) copy-start(f32[1792]{0:T(1024)} %param.18) | copy-start | bytes 21508
  53.8 51.8 %copy-start.11 = (bf16[1,128,1792]{2,1,0:T(8,128)(2,1)S(1)}, bf16[1,128,1792]{2,1,0:T(8,128)(2,1)}, u32[]{:S(2)}) copy-start(bf16[1,128,1792]{2,1,0:T(8,128)(2,1)} %param.21) | copy-start | bytes 1376260
  92.4 13.3 %copy-start.5 = (bf16[1792,3584]{1,0:T(8,128)(2,1)S(1)}, bf16[1792,3584]{1,0:T(8,128)(2,1)}, u32[]{:S(2)}) copy-start(bf16[1792,3584]{1,0:T(8,128)(2,1)} %all-gather.2.cloned.1.call-done) | copy-start | bytes 38535172
  97.9 10.8 %copy-start.6 = (bf16[128,2688]{1,0:T(8,128)(2,1)}, bf16[128,2688]{1,0:T(8,128)(2,1)S(1)}, u32[]{:S(2)}) copy-start(bf16[128,2688]{1,0:T(8,128)(2,1)S(1)} %fusion.4) | copy-start | bytes 2064388
  98.8 14.5 %collective-permute-start.2 = (bf16[96,1792]{1,0:T(8,128)(2,1)}, bf16[96,1792]{1,0:T(8,128)(2,1)S(1)}, u32[]{:S(2)}, u32[]{:S(2)}) collective-permute-start(bf16[96,1792]{1,0:T(8,128)(2,1)} %get-tuple-element.31), channel_id=1, source_target_pairs={{0,1},{1,2},{2,3},{3,4},{4,5},{5,6},{6,7},{7,8},{8,9},{9,10},{10,1... | collective-permute-start | bytes 1032200 | tf_op jit(solution)/shard_map/ppermute | solution.py:16
  101.1 12.2 %collective-permute-start.3 = (bf16[96,1792]{1,0:T(8,128)(2,1)}, bf16[96,1792]{1,0:T(8,128)(2,1)S(1)}, u32[]{:S(2)}, u32[]{:S(2)}) collective-permute-start(bf16[96,1792]{1,0:T(8,128)(2,1)} %get-tuple-element.32), channel_id=1, source_target_pairs={{1,0},{2,1},{3,2},{4,3},{5,4},{6,5},{7,6},{8,7},{9,8},{10,9},{11,1... | collective-permute-start | bytes 1032200 | tf_op jit(solution)/shard_map/ppermute | solution.py:19
  109.0 3.2 %slice-start = ((bf16[128,2688]{1,0:T(8,128)(2,1)}), bf16[128,896]{1,0:T(8,128)(2,1)S(1)}, s32[]{:S(2)}) async-start(bf16[128,2688]{1,0:T(8,128)(2,1)} %copy-done.6), calls=%async_computation.3 | async-start | bytes 458752 | tf_op jit(solution)/shard_map/slice | solution.py:143
  118.6 12.6 %collective-permute-start.4 = (f32[96,1792]{1,0:T(8,128)}, f32[96,1792]{1,0:T(8,128)}, u32[]{:S(2)}, u32[]{:S(2)}) collective-permute-start(f32[96,1792]{1,0:T(8,128)} %fusion.41), channel_id=1, source_target_pairs={{0,1},{1,2},{2,3},{3,4},{4,5},{5,6},{6,7},{7,8},{8,9},{9,10},{10,1... | collective-permute-start | bytes 2064392 | tf_op jit(solution)/shard_map/ppermute | solution.py:16
  122.2 13.2 %copy-start.8 = (bf16[320,1792]{1,0:T(8,128)(2,1)S(1)}, bf16[320,1792]{1,0:T(8,128)(2,1)}, u32[]{:S(2)}) copy-start(bf16[320,1792]{1,0:T(8,128)(2,1)} %copy-done.7) | copy-start | bytes 3440644
  122.2 13.2 %copy-start.10 = (bf16[1024,320]{0,1:T(8,128)(2,1)S(1)}, bf16[1024,320]{0,1:T(8,128)(2,1)}, u32[]{:S(2)}) copy-start(bf16[1024,320]{0,1:T(8,128)(2,1)} %copy-done.9) | copy-start | bytes 1966084
  133.2 4.9 %copy-start.1 = (f32[128,1792]{1,0:T(8,128)}, f32[128,1792]{1,0:T(8,128)S(1)}, u32[]{:S(2)}) copy-start(f32[128,1792]{1,0:T(8,128)S(1)} %get-tuple-element.30) | copy-start | bytes 2752516
  133.2 10.7 %collective-permute-start.5 = (f32[96,1792]{1,0:T(8,128)}, f32[96,1792]{1,0:T(8,128)S(1)}, u32[]{:S(2)}, u32[]{:S(2)}) collective-permute-start(f32[96,1792]{1,0:T(8,128)} %get-tuple-element.29), channel_id=1, source_target_pairs={{1,0},{2,1},{3,2},{4,3},{5,4},{6,5},{7,6},{8,7},{9,8},{10,9},{11,1... | collective-permute-start | bytes 2064392 | tf_op jit(solution)/shard_map/ppermute | solution.py:19
  138.2 5.7 %copy-start.2 = (f32[128,1792]{1,0:T(8,128)S(1)}, f32[128,1792]{1,0:T(8,128)}, u32[]{:S(2)}) copy-start(f32[128,1792]{1,0:T(8,128)} %copy-done.1) | copy-start | bytes 2752516
  144.1 5.6 %copy-start.12 = (bf16[1,128,1792]{2,1,0:T(8,128)(2,1)S(1)}, bf16[1,128,1792]{2,1,0:T(8,128)(2,1)}, u32[]{:S(2)}) copy-start(bf16[1,128,1792]{2,1,0:T(8,128)(2,1)} %param.21) | copy-start | bytes 1376260
  152.2 13.2 %copy-start.4 = (f32[1024,320]{0,1:T(8,128)S(1)}, f32[1024,320]{0,1:T(8,128)}, u32[]{:S(2)}) copy-start(f32[1024,320]{0,1:T(8,128)} %copy-done.3) | copy-start | bytes 3932164
  155.6 32.0 %all-to-all-start.1 = ((bf16[32,84,128]{2,1,0:T(8,128)(2,1)}), bf16[32,84,128]{2,1,0:T(8,128)(2,1)S(1)}, u32[]{:S(2)}, u32[]{:S(2)}) async-start(bf16[32,84,128]{2,1,0:T(8,128)(2,1)} %broadcast_select_fusion), calls=%async_computation.1 | async-start | bytes 1441792 | tf_op jit(solution)/shard_map/all_to_all | solution.py:182
  (4 other events, 6.1 us)
Sparse Core Ops, SparseCore 0:
  10.5 81.7 all-gather.1

commit v8 on v4

--- a/solution.py
+++ b/solution.py
@@ -128,6 +128,10 @@
         groups * slot_count, features
     )
     pick_rows = take_rows[0]
+    slot_total = groups * slot_count
+    row_slot = jnp.full((src_count + 1,), slot_total, jnp.int32).at[send_flat].set(
+        jnp.arange(slot_total, dtype=jnp.int32)
+    )[:src_count]
     packed = jnp.take(incoming, pick_rows, axis=0)
     full_qkv, full_out = gather_weights(qkv_weight, out_weight)
     values, unit_rows, inv_dev, normed = normalize(packed, norm_gain)
@@ -158,9 +162,8 @@
     arrived = extended(rim_parts, (("tensor", 0),), MOST)
     center = center.at[:MOST].add(arrived[:MOST])
     center = center.at[own_rows - MOST :].add(arrived[3 * MOST :])
-    grad_proj = jnp.concatenate([grad_query, center], axis=1).astype(jnp.bfloat16)
-    grad_normed = lax.dot_general(
-        grad_proj, full_qkv, (((1,), (1,)), ((), ())), preferred_element_type=jnp.float32
+    grad_normed = rows_dot(grad_query.astype(jnp.bfloat16), full_qkv[:, :all_heads]) + rows_dot(
+        center.astype(jnp.bfloat16), full_qkv[:, all_heads:]
     )
     scaled = grad_normed * norm_gain
     grad_unit = (
@@ -170,14 +173,13 @@
     )
     grad_packed = (grad_rows.astype(jnp.float32) + inv_dev * grad_unit).astype(jnp.bfloat16)
     back_slots = (
-        jnp.zeros((groups * slot_count, features), jnp.bfloat16).at[pick_rows].set(grad_packed)
-    )
-    back_slots = back_slots.reshape(groups, slot_count, features)
-    returned = lax.all_to_all(back_slots, "dp", split_axis=0, concat_axis=0, tiled=True).reshape(
-        groups * slot_count, features
-    )
-    patch_grad = (
-        jnp.zeros((src_count + 1, features), jnp.bfloat16).at[send_flat].add(returned)[:src_count]
+        jnp.zeros((groups, slot_count, features), jnp.bfloat16)
+        .at[pick_rows // slot_count, pick_rows % slot_count]
+        .set(grad_packed)
+    )
+    returned = lax.all_to_all(back_slots, "dp", split_axis=0, concat_axis=0, tiled=True)
+    patch_grad = returned.at[row_slot // slot_count, row_slot % slot_count].get(
+        mode="fill", fill_value=0
     )
     return (layer_out[None], patch_grad[None])
 

time: 199 us -> 218 us (1.095)
  local copies, waits for them, and re-layouts: 13.8 us -> 35.9 us
  waiting for transfers between devices: 86.4 us -> 81.8 us
  matrix products: 29.4 us -> 32.2 us
  other arithmetic: 17.8 us -> 15.6 us
    scatter x0 -> x3, local copies, waits for them, and re-layouts: none -> 18.7 us  [the longest x2 17.5 us: local(): back_slots = jnp.zeros((groups, slot_count, features), jnp.bfloat16).at[p...]
    dot_general x2 -> x4, matrix products: 1.84 us -> 10.2 us  [rows_dot(): lax.dot_general(a, b, (((1,), (1,)), ((), ())), preferred_element_type=jn...]
    all_to_all x1, waiting for transfers between devices: 25.9 us -> 18 us  [local(): lax.all_to_all(outgoing, 'dp', split_axis=0, concat_axis=0, tiled=True)]
    all_gather x1, waiting for transfers between devices: 35.2 us -> 41.5 us  [gather_weights(): lax.all_gather(jnp.concatenate([qkv_weight, out_wide], axis=1), 'tensor',...]
    dot_general x1 -> x0, matrix products: 5.53 us -> none  [local(): lax.dot_general(grad_proj, full_qkv, (((1,), (1,)), ((), ())), preferred_...]
    gather x0 -> x1, local copies, waits for them, and re-layouts: none -> 4.2 us  [local(): returned.at[row_slot // slot_count, row_slot % slot_count]]
    scatter-add x1 -> x0, other arithmetic: 3.1 us -> none  [local(): jnp.zeros((src_count + 1, features), jnp.bfloat16).at[send_flat]]
    ppermute x3, waiting for transfers between devices: 2.71 us -> 0.01 us  [extended(): lax.ppermute(lax.slice_in_dim(block, 0, width, axis=dim), axis, backward)]
  transfers between devices with their start and end apart: 9 -> 9, of which waited for: 5 -> 4; matrix products, arithmetic and copies ran while one was open for 16% -> 17% of each run, Pallas kernels for 0% -> 0%
where the time goes in v8:
time: 218 us; the launch traced here: 217 us
  waiting for transfers between devices  81.8 us (38%)
  starting transfers between devices  36.6 us (17%)
  local copies, waits for them, and re-layouts  35.9 us (16%)
  matrix products  32.2 us (15%)
  other arithmetic  15.6 us (7%)
  between operations  14.7 us (7%)
    all_gather x1, waiting for transfers between devices, gather_weights(): lax.all_gather(jnp.concatenate([qkv_weight, out_wide], axis=1), 'tensor',...  41.5 us
    all_to_all x1, waiting for transfers between devices, local(): lax.all_to_all(outgoing, 'dp', split_axis=0, concat_axis=0, tiled=True)  18 us
    scatter x2, local copies, waits for them, and re-layouts, local(): back_slots = jnp.zeros((groups, slot_count, features), jnp.bfloat16).at[p...  17.5 us
    all_to_all x1, waiting for transfers between devices, local(): lax.all_to_all(back_slots, 'dp', split_axis=0, concat_axis=0, tiled=True)  12.1 us
    ppermute x3, starting transfers between devices, extended(): lax.ppermute(lax.slice_in_dim(block, 0, width, axis=dim), axis, backward)  10.3 us
    all_to_all x1, starting transfers between devices, local(): lax.all_to_all(outgoing, 'dp', split_axis=0, concat_axis=0, tiled=True)  10.2 us
    dot_general x4, matrix products, rows_dot(): lax.dot_general(a, b, (((1,), (1,)), ((), ())), preferred_element_type=jn...  10.2 us
    ppermute x3, waiting for transfers between devices, extended(): lax.ppermute(lax.slice_in_dim(block, block.shape[dim] - width, None, axis...  10.1 us
  transfers between devices with their start and end apart: 9, of which 4 were waited for; matrix products, arithmetic and copies ran while one was open for 17% of the time, Pallas kernels for 0%

profile of v8, /device:TPU:66, one launch (start us, length us, event | category | flops | bytes accessed | tf_op | source)
XLA Modules:
  0.0 216.7 jit_solution(49907777801493543)
XLA Ops:
  8.3 2.0 pad_maximum_fusion.1
  13.5 10.2 %all-to-all-start = ((bf16[32,6,1792]{2,1,0:T(8,128)(2,1)}), bf16[32,6,1792]{2,1,0:T(8,128)(2,1)S(1)}, u32[]{:S(2)}, u32[]{:S(2)}) async-start(bf16[32,6,1792]{2,1,0:T(8,128)(2,1)} %copy.27), calls=%async_computation | async-start | bytes 1835008 | tf_op jit(solution)/shard_map/all_to_all | solution.py:127
  25.8 3.6 %collective-permute-start.1 = (s32[96]{0:T(128)S(1)}, s32[96]{0:T(128)S(1)}, u32[]{:S(2)}, u32[]{:S(2)}) collective-permute-start(s32[96]{0:T(128)S(1)} %get-tuple-element.43), channel_id=1, source_target_pairs={{1,0},{2,1},{3,2},{4,3},{5,4},{6,5},{7,6},{8,7},{9,8},{10,9},{11,1... | collective-permute-start | bytes 1160 | tf_op jit(solution)/shard_map/ppermute | solution.py:19
  31.0 18.0 %all-to-all-done = bf16[32,6,1792]{2,1,0:T(8,128)(2,1)S(1)} async-done(((bf16[32,6,1792]{2,1,0:T(8,128)(2,1)}), bf16[32,6,1792]{2,1,0:T(8,128)(2,1)S(1)}, u32[]{:S(2)}, u32[]{:S(2)}) %all-to-all-start) | async-done | bytes 688160 | tf_op jit(solution)/shard_map/all_to_all | solution.py:127
  50.8 41.5 %all-gather.2.cloned.1.call-done = bf16[1792,3584]{1,0:T(8,128)(2,1)} async-done(((bf16[112,3584]{1,0:T(8,128)(2,1)}), bf16[1792,3584]{1,0:T(8,128)(2,1)}) %all-gather.2.cloned.1.call-update) | async-done | bytes 12845072 | tf_op jit(solution)/shard_map/all_gather | solution.py:28
  92.3 5.5 %fusion.4 = bf16[128,2688]{1,0:T(8,128)(2,1)S(1)} fusion(bf16[1792,3584]{1,0:T(8,128)(2,1)} %all-gather.2.cloned.1.call-done, f32[1792]{0:T(1024)S(1)} %copy-done.8, f32[128]{0:T(128)S(1)} %add_rsqrt_fusion, f32[128]{0:T(128)S(1)} %broadcast_multiply_fusion.2, bf16[128,1792]{1,0:T(8,128)(2,1)S(1)} %gather_fusion.1, pred[128]{0:T(512)(128)(4,1)S(1)} %compare_and_fusion.1), kind=kOutput, calls=%fused_computation.10 | convolution fusion | flops 1234845696 | bytes 10788992 | tf_op jit(solution)/shard_map/dot_general | solution.py:138
  98.8 2.3 %collective-permute-start.2 = (bf16[96,1792]{1,0:T(8,128)(2,1)}, bf16[96,1792]{1,0:T(8,128)(2,1)S(1)}, u32[]{:S(2)}, u32[]{:S(2)}) collective-permute-start(bf16[96,1792]{1,0:T(8,128)(2,1)} %get-tuple-element.30), channel_id=1, source_target_pairs={{0,1},{1,2},{2,3},{3,4},{4,5},{5,6},{6,7},{7,8},{8,9},{9,10},{10,1... | collective-permute-start | bytes 1032200 | tf_op jit(solution)/shard_map/ppermute | solution.py:16
  101.0 4.5 %collective-permute-start.3 = (bf16[96,1792]{1,0:T(8,128)(2,1)}, bf16[96,1792]{1,0:T(8,128)(2,1)S(1)}, u32[]{:S(2)}, u32[]{:S(2)}) collective-permute-start(bf16[96,1792]{1,0:T(8,128)(2,1)} %get-tuple-element.31), channel_id=1, source_target_pairs={{1,0},{2,1},{3,2},{4,3},{5,4},{6,5},{7,6},{8,7},{9,8},{10,9},{11,1... | collective-permute-start | bytes 1032200 | tf_op jit(solution)/shard_map/ppermute | solution.py:19
  106.6 2.0 fusion.15
  117.7 1.9 collective-permute-start.4
  119.8 10.1 %collective-permute-done.4 = f32[96,1792]{1,0:T(8,128)S(1)} collective-permute-done((f32[96,1792]{1,0:T(8,128)S(1)}, f32[96,1792]{1,0:T(8,128)S(1)}, u32[]{:S(2)}, u32[]{:S(2)}) %collective-permute-start.4) | collective-permute-done | bytes 688160 | tf_op jit(solution)/shard_map/ppermute | solution.py:16
  130.9 2.1 collective-permute-start.5
  133.1 2.7 %convolution_select_fusion = f32[1024,896]{1,0:T(8,128)} fusion(bf16[1024,320]{0,1:T(8,128)(2,1)S(1)} %multiply_convert_fusion, bf16[320,1792]{1,0:T(8,128)(2,1)S(1)} %pad_maximum_fusion, s32[896]{0:T(1024)S(1)} %get-tuple-element.51, s32[896]{0:T(1024)S(1)} %get-tuple-element.52, pred[896]{0:T(1024)(128)(4,1)S(1)} %fusion.72, ...), kind=kOutput, calls=%fused_computation.29 | convolution fusion | flops 590872576 | bytes 4917248 | tf_op jit(solution)/shard_map/dot_general | solution.py:155
  135.8 3.0 %reduce_sum.77 = bf16[128,896]{1,0:T(8,128)(2,1)} reduce(f32[8,128,896]{2,1,0:T(8,128)} %bitcast.85, f32[]{:T(128)} %constant.174.clone.1), dimensions={0}, to_apply=%region_8.9 | reduce | flops 802816 | bytes 3899396 | tf_op jit(solution)/shard_map/reduce_sum | solution.py:85
  138.8 3.0 %fusion.7 = f32[128,1792]{1,0:T(8,128)S(1)} fusion(bf16[1792,3584]{1,0:T(8,128)(2,1)} %all-gather.2.cloned.1.call-done, bf16[128,896]{1,0:T(8,128)(2,1)} %reduce_sum.77), kind=kOutput, calls=%fused_computation.11 | convolution fusion | flops 411041792 | bytes 4358144 | tf_op jit(solution)/shard_map/dot_general | solution.py:89
  143.1 5.3 %fusion.82 = (f32[128]{0:T(128)S(1)}, f32[128]{0:T(128)S(1)}, f32[128,1792]{1,0:T(8,128)S(1)}) fusion(f32[128]{0:T(128)S(1)} %add_rsqrt_fusion, f32[128]{0:T(128)S(1)} %broadcast_multiply_fusion.2, bf16[128,1792]{1,0:T(8,128)(2,1)S(1)} %gather_fusion.1, pred[128]{0:T(512)(128)(4,1)S(1)} %compare_and_fusion.1, f32[1792]{0:T(1024)S(1)} %copy-done.8, ...), kind=kOutput, calls=%fused_computation.144 | convolution fusion | flops 824377088 | bytes 9643136 | tf_op jit(solution)/shard_map/dot_general | solution.py:89
  149.7 16.2 %scatter_fusion = bf16[32,6,1792]{2,0,1:T(8,128)(2,1)S(1)} fusion(bf16[32,6,1792]{2,0,1:T(8,128)(2,1)S(1)} %broadcast_in_dim.62, s32[128]{0:T(128)S(1)} %get-tuple-element.40, bf16[128,1792]{1,0:T(8,128)(2,1)} %fusion.42), kind=kCustom, calls=%fused_computation.4 | custom fusion | bytes 1377280 | tf_op jit(solution)/shard_map/scatter | solution.py:178
  167.2 9.9 %all-to-all-start.1 = ((bf16[32,6,1792]{2,1,0:T(8,128)(2,1)}), bf16[32,6,1792]{2,1,0:T(8,128)(2,1)}, u32[]{:S(2)}, u32[]{:S(2)}) async-start(bf16[32,6,1792]{2,1,0:T(8,128)(2,1)} %copy.32), calls=%async_computation.1 | async-start | bytes 1835008 | tf_op jit(solution)/shard_map/all_to_all | solution.py:180
  177.2 3.8 %convolution_select_fusion.1 = f32[1024,896]{1,0:T(8,128)} fusion(bf16[320,1792]{1,0:T(8,128)(2,1)} %copy-done.3, f32[1024,320]{0,1:T(8,128)S(1)} %get-tuple-element.47, f32[1024]{0:T(1024)S(1)} %fusion.31, f32[1024]{0:T(1024)S(1)} %get-tuple-element.46, s32[896]{0:T(1024)S(1)} %get-tuple-element.51, s32[896]{0:T(1024)S(1)} %get-tuple-element.52, ...), kind=kOutput, calls=%fused_computation.30 | convolution fusion | flops 591855616 | bytes 5579648 | tf_op jit(solution)/shard_map/dot_general | solution.py:109
  181.0 2.2 %reduce_sum.75 = bf16[128,896]{1,0:T(8,128)(2,1)S(1)} reduce(f32[8,128,896]{2,1,0:T(8,128)} %bitcast.84, f32[]{:T(128)} %constant.174.clone.1), dimensions={0}, to_apply=%region_4.5 | reduce | flops 802816 | bytes 3899396 | tf_op jit(solution)/shard_map/reduce_sum | solution.py:85
  185.1 2.6 %fusion.24 = f32[1,128,896]{2,1,0:T(8,128)S(1)} fusion(bf16[128,1792]{0,1:T(8,128)(2,1)S(1)} %bitcast.87, bf16[1792,3584]{1,0:T(8,128)(2,1)} %all-gather.2.cloned.1.call-done), kind=kOutput, calls=%fused_computation.38 | convolution fusion | flops 411041792 | bytes 4128768 | tf_op jit(solution)/shard_map/dot_general | solution.py:45
  187.7 2.6 %fusion.27 = f32[1,128,896]{2,1,0:T(8,128)S(1)} fusion(bf16[128,1792]{0,1:T(8,128)(2,1)S(1)} %bitcast.86, bf16[1792,3584]{1,0:T(8,128)(2,1)} %all-gather.2.cloned.1.call-done), kind=kOutput, calls=%fused_computation.39 | convolution fusion | flops 411041792 | bytes 4128768 | tf_op jit(solution)/shard_map/dot_general | solution.py:45
  191.3 12.1 %all-to-all-done.1 = bf16[32,6,1792]{2,1,0:T(8,128)(2,1)} async-done(((bf16[32,6,1792]{2,1,0:T(8,128)(2,1)}), bf16[32,6,1792]{2,1,0:T(8,128)(2,1)}, u32[]{:S(2)}, u32[]{:S(2)}) %all-to-all-start.1) | async-done | bytes 688160 | tf_op jit(solution)/shard_map/all_to_all | solution.py:180
  204.7 4.2 %gather_fusion.2 = bf16[192,1792]{1,0:T(8,128)(2,1)S(1)} fusion(bf16[32,6,1792]{2,0,1:T(8,128)(2,1)S(1)} %copy.33, s32[192]{0:T(256)S(1)} %bitcast.83), kind=kCustom, calls=%fused_computation.2 | custom fusion | bytes 1377792 | tf_op jit(solution)/shard_map/gather | solution.py:181
  (96 shorter events, 30.5 us)
Async XLA Ops:
  7.2 3.4 %copy-start = (bf16[1,192,1792]{2,1,0:T(8,128)(2,1)S(1)}, bf16[1,192,1792]{2,1,0:T(8,128)(2,1)}, u32[]{:S(2)}) copy-start(bf16[1,192,1792]{2,1,0:T(8,128)(2,1)} %param.12) | copy-start | bytes 2064388
  7.2 3.2 %copy-start.6 = (s32[1,1,32,6]{2,1,3,0:T(1,128)S(1)}, s32[1,1,32,6]{2,1,3,0:T(1,128)}, u32[]{:S(2)}) copy-start(s32[1,1,32,6]{2,1,3,0:T(1,128)} %param.13) | copy-start | bytes 2308
  7.2 85.1 %all-gather.2.cloned.1.call-start = ((), (), s32[]{:S(2)}) async-start(), calls=%async_computation.2 | async-start | bytes 13647872 | tf_op jit(solution)/shard_map/all_gather | solution.py:28
  12.1 11.7 %copy-start.9 = (s32[1,128]{1,0:T(1,128)S(1)}, s32[1,128]{1,0:T(1,128)}, u32[]{:S(2)}) copy-start(s32[1,128]{1,0:T(1,128)} %param.15) | copy-start | bytes 1540
  12.2 17.3 %copy-start.10 = (s32[1,128]{1,0:T(1,128)S(1)}, s32[1,128]{1,0:T(1,128)}, u32[]{:S(2)}) copy-start(s32[1,128]{1,0:T(1,128)} %param.14) | copy-start | bytes 1540
  13.5 35.5 %all-to-all-start = ((bf16[32,6,1792]{2,1,0:T(8,128)(2,1)}), bf16[32,6,1792]{2,1,0:T(8,128)(2,1)S(1)}, u32[]{:S(2)}, u32[]{:S(2)}) async-start(bf16[32,6,1792]{2,1,0:T(8,128)(2,1)} %copy.27), calls=%async_computation | async-start | bytes 1835008 | tf_op jit(solution)/shard_map/all_to_all | solution.py:127
  23.9 6.9 %collective-permute-start = (s32[96]{0:T(128)S(1)}, s32[96]{0:T(128)S(1)}, u32[]{:S(2)}, u32[]{:S(2)}) collective-permute-start(s32[96]{0:T(128)S(1)} %get-tuple-element.42), channel_id=1, source_target_pairs={{0,1},{1,2},{2,3},{3,4},{4,5},{5,6},{6,7},{7,8},{8,9},{9,10},{10,1... | collective-permute-start | bytes 1160 | tf_op jit(solution)/shard_map/ppermute | solution.py:16
  25.8 5.0 %collective-permute-start.1 = (s32[96]{0:T(128)S(1)}, s32[96]{0:T(128)S(1)}, u32[]{:S(2)}, u32[]{:S(2)}) collective-permute-start(s32[96]{0:T(128)S(1)} %get-tuple-element.43), channel_id=1, source_target_pairs={{1,0},{2,1},{3,2},{4,3},{5,4},{6,5},{7,6},{8,7},{9,8},{10,9},{11,1... | collective-permute-start | bytes 1160 | tf_op jit(solution)/shard_map/ppermute | solution.py:19
  49.3 43.0 %copy-start.8 = (f32[1792]{0:T(1024)S(1)}, f32[1792]{0:T(1024)}, u32[]{:S(2)}) copy-start(f32[1792]{0:T(1024)} %param.16) | copy-start | bytes 21508
  50.8 54.8 %copy-start.4 = (bf16[1,128,1792]{2,1,0:T(8,128)(2,1)S(1)}, bf16[1,128,1792]{2,1,0:T(8,128)(2,1)}, u32[]{:S(2)}) copy-start(bf16[1,128,1792]{2,1,0:T(8,128)(2,1)} %param.19) | copy-start | bytes 1376260
  92.3 13.3 %copy-start.1 = (bf16[1792,3584]{1,0:T(8,128)(2,1)S(1)}, bf16[1792,3584]{1,0:T(8,128)(2,1)}, u32[]{:S(2)}) copy-start(bf16[1792,3584]{1,0:T(8,128)(2,1)} %all-gather.2.cloned.1.call-done) | copy-start | bytes 38535172
  97.9 10.8 %copy-start.2 = (bf16[128,2688]{1,0:T(8,128)(2,1)}, bf16[128,2688]{1,0:T(8,128)(2,1)S(1)}, u32[]{:S(2)}) copy-start(bf16[128,2688]{1,0:T(8,128)(2,1)S(1)} %fusion.4) | copy-start | bytes 2064388
  98.8 14.4 %collective-permute-start.2 = (bf16[96,1792]{1,0:T(8,128)(2,1)}, bf16[96,1792]{1,0:T(8,128)(2,1)S(1)}, u32[]{:S(2)}, u32[]{:S(2)}) collective-permute-start(bf16[96,1792]{1,0:T(8,128)(2,1)} %get-tuple-element.30), channel_id=1, source_target_pairs={{0,1},{1,2},{2,3},{3,4},{4,5},{5,6},{6,7},{7,8},{8,9},{9,10},{10,1... | collective-permute-start | bytes 1032200 | tf_op jit(solution)/shard_map/ppermute | solution.py:16
  101.0 12.2 %collective-permute-start.3 = (bf16[96,1792]{1,0:T(8,128)(2,1)}, bf16[96,1792]{1,0:T(8,128)(2,1)S(1)}, u32[]{:S(2)}, u32[]{:S(2)}) collective-permute-start(bf16[96,1792]{1,0:T(8,128)(2,1)} %get-tuple-element.31), channel_id=1, source_target_pairs={{1,0},{2,1},{3,2},{4,3},{5,4},{6,5},{7,6},{8,7},{9,8},{10,9},{11,1... | collective-permute-start | bytes 1032200 | tf_op jit(solution)/shard_map/ppermute | solution.py:19
  108.9 3.2 %slice-start.1 = ((bf16[128,2688]{1,0:T(8,128)(2,1)}), bf16[128,896]{1,0:T(8,128)(2,1)S(1)}, s32[]{:S(2)}) async-start(bf16[128,2688]{1,0:T(8,128)(2,1)} %copy-done.2), calls=%async_computation.4 | async-start | bytes 458752 | tf_op jit(solution)/shard_map/slice | solution.py:139
  112.1 1.1 slice-start
  113.3 19.8 %copy-start.3 = (bf16[320,1792]{1,0:T(8,128)(2,1)}, bf16[320,1792]{1,0:T(8,128)(2,1)S(1)}, u32[]{:S(2)}) copy-start(bf16[320,1792]{1,0:T(8,128)(2,1)S(1)} %pad_maximum_fusion) | copy-start | bytes 3440644
  117.7 2.0 copy-start.7
  117.7 12.3 %collective-permute-start.4 = (f32[96,1792]{1,0:T(8,128)S(1)}, f32[96,1792]{1,0:T(8,128)S(1)}, u32[]{:S(2)}, u32[]{:S(2)}) collective-permute-start(f32[96,1792]{1,0:T(8,128)S(1)} %fusion.46), channel_id=1, source_target_pairs={{0,1},{1,2},{2,3},{3,4},{4,5},{5,6},{6,7},{7,8},{8,9},{9,10},{10,1... | collective-permute-start | bytes 2064392 | tf_op jit(solution)/shard_map/ppermute | solution.py:16
  130.9 10.9 %collective-permute-start.5 = (f32[96,1792]{1,0:T(8,128)}, f32[96,1792]{1,0:T(8,128)}, u32[]{:S(2)}, u32[]{:S(2)}) collective-permute-start(f32[96,1792]{1,0:T(8,128)} %get-tuple-element.28), channel_id=1, source_target_pairs={{1,0},{2,1},{3,2},{4,3},{5,4},{6,5},{7,6},{8,7},{9,8},{10,9},{11,1... | collective-permute-start | bytes 2064392 | tf_op jit(solution)/shard_map/ppermute | solution.py:19
  143.1 5.3 %copy-start.5 = (bf16[1,128,1792]{2,1,0:T(8,128)(2,1)S(1)}, bf16[1,128,1792]{2,1,0:T(8,128)(2,1)}, u32[]{:S(2)}) copy-start(bf16[1,128,1792]{2,1,0:T(8,128)(2,1)} %param.19) | copy-start | bytes 1376260
  167.2 36.1 %all-to-all-start.1 = ((bf16[32,6,1792]{2,1,0:T(8,128)(2,1)}), bf16[32,6,1792]{2,1,0:T(8,128)(2,1)}, u32[]{:S(2)}, u32[]{:S(2)}) async-start(bf16[32,6,1792]{2,1,0:T(8,128)(2,1)} %copy.32), calls=%async_computation.1 | async-start | bytes 1835008 | tf_op jit(solution)/shard_map/all_to_all | solution.py:180
Sparse Core Ops, SparseCore 0:
  10.5 81.7 all-gather.1

commit v9 on v8

--- a/solution.py
+++ b/solution.py
@@ -173,14 +173,13 @@
     )
     grad_packed = (grad_rows.astype(jnp.float32) + inv_dev * grad_unit).astype(jnp.bfloat16)
     back_slots = (
-        jnp.zeros((groups, slot_count, features), jnp.bfloat16)
-        .at[pick_rows // slot_count, pick_rows % slot_count]
-        .set(grad_packed)
-    )
-    returned = lax.all_to_all(back_slots, "dp", split_axis=0, concat_axis=0, tiled=True)
-    patch_grad = returned.at[row_slot // slot_count, row_slot % slot_count].get(
-        mode="fill", fill_value=0
-    )
+        jnp.zeros((groups * slot_count, features), jnp.bfloat16).at[pick_rows].set(grad_packed)
+    )
+    back_slots = back_slots.reshape(groups, slot_count, features)
+    returned = lax.all_to_all(back_slots, "dp", split_axis=0, concat_axis=0, tiled=True).reshape(
+        groups * slot_count, features
+    )
+    patch_grad = jnp.take(returned, row_slot, axis=0, mode="fill", fill_value=0)
     return (layer_out[None], patch_grad[None])
 
 

time: 218 us -> 200 us (0.917)
  local copies, waits for them, and re-layouts: 35.9 us -> 16.2 us
    scatter x2 -> x0, local copies, waits for them, and re-layouts: 17.5 us -> none  [local(): back_slots = jnp.zeros((groups, slot_count, features), jnp.bfloat16).at[p...]
    all_to_all x1, waiting for transfers between devices: 18 us -> 24.5 us  [local(): lax.all_to_all(outgoing, 'dp', split_axis=0, concat_axis=0, tiled=True)]
    all_gather x1, waiting for transfers between devices: 41.5 us -> 35.4 us  [gather_weights(): lax.all_gather(jnp.concatenate([qkv_weight, out_wide], axis=1), 'tensor',...]
    reshape x0 -> x3, local copies, waits for them, and re-layouts: none -> 3.78 us  [the longest x1 1.38 us: local(): lax.all_to_all(back_slots, 'dp', split_axis=0, concat_axis=0, tiled=True)]
    gather x1, local copies, waits for them, and re-layouts: 4.2 us -> 1.14 us  [local(): patch_grad = jnp.take(returned, row_slot, axis=0, mode='fill', fill_value=0)]
    scatter x0 -> x1, other arithmetic: none -> 2.85 us  [local(): jnp.zeros((groups * slot_count, features), jnp.bfloat16).at[pick_rows]]
  transfers between devices with their start and end apart: 9 -> 9, of which waited for: 4 -> 4; matrix products, arithmetic and copies ran while one was open for 17% -> 18% of each run, Pallas kernels for 0% -> 0%
where the time goes in v9:
time: 200 us
  waiting for transfers between devices  82.5 us (41%)
  starting transfers between devices  36.4 us (18%)
  matrix products  32.9 us (16%)
  other arithmetic  17 us (8%)
  local copies, waits for them, and re-layouts  16.2 us (8%)
  between operations  14.6 us (7%)
    all_gather x1, waiting for transfers between devices, gather_weights(): lax.all_gather(jnp.concatenate([qkv_weight, out_wide], axis=1), 'tensor',...  35.4 us
    all_to_all x1, waiting for transfers between devices, local(): lax.all_to_all(outgoing, 'dp', split_axis=0, concat_axis=0, tiled=True)  24.5 us
    all_to_all x1, waiting for transfers between devices, local(): lax.all_to_all(back_slots, 'dp', split_axis=0, concat_axis=0, tiled=True)  12.4 us
    dot_general x4, matrix products, rows_dot(): lax.dot_general(a, b, (((1,), (1,)), ((), ())), preferred_element_type=jn...  10.9 us
    all_to_all x1, starting transfers between devices, local(): lax.all_to_all(outgoing, 'dp', split_axis=0, concat_axis=0, tiled=True)  10.2 us
    ppermute x3, waiting for transfers between devices, extended(): lax.ppermute(lax.slice_in_dim(block, block.shape[dim] - width, None, axis...  10.2 us
    ppermute x3, starting transfers between devices, extended(): lax.ppermute(lax.slice_in_dim(block, 0, width, axis=dim), axis, backward)  10.1 us
    all_to_all x1, starting transfers between devices, local(): lax.all_to_all(back_slots, 'dp', split_axis=0, concat_axis=0, tiled=True)  9.91 us
  transfers between devices with their start and end apart: 9, of which 4 were waited for; matrix products, arithmetic and copies ran while one was open for 18% of the time, Pallas kernels for 0%

profile of v9, /device:TPU:66, one launch (start us, length us, event | category | flops | bytes accessed | tf_op | source)
XLA Modules:
  0.0 199.6 jit_solution(11111978883086082957)
XLA Ops:
  8.3 2.0 %pad_maximum_fusion.1 = bf16[112,3584]{1,0:T(8,128)(2,1)} fusion(bf16[112,896]{1,0:T(8,128)(2,1)S(1)} %reshape.308, bf16[112,2688]{1,0:T(8,128)(2,1)} %param.19), kind=kLoop, calls=%fused_computation.60 | loop fusion | flops 1605632 | bytes 1605632 | tf_op jit(solution)/shard_map/concatenate | solution.py:29
  10.4 1.9 collective-permute-start
  12.4 3.6 %collective-permute-start.1 = (s32[96]{0:T(128)S(1)}, s32[96]{0:T(128)S(1)}, u32[]{:S(2)}, u32[]{:S(2)}) collective-permute-start(s32[96]{0:T(128)S(1)} %get-tuple-element.38), channel_id=1, source_target_pairs={{1,0},{2,1},{3,2},{4,3},{5,4},{6,5},{7,6},{8,7},{9,8},{10,9},{11,1... | collective-permute-start | bytes 1160 | tf_op jit(solution)/shard_map/ppermute | solution.py:19
  18.8 10.2 %all-to-all-start = ((bf16[32,6,1792]{2,1,0:T(8,128)(2,1)}), bf16[32,6,1792]{2,1,0:T(8,128)(2,1)S(1)}, u32[]{:S(2)}, u32[]{:S(2)}) async-start(bf16[32,6,1792]{2,1,0:T(8,128)(2,1)} %reshape.306), calls=%async_computation | async-start | bytes 1835008 | tf_op jit(solution)/shard_map/all_to_all | solution.py:127
  30.7 24.5 %all-to-all-done = bf16[32,6,1792]{2,1,0:T(8,128)(2,1)S(1)} async-done(((bf16[32,6,1792]{2,1,0:T(8,128)(2,1)}), bf16[32,6,1792]{2,1,0:T(8,128)(2,1)S(1)}, u32[]{:S(2)}, u32[]{:S(2)}) %all-to-all-start) | async-done | bytes 688160 | tf_op jit(solution)/shard_map/all_to_all | solution.py:127
  57.0 35.4 %all-gather.2.cloned.1.call-done = bf16[1792,3584]{1,0:T(8,128)(2,1)} async-done(((bf16[112,3584]{1,0:T(8,128)(2,1)}), bf16[1792,3584]{1,0:T(8,128)(2,1)}) %all-gather.2.cloned.1.call-update) | async-done | bytes 12845072 | tf_op jit(solution)/shard_map/all_gather | solution.py:28
  92.3 5.5 %fusion.4 = bf16[128,2688]{1,0:T(8,128)(2,1)S(1)} fusion(bf16[1792,3584]{1,0:T(8,128)(2,1)} %all-gather.2.cloned.1.call-done, f32[1792]{0:T(1024)S(1)} %copy-done.6, f32[128]{0:T(128)S(1)} %add_rsqrt_fusion, f32[128]{0:T(128)S(1)} %broadcast_multiply_fusion.2, bf16[128,1792]{1,0:T(8,128)(2,1)S(1)} %gather_fusion, pred[128]{0:T(512)(128)(4,1)S(1)} %compare_and_fusion.2), kind=kOutput, calls=%fused_computation.10 | convolution fusion | flops 1234845696 | bytes 10788992 | tf_op jit(solution)/shard_map/dot_general | solution.py:138
  98.8 2.3 %collective-permute-start.2 = (bf16[96,1792]{1,0:T(8,128)(2,1)}, bf16[96,1792]{1,0:T(8,128)(2,1)S(1)}, u32[]{:S(2)}, u32[]{:S(2)}) collective-permute-start(bf16[96,1792]{1,0:T(8,128)(2,1)} %get-tuple-element.31), channel_id=1, source_target_pairs={{0,1},{1,2},{2,3},{3,4},{4,5},{5,6},{6,7},{7,8},{8,9},{9,10},{10,1... | collective-permute-start | bytes 1032200 | tf_op jit(solution)/shard_map/ppermute | solution.py:16
  101.1 4.5 %collective-permute-start.3 = (bf16[96,1792]{1,0:T(8,128)(2,1)}, bf16[96,1792]{1,0:T(8,128)(2,1)S(1)}, u32[]{:S(2)}, u32[]{:S(2)}) collective-permute-start(bf16[96,1792]{1,0:T(8,128)(2,1)} %get-tuple-element.32), channel_id=1, source_target_pairs={{1,0},{2,1},{3,2},{4,3},{5,4},{6,5},{7,6},{8,7},{9,8},{10,9},{11,1... | collective-permute-start | bytes 1032200 | tf_op jit(solution)/shard_map/ppermute | solution.py:19
  106.6 2.0 fusion.15
  117.7 1.9 collective-permute-start.4
  119.7 10.2 %collective-permute-done.4 = f32[96,1792]{1,0:T(8,128)S(1)} collective-permute-done((f32[96,1792]{1,0:T(8,128)S(1)}, f32[96,1792]{1,0:T(8,128)S(1)}, u32[]{:S(2)}, u32[]{:S(2)}) %collective-permute-start.4) | collective-permute-done | bytes 688160 | tf_op jit(solution)/shard_map/ppermute | solution.py:16
  130.9 1.9 collective-permute-start.5
  132.8 2.7 %convolution_select_fusion = f32[1024,896]{1,0:T(8,128)} fusion(bf16[1024,320]{0,1:T(8,128)(2,1)S(1)} %multiply_convert_fusion, bf16[320,1792]{1,0:T(8,128)(2,1)S(1)} %pad_maximum_fusion, s32[896]{0:T(1024)S(1)} %get-tuple-element.46, s32[896]{0:T(1024)S(1)} %get-tuple-element.47, pred[896]{0:T(1024)(128)(4,1)S(1)} %fusion.79, ...), kind=kOutput, calls=%fused_computation.29 | convolution fusion | flops 590872576 | bytes 4917248 | tf_op jit(solution)/shard_map/dot_general | solution.py:155
  135.5 3.0 %reduce_sum.77 = bf16[128,896]{1,0:T(8,128)(2,1)} reduce(f32[8,128,896]{2,1,0:T(8,128)} %bitcast.70, f32[]{:T(128)} %constant.136.clone.1), dimensions={0}, to_apply=%region_6.8 | reduce | flops 802816 | bytes 3899396 | tf_op jit(solution)/shard_map/reduce_sum | solution.py:85
  138.5 3.0 %fusion.7 = f32[128,1792]{1,0:T(8,128)S(1)} fusion(bf16[1792,3584]{1,0:T(8,128)(2,1)} %all-gather.2.cloned.1.call-done, bf16[128,896]{1,0:T(8,128)(2,1)} %reduce_sum.77), kind=kOutput, calls=%fused_computation.11 | convolution fusion | flops 411041792 | bytes 4358144 | tf_op jit(solution)/shard_map/dot_general | solution.py:89
  142.8 6.1 %fusion.88 = (f32[128]{0:T(128)S(1)}, f32[128]{0:T(128)S(1)}, f32[128,1792]{1,0:T(8,128)}) fusion(f32[128]{0:T(128)S(1)} %add_rsqrt_fusion, f32[128]{0:T(128)S(1)} %broadcast_multiply_fusion.2, bf16[128,1792]{1,0:T(8,128)(2,1)S(1)} %gather_fusion, pred[128]{0:T(512)(128)(4,1)S(1)} %compare_and_fusion.2, f32[1792]{0:T(1024)S(1)} %copy-done.6, ...), kind=kOutput, calls=%fused_computation.135 | convolution fusion | flops 824377088 | bytes 9643136 | tf_op jit(solution)/shard_map/dot_general | solution.py:89
  148.9 2.8 %scatter_custom_fusion = bf16[192,1792]{1,0:T(8,128)(2,1)S(1)} fusion(s32[128]{0:T(128)S(1)} %fusion.81, f32[128,1792]{1,0:T(8,128)} %get-tuple-element.45, f32[128]{0:T(128)S(1)} %broadcast_multiply_fusion, f32[128]{0:T(128)S(1)} %broadcast_multiply_fusion.1, f32[128]{0:T(128)S(1)} %add_rsqrt_fusion, f32[128]{0:T(128)S(1)} %broadcast_multiply_fusion.2, ...), kind=kCustom, calls=%fused_computation.75 | custom fusion | flops 2523136 | bytes 2525698 | tf_op jit(solution)/shard_map/scatter | solution.py:176
  152.9 9.9 %all-to-all-start.1 = ((bf16[32,6,1792]{2,1,0:T(8,128)(2,1)}), bf16[32,6,1792]{2,1,0:T(8,128)(2,1)}, u32[]{:S(2)}, u32[]{:S(2)}) async-start(bf16[32,6,1792]{2,1,0:T(8,128)(2,1)} %reshape.315), calls=%async_computation.1 | async-start | bytes 1835008 | tf_op jit(solution)/shard_map/all_to_all | solution.py:179
  162.9 3.8 %convolution_select_fusion.1 = f32[1024,896]{1,0:T(8,128)} fusion(bf16[320,1792]{1,0:T(8,128)(2,1)} %copy-done.3, f32[1024,320]{0,1:T(8,128)S(1)} %get-tuple-element.42, f32[1024]{0:T(1024)S(1)} %fusion.31, f32[1024]{0:T(1024)S(1)} %get-tuple-element.41, s32[896]{0:T(1024)S(1)} %get-tuple-element.46, s32[896]{0:T(1024)S(1)} %get-tuple-element.47, ...), kind=kOutput, calls=%fused_computation.30 | convolution fusion | flops 591855616 | bytes 5579648 | tf_op jit(solution)/shard_map/dot_general | solution.py:109
  166.7 2.2 %reduce_sum.75 = bf16[128,896]{1,0:T(8,128)(2,1)S(1)} reduce(f32[8,128,896]{2,1,0:T(8,128)} %bitcast.69, f32[]{:T(128)} %constant.136.clone.1), dimensions={0}, to_apply=%region_4.6 | reduce | flops 802816 | bytes 3899396 | tf_op jit(solution)/shard_map/reduce_sum | solution.py:85
  170.8 2.6 %fusion.24 = f32[1,128,896]{2,1,0:T(8,128)S(1)} fusion(bf16[128,1792]{0,1:T(8,128)(2,1)S(1)} %bitcast.72, bf16[1792,3584]{1,0:T(8,128)(2,1)} %all-gather.2.cloned.1.call-done), kind=kOutput, calls=%fused_computation.38 | convolution fusion | flops 411041792 | bytes 4128768 | tf_op jit(solution)/shard_map/dot_general | solution.py:45
  173.4 2.6 %fusion.27 = f32[1,128,896]{2,1,0:T(8,128)S(1)} fusion(bf16[128,1792]{0,1:T(8,128)(2,1)S(1)} %bitcast.71, bf16[1792,3584]{1,0:T(8,128)(2,1)} %all-gather.2.cloned.1.call-done), kind=kOutput, calls=%fused_computation.39 | convolution fusion | flops 411041792 | bytes 4128768 | tf_op jit(solution)/shard_map/dot_general | solution.py:45
  176.9 12.4 %all-to-all-done.1 = bf16[32,6,1792]{2,1,0:T(8,128)(2,1)} async-done(((bf16[32,6,1792]{2,1,0:T(8,128)(2,1)}), bf16[32,6,1792]{2,1,0:T(8,128)(2,1)}, u32[]{:S(2)}, u32[]{:S(2)}) %all-to-all-start.1) | async-done | bytes 688160 | tf_op jit(solution)/shard_map/all_to_all | solution.py:179
  (91 shorter events, 27.8 us)
Async XLA Ops:
  7.2 9.1 %copy-start = (bf16[1,192,1792]{2,1,0:T(8,128)(2,1)S(1)}, bf16[1,192,1792]{2,1,0:T(8,128)(2,1)}, u32[]{:S(2)}) copy-start(bf16[1,192,1792]{2,1,0:T(8,128)(2,1)} %param.14) | copy-start | bytes 2064388
  7.2 3.2 %copy-start.7 = (s32[1,128]{1,0:T(1,128)S(1)}, s32[1,128]{1,0:T(1,128)}, u32[]{:S(2)}) copy-start(s32[1,128]{1,0:T(1,128)} %param.17) | copy-start | bytes 1540
  7.2 8.8 %copy-start.5 = (s32[1,1,32,6]{2,1,3,0:T(1,128)S(1)}, s32[1,1,32,6]{2,1,3,0:T(1,128)}, u32[]{:S(2)}) copy-start(s32[1,1,32,6]{2,1,3,0:T(1,128)} %param.15) | copy-start | bytes 2308
  7.2 85.1 %all-gather.2.cloned.1.call-start = ((), (), s32[]{:S(2)}) async-start(), calls=%async_computation.2 | async-start | bytes 13647872 | tf_op jit(solution)/shard_map/all_gather | solution.py:28
  10.4 20.0 %collective-permute-start = (s32[96]{0:T(128)S(1)}, s32[96]{0:T(128)S(1)}, u32[]{:S(2)}, u32[]{:S(2)}) collective-permute-start(s32[96]{0:T(128)S(1)} %get-tuple-element.37), channel_id=1, source_target_pairs={{0,1},{1,2},{2,3},{3,4},{4,5},{5,6},{6,7},{7,8},{8,9},{9,10},{10,1... | collective-permute-start | bytes 1160 | tf_op jit(solution)/shard_map/ppermute | solution.py:16
  12.4 18.1 %collective-permute-start.1 = (s32[96]{0:T(128)S(1)}, s32[96]{0:T(128)S(1)}, u32[]{:S(2)}, u32[]{:S(2)}) collective-permute-start(s32[96]{0:T(128)S(1)} %get-tuple-element.38), channel_id=1, source_target_pairs={{1,0},{2,1},{3,2},{4,3},{5,4},{6,5},{7,6},{8,7},{9,8},{10,9},{11,1... | collective-permute-start | bytes 1160 | tf_op jit(solution)/shard_map/ppermute | solution.py:19
  17.5 11.6 %copy-start.8 = (s32[1,128]{1,0:T(1,128)S(1)}, s32[1,128]{1,0:T(1,128)}, u32[]{:S(2)}) copy-start(s32[1,128]{1,0:T(1,128)} %param.16) | copy-start | bytes 1540
  18.8 36.4 %all-to-all-start = ((bf16[32,6,1792]{2,1,0:T(8,128)(2,1)}), bf16[32,6,1792]{2,1,0:T(8,128)(2,1)S(1)}, u32[]{:S(2)}, u32[]{:S(2)}) async-start(bf16[32,6,1792]{2,1,0:T(8,128)(2,1)} %reshape.306), calls=%async_computation | async-start | bytes 1835008 | tf_op jit(solution)/shard_map/all_to_all | solution.py:127
  55.4 36.9 %copy-start.6 = (f32[1792]{0:T(1024)S(1)}, f32[1792]{0:T(1024)}, u32[]{:S(2)}) copy-start(f32[1792]{0:T(1024)} %param.18) | copy-start | bytes 21508
  56.9 48.7 %copy-start.4 = (bf16[1,128,1792]{2,1,0:T(8,128)(2,1)S(1)}, bf16[1,128,1792]{2,1,0:T(8,128)(2,1)}, u32[]{:S(2)}) copy-start(bf16[1,128,1792]{2,1,0:T(8,128)(2,1)} %param.21) | copy-start | bytes 1376260
  92.3 13.3 %copy-start.1 = (bf16[1792,3584]{1,0:T(8,128)(2,1)S(1)}, bf16[1792,3584]{1,0:T(8,128)(2,1)}, u32[]{:S(2)}) copy-start(bf16[1792,3584]{1,0:T(8,128)(2,1)} %all-gather.2.cloned.1.call-done) | copy-start | bytes 38535172
  97.9 10.8 %copy-start.2 = (bf16[128,2688]{1,0:T(8,128)(2,1)}, bf16[128,2688]{1,0:T(8,128)(2,1)S(1)}, u32[]{:S(2)}) copy-start(bf16[128,2688]{1,0:T(8,128)(2,1)S(1)} %fusion.4) | copy-start | bytes 2064388
  98.8 14.4 %collective-permute-start.2 = (bf16[96,1792]{1,0:T(8,128)(2,1)}, bf16[96,1792]{1,0:T(8,128)(2,1)S(1)}, u32[]{:S(2)}, u32[]{:S(2)}) collective-permute-start(bf16[96,1792]{1,0:T(8,128)(2,1)} %get-tuple-element.31), channel_id=1, source_target_pairs={{0,1},{1,2},{2,3},{3,4},{4,5},{5,6},{6,7},{7,8},{8,9},{9,10},{10,1... | collective-permute-start | bytes 1032200 | tf_op jit(solution)/shard_map/ppermute | solution.py:16
  101.1 12.2 %collective-permute-start.3 = (bf16[96,1792]{1,0:T(8,128)(2,1)}, bf16[96,1792]{1,0:T(8,128)(2,1)S(1)}, u32[]{:S(2)}, u32[]{:S(2)}) collective-permute-start(bf16[96,1792]{1,0:T(8,128)(2,1)} %get-tuple-element.32), channel_id=1, source_target_pairs={{1,0},{2,1},{3,2},{4,3},{5,4},{6,5},{7,6},{8,7},{9,8},{10,9},{11,1... | collective-permute-start | bytes 1032200 | tf_op jit(solution)/shard_map/ppermute | solution.py:19
  109.0 3.2 %slice-start = ((bf16[128,2688]{1,0:T(8,128)(2,1)}), bf16[128,896]{1,0:T(8,128)(2,1)S(1)}, s32[]{:S(2)}) async-start(bf16[128,2688]{1,0:T(8,128)(2,1)} %copy-done.2), calls=%async_computation.3 | async-start | bytes 458752 | tf_op jit(solution)/shard_map/slice | solution.py:139
  112.1 1.1 slice-start.1
  113.3 19.5 %copy-start.3 = (bf16[320,1792]{1,0:T(8,128)(2,1)}, bf16[320,1792]{1,0:T(8,128)(2,1)S(1)}, u32[]{:S(2)}) copy-start(bf16[320,1792]{1,0:T(8,128)(2,1)S(1)} %pad_maximum_fusion) | copy-start | bytes 3440644
  117.7 12.3 %collective-permute-start.4 = (f32[96,1792]{1,0:T(8,128)S(1)}, f32[96,1792]{1,0:T(8,128)S(1)}, u32[]{:S(2)}, u32[]{:S(2)}) collective-permute-start(f32[96,1792]{1,0:T(8,128)S(1)} %fusion.46), channel_id=1, source_target_pairs={{0,1},{1,2},{2,3},{3,4},{4,5},{5,6},{6,7},{7,8},{8,9},{9,10},{10,1... | collective-permute-start | bytes 2064392 | tf_op jit(solution)/shard_map/ppermute | solution.py:16
  130.9 10.7 %collective-permute-start.5 = (f32[96,1792]{1,0:T(8,128)}, f32[96,1792]{1,0:T(8,128)}, u32[]{:S(2)}, u32[]{:S(2)}) collective-permute-start(f32[96,1792]{1,0:T(8,128)} %get-tuple-element.29), channel_id=1, source_target_pairs={{1,0},{2,1},{3,2},{4,3},{5,4},{6,5},{7,6},{8,7},{9,8},{10,9},{11,1... | collective-permute-start | bytes 2064392 | tf_op jit(solution)/shard_map/ppermute | solution.py:19
  152.9 36.4 %all-to-all-start.1 = ((bf16[32,6,1792]{2,1,0:T(8,128)(2,1)}), bf16[32,6,1792]{2,1,0:T(8,128)(2,1)}, u32[]{:S(2)}, u32[]{:S(2)}) async-start(bf16[32,6,1792]{2,1,0:T(8,128)(2,1)} %reshape.315), calls=%async_computation.1 | async-start | bytes 1835008 | tf_op jit(solution)/shard_map/all_to_all | solution.py:179
Sparse Core Ops, SparseCore 0:
  10.5 81.8 all-gather.1

commit v10 on v4

--- a/solution.py
+++ b/solution.py
@@ -147,8 +147,12 @@
     dprobs = rows_dot(grad_blocks, wide_kv[:, all_heads:])
     row_inner = jnp.sum(attn_probs * dprobs, axis=1, keepdims=True)
     dscore = (attn_probs * (dprobs - row_inner) * score_scale).astype(jnp.bfloat16)
-    grad_query = own_heads(
-        jnp.dot(dscore, wide_kv[:, :all_heads], preferred_element_type=jnp.float32), own_rows
+    window_rows = wide_kv.shape[0]
+    score_rows = dscore.reshape(HEADS, own_rows, window_rows).transpose(1, 0, 2)
+    grad_query = jnp.dot(
+        score_rows.reshape(own_rows, HEADS * window_rows),
+        head_blocks(wide_kv[:, :all_heads], window_rows),
+        preferred_element_type=jnp.float32,
     )
     grad_key = cols_dot(dscore, query_blocks)
     grad_value = cols_dot(prob_low, grad_blocks)

time: 199 us -> 199 us (level)
  matrix products: 29.4 us -> 25.6 us
  waiting for transfers between devices: 86.4 us -> 88.5 us
  local copies, waits for them, and re-layouts: 13.8 us -> 15.8 us
    all_to_all x1, waiting for transfers between devices: 25.9 us -> 18.1 us  [local(): lax.all_to_all(outgoing, 'dp', split_axis=0, concat_axis=0, tiled=True)]
    all_gather x1, waiting for transfers between devices: 35.2 us -> 41.9 us  [gather_weights(): lax.all_gather(jnp.concatenate([qkv_weight, out_wide], axis=1), 'tensor',...]
    ppermute x3, waiting for transfers between devices: 2.71 us -> 5.98 us  [extended(): lax.ppermute(lax.slice_in_dim(block, 0, width, axis=dim), axis, backward)]
    reduce_sum x2 -> x1, other arithmetic: 5.2 us -> 2.23 us  [own_heads(): return kept.reshape(HEADS, count, stacked.shape[1]).sum(axis=0)]
    dot_general x1, matrix products: 5.53 us -> 2.86 us  [local(): lax.dot_general(grad_proj, full_qkv, (((1,), (1,)), ((), ())), preferred_...]
  transfers between devices with their start and end apart: 9 -> 9, of which waited for: 5 -> 6; matrix products, arithmetic and copies ran while one was open for 16% -> 15% of each run, Pallas kernels for 0% -> 0%
where the time goes in v10:
time: 199 us; the launch traced here: 198 us
  waiting for transfers between devices  88.5 us (44%)
  starting transfers between devices  36.7 us (18%)
  matrix products  25.6 us (13%)
  other arithmetic  16.7 us (8%)
  local copies, waits for them, and re-layouts  15.8 us (8%)
  between operations  14.7 us (7%)
    all_gather x1, waiting for transfers between devices, gather_weights(): lax.all_gather(jnp.concatenate([qkv_weight, out_wide], axis=1), 'tensor',...  41.9 us
    all_to_all x1, waiting for transfers between devices, local(): lax.all_to_all(outgoing, 'dp', split_axis=0, concat_axis=0, tiled=True)  18.1 us
    all_to_all x1, waiting for transfers between devices, local(): lax.all_to_all(back_slots, 'dp', split_axis=0, concat_axis=0, tiled=True)  12.3 us
    ppermute x3, starting transfers between devices, extended(): lax.ppermute(lax.slice_in_dim(block, 0, width, axis=dim), axis, backward)  10.4 us
    all_to_all x1, starting transfers between devices, local(): lax.all_to_all(outgoing, 'dp', split_axis=0, concat_axis=0, tiled=True)  10.3 us
    ppermute x3, waiting for transfers between devices, extended(): lax.ppermute(lax.slice_in_dim(block, block.shape[dim] - width, None, axis...  10.2 us
    all_to_all x1, starting transfers between devices, local(): lax.all_to_all(back_slots, 'dp', split_axis=0, concat_axis=0, tiled=True)  9.91 us
    ppermute x3, starting transfers between devices, extended(): lax.ppermute(lax.slice_in_dim(block, block.shape[dim] - width, None, axis...  6.1 us
  transfers between devices with their start and end apart: 9, of which 6 were waited for; matrix products, arithmetic and copies ran while one was open for 15% of the time, Pallas kernels for 0%

profile of v10, /device:TPU:66, one launch (start us, length us, event | category | flops | bytes accessed | tf_op | source)
XLA Modules:
  0.0 198.0 jit_solution(6391168330520379361)
XLA Ops:
  8.3 2.0 %pad_maximum_fusion.1 = bf16[112,3584]{1,0:T(8,128)(2,1)} fusion(bf16[112,896]{1,0:T(8,128)(2,1)S(1)} %reshape.431, bf16[112,2688]{1,0:T(8,128)(2,1)} %param.17), kind=kLoop, calls=%fused_computation.65 | loop fusion | flops 1605632 | bytes 1605632 | tf_op jit(solution)/shard_map/concatenate | solution.py:29
  13.2 10.3 %all-to-all-start = ((bf16[32,6,1792]{2,1,0:T(8,128)(2,1)}), bf16[32,6,1792]{2,1,0:T(8,128)(2,1)S(1)}, u32[]{:S(2)}, u32[]{:S(2)}) async-start(bf16[32,6,1792]{2,1,0:T(8,128)(2,1)} %broadcast_select_fusion), calls=%async_computation | async-start | bytes 1835008 | tf_op jit(solution)/shard_map/all_to_all | solution.py:127
  23.5 1.9 collective-permute-start
  25.4 3.6 %collective-permute-start.1 = (s32[96]{0:T(128)S(1)}, s32[96]{0:T(128)S(1)}, u32[]{:S(2)}, u32[]{:S(2)}) collective-permute-start(s32[96]{0:T(128)S(1)} %get-tuple-element.39), channel_id=1, source_target_pairs={{1,0},{2,1},{3,2},{4,3},{5,4},{6,5},{7,6},{8,7},{9,8},{10,9},{11,1... | collective-permute-start | bytes 1160 | tf_op jit(solution)/shard_map/ppermute | solution.py:19
  30.6 18.1 %all-to-all-done = bf16[32,6,1792]{2,1,0:T(8,128)(2,1)S(1)} async-done(((bf16[32,6,1792]{2,1,0:T(8,128)(2,1)}), bf16[32,6,1792]{2,1,0:T(8,128)(2,1)S(1)}, u32[]{:S(2)}, u32[]{:S(2)}) %all-to-all-start) | async-done | bytes 688160 | tf_op jit(solution)/shard_map/all_to_all | solution.py:127
  50.4 41.9 %all-gather.2.cloned.1.call-done = bf16[1792,3584]{1,0:T(8,128)(2,1)} async-done(((bf16[112,3584]{1,0:T(8,128)(2,1)}), bf16[1792,3584]{1,0:T(8,128)(2,1)}) %all-gather.2.cloned.1.call-update) | async-done | bytes 12845072 | tf_op jit(solution)/shard_map/all_gather | solution.py:28
  92.3 5.5 %fusion.9 = bf16[128,2688]{1,0:T(8,128)(2,1)S(1)} fusion(bf16[1792,3584]{1,0:T(8,128)(2,1)} %all-gather.2.cloned.1.call-done, f32[1792]{0:T(1024)S(1)} %copy-done.9, f32[128]{0:T(128)S(1)} %add_rsqrt_fusion, f32[128]{0:T(128)S(1)} %broadcast_multiply_fusion.2, bf16[128,1792]{1,0:T(8,128)(2,1)S(1)} %gather_fusion.1, pred[128]{0:T(512)(128)(4,1)S(1)} %compare_and_fusion.1), kind=kOutput, calls=%fused_computation.14 | convolution fusion | flops 1234845696 | bytes 10788992 | tf_op jit(solution)/shard_map/dot_general | solution.py:134
  98.8 2.3 %collective-permute-start.2 = (bf16[96,1792]{1,0:T(8,128)(2,1)}, bf16[96,1792]{1,0:T(8,128)(2,1)S(1)}, u32[]{:S(2)}, u32[]{:S(2)}) collective-permute-start(bf16[96,1792]{1,0:T(8,128)(2,1)} %get-tuple-element.30), channel_id=1, source_target_pairs={{0,1},{1,2},{2,3},{3,4},{4,5},{5,6},{6,7},{7,8},{8,9},{9,10},{10,1... | collective-permute-start | bytes 1032200 | tf_op jit(solution)/shard_map/ppermute | solution.py:16
  101.0 4.5 %collective-permute-start.3 = (bf16[96,1792]{1,0:T(8,128)(2,1)}, bf16[96,1792]{1,0:T(8,128)(2,1)S(1)}, u32[]{:S(2)}, u32[]{:S(2)}) collective-permute-start(bf16[96,1792]{1,0:T(8,128)(2,1)} %get-tuple-element.31), channel_id=1, source_target_pairs={{1,0},{2,1},{3,2},{4,3},{5,4},{6,5},{7,6},{8,7},{9,8},{10,9},{11,1... | collective-permute-start | bytes 1032200 | tf_op jit(solution)/shard_map/ppermute | solution.py:19
  106.6 1.9 fusion.20
  117.6 1.9 collective-permute-start.4
  119.6 10.2 %collective-permute-done.4 = f32[96,1792]{1,0:T(8,128)S(1)} collective-permute-done((f32[96,1792]{1,0:T(8,128)S(1)}, f32[96,1792]{1,0:T(8,128)S(1)}, u32[]{:S(2)}, u32[]{:S(2)}) %collective-permute-start.4) | collective-permute-done | bytes 688160 | tf_op jit(solution)/shard_map/ppermute | solution.py:16
  130.8 2.3 %collective-permute-start.5 = (f32[96,1792]{1,0:T(8,128)}, f32[96,1792]{1,0:T(8,128)}, u32[]{:S(2)}, u32[]{:S(2)}) collective-permute-start(f32[96,1792]{1,0:T(8,128)} %get-tuple-element.28), channel_id=1, source_target_pairs={{1,0},{2,1},{3,2},{4,3},{5,4},{6,5},{7,6},{8,7},{9,8},{10,9},{11,1... | collective-permute-start | bytes 2064392 | tf_op jit(solution)/shard_map/ppermute | solution.py:19
  135.2 1.7 fusion.38
  136.9 4.7 %collective-permute-done.5 = f32[96,1792]{1,0:T(8,128)} collective-permute-done((f32[96,1792]{1,0:T(8,128)}, f32[96,1792]{1,0:T(8,128)}, u32[]{:S(2)}, u32[]{:S(2)}) %collective-permute-start.5) | collective-permute-done | bytes 688160 | tf_op jit(solution)/shard_map/ppermute | solution.py:19
  143.0 2.9 %fusion.104 = (f32[128]{0:T(128)S(1)}, f32[128]{0:T(128)S(1)}, f32[128,1792]{1,0:T(8,128)S(1)}) fusion(f32[128]{0:T(128)S(1)} %add_rsqrt_fusion, f32[128]{0:T(128)S(1)} %broadcast_multiply_fusion.2, bf16[128,1792]{1,0:T(8,128)(2,1)S(1)} %gather_fusion.1, pred[128]{0:T(512)(128)(4,1)S(1)} %compare_and_fusion.1, f32[1792]{0:T(1024)S(1)} %copy-done.10, ...), kind=kOutput, calls=%fused_computation.146 | convolution fusion | flops 1236336384 | bytes 11708928 | tf_op jit(solution)/shard_map/dot_general | solution.py:166
  145.9 2.4 %scatter_custom_fusion = bf16[192,1792]{1,0:T(8,128)(2,1)S(1)} fusion(s32[128]{0:T(128)S(1)} %fusion.96, f32[128,1792]{1,0:T(8,128)S(1)} %get-tuple-element.46, f32[128]{0:T(128)S(1)} %broadcast_multiply_fusion, f32[128]{0:T(128)S(1)} %broadcast_multiply_fusion.1, f32[128]{0:T(128)S(1)} %add_rsqrt_fusion, f32[128]{0:T(128)S(1)} %broadcast_multiply_fusion.2, ...), kind=kCustom, calls=%fused_computation.81 | custom fusion | flops 2523136 | bytes 2525698 | tf_op jit(solution)/shard_map/scatter | solution.py:177
  149.4 9.9 %all-to-all-start.1 = ((bf16[32,6,1792]{2,1,0:T(8,128)(2,1)}), bf16[32,6,1792]{2,1,0:T(8,128)(2,1)}, u32[]{:S(2)}, u32[]{:S(2)}) async-start(bf16[32,6,1792]{2,1,0:T(8,128)(2,1)} %reshape.438), calls=%async_computation.1 | async-start | bytes 1835008 | tf_op jit(solution)/shard_map/all_to_all | solution.py:180
  159.4 3.8 %fusion.18 = f32[1024,896]{1,0:T(8,128)} fusion(s32[896]{0:T(1024)S(1)} %get-tuple-element.47, s32[896]{0:T(1024)S(1)} %get-tuple-element.48, s32[1024]{0:T(1024)S(1)} %get-tuple-element.49, s32[1024]{0:T(1024)S(1)} %get-tuple-element.50, pred[1024]{0:T(1024)(128)(4,1)S(1)} %fusion.95, pred[896]{0:T(1024)(128)(4,1)S(1)} %fusion.94, ...), kind=kOutput, calls=%fused_computation.25 | convolution fusion | flops 591855616 | bytes 5579648 | tf_op jit(solution)/shard_map/dot_general | solution.py:109
  163.2 2.2 %reduce_sum.66 = bf16[128,896]{1,0:T(8,128)(2,1)S(1)} reduce(f32[8,128,896]{2,1,0:T(8,128)} %bitcast.78, f32[]{:T(128)} %constant.150.clone.1), dimensions={0}, to_apply=%region_4.5 | reduce | flops 802816 | bytes 3899396 | tf_op jit(solution)/shard_map/reduce_sum | solution.py:85
  167.3 2.6 %fusion.29 = f32[1,128,896]{2,1,0:T(8,128)S(1)} fusion(bf16[128,1792]{0,1:T(8,128)(2,1)S(1)} %bitcast.83, bf16[1792,3584]{1,0:T(8,128)(2,1)} %all-gather.2.cloned.1.call-done), kind=kOutput, calls=%fused_computation.40 | convolution fusion | flops 411041792 | bytes 4128768 | tf_op jit(solution)/shard_map/dot_general | solution.py:45
  169.9 2.6 %fusion.32 = f32[1,128,896]{2,1,0:T(8,128)S(1)} fusion(bf16[128,1792]{0,1:T(8,128)(2,1)S(1)} %bitcast.82, bf16[1792,3584]{1,0:T(8,128)(2,1)} %all-gather.2.cloned.1.call-done), kind=kOutput, calls=%fused_computation.41 | convolution fusion | flops 411041792 | bytes 4128768 | tf_op jit(solution)/shard_map/dot_general | solution.py:45
  173.5 12.3 %all-to-all-done.1 = bf16[32,6,1792]{2,1,0:T(8,128)(2,1)} async-done(((bf16[32,6,1792]{2,1,0:T(8,128)(2,1)}), bf16[32,6,1792]{2,1,0:T(8,128)(2,1)}, u32[]{:S(2)}, u32[]{:S(2)}) %all-to-all-start.1) | async-done | bytes 688160 | tf_op jit(solution)/shard_map/all_to_all | solution.py:180
  187.2 3.1 %scatter_custom_fusion.1 = bf16[193,1792]{1,0:T(8,128)(2,1)S(1)} fusion(s32[192]{0:T(256)S(1)} %bitcast.92, bf16[192,1792]{1,0:T(8,128)(2,1)S(1)} %reshape.468, bf16[]{:T(256)} %constant.143.clone.1), kind=kCustom, calls=%fused_computation.92 | custom fusion | flops 344064 | bytes 691714 | tf_op jit(solution)/shard_map/scatter-add | solution.py:184
  (110 shorter events, 28.7 us)
Async XLA Ops:
  7.2 3.4 %copy-start = (bf16[1,192,1792]{2,1,0:T(8,128)(2,1)S(1)}, bf16[1,192,1792]{2,1,0:T(8,128)(2,1)}, u32[]{:S(2)}) copy-start(bf16[1,192,1792]{2,1,0:T(8,128)(2,1)} %param.12) | copy-start | bytes 2064388
  7.2 85.1 %all-gather.2.cloned.1.call-start = ((), (), s32[]{:S(2)}) async-start(), calls=%async_computation.2 | async-start | bytes 13647872 | tf_op jit(solution)/shard_map/all_gather | solution.py:28
  12.1 11.3 %copy-start.11 = (s32[1,128]{1,0:T(1,128)S(1)}, s32[1,128]{1,0:T(1,128)}, u32[]{:S(2)}) copy-start(s32[1,128]{1,0:T(1,128)} %param.15) | copy-start | bytes 1540
  12.1 17.0 %copy-start.12 = (s32[1,128]{1,0:T(1,128)S(1)}, s32[1,128]{1,0:T(1,128)}, u32[]{:S(2)}) copy-start(s32[1,128]{1,0:T(1,128)} %param.14) | copy-start | bytes 1540
  13.2 35.5 %all-to-all-start = ((bf16[32,6,1792]{2,1,0:T(8,128)(2,1)}), bf16[32,6,1792]{2,1,0:T(8,128)(2,1)S(1)}, u32[]{:S(2)}, u32[]{:S(2)}) async-start(bf16[32,6,1792]{2,1,0:T(8,128)(2,1)} %broadcast_select_fusion), calls=%async_computation | async-start | bytes 1835008 | tf_op jit(solution)/shard_map/all_to_all | solution.py:127
  23.5 5.7 %collective-permute-start = (s32[96]{0:T(128)S(1)}, s32[96]{0:T(128)S(1)}, u32[]{:S(2)}, u32[]{:S(2)}) collective-permute-start(s32[96]{0:T(128)S(1)} %get-tuple-element.38), channel_id=1, source_target_pairs={{0,1},{1,2},{2,3},{3,4},{4,5},{5,6},{6,7},{7,8},{8,9},{9,10},{10,1... | collective-permute-start | bytes 1160 | tf_op jit(solution)/shard_map/ppermute | solution.py:16
  25.4 5.0 %collective-permute-start.1 = (s32[96]{0:T(128)S(1)}, s32[96]{0:T(128)S(1)}, u32[]{:S(2)}, u32[]{:S(2)}) collective-permute-start(s32[96]{0:T(128)S(1)} %get-tuple-element.39), channel_id=1, source_target_pairs={{1,0},{2,1},{3,2},{4,3},{5,4},{6,5},{7,6},{8,7},{9,8},{10,9},{11,1... | collective-permute-start | bytes 1160 | tf_op jit(solution)/shard_map/ppermute | solution.py:19
  48.9 43.4 %copy-start.9 = (f32[1792]{0:T(1024)S(1)}, f32[1792]{0:T(1024)}, u32[]{:S(2)}) copy-start(f32[1792]{0:T(1024)} %param.16) | copy-start | bytes 21508
  50.4 55.2 %copy-start.6 = (bf16[1,128,1792]{2,1,0:T(8,128)(2,1)S(1)}, bf16[1,128,1792]{2,1,0:T(8,128)(2,1)}, u32[]{:S(2)}) copy-start(bf16[1,128,1792]{2,1,0:T(8,128)(2,1)} %param.19) | copy-start | bytes 1376260
  92.3 13.3 %copy-start.3 = (bf16[1792,3584]{1,0:T(8,128)(2,1)S(1)}, bf16[1792,3584]{1,0:T(8,128)(2,1)}, u32[]{:S(2)}) copy-start(bf16[1792,3584]{1,0:T(8,128)(2,1)} %all-gather.2.cloned.1.call-done) | copy-start | bytes 38535172
  97.8 10.7 %copy-start.4 = (bf16[128,2688]{1,0:T(8,128)(2,1)}, bf16[128,2688]{1,0:T(8,128)(2,1)S(1)}, u32[]{:S(2)}) copy-start(bf16[128,2688]{1,0:T(8,128)(2,1)S(1)} %fusion.9) | copy-start | bytes 2064388
  98.8 14.4 %collective-permute-start.2 = (bf16[96,1792]{1,0:T(8,128)(2,1)}, bf16[96,1792]{1,0:T(8,128)(2,1)S(1)}, u32[]{:S(2)}, u32[]{:S(2)}) collective-permute-start(bf16[96,1792]{1,0:T(8,128)(2,1)} %get-tuple-element.30), channel_id=1, source_target_pairs={{0,1},{1,2},{2,3},{3,4},{4,5},{5,6},{6,7},{7,8},{8,9},{9,10},{10,1... | collective-permute-start | bytes 1032200 | tf_op jit(solution)/shard_map/ppermute | solution.py:16
  101.0 12.1 %collective-permute-start.3 = (bf16[96,1792]{1,0:T(8,128)(2,1)}, bf16[96,1792]{1,0:T(8,128)(2,1)S(1)}, u32[]{:S(2)}, u32[]{:S(2)}) collective-permute-start(bf16[96,1792]{1,0:T(8,128)(2,1)} %get-tuple-element.31), channel_id=1, source_target_pairs={{1,0},{2,1},{3,2},{4,3},{5,4},{6,5},{7,6},{8,7},{9,8},{10,9},{11,1... | collective-permute-start | bytes 1032200 | tf_op jit(solution)/shard_map/ppermute | solution.py:19
  108.9 3.2 %slice-start.5 = ((bf16[128,2688]{1,0:T(8,128)(2,1)}), bf16[128,896]{1,0:T(8,128)(2,1)S(1)}, s32[]{:S(2)}) async-start(bf16[128,2688]{1,0:T(8,128)(2,1)} %copy-done.4), calls=%async_computation.8 | async-start | bytes 458752 | tf_op jit(solution)/shard_map/slice | solution.py:135
  117.6 12.3 %collective-permute-start.4 = (f32[96,1792]{1,0:T(8,128)S(1)}, f32[96,1792]{1,0:T(8,128)S(1)}, u32[]{:S(2)}, u32[]{:S(2)}) collective-permute-start(f32[96,1792]{1,0:T(8,128)S(1)} %fusion.57), channel_id=1, source_target_pairs={{0,1},{1,2},{2,3},{3,4},{4,5},{5,6},{6,7},{7,8},{8,9},{9,10},{10,1... | collective-permute-start | bytes 2064392 | tf_op jit(solution)/shard_map/ppermute | solution.py:16
  130.8 3.5 %slice-start.6 = ((bf16[320,1792]{1,0:T(8,128)(2,1)}), bf16[320,896]{1,0:T(8,128)(2,1)S(1)}, s32[]{:S(2)}) async-start(bf16[320,1792]{1,0:T(8,128)(2,1)} %copy-done.5), calls=%async_computation.9 | async-start | bytes 1146880 | tf_op jit(solution)/shard_map/slice | solution.py:101
  130.8 10.8 %collective-permute-start.5 = (f32[96,1792]{1,0:T(8,128)}, f32[96,1792]{1,0:T(8,128)}, u32[]{:S(2)}, u32[]{:S(2)}) collective-permute-start(f32[96,1792]{1,0:T(8,128)} %get-tuple-element.28), channel_id=1, source_target_pairs={{1,0},{2,1},{3,2},{4,3},{5,4},{6,5},{7,6},{8,7},{9,8},{10,9},{11,1... | collective-permute-start | bytes 2064392 | tf_op jit(solution)/shard_map/ppermute | solution.py:19
  134.4 8.6 %slice-start = ((s8[12845056]{0:T(1024)(128)(4,1)}), s8[4194304]{0:T(1024)(128)(4,1)S(1)}, s32[]{:S(2)}) async-start(s8[12845056]{0:T(1024)(128)(4,1)} %bitcast.79), calls=%async_computation.3 | async-start | bytes 8388608
  135.2 7.8 %slice-start.1 = ((s8[12845056]{0:T(1024)(128)(4,1)}), s8[4194304]{0:T(1024)(128)(4,1)S(1)}, s32[]{:S(2)}) async-start(s8[12845056]{0:T(1024)(128)(4,1)} %bitcast.79), calls=%async_computation.4 | async-start | bytes 8388608
  135.2 7.8 %slice-start.2 = ((s8[12845056]{0:T(1024)(128)(4,1)}), s8[4194304]{0:T(1024)(128)(4,1)S(1)}, s32[]{:S(2)}) async-start(s8[12845056]{0:T(1024)(128)(4,1)} %bitcast.79), calls=%async_computation.5 | async-start | bytes 8388608
  135.2 7.8 %slice-start.3 = ((s8[12845056]{0:T(1024)(128)(4,1)}), s8[262144]{0:T(1024)(128)(4,1)S(1)}, s32[]{:S(2)}) async-start(s8[12845056]{0:T(1024)(128)(4,1)} %bitcast.79), calls=%async_computation.6 | async-start | bytes 524288
  136.9 6.1 %copy-start.10 = (f32[1792]{0:T(1024)S(1)}, f32[1792]{0:T(1024)}, u32[]{:S(2)}) copy-start(f32[1792]{0:T(1024)} %param.16) | copy-start | bytes 21508
  148.2 11.1 %copy-start.2 = (f32[1024,320]{0,1:T(8,128)S(1)}, f32[1024,320]{0,1:T(8,128)}, u32[]{:S(2)}) copy-start(f32[1024,320]{0,1:T(8,128)} %copy-done.1) | copy-start | bytes 3932164
  149.4 36.4 %all-to-all-start.1 = ((bf16[32,6,1792]{2,1,0:T(8,128)(2,1)}), bf16[32,6,1792]{2,1,0:T(8,128)(2,1)}, u32[]{:S(2)}, u32[]{:S(2)}) async-start(bf16[32,6,1792]{2,1,0:T(8,128)(2,1)} %reshape.438), calls=%async_computation.1 | async-start | bytes 1835008 | tf_op jit(solution)/shard_map/all_to_all | solution.py:180
  (5 other events, 8.5 us)
Sparse Core Ops, SparseCore 0:
  10.4 81.8 all-gather.1

commit v11 on v10

--- a/solution.py
+++ b/solution.py
@@ -128,6 +128,10 @@
         groups * slot_count, features
     )
     pick_rows = take_rows[0]
+    slot_total = groups * slot_count
+    row_slot = jnp.full((src_count + 1,), slot_total, jnp.int32).at[send_flat].set(
+        jnp.arange(slot_total, dtype=jnp.int32)
+    )[:src_count]
     packed = jnp.take(incoming, pick_rows, axis=0)
     full_qkv, full_out = gather_weights(qkv_weight, out_weight)
     values, unit_rows, inv_dev, normed = normalize(packed, norm_gain)
@@ -180,9 +184,7 @@
     returned = lax.all_to_all(back_slots, "dp", split_axis=0, concat_axis=0, tiled=True).reshape(
         groups * slot_count, features
     )
-    patch_grad = (
-        jnp.zeros((src_count + 1, features), jnp.bfloat16).at[send_flat].add(returned)[:src_count]
-    )
+    patch_grad = jnp.take(returned, row_slot, axis=0, mode="fill", fill_value=0)
     return (layer_out[None], patch_grad[None])
 
 

time: 199 us -> 197 us (0.990)
  other arithmetic: 16.7 us -> 13.6 us
  local copies, waits for them, and re-layouts: 15.8 us -> 18.7 us
    scatter-add x1 -> x0, other arithmetic: 3.1 us -> none  [local(): jnp.zeros((src_count + 1, features), jnp.bfloat16).at[send_flat]]
  transfers between devices with their start and end apart: 9 -> 9, of which waited for: 6 -> 5; matrix products, arithmetic and copies ran while one was open for 15% -> 16% of each run, Pallas kernels for 0% -> 0%
where the time goes in v11:
time: 197 us; the launch traced here: 196 us
  waiting for transfers between devices  86.7 us (44%)
  starting transfers between devices  36.7 us (19%)
  matrix products  25.6 us (13%)
  local copies, waits for them, and re-layouts  18.7 us (9%)
  between operations  14.8 us (8%)
  other arithmetic  13.6 us (7%)
    all_gather x1, waiting for transfers between devices, gather_weights(): lax.all_gather(jnp.concatenate([qkv_weight, out_wide], axis=1), 'tensor',...  42 us
    all_to_all x1, waiting for transfers between devices, local(): lax.all_to_all(outgoing, 'dp', split_axis=0, concat_axis=0, tiled=True)  17.4 us
    all_to_all x1, waiting for transfers between devices, local(): lax.all_to_all(back_slots, 'dp', split_axis=0, concat_axis=0, tiled=True)  12.4 us
    ppermute x3, starting transfers between devices, extended(): lax.ppermute(lax.slice_in_dim(block, 0, width, axis=dim), axis, backward)  10.4 us
    all_to_all x1, starting transfers between devices, local(): lax.all_to_all(outgoing, 'dp', split_axis=0, concat_axis=0, tiled=True)  10.2 us
    ppermute x3, waiting for transfers between devices, extended(): lax.ppermute(lax.slice_in_dim(block, block.shape[dim] - width, None, axis...  10.2 us
    all_to_all x1, starting transfers between devices, local(): lax.all_to_all(back_slots, 'dp', split_axis=0, concat_axis=0, tiled=True)  9.91 us
    ppermute x3, starting transfers between devices, extended(): lax.ppermute(lax.slice_in_dim(block, block.shape[dim] - width, None, axis...  6.1 us
  transfers between devices with their start and end apart: 9, of which 5 were waited for; matrix products, arithmetic and copies ran while one was open for 16% of the time, Pallas kernels for 0%

profile of v11, /device:TPU:66, one launch (start us, length us, event | category | flops | bytes accessed | tf_op | source)
XLA Modules:
  0.0 196.2 jit_solution(1818274584542503904)
XLA Ops:
  8.3 2.0 %pad_maximum_fusion.1 = bf16[112,3584]{1,0:T(8,128)(2,1)} fusion(bf16[112,896]{1,0:T(8,128)(2,1)S(1)} %reshape.404, bf16[112,2688]{1,0:T(8,128)(2,1)} %param.19), kind=kLoop, calls=%fused_computation.65 | loop fusion | flops 1605632 | bytes 1605632 | tf_op jit(solution)/shard_map/concatenate | solution.py:29
  13.0 10.2 %all-to-all-start = ((bf16[32,6,1792]{2,1,0:T(8,128)(2,1)}), bf16[32,6,1792]{2,1,0:T(8,128)(2,1)S(1)}, u32[]{:S(2)}, u32[]{:S(2)}) async-start(bf16[32,6,1792]{2,1,0:T(8,128)(2,1)} %reshape.402), calls=%async_computation | async-start | bytes 1835008 | tf_op jit(solution)/shard_map/all_to_all | solution.py:127
  23.4 1.9 collective-permute-start
  25.3 3.6 %collective-permute-start.1 = (s32[96]{0:T(128)S(1)}, s32[96]{0:T(128)S(1)}, u32[]{:S(2)}, u32[]{:S(2)}) collective-permute-start(s32[96]{0:T(128)S(1)} %get-tuple-element.38), channel_id=1, source_target_pairs={{1,0},{2,1},{3,2},{4,3},{5,4},{6,5},{7,6},{8,7},{9,8},{10,9},{11,1... | collective-permute-start | bytes 1160 | tf_op jit(solution)/shard_map/ppermute | solution.py:19
  31.2 17.4 %all-to-all-done = bf16[32,6,1792]{2,1,0:T(8,128)(2,1)S(1)} async-done(((bf16[32,6,1792]{2,1,0:T(8,128)(2,1)}), bf16[32,6,1792]{2,1,0:T(8,128)(2,1)S(1)}, u32[]{:S(2)}, u32[]{:S(2)}) %all-to-all-start) | async-done | bytes 688160 | tf_op jit(solution)/shard_map/all_to_all | solution.py:127
  50.3 42.0 %all-gather.2.cloned.1.call-done = bf16[1792,3584]{1,0:T(8,128)(2,1)} async-done(((bf16[112,3584]{1,0:T(8,128)(2,1)}), bf16[1792,3584]{1,0:T(8,128)(2,1)}) %all-gather.2.cloned.1.call-update) | async-done | bytes 12845072 | tf_op jit(solution)/shard_map/all_gather | solution.py:28
  92.3 5.5 %fusion.9 = bf16[128,2688]{1,0:T(8,128)(2,1)S(1)} fusion(bf16[1792,3584]{1,0:T(8,128)(2,1)} %all-gather.2.cloned.1.call-done, f32[1792]{0:T(1024)S(1)} %copy-done.12, f32[128]{0:T(128)S(1)} %add_rsqrt_fusion, f32[128]{0:T(128)S(1)} %broadcast_multiply_fusion.2, bf16[128,1792]{1,0:T(8,128)(2,1)S(1)} %gather_fusion, pred[128]{0:T(512)(128)(4,1)S(1)} %compare_and_fusion.2), kind=kOutput, calls=%fused_computation.15 | convolution fusion | flops 1234845696 | bytes 10788992 | tf_op jit(solution)/shard_map/dot_general | solution.py:138
  98.8 2.3 %collective-permute-start.2 = (bf16[96,1792]{1,0:T(8,128)(2,1)}, bf16[96,1792]{1,0:T(8,128)(2,1)S(1)}, u32[]{:S(2)}, u32[]{:S(2)}) collective-permute-start(bf16[96,1792]{1,0:T(8,128)(2,1)} %get-tuple-element.31), channel_id=1, source_target_pairs={{0,1},{1,2},{2,3},{3,4},{4,5},{5,6},{6,7},{7,8},{8,9},{9,10},{10,1... | collective-permute-start | bytes 1032200 | tf_op jit(solution)/shard_map/ppermute | solution.py:16
  101.0 4.5 %collective-permute-start.3 = (bf16[96,1792]{1,0:T(8,128)(2,1)}, bf16[96,1792]{1,0:T(8,128)(2,1)S(1)}, u32[]{:S(2)}, u32[]{:S(2)}) collective-permute-start(bf16[96,1792]{1,0:T(8,128)(2,1)} %get-tuple-element.32), channel_id=1, source_target_pairs={{1,0},{2,1},{3,2},{4,3},{5,4},{6,5},{7,6},{8,7},{9,8},{10,9},{11,1... | collective-permute-start | bytes 1032200 | tf_op jit(solution)/shard_map/ppermute | solution.py:19
  106.6 1.9 fusion.20
  109.6 1.7 slice.142
  117.7 1.9 collective-permute-start.4
  119.7 10.2 %collective-permute-done.4 = f32[96,1792]{1,0:T(8,128)S(1)} collective-permute-done((f32[96,1792]{1,0:T(8,128)S(1)}, f32[96,1792]{1,0:T(8,128)S(1)}, u32[]{:S(2)}, u32[]{:S(2)}) %collective-permute-start.4) | collective-permute-done | bytes 688160 | tf_op jit(solution)/shard_map/ppermute | solution.py:16
  130.9 2.3 %collective-permute-start.5 = (f32[96,1792]{1,0:T(8,128)}, f32[96,1792]{1,0:T(8,128)}, u32[]{:S(2)}, u32[]{:S(2)}) collective-permute-start(f32[96,1792]{1,0:T(8,128)} %get-tuple-element.29), channel_id=1, source_target_pairs={{1,0},{2,1},{3,2},{4,3},{5,4},{6,5},{7,6},{8,7},{9,8},{10,9},{11,1... | collective-permute-start | bytes 2064392 | tf_op jit(solution)/shard_map/ppermute | solution.py:19
  135.2 1.7 fusion.38
  136.9 4.7 %collective-permute-done.5 = f32[96,1792]{1,0:T(8,128)} collective-permute-done((f32[96,1792]{1,0:T(8,128)}, f32[96,1792]{1,0:T(8,128)}, u32[]{:S(2)}, u32[]{:S(2)}) %collective-permute-start.5) | collective-permute-done | bytes 688160 | tf_op jit(solution)/shard_map/ppermute | solution.py:19
  143.0 2.9 %fusion.104 = (f32[128]{0:T(128)S(1)}, f32[128]{0:T(128)S(1)}, f32[128,1792]{1,0:T(8,128)S(1)}) fusion(f32[128]{0:T(128)S(1)} %copy-done.11, f32[128]{0:T(128)S(1)} %broadcast_multiply_fusion.2, bf16[128,1792]{1,0:T(8,128)(2,1)S(1)} %gather_fusion, pred[128]{0:T(512)(128)(4,1)S(1)} %compare_and_fusion.2, f32[1792]{0:T(1024)S(1)} %copy-done.13, ...), kind=kOutput, calls=%fused_computation.149 | convolution fusion | flops 1236336384 | bytes 11708928 | tf_op jit(solution)/shard_map/dot_general | solution.py:170
  145.9 2.4 %scatter_custom_fusion = bf16[192,1792]{1,0:T(8,128)(2,1)S(1)} fusion(s32[128]{0:T(128)} %copy-done.9, f32[128,1792]{1,0:T(8,128)S(1)} %get-tuple-element.45, f32[128]{0:T(128)S(1)} %broadcast_multiply_fusion, f32[128]{0:T(128)S(1)} %broadcast_multiply_fusion.1, f32[128]{0:T(128)S(1)} %copy-done.11, f32[128]{0:T(128)S(1)} %broadcast_multiply_fusion.2, ...), kind=kCustom, calls=%fused_computation.82 | custom fusion | flops 2523136 | bytes 2525824 | tf_op jit(solution)/shard_map/scatter | solution.py:181
  149.5 9.9 %all-to-all-start.1 = ((bf16[32,6,1792]{2,1,0:T(8,128)(2,1)}), bf16[32,6,1792]{2,1,0:T(8,128)(2,1)}, u32[]{:S(2)}, u32[]{:S(2)}) async-start(bf16[32,6,1792]{2,1,0:T(8,128)(2,1)} %reshape.411), calls=%async_computation.1 | async-start | bytes 1835008 | tf_op jit(solution)/shard_map/all_to_all | solution.py:184
  159.4 3.8 %fusion.18 = f32[1024,896]{1,0:T(8,128)} fusion(s32[896]{0:T(1024)S(1)} %get-tuple-element.46, s32[896]{0:T(1024)S(1)} %get-tuple-element.47, s32[1024]{0:T(1024)S(1)} %get-tuple-element.48, s32[1024]{0:T(1024)S(1)} %get-tuple-element.49, pred[1024]{0:T(1024)(128)(4,1)S(1)} %fusion.93, pred[896]{0:T(1024)(128)(4,1)S(1)} %fusion.92, ...), kind=kOutput, calls=%fused_computation.26 | convolution fusion | flops 591855616 | bytes 5579648 | tf_op jit(solution)/shard_map/dot_general | solution.py:109
  163.2 2.2 %reduce_sum.66 = bf16[128,896]{1,0:T(8,128)(2,1)S(1)} reduce(f32[8,128,896]{2,1,0:T(8,128)} %bitcast.75, f32[]{:T(128)} %constant.147.clone.1), dimensions={0}, to_apply=%region_4.6 | reduce | flops 802816 | bytes 3899396 | tf_op jit(solution)/shard_map/reduce_sum | solution.py:85
  167.3 2.6 %fusion.29 = f32[1,128,896]{2,1,0:T(8,128)S(1)} fusion(bf16[128,1792]{0,1:T(8,128)(2,1)S(1)} %bitcast.80, bf16[1792,3584]{1,0:T(8,128)(2,1)} %all-gather.2.cloned.1.call-done), kind=kOutput, calls=%fused_computation.41 | convolution fusion | flops 411041792 | bytes 4128768 | tf_op jit(solution)/shard_map/dot_general | solution.py:45
  169.9 2.6 %fusion.32 = f32[1,128,896]{2,1,0:T(8,128)S(1)} fusion(bf16[128,1792]{0,1:T(8,128)(2,1)S(1)} %bitcast.79, bf16[1792,3584]{1,0:T(8,128)(2,1)} %all-gather.2.cloned.1.call-done), kind=kOutput, calls=%fused_computation.42 | convolution fusion | flops 411041792 | bytes 4128768 | tf_op jit(solution)/shard_map/dot_general | solution.py:45
  173.5 12.4 %all-to-all-done.1 = bf16[32,6,1792]{2,1,0:T(8,128)(2,1)} async-done(((bf16[32,6,1792]{2,1,0:T(8,128)(2,1)}), bf16[32,6,1792]{2,1,0:T(8,128)(2,1)}, u32[]{:S(2)}, u32[]{:S(2)}) %all-to-all-start.1) | async-done | bytes 688160 | tf_op jit(solution)/shard_map/all_to_all | solution.py:184
  (122 shorter events, 28.7 us)
Async XLA Ops:
  7.2 85.1 %all-gather.2.cloned.1.call-start = ((), (), s32[]{:S(2)}) async-start(), calls=%async_computation.2 | async-start | bytes 13647872 | tf_op jit(solution)/shard_map/all_gather | solution.py:28
  11.9 11.5 %copy-start.14 = (s32[1,128]{1,0:T(1,128)S(1)}, s32[1,128]{1,0:T(1,128)}, u32[]{:S(2)}) copy-start(s32[1,128]{1,0:T(1,128)} %param.17) | copy-start | bytes 1540
  11.9 18.4 %copy-start.15 = (s32[1,128]{1,0:T(1,128)S(1)}, s32[1,128]{1,0:T(1,128)}, u32[]{:S(2)}) copy-start(s32[1,128]{1,0:T(1,128)} %param.16) | copy-start | bytes 1540
  13.0 35.5 %all-to-all-start = ((bf16[32,6,1792]{2,1,0:T(8,128)(2,1)}), bf16[32,6,1792]{2,1,0:T(8,128)(2,1)S(1)}, u32[]{:S(2)}, u32[]{:S(2)}) async-start(bf16[32,6,1792]{2,1,0:T(8,128)(2,1)} %reshape.402), calls=%async_computation | async-start | bytes 1835008 | tf_op jit(solution)/shard_map/all_to_all | solution.py:127
  23.4 7.5 %collective-permute-start = (s32[96]{0:T(128)S(1)}, s32[96]{0:T(128)S(1)}, u32[]{:S(2)}, u32[]{:S(2)}) collective-permute-start(s32[96]{0:T(128)S(1)} %get-tuple-element.37), channel_id=1, source_target_pairs={{0,1},{1,2},{2,3},{3,4},{4,5},{5,6},{6,7},{7,8},{8,9},{9,10},{10,1... | collective-permute-start | bytes 1160 | tf_op jit(solution)/shard_map/ppermute | solution.py:16
  25.3 5.6 %collective-permute-start.1 = (s32[96]{0:T(128)S(1)}, s32[96]{0:T(128)S(1)}, u32[]{:S(2)}, u32[]{:S(2)}) collective-permute-start(s32[96]{0:T(128)S(1)} %get-tuple-element.38), channel_id=1, source_target_pairs={{1,0},{2,1},{3,2},{4,3},{5,4},{6,5},{7,6},{8,7},{9,8},{10,9},{11,1... | collective-permute-start | bytes 1160 | tf_op jit(solution)/shard_map/ppermute | solution.py:19
  48.8 43.5 %copy-start.12 = (f32[1792]{0:T(1024)S(1)}, f32[1792]{0:T(1024)}, u32[]{:S(2)}) copy-start(f32[1792]{0:T(1024)} %param.18) | copy-start | bytes 21508
  50.3 47.5 %copy-start.10 = (f32[128]{0:T(128)}, f32[128]{0:T(128)S(1)}, u32[]{:S(2)}) copy-start(f32[128]{0:T(128)S(1)} %add_rsqrt_fusion) | copy-start | bytes 1540
  50.3 55.3 %copy-start.6 = (bf16[1,128,1792]{2,1,0:T(8,128)(2,1)S(1)}, bf16[1,128,1792]{2,1,0:T(8,128)(2,1)}, u32[]{:S(2)}) copy-start(bf16[1,128,1792]{2,1,0:T(8,128)(2,1)} %param.21) | copy-start | bytes 1376260
  92.3 13.3 %copy-start.3 = (bf16[1792,3584]{1,0:T(8,128)(2,1)S(1)}, bf16[1792,3584]{1,0:T(8,128)(2,1)}, u32[]{:S(2)}) copy-start(bf16[1792,3584]{1,0:T(8,128)(2,1)} %all-gather.2.cloned.1.call-done) | copy-start | bytes 38535172
  97.9 10.7 %copy-start.4 = (bf16[128,2688]{1,0:T(8,128)(2,1)}, bf16[128,2688]{1,0:T(8,128)(2,1)S(1)}, u32[]{:S(2)}) copy-start(bf16[128,2688]{1,0:T(8,128)(2,1)S(1)} %fusion.9) | copy-start | bytes 2064388
  98.8 14.4 %collective-permute-start.2 = (bf16[96,1792]{1,0:T(8,128)(2,1)}, bf16[96,1792]{1,0:T(8,128)(2,1)S(1)}, u32[]{:S(2)}, u32[]{:S(2)}) collective-permute-start(bf16[96,1792]{1,0:T(8,128)(2,1)} %get-tuple-element.31), channel_id=1, source_target_pairs={{0,1},{1,2},{2,3},{3,4},{4,5},{5,6},{6,7},{7,8},{8,9},{9,10},{10,1... | collective-permute-start | bytes 1032200 | tf_op jit(solution)/shard_map/ppermute | solution.py:16
  101.0 12.1 %collective-permute-start.3 = (bf16[96,1792]{1,0:T(8,128)(2,1)}, bf16[96,1792]{1,0:T(8,128)(2,1)S(1)}, u32[]{:S(2)}, u32[]{:S(2)}) collective-permute-start(bf16[96,1792]{1,0:T(8,128)(2,1)} %get-tuple-element.32), channel_id=1, source_target_pairs={{1,0},{2,1},{3,2},{4,3},{5,4},{6,5},{7,6},{8,7},{9,8},{10,9},{11,1... | collective-permute-start | bytes 1032200 | tf_op jit(solution)/shard_map/ppermute | solution.py:19
  117.7 12.3 %collective-permute-start.4 = (f32[96,1792]{1,0:T(8,128)S(1)}, f32[96,1792]{1,0:T(8,128)S(1)}, u32[]{:S(2)}, u32[]{:S(2)}) collective-permute-start(f32[96,1792]{1,0:T(8,128)S(1)} %fusion.57), channel_id=1, source_target_pairs={{0,1},{1,2},{2,3},{3,4},{4,5},{5,6},{6,7},{7,8},{8,9},{9,10},{10,1... | collective-permute-start | bytes 2064392 | tf_op jit(solution)/shard_map/ppermute | solution.py:16
  130.9 3.5 %slice-start.6 = ((bf16[320,1792]{1,0:T(8,128)(2,1)}), bf16[320,896]{1,0:T(8,128)(2,1)S(1)}, s32[]{:S(2)}) async-start(bf16[320,1792]{1,0:T(8,128)(2,1)} %copy-done.5), calls=%async_computation.9 | async-start | bytes 1146880 | tf_op jit(solution)/shard_map/slice | solution.py:101
  130.9 10.8 %collective-permute-start.5 = (f32[96,1792]{1,0:T(8,128)}, f32[96,1792]{1,0:T(8,128)}, u32[]{:S(2)}, u32[]{:S(2)}) collective-permute-start(f32[96,1792]{1,0:T(8,128)} %get-tuple-element.29), channel_id=1, source_target_pairs={{1,0},{2,1},{3,2},{4,3},{5,4},{6,5},{7,6},{8,7},{9,8},{10,9},{11,1... | collective-permute-start | bytes 2064392 | tf_op jit(solution)/shard_map/ppermute | solution.py:19
  134.4 8.6 %slice-start = ((s8[12845056]{0:T(1024)(128)(4,1)}), s8[4194304]{0:T(1024)(128)(4,1)S(1)}, s32[]{:S(2)}) async-start(s8[12845056]{0:T(1024)(128)(4,1)} %bitcast.76), calls=%async_computation.3 | async-start | bytes 8388608
  135.2 7.8 %slice-start.1 = ((s8[12845056]{0:T(1024)(128)(4,1)}), s8[4194304]{0:T(1024)(128)(4,1)S(1)}, s32[]{:S(2)}) async-start(s8[12845056]{0:T(1024)(128)(4,1)} %bitcast.76), calls=%async_computation.4 | async-start | bytes 8388608
  135.2 7.8 %slice-start.2 = ((s8[12845056]{0:T(1024)(128)(4,1)}), s8[4194304]{0:T(1024)(128)(4,1)S(1)}, s32[]{:S(2)}) async-start(s8[12845056]{0:T(1024)(128)(4,1)} %bitcast.76), calls=%async_computation.5 | async-start | bytes 8388608
  135.2 7.8 %slice-start.3 = ((s8[12845056]{0:T(1024)(128)(4,1)}), s8[262144]{0:T(1024)(128)(4,1)S(1)}, s32[]{:S(2)}) async-start(s8[12845056]{0:T(1024)(128)(4,1)} %bitcast.76), calls=%async_computation.6 | async-start | bytes 524288
  136.9 6.1 %copy-start.11 = (f32[128]{0:T(128)S(1)}, f32[128]{0:T(128)}, u32[]{:S(2)}) copy-start(f32[128]{0:T(128)} %copy-done.10) | copy-start | bytes 1540
  136.9 6.1 %copy-start.13 = (f32[1792]{0:T(1024)S(1)}, f32[1792]{0:T(1024)}, u32[]{:S(2)}) copy-start(f32[1792]{0:T(1024)} %param.18) | copy-start | bytes 21508
  148.3 11.1 %copy-start.2 = (f32[1024,320]{0,1:T(8,128)S(1)}, f32[1024,320]{0,1:T(8,128)}, u32[]{:S(2)}) copy-start(f32[1024,320]{0,1:T(8,128)} %copy-done.1) | copy-start | bytes 3932164
  149.5 36.4 %all-to-all-start.1 = ((bf16[32,6,1792]{2,1,0:T(8,128)(2,1)}), bf16[32,6,1792]{2,1,0:T(8,128)(2,1)}, u32[]{:S(2)}, u32[]{:S(2)}) async-start(bf16[32,6,1792]{2,1,0:T(8,128)(2,1)} %reshape.411), calls=%async_computation.1 | async-start | bytes 1835008 | tf_op jit(solution)/shard_map/all_to_all | solution.py:184
  (8 other events, 15.7 us)
Sparse Core Ops, SparseCore 0:
  10.5 81.8 all-gather.1

commit v12 on v11

--- a/solution.py
+++ b/solution.py
@@ -162,10 +162,14 @@
     grad_value = cols_dot(prob_low, grad_blocks)
     grad_window = jnp.concatenate([grad_key, grad_value], axis=1)
     center = grad_window[MOST : MOST + own_rows]
-    rim_parts = jnp.concatenate([grad_window[:MOST], grad_window[MOST + own_rows :]], axis=0)
-    arrived = extended(rim_parts, (("tensor", 0),), MOST)
-    center = center.at[:MOST].add(arrived[:MOST])
-    center = center.at[own_rows - MOST :].add(arrived[3 * MOST :])
+    blocks = lax.axis_size("tensor")
+    ahead = [(i, i + 1) for i in range(blocks - 1)]
+    behind = [(target, source) for source, target in ahead]
+    high_rim, low_rim = lax.optimization_barrier((grad_window[MOST + own_rows :], grad_window[:MOST]))
+    from_prev = lax.ppermute(high_rim, "tensor", ahead)
+    from_next = lax.ppermute(low_rim, "tensor", behind)
+    center = center.at[:MOST].add(from_prev)
+    center = center.at[own_rows - MOST :].add(from_next)
     grad_proj = jnp.concatenate([grad_query, center], axis=1).astype(jnp.bfloat16)
     grad_normed = lax.dot_general(
         grad_proj, full_qkv, (((1,), (1,)), ((), ())), preferred_element_type=jnp.float32

time: 197 us -> 188 us (0.954)
  waiting for transfers between devices: 86.7 us -> 75 us
    ppermute x3 -> x2, waiting for transfers between devices: 10.2 us -> 0.01 us  [extended(): lax.ppermute(lax.slice_in_dim(block, block.shape[dim] - width, None, axis...]
    ppermute x0 -> x2, waiting for transfers between devices: none -> 6.18 us  [the longest x1 4.52 us: local(): from_prev = lax.ppermute(high_rim, 'tensor', ahead)]
    ppermute x0 -> x2, starting transfers between devices: none -> 5.91 us  [the longest x1 3.86 us: local(): from_next = lax.ppermute(low_rim, 'tensor', behind)]
    ppermute x3 -> x2, waiting for transfers between devices: 4.74 us -> 0.01 us  [extended(): lax.ppermute(lax.slice_in_dim(block, 0, width, axis=dim), axis, backward)]
    all_to_all x1, waiting for transfers between devices: 17.4 us -> 14.5 us  [local(): lax.all_to_all(outgoing, 'dp', split_axis=0, concat_axis=0, tiled=True)]
    ppermute x3 -> x2, starting transfers between devices: 10.4 us -> 8.16 us  [extended(): lax.ppermute(lax.slice_in_dim(block, 0, width, axis=dim), axis, backward)]
    ppermute x3 -> x2, starting transfers between devices: 6.1 us -> 4.18 us  [extended(): lax.ppermute(lax.slice_in_dim(block, block.shape[dim] - width, None, axis...]
  transfers between devices with their start and end apart: 9 -> 9, of which waited for: 5 -> 5; matrix products, arithmetic and copies ran while one was open for 16% -> 18% of each run, Pallas kernels for 0% -> 0%
where the time goes in v12:
time: 188 us; the launch traced here: 187 us
  waiting for transfers between devices  75 us (40%)
  starting transfers between devices  38.5 us (20%)
  matrix products  26.5 us (14%)
  local copies, waits for them, and re-layouts  18.7 us (10%)
  between operations  14.8 us (8%)
  other arithmetic  13.9 us (7%)
    all_gather x1, waiting for transfers between devices, gather_weights(): lax.all_gather(jnp.concatenate([qkv_weight, out_wide], axis=1), 'tensor',...  42 us
    all_to_all x1, waiting for transfers between devices, local(): lax.all_to_all(outgoing, 'dp', split_axis=0, concat_axis=0, tiled=True)  14.5 us
    all_to_all x1, waiting for transfers between devices, local(): lax.all_to_all(back_slots, 'dp', split_axis=0, concat_axis=0, tiled=True)  12.3 us
    all_to_all x1, starting transfers between devices, local(): lax.all_to_all(outgoing, 'dp', split_axis=0, concat_axis=0, tiled=True)  10.2 us
    all_to_all x1, starting transfers between devices, local(): lax.all_to_all(back_slots, 'dp', split_axis=0, concat_axis=0, tiled=True)  9.91 us
    ppermute x2, starting transfers between devices, extended(): lax.ppermute(lax.slice_in_dim(block, 0, width, axis=dim), axis, backward)  8.16 us
    dot_general x1, matrix products, local(): jnp.dot(normed, full_qkv, preferred_element_type=jnp.float32)  5.54 us
    dot_general x2, matrix products, times_out(): jnp.dot(spread(attended, side), out_pairs, preferred_element_type=jnp.flo...  5.19 us
  transfers between devices with their start and end apart: 9, of which 5 were waited for; matrix products, arithmetic and copies ran while one was open for 18% of the time, Pallas kernels for 0%

profile of v12, /device:TPU:66, one launch (start us, length us, event | category | flops | bytes accessed | tf_op | source)
XLA Modules:
  0.0 187.4 jit_solution(8856561315826569764)
XLA Ops:
  8.3 2.0 %pad_maximum_fusion.1 = bf16[112,3584]{1,0:T(8,128)(2,1)} fusion(bf16[112,896]{1,0:T(8,128)(2,1)S(1)} %reshape.404, bf16[112,2688]{1,0:T(8,128)(2,1)} %param.19), kind=kLoop, calls=%fused_computation.65 | loop fusion | flops 1605632 | bytes 1605632 | tf_op jit(solution)/shard_map/concatenate | solution.py:29
  13.1 10.2 %all-to-all-start = ((bf16[32,6,1792]{2,1,0:T(8,128)(2,1)}), bf16[32,6,1792]{2,1,0:T(8,128)(2,1)S(1)}, u32[]{:S(2)}, u32[]{:S(2)}) async-start(bf16[32,6,1792]{2,1,0:T(8,128)(2,1)} %reshape.402), calls=%async_computation | async-start | bytes 1835008 | tf_op jit(solution)/shard_map/all_to_all | solution.py:127
  23.4 1.9 %collective-permute-start = (s32[96]{0:T(128)S(1)}, s32[96]{0:T(128)S(1)}, u32[]{:S(2)}, u32[]{:S(2)}) collective-permute-start(s32[96]{0:T(128)S(1)} %get-tuple-element.41), channel_id=1, source_target_pairs={{0,1},{1,2},{2,3},{3,4},{4,5},{5,6},{6,7},{7,8},{8,9},{9,10},{10,1... | collective-permute-start | bytes 1160 | tf_op jit(solution)/shard_map/ppermute | solution.py:16
  25.3 3.6 %collective-permute-start.1 = (s32[96]{0:T(128)S(1)}, s32[96]{0:T(128)S(1)}, u32[]{:S(2)}, u32[]{:S(2)}) collective-permute-start(s32[96]{0:T(128)S(1)} %get-tuple-element.42), channel_id=1, source_target_pairs={{1,0},{2,1},{3,2},{4,3},{5,4},{6,5},{7,6},{8,7},{9,8},{10,9},{11,1... | collective-permute-start | bytes 1160 | tf_op jit(solution)/shard_map/ppermute | solution.py:19
  34.1 14.5 %all-to-all-done = bf16[32,6,1792]{2,1,0:T(8,128)(2,1)S(1)} async-done(((bf16[32,6,1792]{2,1,0:T(8,128)(2,1)}), bf16[32,6,1792]{2,1,0:T(8,128)(2,1)S(1)}, u32[]{:S(2)}, u32[]{:S(2)}) %all-to-all-start) | async-done | bytes 688160 | tf_op jit(solution)/shard_map/all_to_all | solution.py:127
  50.3 42.0 %all-gather.2.cloned.1.call-done = bf16[1792,3584]{1,0:T(8,128)(2,1)} async-done(((bf16[112,3584]{1,0:T(8,128)(2,1)}), bf16[1792,3584]{1,0:T(8,128)(2,1)}) %all-gather.2.cloned.1.call-update) | async-done | bytes 12845072 | tf_op jit(solution)/shard_map/all_gather | solution.py:28
  92.3 5.5 %fusion.9 = bf16[128,2688]{1,0:T(8,128)(2,1)S(1)} fusion(bf16[1792,3584]{1,0:T(8,128)(2,1)} %all-gather.2.cloned.1.call-done, f32[1792]{0:T(1024)S(1)} %copy-done.13, f32[128]{0:T(128)S(1)} %add_rsqrt_fusion, f32[128]{0:T(128)S(1)} %broadcast_multiply_fusion.2, bf16[128,1792]{1,0:T(8,128)(2,1)S(1)} %gather_fusion, pred[128]{0:T(512)(128)(4,1)S(1)} %compare_and_fusion.2), kind=kOutput, calls=%fused_computation.15 | convolution fusion | flops 1234845696 | bytes 10788992 | tf_op jit(solution)/shard_map/dot_general | solution.py:138
  98.8 2.3 %collective-permute-start.2 = (bf16[96,1792]{1,0:T(8,128)(2,1)}, bf16[96,1792]{1,0:T(8,128)(2,1)S(1)}, u32[]{:S(2)}, u32[]{:S(2)}) collective-permute-start(bf16[96,1792]{1,0:T(8,128)(2,1)} %get-tuple-element.35), channel_id=1, source_target_pairs={{0,1},{1,2},{2,3},{3,4},{4,5},{5,6},{6,7},{7,8},{8,9},{9,10},{10,1... | collective-permute-start | bytes 1032200 | tf_op jit(solution)/shard_map/ppermute | solution.py:16
  101.1 4.5 %collective-permute-start.3 = (bf16[96,1792]{1,0:T(8,128)(2,1)}, bf16[96,1792]{1,0:T(8,128)(2,1)S(1)}, u32[]{:S(2)}, u32[]{:S(2)}) collective-permute-start(bf16[96,1792]{1,0:T(8,128)(2,1)} %get-tuple-element.36), channel_id=1, source_target_pairs={{1,0},{2,1},{3,2},{4,3},{5,4},{6,5},{7,6},{8,7},{9,8},{10,9},{11,1... | collective-permute-start | bytes 1032200 | tf_op jit(solution)/shard_map/ppermute | solution.py:19
  106.7 1.9 %fusion.20 = f32[1792,128]{1,0:T(8,128)} fusion(bf16[1792,3584]{1,0:T(8,128)(2,1)S(1)} %copy-done.1, bf16[128,1792]{1,0:T(8,128)(2,1)S(1)} %bitcast.84), kind=kOutput, calls=%fused_computation.28 | convolution fusion | flops 411041792 | bytes 4358144 | tf_op jit(solution)/shard_map/dot_general | solution.py:55
  112.1 1.9 %fusion.17 = (bf16[1024,896]{1,0:T(8,128)(2,1)S(1)}, bf16[1024,896]{1,0:T(8,128)(2,1)S(1)}) fusion(s32[896]{0:T(1024)S(1)} %get-tuple-element.50, s32[896]{0:T(1024)S(1)} %get-tuple-element.51, s32[1024]{0:T(1024)S(1)} %get-tuple-element.52, s32[1024]{0:T(1024)S(1)} %get-tuple-element.53, pred[1024]{0:T(1024)(128)(4,1)} %fusion.93, ...), kind=kLoop, calls=%fused_computation.25 | loop fusion | flops 4587520 | bytes 4146048 | tf_op jit(solution)/shard_map/jit(_where)/select_n | solution.py:78
  118.7 2.1 %collective-permute-start.4 = (f32[96,1792]{1,0:T(8,128)S(1)}, f32[96,1792]{1,0:T(8,128)S(1)}, u32[]{:S(2)}, u32[]{:S(2)}) collective-permute-start(f32[96,1792]{1,0:T(8,128)S(1)} %get-tuple-element.29), channel_id=1, source_target_pairs={{0,1},{1,2},{2,3},{3,4},{4,5},{5,6},{6,7},{7,8},{8,9},{9,10},{10,1... | collective-permute-start | bytes 2064392 | tf_op jit(solution)/shard_map/ppermute | solution.py:169
  120.8 3.9 %collective-permute-start.5 = (f32[96,1792]{1,0:T(8,128)S(1)}, f32[96,1792]{1,0:T(8,128)S(1)}, u32[]{:S(2)}, u32[]{:S(2)}) collective-permute-start(f32[96,1792]{1,0:T(8,128)S(1)} %get-tuple-element.30), channel_id=1, source_target_pairs={{1,0},{2,1},{3,2},{4,3},{5,4},{6,5},{7,6},{8,7},{9,8},{10,9},{11,1... | collective-permute-start | bytes 2064392 | tf_op jit(solution)/shard_map/ppermute | solution.py:170
  124.7 1.8 fusion.38
  126.6 4.5 %collective-permute-done.4 = f32[96,1792]{1,0:T(8,128)S(1)} collective-permute-done((f32[96,1792]{1,0:T(8,128)S(1)}, f32[96,1792]{1,0:T(8,128)S(1)}, u32[]{:S(2)}, u32[]{:S(2)}) %collective-permute-start.4) | collective-permute-done | bytes 688160 | tf_op jit(solution)/shard_map/ppermute | solution.py:169
  131.2 1.7 collective-permute-done.5
  133.2 3.7 %fusion.104 = (f32[128]{0:T(128)S(1)}, f32[128]{0:T(128)S(1)}, f32[128,1792]{1,0:T(8,128)}) fusion(f32[128]{0:T(128)S(1)} %copy-done.12, f32[128]{0:T(128)S(1)} %broadcast_multiply_fusion.2, bf16[128,1792]{1,0:T(8,128)(2,1)S(1)} %gather_fusion, pred[128]{0:T(512)(128)(4,1)S(1)} %compare_and_fusion.2, f32[1792]{0:T(1024)S(1)} %copy-done.14, ...), kind=kOutput, calls=%fused_computation.149 | convolution fusion | flops 1236336384 | bytes 11708928 | tf_op jit(solution)/shard_map/dot_general | solution.py:174
  136.8 2.6 %scatter_custom_fusion = bf16[192,1792]{1,0:T(8,128)(2,1)S(1)} fusion(s32[128]{0:T(128)} %copy-done.10, f32[128,1792]{1,0:T(8,128)} %get-tuple-element.49, f32[128]{0:T(128)S(1)} %broadcast_multiply_fusion, f32[128]{0:T(128)S(1)} %broadcast_multiply_fusion.1, f32[128]{0:T(128)S(1)} %copy-done.12, f32[128]{0:T(128)S(1)} %broadcast_multiply_fusion.2, ...), kind=kCustom, calls=%fused_computation.82 | custom fusion | flops 2523136 | bytes 2525824 | tf_op jit(solution)/shard_map/scatter | solution.py:185
  140.6 9.9 %all-to-all-start.1 = ((bf16[32,6,1792]{2,1,0:T(8,128)(2,1)}), bf16[32,6,1792]{2,1,0:T(8,128)(2,1)}, u32[]{:S(2)}, u32[]{:S(2)}) async-start(bf16[32,6,1792]{2,1,0:T(8,128)(2,1)} %reshape.411), calls=%async_computation.1 | async-start | bytes 1835008 | tf_op jit(solution)/shard_map/all_to_all | solution.py:188
  150.6 3.8 %fusion.18 = f32[1024,896]{1,0:T(8,128)} fusion(s32[896]{0:T(1024)S(1)} %get-tuple-element.50, s32[896]{0:T(1024)S(1)} %get-tuple-element.51, s32[1024]{0:T(1024)S(1)} %get-tuple-element.52, s32[1024]{0:T(1024)S(1)} %get-tuple-element.53, pred[1024]{0:T(1024)(128)(4,1)S(1)} %copy-done.8, pred[896]{0:T(1024)(128)(4,1)S(1)} %fusion.92, ...), kind=kOutput, calls=%fused_computation.26 | convolution fusion | flops 591855616 | bytes 5579648 | tf_op jit(solution)/shard_map/dot_general | solution.py:109
  154.4 2.2 %reduce_sum.66 = bf16[128,896]{1,0:T(8,128)(2,1)S(1)} reduce(f32[8,128,896]{2,1,0:T(8,128)} %bitcast.75, f32[]{:T(128)} %constant.147.clone.1), dimensions={0}, to_apply=%region_4.6 | reduce | flops 802816 | bytes 3899396 | tf_op jit(solution)/shard_map/reduce_sum | solution.py:85
  158.5 2.6 %fusion.29 = f32[1,128,896]{2,1,0:T(8,128)S(1)} fusion(bf16[128,1792]{0,1:T(8,128)(2,1)S(1)} %bitcast.80, bf16[1792,3584]{1,0:T(8,128)(2,1)} %all-gather.2.cloned.1.call-done), kind=kOutput, calls=%fused_computation.41 | convolution fusion | flops 411041792 | bytes 4128768 | tf_op jit(solution)/shard_map/dot_general | solution.py:45
  161.1 2.6 %fusion.32 = f32[1,128,896]{2,1,0:T(8,128)S(1)} fusion(bf16[128,1792]{0,1:T(8,128)(2,1)S(1)} %bitcast.79, bf16[1792,3584]{1,0:T(8,128)(2,1)} %all-gather.2.cloned.1.call-done), kind=kOutput, calls=%fused_computation.42 | convolution fusion | flops 411041792 | bytes 4128768 | tf_op jit(solution)/shard_map/dot_general | solution.py:45
  164.7 12.3 %all-to-all-done.1 = bf16[32,6,1792]{2,1,0:T(8,128)(2,1)} async-done(((bf16[32,6,1792]{2,1,0:T(8,128)(2,1)}), bf16[32,6,1792]{2,1,0:T(8,128)(2,1)}, u32[]{:S(2)}, u32[]{:S(2)}) %all-to-all-start.1) | async-done | bytes 688160 | tf_op jit(solution)/shard_map/all_to_all | solution.py:188
  (124 shorter events, 28.4 us)
Async XLA Ops:
  7.2 85.1 %all-gather.2.cloned.1.call-start = ((), (), s32[]{:S(2)}) async-start(), calls=%async_computation.2 | async-start | bytes 13647872 | tf_op jit(solution)/shard_map/all_gather | solution.py:28
  11.9 11.4 %copy-start.15 = (s32[1,128]{1,0:T(1,128)S(1)}, s32[1,128]{1,0:T(1,128)}, u32[]{:S(2)}) copy-start(s32[1,128]{1,0:T(1,128)} %param.17) | copy-start | bytes 1540
  11.9 18.4 %copy-start.16 = (s32[1,128]{1,0:T(1,128)S(1)}, s32[1,128]{1,0:T(1,128)}, u32[]{:S(2)}) copy-start(s32[1,128]{1,0:T(1,128)} %param.16) | copy-start | bytes 1540
  13.1 35.5 %all-to-all-start = ((bf16[32,6,1792]{2,1,0:T(8,128)(2,1)}), bf16[32,6,1792]{2,1,0:T(8,128)(2,1)S(1)}, u32[]{:S(2)}, u32[]{:S(2)}) async-start(bf16[32,6,1792]{2,1,0:T(8,128)(2,1)} %reshape.402), calls=%async_computation | async-start | bytes 1835008 | tf_op jit(solution)/shard_map/all_to_all | solution.py:127
  23.4 10.5 %collective-permute-start = (s32[96]{0:T(128)S(1)}, s32[96]{0:T(128)S(1)}, u32[]{:S(2)}, u32[]{:S(2)}) collective-permute-start(s32[96]{0:T(128)S(1)} %get-tuple-element.41), channel_id=1, source_target_pairs={{0,1},{1,2},{2,3},{3,4},{4,5},{5,6},{6,7},{7,8},{8,9},{9,10},{10,1... | collective-permute-start | bytes 1160 | tf_op jit(solution)/shard_map/ppermute | solution.py:16
  25.3 8.6 %collective-permute-start.1 = (s32[96]{0:T(128)S(1)}, s32[96]{0:T(128)S(1)}, u32[]{:S(2)}, u32[]{:S(2)}) collective-permute-start(s32[96]{0:T(128)S(1)} %get-tuple-element.42), channel_id=1, source_target_pairs={{1,0},{2,1},{3,2},{4,3},{5,4},{6,5},{7,6},{8,7},{9,8},{10,9},{11,1... | collective-permute-start | bytes 1160 | tf_op jit(solution)/shard_map/ppermute | solution.py:19
  48.8 43.5 %copy-start.13 = (f32[1792]{0:T(1024)S(1)}, f32[1792]{0:T(1024)}, u32[]{:S(2)}) copy-start(f32[1792]{0:T(1024)} %param.18) | copy-start | bytes 21508
  50.3 47.6 %copy-start.11 = (f32[128]{0:T(128)}, f32[128]{0:T(128)S(1)}, u32[]{:S(2)}) copy-start(f32[128]{0:T(128)S(1)} %add_rsqrt_fusion) | copy-start | bytes 1540
  50.3 55.3 %copy-start.4 = (bf16[1,128,1792]{2,1,0:T(8,128)(2,1)S(1)}, bf16[1,128,1792]{2,1,0:T(8,128)(2,1)}, u32[]{:S(2)}) copy-start(bf16[1,128,1792]{2,1,0:T(8,128)(2,1)} %param.21) | copy-start | bytes 1376260
  92.3 13.3 %copy-start.1 = (bf16[1792,3584]{1,0:T(8,128)(2,1)S(1)}, bf16[1792,3584]{1,0:T(8,128)(2,1)}, u32[]{:S(2)}) copy-start(bf16[1792,3584]{1,0:T(8,128)(2,1)} %all-gather.2.cloned.1.call-done) | copy-start | bytes 38535172
  97.9 10.7 %copy-start.2 = (bf16[128,2688]{1,0:T(8,128)(2,1)}, bf16[128,2688]{1,0:T(8,128)(2,1)S(1)}, u32[]{:S(2)}) copy-start(bf16[128,2688]{1,0:T(8,128)(2,1)S(1)} %fusion.9) | copy-start | bytes 2064388
  98.8 15.2 %collective-permute-start.2 = (bf16[96,1792]{1,0:T(8,128)(2,1)}, bf16[96,1792]{1,0:T(8,128)(2,1)S(1)}, u32[]{:S(2)}, u32[]{:S(2)}) collective-permute-start(bf16[96,1792]{1,0:T(8,128)(2,1)} %get-tuple-element.35), channel_id=1, source_target_pairs={{0,1},{1,2},{2,3},{3,4},{4,5},{5,6},{6,7},{7,8},{8,9},{9,10},{10,1... | collective-permute-start | bytes 1032200 | tf_op jit(solution)/shard_map/ppermute | solution.py:16
  101.1 12.9 %collective-permute-start.3 = (bf16[96,1792]{1,0:T(8,128)(2,1)}, bf16[96,1792]{1,0:T(8,128)(2,1)S(1)}, u32[]{:S(2)}, u32[]{:S(2)}) collective-permute-start(bf16[96,1792]{1,0:T(8,128)(2,1)} %get-tuple-element.36), channel_id=1, source_target_pairs={{1,0},{2,1},{3,2},{4,3},{5,4},{6,5},{7,6},{8,7},{9,8},{10,9},{11,1... | collective-permute-start | bytes 1032200 | tf_op jit(solution)/shard_map/ppermute | solution.py:19
  118.6 6.1 %slice-start.6 = ((bf16[320,1792]{1,0:T(8,128)(2,1)}), bf16[320,896]{1,0:T(8,128)(2,1)S(1)}, s32[]{:S(2)}) async-start(bf16[320,1792]{1,0:T(8,128)(2,1)} %copy-done.3), calls=%async_computation.9 | async-start | bytes 1146880 | tf_op jit(solution)/shard_map/slice | solution.py:101
  118.6 6.1 %copy-start.5 = (s32[8,320]{0,1:T(8,128)S(1)}, s32[8,320]{0,1:T(8,128)}, u32[]{:S(2)}) copy-start(s32[8,320]{0,1:T(8,128)} %copy.28) | copy-start | bytes 30724
  118.6 6.1 %copy-start.6 = (s32[8,320]{0,1:T(8,128)S(1)}, s32[8,320]{0,1:T(8,128)}, u32[]{:S(2)}) copy-start(s32[8,320]{0,1:T(8,128)} %copy.29) | copy-start | bytes 30724
  118.7 12.4 %collective-permute-start.4 = (f32[96,1792]{1,0:T(8,128)S(1)}, f32[96,1792]{1,0:T(8,128)S(1)}, u32[]{:S(2)}, u32[]{:S(2)}) collective-permute-start(f32[96,1792]{1,0:T(8,128)S(1)} %get-tuple-element.29), channel_id=1, source_target_pairs={{0,1},{1,2},{2,3},{3,4},{4,5},{5,6},{6,7},{7,8},{8,9},{9,10},{10,1... | collective-permute-start | bytes 2064392 | tf_op jit(solution)/shard_map/ppermute | solution.py:169
  120.8 12.1 %collective-permute-start.5 = (f32[96,1792]{1,0:T(8,128)S(1)}, f32[96,1792]{1,0:T(8,128)S(1)}, u32[]{:S(2)}, u32[]{:S(2)}) collective-permute-start(f32[96,1792]{1,0:T(8,128)S(1)} %get-tuple-element.30), channel_id=1, source_target_pairs={{1,0},{2,1},{3,2},{4,3},{5,4},{6,5},{7,6},{8,7},{9,8},{10,9},{11,1... | collective-permute-start | bytes 2064392 | tf_op jit(solution)/shard_map/ppermute | solution.py:170
  124.7 8.4 %slice-start = ((s8[12845056]{0:T(1024)(128)(4,1)}), s8[4194304]{0:T(1024)(128)(4,1)S(1)}, s32[]{:S(2)}) async-start(s8[12845056]{0:T(1024)(128)(4,1)} %bitcast.76), calls=%async_computation.3 | async-start | bytes 8388608
  124.7 8.4 %slice-start.1 = ((s8[12845056]{0:T(1024)(128)(4,1)}), s8[4194304]{0:T(1024)(128)(4,1)S(1)}, s32[]{:S(2)}) async-start(s8[12845056]{0:T(1024)(128)(4,1)} %bitcast.76), calls=%async_computation.4 | async-start | bytes 8388608
  124.7 8.4 %slice-start.2 = ((s8[12845056]{0:T(1024)(128)(4,1)}), s8[4194304]{0:T(1024)(128)(4,1)S(1)}, s32[]{:S(2)}) async-start(s8[12845056]{0:T(1024)(128)(4,1)} %bitcast.76), calls=%async_computation.5 | async-start | bytes 8388608
  126.5 6.6 %slice-start.3 = ((s8[12845056]{0:T(1024)(128)(4,1)}), s8[262144]{0:T(1024)(128)(4,1)S(1)}, s32[]{:S(2)}) async-start(s8[12845056]{0:T(1024)(128)(4,1)} %bitcast.76), calls=%async_computation.6 | async-start | bytes 524288
  139.5 11.1 %copy-start.8 = (pred[1024]{0:T(1024)(128)(4,1)S(1)}, pred[1024]{0:T(1024)(128)(4,1)}, u32[]{:S(2)}) copy-start(pred[1024]{0:T(1024)(128)(4,1)} %fusion.93) | copy-start | bytes 3076
  140.6 36.4 %all-to-all-start.1 = ((bf16[32,6,1792]{2,1,0:T(8,128)(2,1)}), bf16[32,6,1792]{2,1,0:T(8,128)(2,1)}, u32[]{:S(2)}, u32[]{:S(2)}) async-start(bf16[32,6,1792]{2,1,0:T(8,128)(2,1)} %reshape.411), calls=%async_computation.1 | async-start | bytes 1835008 | tf_op jit(solution)/shard_map/all_to_all | solution.py:188
  (9 other events, 18.7 us)
Sparse Core Ops, SparseCore 0:
  10.5 81.8 all-gather.1

commit v13 on v12

--- a/solution.py
+++ b/solution.py
@@ -135,14 +135,15 @@
     packed = jnp.take(incoming, pick_rows, axis=0)
     full_qkv, full_out = gather_weights(qkv_weight, out_weight)
     values, unit_rows, inv_dev, normed = normalize(packed, norm_gain)
-    projected = jnp.dot(normed, full_qkv, preferred_element_type=jnp.float32).astype(jnp.bfloat16)
-    queries = projected[:, :all_heads]
-    keyval = projected[:, all_heads:]
+    wide_normed = extended(normed, (("tensor", 0),), MOST)
+    queries = jnp.dot(
+        normed, full_qkv[:, :all_heads], preferred_element_type=jnp.float32
+    ).astype(jnp.bfloat16)
+    wide_kv = jnp.dot(
+        wide_normed, full_qkv[:, all_heads:], preferred_element_type=jnp.float32
+    ).astype(jnp.bfloat16)
     seg_plus = segments[0] + 1
-    wide_kv, wide_seg = (
-        extended(keyval, (("tensor", 0),), MOST),
-        extended(seg_plus, (("tensor", 0),), MOST),
-    )
+    wide_seg = extended(seg_plus, (("tensor", 0),), MOST)
     attn_probs, prob_low, attended, query_blocks = attend(queries, wide_kv, seg_plus, wide_seg)
     layer_out = (values + times_out(attended, full_out)).astype(jnp.bfloat16)
     grad_rows = grad_out[0]

time: 188 us -> 188 us (level)
  matrix products: 26.5 us -> 32 us
  waiting for transfers between devices: 75 us -> 70 us
    all_gather x1, waiting for transfers between devices: 42 us -> 38 us  [gather_weights(): lax.all_gather(jnp.concatenate([qkv_weight, out_wide], axis=1), 'tensor',...]
    dot_general x2, matrix products: 2.94 us -> 5.82 us  [times_out_t(): lax.dot_general(grad_rows[:, side * half:(side + 1) * half], out_pairs, (...]
    dot_general x1 -> x2, matrix products: 5.54 us -> 8.22 us  [the longest x1 5.3 us: local(): jnp.dot(wide_normed, full_qkv[:, all_heads:], preferred_element_type=jnp....]
    unnamed x47 -> x49, local copies, waits for them, and re-layouts: 3.07 us -> 3.81 us
  transfers between devices with their start and end apart: 9 -> 9, of which waited for: 5 -> 5; matrix products, arithmetic and copies ran while one was open for 18% -> 19% of each run, Pallas kernels for 0% -> 0%
where the time goes in v13:
time: 188 us; the launch traced here: 186 us
  waiting for transfers between devices  70 us (37%)
  starting transfers between devices  37.4 us (20%)
  matrix products  32 us (17%)
  local copies, waits for them, and re-layouts  18 us (10%)
  between operations  14.8 us (8%)
  other arithmetic  13.9 us (7%)
    all_gather x1, waiting for transfers between devices, gather_weights(): lax.all_gather(jnp.concatenate([qkv_weight, out_wide], axis=1), 'tensor',...  38 us
    all_to_all x1, waiting for transfers between devices, local(): lax.all_to_all(outgoing, 'dp', split_axis=0, concat_axis=0, tiled=True)  14 us
    all_to_all x1, waiting for transfers between devices, local(): lax.all_to_all(back_slots, 'dp', split_axis=0, concat_axis=0, tiled=True)  11.7 us
    all_to_all x1, starting transfers between devices, local(): lax.all_to_all(outgoing, 'dp', split_axis=0, concat_axis=0, tiled=True)  10.3 us
    all_to_all x1, starting transfers between devices, local(): lax.all_to_all(back_slots, 'dp', split_axis=0, concat_axis=0, tiled=True)  9.91 us
    ppermute x2, starting transfers between devices, extended(): lax.ppermute(lax.slice_in_dim(block, 0, width, axis=dim), axis, backward)  7.47 us
    dot_general x2, matrix products, times_out_t(): lax.dot_general(grad_rows[:, side * half:(side + 1) * half], out_pairs, (...  5.82 us
    dot_general x1, matrix products, local(): jnp.dot(wide_normed, full_qkv[:, all_heads:], preferred_element_type=jnp....  5.3 us
  transfers between devices with their start and end apart: 9, of which 5 were waited for; matrix products, arithmetic and copies ran while one was open for 19% of the time, Pallas kernels for 0%

profile of v13, /device:TPU:66, one launch (start us, length us, event | category | flops | bytes accessed | tf_op | source)
XLA Modules:
  0.0 186.1 jit_solution(10013343516257067271)
XLA Ops:
  8.3 2.0 %pad_maximum_fusion = bf16[112,3584]{1,0:T(8,128)(2,1)} fusion(bf16[112,896]{1,0:T(8,128)(2,1)S(1)} %reshape.404, bf16[112,2688]{1,0:T(8,128)(2,1)} %param.19), kind=kLoop, calls=%fused_computation.72 | loop fusion | flops 1605632 | bytes 1605632 | tf_op jit(solution)/shard_map/concatenate | solution.py:29
  13.0 10.3 %all-to-all-start = ((bf16[32,6,1792]{2,1,0:T(8,128)(2,1)}), bf16[32,6,1792]{2,1,0:T(8,128)(2,1)S(1)}, u32[]{:S(2)}, u32[]{:S(2)}) async-start(bf16[32,6,1792]{2,1,0:T(8,128)(2,1)} %reshape.402), calls=%async_computation | async-start | bytes 1835008 | tf_op jit(solution)/shard_map/all_to_all | solution.py:127
  23.4 1.9 %collective-permute-start = (s32[96]{0:T(128)S(1)}, s32[96]{0:T(128)S(1)}, u32[]{:S(2)}, u32[]{:S(2)}) collective-permute-start(s32[96]{0:T(128)S(1)} %get-tuple-element.41), channel_id=1, source_target_pairs={{0,1},{1,2},{2,3},{3,4},{4,5},{5,6},{6,7},{7,8},{8,9},{9,10},{10,1... | collective-permute-start | bytes 1160 | tf_op jit(solution)/shard_map/ppermute | solution.py:16
  25.3 3.6 %collective-permute-start.1 = (s32[96]{0:T(128)S(1)}, s32[96]{0:T(128)S(1)}, u32[]{:S(2)}, u32[]{:S(2)}) collective-permute-start(s32[96]{0:T(128)S(1)} %get-tuple-element.42), channel_id=1, source_target_pairs={{1,0},{2,1},{3,2},{4,3},{5,4},{6,5},{7,6},{8,7},{9,8},{10,9},{11,1... | collective-permute-start | bytes 1160 | tf_op jit(solution)/shard_map/ppermute | solution.py:19
  34.5 14.0 %all-to-all-done = bf16[32,6,1792]{2,1,0:T(8,128)(2,1)S(1)} async-done(((bf16[32,6,1792]{2,1,0:T(8,128)(2,1)}), bf16[32,6,1792]{2,1,0:T(8,128)(2,1)S(1)}, u32[]{:S(2)}, u32[]{:S(2)}) %all-to-all-start) | async-done | bytes 688160 | tf_op jit(solution)/shard_map/all_to_all | solution.py:127
  52.2 1.9 %collective-permute-start.2 = (bf16[96,1792]{1,0:T(8,128)(2,1)}, bf16[96,1792]{1,0:T(8,128)(2,1)}, u32[]{:S(2)}, u32[]{:S(2)}) collective-permute-start(bf16[96,1792]{1,0:T(8,128)(2,1)} %get-tuple-element.37), channel_id=1, source_target_pairs={{0,1},{1,2},{2,3},{3,4},{4,5},{5,6},{6,7},{7,8},{8,9},{9,10},{10,1... | collective-permute-start | bytes 1032200 | tf_op jit(solution)/shard_map/ppermute | solution.py:16
  54.1 3.8 %collective-permute-start.3 = (bf16[96,1792]{1,0:T(8,128)(2,1)S(1)}, bf16[96,1792]{1,0:T(8,128)(2,1)}, u32[]{:S(2)}, u32[]{:S(2)}) collective-permute-start(bf16[96,1792]{1,0:T(8,128)(2,1)S(1)} %get-tuple-element.38), channel_id=1, source_target_pairs={{1,0},{2,1},{3,2},{4,3},{5,4},{6,5},{7,6},{8,7},{9,8},{10,9},{11,1... | collective-permute-start | bytes 1032200 | tf_op jit(solution)/shard_map/ppermute | solution.py:19
  58.0 38.0 %all-gather.2.cloned.1.call-done = bf16[1792,3584]{1,0:T(8,128)(2,1)} async-done(((bf16[112,3584]{1,0:T(8,128)(2,1)}), bf16[1792,3584]{1,0:T(8,128)(2,1)}) %all-gather.2.cloned.1.call-update) | async-done | bytes 12845072 | tf_op jit(solution)/shard_map/all_gather | solution.py:28
  96.0 2.9 %fusion.24 = f32[1792,128]{1,0:T(8,128)S(1)} fusion(bf16[1792,3584]{1,0:T(8,128)(2,1)} %all-gather.2.cloned.1.call-done, bf16[128,1792]{1,0:T(8,128)(2,1)S(1)} %bitcast.84), kind=kOutput, calls=%fused_computation.32 | convolution fusion | flops 411041792 | bytes 4358144 | tf_op jit(solution)/shard_map/dot_general | solution.py:55
  99.9 2.9 %fusion.22 = f32[1792,128]{1,0:T(8,128)S(1)} fusion(bf16[1792,3584]{1,0:T(8,128)(2,1)} %all-gather.2.cloned.1.call-done, bf16[128,1792]{1,0:T(8,128)(2,1)S(1)} %bitcast.85), kind=kOutput, calls=%fused_computation.30 | convolution fusion | flops 411041792 | bytes 4358144 | tf_op jit(solution)/shard_map/dot_general | solution.py:55
  104.1 5.3 %fusion.11 = bf16[320,1792]{1,0:T(8,128)(2,1)S(1)} fusion(bf16[1792,3584]{1,0:T(8,128)(2,1)} %all-gather.2.cloned.1.call-done, bf16[96,1792]{1,0:T(8,128)(2,1)} %collective-permute-done.3, bf16[128,1792]{1,0:T(8,128)(2,1)S(1)} %fusion.58, bf16[96,1792]{1,0:T(8,128)(2,1)} %collective-permute-done.2), kind=kOutput, calls=%fused_computation.23 | convolution fusion | flops 2059223040 | bytes 8716288 | tf_op jit(solution)/shard_map/dot_general | solution.py:142
  109.5 2.9 %fusion.40 = bf16[128,896]{1,0:T(8,128)(2,1)S(1)} fusion(bf16[128,1792]{1,0:T(8,128)(2,1)S(1)} %fusion.58, bf16[1792,3584]{1,0:T(8,128)(2,1)} %all-gather.2.cloned.1.call-done), kind=kOutput, calls=%fused_computation.46 | convolution fusion | flops 411156480 | bytes 3899392 | tf_op jit(solution)/shard_map/dot_general | solution.py:139
  118.0 2.3 %collective-permute-start.4 = (f32[96,1792]{1,0:T(8,128)S(1)}, f32[96,1792]{1,0:T(8,128)S(1)}, u32[]{:S(2)}, u32[]{:S(2)}) collective-permute-start(f32[96,1792]{1,0:T(8,128)S(1)} %get-tuple-element.29), channel_id=1, source_target_pairs={{0,1},{1,2},{2,3},{3,4},{4,5},{5,6},{6,7},{7,8},{8,9},{9,10},{10,1... | collective-permute-start | bytes 2064392 | tf_op jit(solution)/shard_map/ppermute | solution.py:170
  120.3 3.6 %collective-permute-start.5 = (f32[96,1792]{1,0:T(8,128)S(1)}, f32[96,1792]{1,0:T(8,128)S(1)}, u32[]{:S(2)}, u32[]{:S(2)}) collective-permute-start(f32[96,1792]{1,0:T(8,128)S(1)} %get-tuple-element.30), channel_id=1, source_target_pairs={{1,0},{2,1},{3,2},{4,3},{5,4},{6,5},{7,6},{8,7},{9,8},{10,9},{11,1... | collective-permute-start | bytes 2064392 | tf_op jit(solution)/shard_map/ppermute | solution.py:171
  124.0 1.8 fusion.43
  125.9 4.6 %collective-permute-done.4 = f32[96,1792]{1,0:T(8,128)S(1)} collective-permute-done((f32[96,1792]{1,0:T(8,128)S(1)}, f32[96,1792]{1,0:T(8,128)S(1)}, u32[]{:S(2)}, u32[]{:S(2)}) %collective-permute-start.4) | collective-permute-done | bytes 688160 | tf_op jit(solution)/shard_map/ppermute | solution.py:170
  132.5 3.7 %fusion.111 = (f32[128]{0:T(128)S(1)}, f32[128]{0:T(128)S(1)}, f32[128,1792]{1,0:T(8,128)}) fusion(f32[128]{0:T(128)S(1)} %copy-done.11, f32[128]{0:T(128)S(1)} %copy-done.8, bf16[128,1792]{1,0:T(8,128)(2,1)S(1)} %gather_fusion, pred[128]{0:T(512)(128)(4,1)S(1)} %compare_and_fusion.2, f32[1792]{0:T(1024)S(1)} %copy-done.6, ...), kind=kOutput, calls=%fused_computation.154 | convolution fusion | flops 1236336384 | bytes 11708928 | tf_op jit(solution)/shard_map/dot_general | solution.py:175
  136.2 2.6 %scatter_custom_fusion = bf16[192,1792]{1,0:T(8,128)(2,1)S(1)} fusion(s32[128]{0:T(128)} %copy-done.15, f32[128,1792]{1,0:T(8,128)} %get-tuple-element.49, f32[128]{0:T(128)S(1)} %broadcast_multiply_fusion, f32[128]{0:T(128)S(1)} %broadcast_multiply_fusion.1, f32[128]{0:T(128)S(1)} %copy-done.11, f32[128]{0:T(128)S(1)} %copy-done.8, ...), kind=kCustom, calls=%fused_computation.89 | custom fusion | flops 2523136 | bytes 2525824 | tf_op jit(solution)/shard_map/scatter | solution.py:186
  140.0 9.9 %all-to-all-start.1 = ((bf16[32,6,1792]{2,1,0:T(8,128)(2,1)}), bf16[32,6,1792]{2,1,0:T(8,128)(2,1)}, u32[]{:S(2)}, u32[]{:S(2)}) async-start(bf16[32,6,1792]{2,1,0:T(8,128)(2,1)} %reshape.411), calls=%async_computation.1 | async-start | bytes 1835008 | tf_op jit(solution)/shard_map/all_to_all | solution.py:189
  149.9 3.8 %fusion.20 = f32[1024,896]{1,0:T(8,128)} fusion(s32[896]{0:T(1024)S(1)} %get-tuple-element.50, s32[896]{0:T(1024)S(1)} %get-tuple-element.51, s32[1024]{0:T(1024)S(1)} %get-tuple-element.52, s32[1024]{0:T(1024)S(1)} %get-tuple-element.53, pred[1024]{0:T(1024)(128)(4,1)S(1)} %copy-done.13, pred[896]{0:T(1024)(128)(4,1)S(1)} %copy-done.12, ...), kind=kOutput, calls=%fused_computation.28 | convolution fusion | flops 591855616 | bytes 5579648 | tf_op jit(solution)/shard_map/dot_general | solution.py:109
  153.7 2.2 %reduce_sum.66 = bf16[128,896]{1,0:T(8,128)(2,1)S(1)} reduce(f32[8,128,896]{2,1,0:T(8,128)} %bitcast.76, f32[]{:T(128)} %constant.147.clone.1), dimensions={0}, to_apply=%region_4.6 | reduce | flops 802816 | bytes 3899396 | tf_op jit(solution)/shard_map/reduce_sum | solution.py:85
  157.8 2.6 %fusion.31 = f32[1,128,896]{2,1,0:T(8,128)S(1)} fusion(bf16[128,1792]{0,1:T(8,128)(2,1)S(1)} %bitcast.81, bf16[1792,3584]{1,0:T(8,128)(2,1)} %all-gather.2.cloned.1.call-done), kind=kOutput, calls=%fused_computation.43 | convolution fusion | flops 411041792 | bytes 4128768 | tf_op jit(solution)/shard_map/dot_general | solution.py:45
  160.4 2.6 %fusion.34 = f32[1,128,896]{2,1,0:T(8,128)S(1)} fusion(bf16[128,1792]{0,1:T(8,128)(2,1)S(1)} %bitcast.80, bf16[1792,3584]{1,0:T(8,128)(2,1)} %all-gather.2.cloned.1.call-done), kind=kOutput, calls=%fused_computation.44 | convolution fusion | flops 411041792 | bytes 4128768 | tf_op jit(solution)/shard_map/dot_general | solution.py:45
  164.0 11.7 %all-to-all-done.1 = bf16[32,6,1792]{2,1,0:T(8,128)(2,1)} async-done(((bf16[32,6,1792]{2,1,0:T(8,128)(2,1)}), bf16[32,6,1792]{2,1,0:T(8,128)(2,1)}, u32[]{:S(2)}, u32[]{:S(2)}) %all-to-all-start.1) | async-done | bytes 688160 | tf_op jit(solution)/shard_map/all_to_all | solution.py:189
  (123 shorter events, 30.3 us)
Async XLA Ops:
  7.2 3.4 %copy-start = (bf16[1,192,1792]{2,1,0:T(8,128)(2,1)S(1)}, bf16[1,192,1792]{2,1,0:T(8,128)(2,1)}, u32[]{:S(2)}) copy-start(bf16[1,192,1792]{2,1,0:T(8,128)(2,1)} %param.14) | copy-start | bytes 2064388
  7.2 3.1 %copy-start.9 = (s32[1,1,32,6]{2,1,3,0:T(1,128)S(1)}, s32[1,1,32,6]{2,1,3,0:T(1,128)}, u32[]{:S(2)}) copy-start(s32[1,1,32,6]{2,1,3,0:T(1,128)} %param.15) | copy-start | bytes 2308
  7.2 88.8 %all-gather.2.cloned.1.call-start = ((), (), s32[]{:S(2)}) async-start(), calls=%async_computation.2 | async-start | bytes 13647872 | tf_op jit(solution)/shard_map/all_gather | solution.py:28
  11.8 11.4 %copy-start.16 = (s32[1,128]{1,0:T(1,128)S(1)}, s32[1,128]{1,0:T(1,128)}, u32[]{:S(2)}) copy-start(s32[1,128]{1,0:T(1,128)} %param.17) | copy-start | bytes 1540
  11.9 18.4 %copy-start.17 = (s32[1,128]{1,0:T(1,128)S(1)}, s32[1,128]{1,0:T(1,128)}, u32[]{:S(2)}) copy-start(s32[1,128]{1,0:T(1,128)} %param.16) | copy-start | bytes 1540
  13.0 35.5 %all-to-all-start = ((bf16[32,6,1792]{2,1,0:T(8,128)(2,1)}), bf16[32,6,1792]{2,1,0:T(8,128)(2,1)S(1)}, u32[]{:S(2)}, u32[]{:S(2)}) async-start(bf16[32,6,1792]{2,1,0:T(8,128)(2,1)} %reshape.402), calls=%async_computation | async-start | bytes 1835008 | tf_op jit(solution)/shard_map/all_to_all | solution.py:127
  23.4 10.9 %collective-permute-start = (s32[96]{0:T(128)S(1)}, s32[96]{0:T(128)S(1)}, u32[]{:S(2)}, u32[]{:S(2)}) collective-permute-start(s32[96]{0:T(128)S(1)} %get-tuple-element.41), channel_id=1, source_target_pairs={{0,1},{1,2},{2,3},{3,4},{4,5},{5,6},{6,7},{7,8},{8,9},{9,10},{10,1... | collective-permute-start | bytes 1160 | tf_op jit(solution)/shard_map/ppermute | solution.py:16
  25.3 9.0 %collective-permute-start.1 = (s32[96]{0:T(128)S(1)}, s32[96]{0:T(128)S(1)}, u32[]{:S(2)}, u32[]{:S(2)}) collective-permute-start(s32[96]{0:T(128)S(1)} %get-tuple-element.42), channel_id=1, source_target_pairs={{1,0},{2,1},{3,2},{4,3},{5,4},{6,5},{7,6},{8,7},{9,8},{10,9},{11,1... | collective-permute-start | bytes 1160 | tf_op jit(solution)/shard_map/ppermute | solution.py:19
  49.7 46.3 %copy-start.2 = (bf16[1,128,1792]{2,1,0:T(8,128)(2,1)S(1)}, bf16[1,128,1792]{2,1,0:T(8,128)(2,1)}, u32[]{:S(2)}) copy-start(bf16[1,128,1792]{2,1,0:T(8,128)(2,1)} %param.21) | copy-start | bytes 1376260
  52.2 51.9 %collective-permute-start.2 = (bf16[96,1792]{1,0:T(8,128)(2,1)}, bf16[96,1792]{1,0:T(8,128)(2,1)}, u32[]{:S(2)}, u32[]{:S(2)}) collective-permute-start(bf16[96,1792]{1,0:T(8,128)(2,1)} %get-tuple-element.37), channel_id=1, source_target_pairs={{0,1},{1,2},{2,3},{3,4},{4,5},{5,6},{6,7},{7,8},{8,9},{9,10},{10,1... | collective-permute-start | bytes 1032200 | tf_op jit(solution)/shard_map/ppermute | solution.py:16
  54.1 50.0 %collective-permute-start.3 = (bf16[96,1792]{1,0:T(8,128)(2,1)S(1)}, bf16[96,1792]{1,0:T(8,128)(2,1)}, u32[]{:S(2)}, u32[]{:S(2)}) collective-permute-start(bf16[96,1792]{1,0:T(8,128)(2,1)S(1)} %get-tuple-element.38), channel_id=1, source_target_pairs={{1,0},{2,1},{3,2},{4,3},{5,4},{6,5},{7,6},{8,7},{9,8},{10,9},{11,1... | collective-permute-start | bytes 1032200 | tf_op jit(solution)/shard_map/ppermute | solution.py:19
  109.4 5.4 %copy-start.1 = (bf16[320,1792]{1,0:T(8,128)(2,1)}, bf16[320,1792]{1,0:T(8,128)(2,1)S(1)}, u32[]{:S(2)}) copy-start(bf16[320,1792]{1,0:T(8,128)(2,1)S(1)} %fusion.11) | copy-start | bytes 3440644
  109.5 2.9 %copy-start.12 = (pred[896]{0:T(1024)(128)(4,1)S(1)}, pred[896]{0:T(1024)(128)(4,1)}, u32[]{:S(2)}) copy-start(pred[896]{0:T(1024)(128)(4,1)} %fusion.98) | copy-start | bytes 2692
  109.5 2.9 %copy-start.13 = (pred[1024]{0:T(1024)(128)(4,1)S(1)}, pred[1024]{0:T(1024)(128)(4,1)}, u32[]{:S(2)}) copy-start(pred[1024]{0:T(1024)(128)(4,1)} %fusion.99) | copy-start | bytes 3076
  117.9 6.1 %slice-start.4 = ((bf16[320,1792]{1,0:T(8,128)(2,1)}), bf16[320,896]{1,0:T(8,128)(2,1)S(1)}, s32[]{:S(2)}) async-start(bf16[320,1792]{1,0:T(8,128)(2,1)} %copy-done.1), calls=%async_computation.7 | async-start | bytes 1146880 | tf_op jit(solution)/shard_map/slice | solution.py:101
  117.9 6.1 %copy-start.3 = (s32[8,320]{0,1:T(8,128)S(1)}, s32[8,320]{0,1:T(8,128)}, u32[]{:S(2)}) copy-start(s32[8,320]{0,1:T(8,128)} %copy.29) | copy-start | bytes 30724
  117.9 6.1 %copy-start.4 = (pred[8,320]{0,1:T(8,128)(4,1)S(1)}, pred[8,320]{0,1:T(8,128)(4,1)}, u32[]{:S(2)}) copy-start(pred[8,320]{0,1:T(8,128)(4,1)} %copy.27) | copy-start | bytes 7684
  118.0 12.4 %collective-permute-start.4 = (f32[96,1792]{1,0:T(8,128)S(1)}, f32[96,1792]{1,0:T(8,128)S(1)}, u32[]{:S(2)}, u32[]{:S(2)}) collective-permute-start(f32[96,1792]{1,0:T(8,128)S(1)} %get-tuple-element.29), channel_id=1, source_target_pairs={{0,1},{1,2},{2,3},{3,4},{4,5},{5,6},{6,7},{7,8},{8,9},{9,10},{10,1... | collective-permute-start | bytes 2064392 | tf_op jit(solution)/shard_map/ppermute | solution.py:170
  120.3 11.9 %collective-permute-start.5 = (f32[96,1792]{1,0:T(8,128)S(1)}, f32[96,1792]{1,0:T(8,128)S(1)}, u32[]{:S(2)}, u32[]{:S(2)}) collective-permute-start(f32[96,1792]{1,0:T(8,128)S(1)} %get-tuple-element.30), channel_id=1, source_target_pairs={{1,0},{2,1},{3,2},{4,3},{5,4},{6,5},{7,6},{8,7},{9,8},{10,9},{11,1... | collective-permute-start | bytes 2064392 | tf_op jit(solution)/shard_map/ppermute | solution.py:171
  124.0 8.4 %slice-start = ((s8[12845056]{0:T(1024)(128)(4,1)}), s8[4194304]{0:T(1024)(128)(4,1)S(1)}, s32[]{:S(2)}) async-start(s8[12845056]{0:T(1024)(128)(4,1)} %bitcast.77), calls=%async_computation.3 | async-start | bytes 8388608
  124.0 8.4 %slice-start.1 = ((s8[12845056]{0:T(1024)(128)(4,1)}), s8[4194304]{0:T(1024)(128)(4,1)S(1)}, s32[]{:S(2)}) async-start(s8[12845056]{0:T(1024)(128)(4,1)} %bitcast.77), calls=%async_computation.4 | async-start | bytes 8388608
  124.0 8.4 %slice-start.2 = ((s8[12845056]{0:T(1024)(128)(4,1)}), s8[4194304]{0:T(1024)(128)(4,1)S(1)}, s32[]{:S(2)}) async-start(s8[12845056]{0:T(1024)(128)(4,1)} %bitcast.77), calls=%async_computation.5 | async-start | bytes 8388608
  125.8 6.6 %slice-start.3 = ((s8[12845056]{0:T(1024)(128)(4,1)}), s8[262144]{0:T(1024)(128)(4,1)S(1)}, s32[]{:S(2)}) async-start(s8[12845056]{0:T(1024)(128)(4,1)} %bitcast.77), calls=%async_computation.6 | async-start | bytes 524288
  140.0 35.7 %all-to-all-start.1 = ((bf16[32,6,1792]{2,1,0:T(8,128)(2,1)}), bf16[32,6,1792]{2,1,0:T(8,128)(2,1)}, u32[]{:S(2)}, u32[]{:S(2)}) async-start(bf16[32,6,1792]{2,1,0:T(8,128)(2,1)} %reshape.411), calls=%async_computation.1 | async-start | bytes 1835008 | tf_op jit(solution)/shard_map/all_to_all | solution.py:189
  (8 other events, 10.9 us)
Sparse Core Ops, SparseCore 0:
  10.4 85.4 all-gather.1

commit v14 on v12

--- a/solution.py
+++ b/solution.py
@@ -184,10 +184,7 @@
     back_slots = (
         jnp.zeros((groups * slot_count, features), jnp.bfloat16).at[pick_rows].set(grad_packed)
     )
-    back_slots = back_slots.reshape(groups, slot_count, features)
-    returned = lax.all_to_all(back_slots, "dp", split_axis=0, concat_axis=0, tiled=True).reshape(
-        groups * slot_count, features
-    )
+    returned = lax.all_to_all(back_slots, "dp", split_axis=0, concat_axis=0, tiled=True)
     patch_grad = jnp.take(returned, row_slot, axis=0, mode="fill", fill_value=0)
     return (layer_out[None], patch_grad[None])
 

time: 188 us -> 188 us (level)
    all_to_all x0 -> x2, local copies, waits for them, and re-layouts: none -> 2.54 us  [local(): lax.all_to_all(back_slots, 'dp', split_axis=0, concat_axis=0, tiled=True)]
    reshape x2 -> x0, local copies, waits for them, and re-layouts: 2.54 us -> none  [the longest x1 1.38 us: local(): lax.all_to_all(back_slots, 'dp', split_axis=0, concat_axis=0, tiled=True)]
where the time goes in v14:
time: 188 us; the launch traced here: 187 us
  waiting for transfers between devices  75 us (40%)
  starting transfers between devices  38.5 us (20%)
  matrix products  26.5 us (14%)
  local copies, waits for them, and re-layouts  18.7 us (10%)
  between operations  14.8 us (8%)
  other arithmetic  13.9 us (7%)
    all_gather x1, waiting for transfers between devices, gather_weights(): lax.all_gather(jnp.concatenate([qkv_weight, out_wide], axis=1), 'tensor',...  42 us
    all_to_all x1, waiting for transfers between devices, local(): lax.all_to_all(outgoing, 'dp', split_axis=0, concat_axis=0, tiled=True)  14.5 us
    all_to_all x1, waiting for transfers between devices, local(): lax.all_to_all(back_slots, 'dp', split_axis=0, concat_axis=0, tiled=True)  12.3 us
    all_to_all x1, starting transfers between devices, local(): lax.all_to_all(outgoing, 'dp', split_axis=0, concat_axis=0, tiled=True)  10.2 us
    all_to_all x1, starting transfers between devices, local(): lax.all_to_all(back_slots, 'dp', split_axis=0, concat_axis=0, tiled=True)  9.91 us
    ppermute x2, starting transfers between devices, extended(): lax.ppermute(lax.slice_in_dim(block, 0, width, axis=dim), axis, backward)  8.16 us
    dot_general x1, matrix products, local(): jnp.dot(normed, full_qkv, preferred_element_type=jnp.float32)  5.54 us
    dot_general x2, matrix products, times_out(): jnp.dot(spread(attended, side), out_pairs, preferred_element_type=jnp.flo...  5.19 us
  transfers between devices with their start and end apart: 9, of which 5 were waited for; matrix products, arithmetic and copies ran while one was open for 18% of the time, Pallas kernels for 0%

profile of v14, /device:TPU:66, one launch (start us, length us, event | category | flops | bytes accessed | tf_op | source)
XLA Modules:
  0.0 187.4 jit_solution(8856561315826569764)
XLA Ops:
  8.3 2.0 %pad_maximum_fusion.1 = bf16[112,3584]{1,0:T(8,128)(2,1)} fusion(bf16[112,896]{1,0:T(8,128)(2,1)S(1)} %reshape.400, bf16[112,2688]{1,0:T(8,128)(2,1)} %param.19), kind=kLoop, calls=%fused_computation.65 | loop fusion | flops 1605632 | bytes 1605632 | tf_op jit(solution)/shard_map/concatenate | solution.py:29
  13.1 10.2 %all-to-all-start = ((bf16[32,6,1792]{2,1,0:T(8,128)(2,1)}), bf16[32,6,1792]{2,1,0:T(8,128)(2,1)S(1)}, u32[]{:S(2)}, u32[]{:S(2)}) async-start(bf16[32,6,1792]{2,1,0:T(8,128)(2,1)} %reshape.398), calls=%async_computation | async-start | bytes 1835008 | tf_op jit(solution)/shard_map/all_to_all | solution.py:127
  23.4 1.9 %collective-permute-start = (s32[96]{0:T(128)S(1)}, s32[96]{0:T(128)S(1)}, u32[]{:S(2)}, u32[]{:S(2)}) collective-permute-start(s32[96]{0:T(128)S(1)} %get-tuple-element.41), channel_id=1, source_target_pairs={{0,1},{1,2},{2,3},{3,4},{4,5},{5,6},{6,7},{7,8},{8,9},{9,10},{10,1... | collective-permute-start | bytes 1160 | tf_op jit(solution)/shard_map/ppermute | solution.py:16
  25.3 3.6 %collective-permute-start.1 = (s32[96]{0:T(128)S(1)}, s32[96]{0:T(128)S(1)}, u32[]{:S(2)}, u32[]{:S(2)}) collective-permute-start(s32[96]{0:T(128)S(1)} %get-tuple-element.42), channel_id=1, source_target_pairs={{1,0},{2,1},{3,2},{4,3},{5,4},{6,5},{7,6},{8,7},{9,8},{10,9},{11,1... | collective-permute-start | bytes 1160 | tf_op jit(solution)/shard_map/ppermute | solution.py:19
  34.1 14.5 %all-to-all-done = bf16[32,6,1792]{2,1,0:T(8,128)(2,1)S(1)} async-done(((bf16[32,6,1792]{2,1,0:T(8,128)(2,1)}), bf16[32,6,1792]{2,1,0:T(8,128)(2,1)S(1)}, u32[]{:S(2)}, u32[]{:S(2)}) %all-to-all-start) | async-done | bytes 688160 | tf_op jit(solution)/shard_map/all_to_all | solution.py:127
  50.3 42.0 %all-gather.2.cloned.1.call-done = bf16[1792,3584]{1,0:T(8,128)(2,1)} async-done(((bf16[112,3584]{1,0:T(8,128)(2,1)}), bf16[1792,3584]{1,0:T(8,128)(2,1)}) %all-gather.2.cloned.1.call-update) | async-done | bytes 12845072 | tf_op jit(solution)/shard_map/all_gather | solution.py:28
  92.3 5.5 %fusion.9 = bf16[128,2688]{1,0:T(8,128)(2,1)S(1)} fusion(bf16[1792,3584]{1,0:T(8,128)(2,1)} %all-gather.2.cloned.1.call-done, f32[1792]{0:T(1024)S(1)} %copy-done.13, f32[128]{0:T(128)S(1)} %add_rsqrt_fusion, f32[128]{0:T(128)S(1)} %broadcast_multiply_fusion.2, bf16[128,1792]{1,0:T(8,128)(2,1)S(1)} %gather_fusion, pred[128]{0:T(512)(128)(4,1)S(1)} %compare_and_fusion.2), kind=kOutput, calls=%fused_computation.15 | convolution fusion | flops 1234845696 | bytes 10788992 | tf_op jit(solution)/shard_map/dot_general | solution.py:138
  98.8 2.3 %collective-permute-start.2 = (bf16[96,1792]{1,0:T(8,128)(2,1)}, bf16[96,1792]{1,0:T(8,128)(2,1)S(1)}, u32[]{:S(2)}, u32[]{:S(2)}) collective-permute-start(bf16[96,1792]{1,0:T(8,128)(2,1)} %get-tuple-element.35), channel_id=1, source_target_pairs={{0,1},{1,2},{2,3},{3,4},{4,5},{5,6},{6,7},{7,8},{8,9},{9,10},{10,1... | collective-permute-start | bytes 1032200 | tf_op jit(solution)/shard_map/ppermute | solution.py:16
  101.1 4.5 %collective-permute-start.3 = (bf16[96,1792]{1,0:T(8,128)(2,1)}, bf16[96,1792]{1,0:T(8,128)(2,1)S(1)}, u32[]{:S(2)}, u32[]{:S(2)}) collective-permute-start(bf16[96,1792]{1,0:T(8,128)(2,1)} %get-tuple-element.36), channel_id=1, source_target_pairs={{1,0},{2,1},{3,2},{4,3},{5,4},{6,5},{7,6},{8,7},{9,8},{10,9},{11,1... | collective-permute-start | bytes 1032200 | tf_op jit(solution)/shard_map/ppermute | solution.py:19
  106.7 1.9 %fusion.20 = f32[1792,128]{1,0:T(8,128)} fusion(bf16[1792,3584]{1,0:T(8,128)(2,1)S(1)} %copy-done.1, bf16[128,1792]{1,0:T(8,128)(2,1)S(1)} %bitcast.84), kind=kOutput, calls=%fused_computation.28 | convolution fusion | flops 411041792 | bytes 4358144 | tf_op jit(solution)/shard_map/dot_general | solution.py:55
  112.1 1.9 %fusion.17 = (bf16[1024,896]{1,0:T(8,128)(2,1)S(1)}, bf16[1024,896]{1,0:T(8,128)(2,1)S(1)}) fusion(s32[896]{0:T(1024)S(1)} %get-tuple-element.50, s32[896]{0:T(1024)S(1)} %get-tuple-element.51, s32[1024]{0:T(1024)S(1)} %get-tuple-element.52, s32[1024]{0:T(1024)S(1)} %get-tuple-element.53, pred[1024]{0:T(1024)(128)(4,1)} %fusion.93, ...), kind=kLoop, calls=%fused_computation.25 | loop fusion | flops 4587520 | bytes 4146048 | tf_op jit(solution)/shard_map/jit(_where)/select_n | solution.py:78
  118.7 2.1 %collective-permute-start.4 = (f32[96,1792]{1,0:T(8,128)S(1)}, f32[96,1792]{1,0:T(8,128)S(1)}, u32[]{:S(2)}, u32[]{:S(2)}) collective-permute-start(f32[96,1792]{1,0:T(8,128)S(1)} %get-tuple-element.29), channel_id=1, source_target_pairs={{0,1},{1,2},{2,3},{3,4},{4,5},{5,6},{6,7},{7,8},{8,9},{9,10},{10,1... | collective-permute-start | bytes 2064392 | tf_op jit(solution)/shard_map/ppermute | solution.py:169
  120.8 3.9 %collective-permute-start.5 = (f32[96,1792]{1,0:T(8,128)S(1)}, f32[96,1792]{1,0:T(8,128)S(1)}, u32[]{:S(2)}, u32[]{:S(2)}) collective-permute-start(f32[96,1792]{1,0:T(8,128)S(1)} %get-tuple-element.30), channel_id=1, source_target_pairs={{1,0},{2,1},{3,2},{4,3},{5,4},{6,5},{7,6},{8,7},{9,8},{10,9},{11,1... | collective-permute-start | bytes 2064392 | tf_op jit(solution)/shard_map/ppermute | solution.py:170
  124.7 1.8 fusion.38
  126.6 4.5 %collective-permute-done.4 = f32[96,1792]{1,0:T(8,128)S(1)} collective-permute-done((f32[96,1792]{1,0:T(8,128)S(1)}, f32[96,1792]{1,0:T(8,128)S(1)}, u32[]{:S(2)}, u32[]{:S(2)}) %collective-permute-start.4) | collective-permute-done | bytes 688160 | tf_op jit(solution)/shard_map/ppermute | solution.py:169
  131.2 1.7 collective-permute-done.5
  133.2 3.7 %fusion.104 = (f32[128]{0:T(128)S(1)}, f32[128]{0:T(128)S(1)}, f32[128,1792]{1,0:T(8,128)}) fusion(f32[128]{0:T(128)S(1)} %copy-done.12, f32[128]{0:T(128)S(1)} %broadcast_multiply_fusion.2, bf16[128,1792]{1,0:T(8,128)(2,1)S(1)} %gather_fusion, pred[128]{0:T(512)(128)(4,1)S(1)} %compare_and_fusion.2, f32[1792]{0:T(1024)S(1)} %copy-done.14, ...), kind=kOutput, calls=%fused_computation.149 | convolution fusion | flops 1236336384 | bytes 11708928 | tf_op jit(solution)/shard_map/dot_general | solution.py:174
  136.8 2.6 %scatter_custom_fusion = bf16[192,1792]{1,0:T(8,128)(2,1)S(1)} fusion(s32[128]{0:T(128)} %copy-done.10, f32[128,1792]{1,0:T(8,128)} %get-tuple-element.49, f32[128]{0:T(128)S(1)} %broadcast_multiply_fusion, f32[128]{0:T(128)S(1)} %broadcast_multiply_fusion.1, f32[128]{0:T(128)S(1)} %copy-done.12, f32[128]{0:T(128)S(1)} %broadcast_multiply_fusion.2, ...), kind=kCustom, calls=%fused_computation.82 | custom fusion | flops 2523136 | bytes 2525824 | tf_op jit(solution)/shard_map/scatter | solution.py:185
  140.6 9.9 %all-to-all-start.1 = ((bf16[32,6,1792]{2,1,0:T(8,128)(2,1)}), bf16[32,6,1792]{2,1,0:T(8,128)(2,1)}, u32[]{:S(2)}, u32[]{:S(2)}) async-start(bf16[32,6,1792]{2,1,0:T(8,128)(2,1)} %all_to_all.12), calls=%async_computation.1 | async-start | bytes 1835008 | tf_op jit(solution)/shard_map/all_to_all | solution.py:187
  150.6 3.8 %fusion.18 = f32[1024,896]{1,0:T(8,128)} fusion(s32[896]{0:T(1024)S(1)} %get-tuple-element.50, s32[896]{0:T(1024)S(1)} %get-tuple-element.51, s32[1024]{0:T(1024)S(1)} %get-tuple-element.52, s32[1024]{0:T(1024)S(1)} %get-tuple-element.53, pred[1024]{0:T(1024)(128)(4,1)S(1)} %copy-done.8, pred[896]{0:T(1024)(128)(4,1)S(1)} %fusion.92, ...), kind=kOutput, calls=%fused_computation.26 | convolution fusion | flops 591855616 | bytes 5579648 | tf_op jit(solution)/shard_map/dot_general | solution.py:109
  154.4 2.2 %reduce_sum.66 = bf16[128,896]{1,0:T(8,128)(2,1)S(1)} reduce(f32[8,128,896]{2,1,0:T(8,128)} %bitcast.75, f32[]{:T(128)} %constant.147.clone.1), dimensions={0}, to_apply=%region_4.6 | reduce | flops 802816 | bytes 3899396 | tf_op jit(solution)/shard_map/reduce_sum | solution.py:85
  158.5 2.6 %fusion.29 = f32[1,128,896]{2,1,0:T(8,128)S(1)} fusion(bf16[128,1792]{0,1:T(8,128)(2,1)S(1)} %bitcast.80, bf16[1792,3584]{1,0:T(8,128)(2,1)} %all-gather.2.cloned.1.call-done), kind=kOutput, calls=%fused_computation.41 | convolution fusion | flops 411041792 | bytes 4128768 | tf_op jit(solution)/shard_map/dot_general | solution.py:45
  161.1 2.6 %fusion.32 = f32[1,128,896]{2,1,0:T(8,128)S(1)} fusion(bf16[128,1792]{0,1:T(8,128)(2,1)S(1)} %bitcast.79, bf16[1792,3584]{1,0:T(8,128)(2,1)} %all-gather.2.cloned.1.call-done), kind=kOutput, calls=%fused_computation.42 | convolution fusion | flops 411041792 | bytes 4128768 | tf_op jit(solution)/shard_map/dot_general | solution.py:45
  164.7 12.3 %all-to-all-done.1 = bf16[32,6,1792]{2,1,0:T(8,128)(2,1)} async-done(((bf16[32,6,1792]{2,1,0:T(8,128)(2,1)}), bf16[32,6,1792]{2,1,0:T(8,128)(2,1)}, u32[]{:S(2)}, u32[]{:S(2)}) %all-to-all-start.1) | async-done | bytes 688160 | tf_op jit(solution)/shard_map/all_to_all | solution.py:187
  (124 shorter events, 28.4 us)
Async XLA Ops:
  7.2 85.1 %all-gather.2.cloned.1.call-start = ((), (), s32[]{:S(2)}) async-start(), calls=%async_computation.2 | async-start | bytes 13647872 | tf_op jit(solution)/shard_map/all_gather | solution.py:28
  11.9 11.4 %copy-start.15 = (s32[1,128]{1,0:T(1,128)S(1)}, s32[1,128]{1,0:T(1,128)}, u32[]{:S(2)}) copy-start(s32[1,128]{1,0:T(1,128)} %param.17) | copy-start | bytes 1540
  11.9 18.4 %copy-start.16 = (s32[1,128]{1,0:T(1,128)S(1)}, s32[1,128]{1,0:T(1,128)}, u32[]{:S(2)}) copy-start(s32[1,128]{1,0:T(1,128)} %param.16) | copy-start | bytes 1540
  13.1 35.5 %all-to-all-start = ((bf16[32,6,1792]{2,1,0:T(8,128)(2,1)}), bf16[32,6,1792]{2,1,0:T(8,128)(2,1)S(1)}, u32[]{:S(2)}, u32[]{:S(2)}) async-start(bf16[32,6,1792]{2,1,0:T(8,128)(2,1)} %reshape.398), calls=%async_computation | async-start | bytes 1835008 | tf_op jit(solution)/shard_map/all_to_all | solution.py:127
  23.4 10.5 %collective-permute-start = (s32[96]{0:T(128)S(1)}, s32[96]{0:T(128)S(1)}, u32[]{:S(2)}, u32[]{:S(2)}) collective-permute-start(s32[96]{0:T(128)S(1)} %get-tuple-element.41), channel_id=1, source_target_pairs={{0,1},{1,2},{2,3},{3,4},{4,5},{5,6},{6,7},{7,8},{8,9},{9,10},{10,1... | collective-permute-start | bytes 1160 | tf_op jit(solution)/shard_map/ppermute | solution.py:16
  25.3 8.6 %collective-permute-start.1 = (s32[96]{0:T(128)S(1)}, s32[96]{0:T(128)S(1)}, u32[]{:S(2)}, u32[]{:S(2)}) collective-permute-start(s32[96]{0:T(128)S(1)} %get-tuple-element.42), channel_id=1, source_target_pairs={{1,0},{2,1},{3,2},{4,3},{5,4},{6,5},{7,6},{8,7},{9,8},{10,9},{11,1... | collective-permute-start | bytes 1160 | tf_op jit(solution)/shard_map/ppermute | solution.py:19
  48.8 43.5 %copy-start.13 = (f32[1792]{0:T(1024)S(1)}, f32[1792]{0:T(1024)}, u32[]{:S(2)}) copy-start(f32[1792]{0:T(1024)} %param.18) | copy-start | bytes 21508
  50.3 47.6 %copy-start.11 = (f32[128]{0:T(128)}, f32[128]{0:T(128)S(1)}, u32[]{:S(2)}) copy-start(f32[128]{0:T(128)S(1)} %add_rsqrt_fusion) | copy-start | bytes 1540
  50.3 55.3 %copy-start.4 = (bf16[1,128,1792]{2,1,0:T(8,128)(2,1)S(1)}, bf16[1,128,1792]{2,1,0:T(8,128)(2,1)}, u32[]{:S(2)}) copy-start(bf16[1,128,1792]{2,1,0:T(8,128)(2,1)} %param.21) | copy-start | bytes 1376260
  92.3 13.3 %copy-start.1 = (bf16[1792,3584]{1,0:T(8,128)(2,1)S(1)}, bf16[1792,3584]{1,0:T(8,128)(2,1)}, u32[]{:S(2)}) copy-start(bf16[1792,3584]{1,0:T(8,128)(2,1)} %all-gather.2.cloned.1.call-done) | copy-start | bytes 38535172
  97.9 10.7 %copy-start.2 = (bf16[128,2688]{1,0:T(8,128)(2,1)}, bf16[128,2688]{1,0:T(8,128)(2,1)S(1)}, u32[]{:S(2)}) copy-start(bf16[128,2688]{1,0:T(8,128)(2,1)S(1)} %fusion.9) | copy-start | bytes 2064388
  98.8 15.2 %collective-permute-start.2 = (bf16[96,1792]{1,0:T(8,128)(2,1)}, bf16[96,1792]{1,0:T(8,128)(2,1)S(1)}, u32[]{:S(2)}, u32[]{:S(2)}) collective-permute-start(bf16[96,1792]{1,0:T(8,128)(2,1)} %get-tuple-element.35), channel_id=1, source_target_pairs={{0,1},{1,2},{2,3},{3,4},{4,5},{5,6},{6,7},{7,8},{8,9},{9,10},{10,1... | collective-permute-start | bytes 1032200 | tf_op jit(solution)/shard_map/ppermute | solution.py:16
  101.1 12.9 %collective-permute-start.3 = (bf16[96,1792]{1,0:T(8,128)(2,1)}, bf16[96,1792]{1,0:T(8,128)(2,1)S(1)}, u32[]{:S(2)}, u32[]{:S(2)}) collective-permute-start(bf16[96,1792]{1,0:T(8,128)(2,1)} %get-tuple-element.36), channel_id=1, source_target_pairs={{1,0},{2,1},{3,2},{4,3},{5,4},{6,5},{7,6},{8,7},{9,8},{10,9},{11,1... | collective-permute-start | bytes 1032200 | tf_op jit(solution)/shard_map/ppermute | solution.py:19
  118.6 6.1 %slice-start.6 = ((bf16[320,1792]{1,0:T(8,128)(2,1)}), bf16[320,896]{1,0:T(8,128)(2,1)S(1)}, s32[]{:S(2)}) async-start(bf16[320,1792]{1,0:T(8,128)(2,1)} %copy-done.3), calls=%async_computation.9 | async-start | bytes 1146880 | tf_op jit(solution)/shard_map/slice | solution.py:101
  118.6 6.1 %copy-start.5 = (s32[8,320]{0,1:T(8,128)S(1)}, s32[8,320]{0,1:T(8,128)}, u32[]{:S(2)}) copy-start(s32[8,320]{0,1:T(8,128)} %copy.28) | copy-start | bytes 30724
  118.6 6.1 %copy-start.6 = (s32[8,320]{0,1:T(8,128)S(1)}, s32[8,320]{0,1:T(8,128)}, u32[]{:S(2)}) copy-start(s32[8,320]{0,1:T(8,128)} %copy.29) | copy-start | bytes 30724
  118.7 12.4 %collective-permute-start.4 = (f32[96,1792]{1,0:T(8,128)S(1)}, f32[96,1792]{1,0:T(8,128)S(1)}, u32[]{:S(2)}, u32[]{:S(2)}) collective-permute-start(f32[96,1792]{1,0:T(8,128)S(1)} %get-tuple-element.29), channel_id=1, source_target_pairs={{0,1},{1,2},{2,3},{3,4},{4,5},{5,6},{6,7},{7,8},{8,9},{9,10},{10,1... | collective-permute-start | bytes 2064392 | tf_op jit(solution)/shard_map/ppermute | solution.py:169
  120.8 12.1 %collective-permute-start.5 = (f32[96,1792]{1,0:T(8,128)S(1)}, f32[96,1792]{1,0:T(8,128)S(1)}, u32[]{:S(2)}, u32[]{:S(2)}) collective-permute-start(f32[96,1792]{1,0:T(8,128)S(1)} %get-tuple-element.30), channel_id=1, source_target_pairs={{1,0},{2,1},{3,2},{4,3},{5,4},{6,5},{7,6},{8,7},{9,8},{10,9},{11,1... | collective-permute-start | bytes 2064392 | tf_op jit(solution)/shard_map/ppermute | solution.py:170
  124.7 8.4 %slice-start = ((s8[12845056]{0:T(1024)(128)(4,1)}), s8[4194304]{0:T(1024)(128)(4,1)S(1)}, s32[]{:S(2)}) async-start(s8[12845056]{0:T(1024)(128)(4,1)} %bitcast.76), calls=%async_computation.3 | async-start | bytes 8388608
  124.7 8.4 %slice-start.1 = ((s8[12845056]{0:T(1024)(128)(4,1)}), s8[4194304]{0:T(1024)(128)(4,1)S(1)}, s32[]{:S(2)}) async-start(s8[12845056]{0:T(1024)(128)(4,1)} %bitcast.76), calls=%async_computation.4 | async-start | bytes 8388608
  124.7 8.4 %slice-start.2 = ((s8[12845056]{0:T(1024)(128)(4,1)}), s8[4194304]{0:T(1024)(128)(4,1)S(1)}, s32[]{:S(2)}) async-start(s8[12845056]{0:T(1024)(128)(4,1)} %bitcast.76), calls=%async_computation.5 | async-start | bytes 8388608
  126.5 6.6 %slice-start.3 = ((s8[12845056]{0:T(1024)(128)(4,1)}), s8[262144]{0:T(1024)(128)(4,1)S(1)}, s32[]{:S(2)}) async-start(s8[12845056]{0:T(1024)(128)(4,1)} %bitcast.76), calls=%async_computation.6 | async-start | bytes 524288
  139.5 11.1 %copy-start.8 = (pred[1024]{0:T(1024)(128)(4,1)S(1)}, pred[1024]{0:T(1024)(128)(4,1)}, u32[]{:S(2)}) copy-start(pred[1024]{0:T(1024)(128)(4,1)} %fusion.93) | copy-start | bytes 3076
  140.6 36.4 %all-to-all-start.1 = ((bf16[32,6,1792]{2,1,0:T(8,128)(2,1)}), bf16[32,6,1792]{2,1,0:T(8,128)(2,1)}, u32[]{:S(2)}, u32[]{:S(2)}) async-start(bf16[32,6,1792]{2,1,0:T(8,128)(2,1)} %all_to_all.12), calls=%async_computation.1 | async-start | bytes 1835008 | tf_op jit(solution)/shard_map/all_to_all | solution.py:187
  (9 other events, 18.7 us)
Sparse Core Ops, SparseCore 0:
  10.5 81.8 all-gather.1

commit v15 on v12

--- a/solution.py
+++ b/solution.py
@@ -57,10 +57,11 @@
             out_pairs,
             (((1,), (1,)), ((), ())),
             preferred_element_type=jnp.float32,
-        ).reshape(rows, -1, 2)[:, :, side]
+        )
         for side in range(2)
     ]
-    return parts[0] + parts[1]
+    even = lax.broadcasted_iota(jnp.int32, parts[0].shape, 1) % 2 == 0
+    return jnp.where(even, parts[0], parts[1]).reshape(rows, -1, 2).sum(axis=2)
 
 
 def normalize(rows_in, norm_gain):

time: 188 us -> 186 us (0.989)
  other arithmetic: 13.9 us -> 19.1 us
  waiting for transfers between devices: 75 us -> 70.2 us
  local copies, waits for them, and re-layouts: 18.7 us -> 16.7 us
    all_to_all x1, waiting for transfers between devices: 14.5 us -> 9.75 us  [local(): lax.all_to_all(outgoing, 'dp', split_axis=0, concat_axis=0, tiled=True)]
    slice x2 -> x0, local copies, waits for them, and re-layouts: 1.97 us -> none  [times_out_t(): lax.dot_general(grad_rows[:, side * half:(side + 1) * half], out_pairs, (...]
  transfers between devices with their start and end apart: 9 -> 9, of which waited for: 5 -> 5; matrix products, arithmetic and copies ran while one was open for 18% -> 19% of each run, Pallas kernels for 0% -> 0%
where the time goes in v15:
time: 186 us; the launch traced here: 185 us
  waiting for transfers between devices  70.2 us (38%)
  starting transfers between devices  38.5 us (21%)
  matrix products  25.7 us (14%)
  other arithmetic  19.1 us (10%)
  local copies, waits for them, and re-layouts  16.7 us (9%)
  between operations  15 us (8%)
    all_gather x1, waiting for transfers between devices, gather_weights(): lax.all_gather(jnp.concatenate([qkv_weight, out_wide], axis=1), 'tensor',...  42 us
    all_to_all x1, waiting for transfers between devices, local(): lax.all_to_all(back_slots, 'dp', split_axis=0, concat_axis=0, tiled=True)  12.3 us
    all_to_all x1, starting transfers between devices, local(): lax.all_to_all(outgoing, 'dp', split_axis=0, concat_axis=0, tiled=True)  10.3 us
    all_to_all x1, starting transfers between devices, local(): lax.all_to_all(back_slots, 'dp', split_axis=0, concat_axis=0, tiled=True)  9.91 us
    all_to_all x1, waiting for transfers between devices, local(): lax.all_to_all(outgoing, 'dp', split_axis=0, concat_axis=0, tiled=True)  9.75 us
    ppermute x2, starting transfers between devices, extended(): lax.ppermute(lax.slice_in_dim(block, 0, width, axis=dim), axis, backward)  8.16 us
    dot_general x1, matrix products, local(): jnp.dot(normed, full_qkv, preferred_element_type=jnp.float32)  5.54 us
    dot_general x2, matrix products, times_out(): jnp.dot(spread(attended, side), out_pairs, preferred_element_type=jnp.flo...  5.18 us
  transfers between devices with their start and end apart: 9, of which 5 were waited for; matrix products, arithmetic and copies ran while one was open for 19% of the time, Pallas kernels for 0%

profile of v15, /device:TPU:66, one launch (start us, length us, event | category | flops | bytes accessed | tf_op | source)
XLA Modules:
  0.0 185.1 jit_solution(1266978088564810541)
XLA Ops:
  8.3 2.0 %pad_maximum_fusion.1 = bf16[112,3584]{1,0:T(8,128)(2,1)} fusion(bf16[112,896]{1,0:T(8,128)(2,1)S(1)} %reshape.392, bf16[112,2688]{1,0:T(8,128)(2,1)} %param.19), kind=kLoop, calls=%fused_computation.67 | loop fusion | flops 1605632 | bytes 1605632 | tf_op jit(solution)/shard_map/concatenate | solution.py:29
  13.1 10.3 %all-to-all-start = ((bf16[32,6,1792]{2,1,0:T(8,128)(2,1)}), bf16[32,6,1792]{2,1,0:T(8,128)(2,1)S(1)}, u32[]{:S(2)}, u32[]{:S(2)}) async-start(bf16[32,6,1792]{2,1,0:T(8,128)(2,1)} %reshape.390), calls=%async_computation | async-start | bytes 1835008 | tf_op jit(solution)/shard_map/all_to_all | solution.py:128
  23.4 1.9 %collective-permute-start = (s32[96]{0:T(128)S(1)}, s32[96]{0:T(128)S(1)}, u32[]{:S(2)}, u32[]{:S(2)}) collective-permute-start(s32[96]{0:T(128)S(1)} %get-tuple-element.41), channel_id=1, source_target_pairs={{0,1},{1,2},{2,3},{3,4},{4,5},{5,6},{6,7},{7,8},{8,9},{9,10},{10,1... | collective-permute-start | bytes 1160 | tf_op jit(solution)/shard_map/ppermute | solution.py:16
  25.3 3.6 %collective-permute-start.1 = (s32[96]{0:T(128)S(1)}, s32[96]{0:T(128)S(1)}, u32[]{:S(2)}, u32[]{:S(2)}) collective-permute-start(s32[96]{0:T(128)S(1)} %get-tuple-element.42), channel_id=1, source_target_pairs={{1,0},{2,1},{3,2},{4,3},{5,4},{6,5},{7,6},{8,7},{9,8},{10,9},{11,1... | collective-permute-start | bytes 1160 | tf_op jit(solution)/shard_map/ppermute | solution.py:19
  38.8 9.7 %all-to-all-done = bf16[32,6,1792]{2,1,0:T(8,128)(2,1)S(1)} async-done(((bf16[32,6,1792]{2,1,0:T(8,128)(2,1)}), bf16[32,6,1792]{2,1,0:T(8,128)(2,1)S(1)}, u32[]{:S(2)}, u32[]{:S(2)}) %all-to-all-start) | async-done | bytes 688160 | tf_op jit(solution)/shard_map/all_to_all | solution.py:128
  50.3 42.0 %all-gather.2.cloned.1.call-done = bf16[1792,3584]{1,0:T(8,128)(2,1)} async-done(((bf16[112,3584]{1,0:T(8,128)(2,1)}), bf16[1792,3584]{1,0:T(8,128)(2,1)}) %all-gather.2.cloned.1.call-update) | async-done | bytes 12845072 | tf_op jit(solution)/shard_map/all_gather | solution.py:28
  92.3 5.5 %fusion.9 = bf16[128,2688]{1,0:T(8,128)(2,1)S(1)} fusion(bf16[1792,3584]{1,0:T(8,128)(2,1)} %all-gather.2.cloned.1.call-done, f32[1792]{0:T(1024)S(1)} %copy-done.27, f32[128]{0:T(128)S(1)} %add_rsqrt_fusion, f32[128]{0:T(128)S(1)} %broadcast_multiply_fusion.2, bf16[128,1792]{1,0:T(8,128)(2,1)S(1)} %gather_fusion, pred[128]{0:T(512)(128)(4,1)S(1)} %compare_and_fusion.2), kind=kOutput, calls=%fused_computation.15 | convolution fusion | flops 1234845696 | bytes 10788992 | tf_op jit(solution)/shard_map/dot_general | solution.py:139
  98.7 2.3 %collective-permute-start.2 = (bf16[96,1792]{1,0:T(8,128)(2,1)}, bf16[96,1792]{1,0:T(8,128)(2,1)S(1)}, u32[]{:S(2)}, u32[]{:S(2)}) collective-permute-start(bf16[96,1792]{1,0:T(8,128)(2,1)} %get-tuple-element.35), channel_id=1, source_target_pairs={{0,1},{1,2},{2,3},{3,4},{4,5},{5,6},{6,7},{7,8},{8,9},{9,10},{10,1... | collective-permute-start | bytes 1032200 | tf_op jit(solution)/shard_map/ppermute | solution.py:16
  101.0 4.5 %collective-permute-start.3 = (bf16[96,1792]{1,0:T(8,128)(2,1)S(1)}, bf16[96,1792]{1,0:T(8,128)(2,1)S(1)}, u32[]{:S(2)}, u32[]{:S(2)}) collective-permute-start(bf16[96,1792]{1,0:T(8,128)(2,1)S(1)} %get-tuple-element.36), channel_id=1, source_target_pairs={{1,0},{2,1},{3,2},{4,3},{5,4},{6,5},{7,6},{8,7},{9,8},{10,9},{11,1... | collective-permute-start | bytes 1032200 | tf_op jit(solution)/shard_map/ppermute | solution.py:19
  109.1 1.8 fusion.18
  116.3 2.1 %collective-permute-start.4 = (f32[96,1792]{1,0:T(8,128)S(1)}, f32[96,1792]{1,0:T(8,128)S(1)}, u32[]{:S(2)}, u32[]{:S(2)}) collective-permute-start(f32[96,1792]{1,0:T(8,128)S(1)} %get-tuple-element.29), channel_id=1, source_target_pairs={{0,1},{1,2},{2,3},{3,4},{4,5},{5,6},{6,7},{7,8},{8,9},{9,10},{10,1... | collective-permute-start | bytes 2064392 | tf_op jit(solution)/shard_map/ppermute | solution.py:170
  118.3 3.9 %collective-permute-start.5 = (f32[96,1792]{1,0:T(8,128)S(1)}, f32[96,1792]{1,0:T(8,128)S(1)}, u32[]{:S(2)}, u32[]{:S(2)}) collective-permute-start(f32[96,1792]{1,0:T(8,128)S(1)} %get-tuple-element.30), channel_id=1, source_target_pairs={{1,0},{2,1},{3,2},{4,3},{5,4},{6,5},{7,6},{8,7},{9,8},{10,9},{11,1... | collective-permute-start | bytes 2064392 | tf_op jit(solution)/shard_map/ppermute | solution.py:171
  122.3 1.8 fusion.37
  124.2 4.5 %collective-permute-done.4 = f32[96,1792]{1,0:T(8,128)S(1)} collective-permute-done((f32[96,1792]{1,0:T(8,128)S(1)}, f32[96,1792]{1,0:T(8,128)S(1)}, u32[]{:S(2)}, u32[]{:S(2)}) %collective-permute-start.4) | collective-permute-done | bytes 688160 | tf_op jit(solution)/shard_map/ppermute | solution.py:170
  128.8 1.6 collective-permute-done.5
  130.7 3.7 %fusion.106 = (f32[128]{0:T(128)S(1)}, f32[128]{0:T(128)S(1)}, f32[128,1792]{1,0:T(8,128)}) fusion(f32[128]{0:T(128)S(1)} %copy-done.26, f32[128]{0:T(128)S(1)} %copy-done.20, bf16[128,1792]{1,0:T(8,128)(2,1)S(1)} %gather_fusion, pred[128]{0:T(512)(128)(4,1)S(1)} %copy-done.16, f32[1792]{0:T(1024)S(1)} %copy-done.28, bf16[1792,3584]{1,0:T(8,128)(2,1)S(1)} %bitcast.76, ...), kind=kOutput, calls=%fused_computation.154 | convolution fusion | flops 1236336384 | bytes 11708928 | tf_op jit(solution)/shard_map/dot_general | solution.py:175
  134.4 2.6 %scatter_custom_fusion = bf16[192,1792]{1,0:T(8,128)(2,1)S(1)} fusion(s32[128]{0:T(128)} %copy-done.24, f32[128,1792]{1,0:T(8,128)} %get-tuple-element.49, f32[128]{0:T(128)S(1)} %broadcast_multiply_fusion, f32[128]{0:T(128)S(1)} %broadcast_multiply_fusion.1, f32[128]{0:T(128)S(1)} %copy-done.26, f32[128]{0:T(128)S(1)} %copy-done.20, ...), kind=kCustom, calls=%fused_computation.84 | custom fusion | flops 2523136 | bytes 2525824 | tf_op jit(solution)/shard_map/scatter | solution.py:186
  138.2 9.9 %all-to-all-start.1 = ((bf16[32,6,1792]{2,1,0:T(8,128)(2,1)}), bf16[32,6,1792]{2,1,0:T(8,128)(2,1)}, u32[]{:S(2)}, u32[]{:S(2)}) async-start(bf16[32,6,1792]{2,1,0:T(8,128)(2,1)} %reshape.398), calls=%async_computation.1 | async-start | bytes 1835008 | tf_op jit(solution)/shard_map/all_to_all | solution.py:189
  148.2 3.8 %fusion.19 = f32[1024,896]{1,0:T(8,128)} fusion(s32[896]{0:T(1024)S(1)} %copy-done.9, s32[896]{0:T(1024)S(1)} %copy-done.10, s32[1024]{0:T(1024)S(1)} %copy-done.11, s32[1024]{0:T(1024)S(1)} %copy-done.12, pred[1024]{0:T(1024)(128)(4,1)S(1)} %copy-done.22, pred[896]{0:T(1024)(128)(4,1)S(1)} %copy-done.21, bf16[320,1792]{1,0:T(8,128)(2,1)} %copy-done.3, ...), kind=kOutput, calls=%fused_computation.29 | convolution fusion | flops 591855616 | bytes 5579648 | tf_op jit(solution)/shard_map/dot_general | solution.py:110
  152.0 2.2 %reduce_sum.75 = bf16[128,896]{1,0:T(8,128)(2,1)S(1)} reduce(f32[8,128,896]{2,1,0:T(8,128)} %bitcast.74, f32[]{:T(128)} %constant.161.clone.1), dimensions={0}, to_apply=%region_4.6 | reduce | flops 802816 | bytes 3899396 | tf_op jit(solution)/shard_map/reduce_sum | solution.py:86
  156.2 2.6 %fusion.28 = f32[1,128,896]{2,1,0:T(8,128)S(1)} fusion(bf16[128,1792]{0,1:T(8,128)(2,1)S(1)} %bitcast.79, bf16[1792,3584]{1,0:T(8,128)(2,1)} %all-gather.2.cloned.1.call-done), kind=kOutput, calls=%fused_computation.42 | convolution fusion | flops 411041792 | bytes 4128768 | tf_op jit(solution)/shard_map/dot_general | solution.py:45
  158.8 2.6 %fusion.31 = f32[1,128,896]{2,1,0:T(8,128)S(1)} fusion(bf16[128,1792]{0,1:T(8,128)(2,1)S(1)} %bitcast.78, bf16[1792,3584]{1,0:T(8,128)(2,1)} %all-gather.2.cloned.1.call-done), kind=kOutput, calls=%fused_computation.43 | convolution fusion | flops 411041792 | bytes 4128768 | tf_op jit(solution)/shard_map/dot_general | solution.py:45
  162.3 12.3 %all-to-all-done.1 = bf16[32,6,1792]{2,1,0:T(8,128)(2,1)} async-done(((bf16[32,6,1792]{2,1,0:T(8,128)(2,1)}), bf16[32,6,1792]{2,1,0:T(8,128)(2,1)}, u32[]{:S(2)}, u32[]{:S(2)}) %all-to-all-start.1) | async-done | bytes 688160 | tf_op jit(solution)/shard_map/all_to_all | solution.py:189
  174.6 1.4 reshape.399
  (151 shorter events, 31.5 us)
Async XLA Ops:
  7.2 85.1 %all-gather.2.cloned.1.call-start = ((), (), s32[]{:S(2)}) async-start(), calls=%async_computation.2 | async-start | bytes 13647872 | tf_op jit(solution)/shard_map/all_gather | solution.py:28
  11.9 11.4 %copy-start.29 = (s32[1,128]{1,0:T(1,128)S(1)}, s32[1,128]{1,0:T(1,128)}, u32[]{:S(2)}) copy-start(s32[1,128]{1,0:T(1,128)} %param.17) | copy-start | bytes 1540
  11.9 19.0 %copy-start.30 = (s32[1,128]{1,0:T(1,128)S(1)}, s32[1,128]{1,0:T(1,128)}, u32[]{:S(2)}) copy-start(s32[1,128]{1,0:T(1,128)} %param.16) | copy-start | bytes 1540
  13.1 35.5 %all-to-all-start = ((bf16[32,6,1792]{2,1,0:T(8,128)(2,1)}), bf16[32,6,1792]{2,1,0:T(8,128)(2,1)S(1)}, u32[]{:S(2)}, u32[]{:S(2)}) async-start(bf16[32,6,1792]{2,1,0:T(8,128)(2,1)} %reshape.390), calls=%async_computation | async-start | bytes 1835008 | tf_op jit(solution)/shard_map/all_to_all | solution.py:128
  23.4 14.6 %collective-permute-start = (s32[96]{0:T(128)S(1)}, s32[96]{0:T(128)S(1)}, u32[]{:S(2)}, u32[]{:S(2)}) collective-permute-start(s32[96]{0:T(128)S(1)} %get-tuple-element.41), channel_id=1, source_target_pairs={{0,1},{1,2},{2,3},{3,4},{4,5},{5,6},{6,7},{7,8},{8,9},{9,10},{10,1... | collective-permute-start | bytes 1160 | tf_op jit(solution)/shard_map/ppermute | solution.py:16
  25.3 12.7 %collective-permute-start.1 = (s32[96]{0:T(128)S(1)}, s32[96]{0:T(128)S(1)}, u32[]{:S(2)}, u32[]{:S(2)}) collective-permute-start(s32[96]{0:T(128)S(1)} %get-tuple-element.42), channel_id=1, source_target_pairs={{1,0},{2,1},{3,2},{4,3},{5,4},{6,5},{7,6},{8,7},{9,8},{10,9},{11,1... | collective-permute-start | bytes 1160 | tf_op jit(solution)/shard_map/ppermute | solution.py:19
  34.6 57.7 %copy-start.15 = (pred[128]{0:T(512)(128)(4,1)}, pred[128]{0:T(512)(128)(4,1)S(1)}, u32[]{:S(2)}) copy-start(pred[128]{0:T(512)(128)(4,1)S(1)} %compare_and_fusion.2) | copy-start | bytes 388
  48.8 43.5 %copy-start.27 = (f32[1792]{0:T(1024)S(1)}, f32[1792]{0:T(1024)}, u32[]{:S(2)}) copy-start(f32[1792]{0:T(1024)} %param.18) | copy-start | bytes 21508
  50.0 47.9 %copy-start.19 = (f32[128]{0:T(128)}, f32[128]{0:T(128)S(1)}, u32[]{:S(2)}) copy-start(f32[128]{0:T(128)S(1)} %broadcast_multiply_fusion.2) | copy-start | bytes 1540
  50.3 47.6 %copy-start.25 = (f32[128]{0:T(128)}, f32[128]{0:T(128)S(1)}, u32[]{:S(2)}) copy-start(f32[128]{0:T(128)S(1)} %add_rsqrt_fusion) | copy-start | bytes 1540
  92.3 13.2 %copy-start.1 = (bf16[1792,3584]{1,0:T(8,128)(2,1)S(1)}, bf16[1792,3584]{1,0:T(8,128)(2,1)}, u32[]{:S(2)}) copy-start(bf16[1792,3584]{1,0:T(8,128)(2,1)} %all-gather.2.cloned.1.call-done) | copy-start | bytes 38535172
  97.9 8.7 %copy-start.2 = (bf16[128,2688]{1,0:T(8,128)(2,1)}, bf16[128,2688]{1,0:T(8,128)(2,1)S(1)}, u32[]{:S(2)}) copy-start(bf16[128,2688]{1,0:T(8,128)(2,1)S(1)} %fusion.9) | copy-start | bytes 2064388
  97.9 7.6 %copy-start.4 = (bf16[1,128,1792]{2,1,0:T(8,128)(2,1)S(1)}, bf16[1,128,1792]{2,1,0:T(8,128)(2,1)}, u32[]{:S(2)}) copy-start(bf16[1,128,1792]{2,1,0:T(8,128)(2,1)} %param.21) | copy-start | bytes 1376260
  98.7 12.2 %collective-permute-start.2 = (bf16[96,1792]{1,0:T(8,128)(2,1)}, bf16[96,1792]{1,0:T(8,128)(2,1)S(1)}, u32[]{:S(2)}, u32[]{:S(2)}) collective-permute-start(bf16[96,1792]{1,0:T(8,128)(2,1)} %get-tuple-element.35), channel_id=1, source_target_pairs={{0,1},{1,2},{2,3},{3,4},{4,5},{5,6},{6,7},{7,8},{8,9},{9,10},{10,1... | collective-permute-start | bytes 1032200 | tf_op jit(solution)/shard_map/ppermute | solution.py:16
  101.0 9.9 %collective-permute-start.3 = (bf16[96,1792]{1,0:T(8,128)(2,1)S(1)}, bf16[96,1792]{1,0:T(8,128)(2,1)S(1)}, u32[]{:S(2)}, u32[]{:S(2)}) collective-permute-start(bf16[96,1792]{1,0:T(8,128)(2,1)S(1)} %get-tuple-element.36), channel_id=1, source_target_pairs={{1,0},{2,1},{3,2},{4,3},{5,4},{6,5},{7,6},{8,7},{9,8},{10,9},{11,1... | collective-permute-start | bytes 1032200 | tf_op jit(solution)/shard_map/ppermute | solution.py:19
  116.3 12.4 %collective-permute-start.4 = (f32[96,1792]{1,0:T(8,128)S(1)}, f32[96,1792]{1,0:T(8,128)S(1)}, u32[]{:S(2)}, u32[]{:S(2)}) collective-permute-start(f32[96,1792]{1,0:T(8,128)S(1)} %get-tuple-element.29), channel_id=1, source_target_pairs={{0,1},{1,2},{2,3},{3,4},{4,5},{5,6},{6,7},{7,8},{8,9},{9,10},{10,1... | collective-permute-start | bytes 2064392 | tf_op jit(solution)/shard_map/ppermute | solution.py:170
  118.3 12.1 %collective-permute-start.5 = (f32[96,1792]{1,0:T(8,128)S(1)}, f32[96,1792]{1,0:T(8,128)S(1)}, u32[]{:S(2)}, u32[]{:S(2)}) collective-permute-start(f32[96,1792]{1,0:T(8,128)S(1)} %get-tuple-element.30), channel_id=1, source_target_pairs={{1,0},{2,1},{3,2},{4,3},{5,4},{6,5},{7,6},{8,7},{9,8},{10,9},{11,1... | collective-permute-start | bytes 2064392 | tf_op jit(solution)/shard_map/ppermute | solution.py:171
  122.3 8.3 %slice-start = ((s8[12845056]{0:T(1024)(128)(4,1)}), s8[4194304]{0:T(1024)(128)(4,1)S(1)}, s32[]{:S(2)}) async-start(s8[12845056]{0:T(1024)(128)(4,1)} %bitcast.75), calls=%async_computation.3 | async-start | bytes 8388608
  122.3 8.3 %slice-start.1 = ((s8[12845056]{0:T(1024)(128)(4,1)}), s8[4194304]{0:T(1024)(128)(4,1)S(1)}, s32[]{:S(2)}) async-start(s8[12845056]{0:T(1024)(128)(4,1)} %bitcast.75), calls=%async_computation.4 | async-start | bytes 8388608
  122.3 8.3 %slice-start.2 = ((s8[12845056]{0:T(1024)(128)(4,1)}), s8[4194304]{0:T(1024)(128)(4,1)S(1)}, s32[]{:S(2)}) async-start(s8[12845056]{0:T(1024)(128)(4,1)} %bitcast.75), calls=%async_computation.5 | async-start | bytes 8388608
  137.1 11.1 %copy-start.11 = (s32[1024]{0:T(1024)S(1)}, s32[1024]{0:T(1024)}, u32[]{:S(2)}) copy-start(s32[1024]{0:T(1024)} %get-tuple-element.54) | copy-start | bytes 12292
  137.1 11.1 %copy-start.12 = (s32[1024]{0:T(1024)S(1)}, s32[1024]{0:T(1024)}, u32[]{:S(2)}) copy-start(s32[1024]{0:T(1024)} %get-tuple-element.55) | copy-start | bytes 12292
  137.1 11.1 %copy-start.22 = (pred[1024]{0:T(1024)(128)(4,1)S(1)}, pred[1024]{0:T(1024)(128)(4,1)}, u32[]{:S(2)}) copy-start(pred[1024]{0:T(1024)(128)(4,1)} %fusion.95) | copy-start | bytes 3076
  138.2 36.4 %all-to-all-start.1 = ((bf16[32,6,1792]{2,1,0:T(8,128)(2,1)}), bf16[32,6,1792]{2,1,0:T(8,128)(2,1)}, u32[]{:S(2)}, u32[]{:S(2)}) async-start(bf16[32,6,1792]{2,1,0:T(8,128)(2,1)} %reshape.398), calls=%async_computation.1 | async-start | bytes 1835008 | tf_op jit(solution)/shard_map/all_to_all | solution.py:189
  (23 other events, 75.7 us)
Sparse Core Ops, SparseCore 0:
  10.5 81.8 all-gather.1
